TPU v7x, 32 devices: a whole 2x2x4 slice. The times are simulated.
32 devices in a mesh: ctx: 4 (over z), pipe: 8 (over y, x, core).
Axes of the slice: x: 2, y: 2, z: 4, core: 2. Of those that a mesh axis runs over, the one named last changes fastest.
Arguments:
- qkv_in: bfloat16 [8, 512, 3, 256], P('pipe', 'ctx'), may hold values from -6 to 6
- qkv_saved: bfloat16 [8, 512, 3, 256], P('pipe', 'ctx'), may hold values from -6 to 6
- conv_saved: float32 [8, 512, 256], P('pipe', 'ctx'), may hold values from -6 to 6
- out_grad: bfloat16 [8, 512, 256], P('pipe', 'ctx'), may hold values from -6 to 6
- filters: float32 [8, 16, 512], P('pipe', None, 'ctx'), may hold values from -32768 to 32768
Outputs:
- next_input: bfloat16 [8, 512, 256], P('pipe', 'ctx')
- prev_grad: bfloat16 [8, 512, 3, 256], P('pipe', 'ctx')
- filter_grad: float32 [8, 16, 512], P('pipe', None, 'ctx')
All inputs are finite; a program needn't handle non-finite values.
Results may differ from a plain program's by a relative error of at most 0.001.
Values may be sent and summed in bfloat16 or wider, within the bound.
No kernel may reach another device: no remote copies, remote signals or barrier semaphores. Data moves between devices by JAX's collectives and lax.ppermute only.
A program may use at most 64 MiB of HBM per device.

v0:
```python
import math

import jax
import jax.numpy as jnp
from jax import lax
from jax.sharding import PartitionSpec as P

CPF = 16
N1 = 128


highest = lax.Precision.HIGHEST


def from_behind(x, axis, by):
    devices = lax.axis_size(axis)
    pairs = [(i, i + by) for i in range(devices) if 0 <= i + by < devices]
    return lax.ppermute(x, axis, pairs)


def angles(first_ids, second_ids, period):
    product = first_ids[:, None] * second_ids[None, :] % period
    return product.astype(jnp.float32) * (2.0 * math.pi / period)


def turn_table(theta_grid, direction):
    cosine = jnp.cos(theta_grid)
    sine_part = direction * jnp.sin(theta_grid)
    real_row = jnp.stack([cosine, sine_part], axis=-1)
    imag_row = jnp.stack([-sine_part, cosine], axis=-1)
    return jnp.stack([real_row, imag_row], axis=1)


def rotate(values, theta_grid, direction):
    cosine = jnp.cos(theta_grid)[:, :, None]
    sine_part = direction * jnp.sin(theta_grid)[:, :, None]
    real_part = values[:, :, 0]
    imag_part = values[:, :, 1]
    return jnp.stack(
        [real_part * cosine - imag_part * sine_part, real_part * sine_part + imag_part * cosine],
        axis=2,
    )


def spectral_product(left_side, right_side, direction):
    left_re = left_side[..., 0, :]
    left_im = left_side[..., 1, :]
    right_re = right_side[..., 0, :]
    right_im = direction * right_side[..., 1, :]
    return jnp.stack(
        [left_re * right_re - left_im * right_im, left_re * right_im + left_im * right_re], axis=-2
    )


def split_time(blocks):
    return lax.all_to_all(blocks, "ctx", split_axis=1, concat_axis=0, tiled=True)


def split_freq(blocks):
    return lax.all_to_all(blocks, "ctx", split_axis=0, concat_axis=1, tiled=True)


def spectrum(signal_in, tables):
    outer_fwd, twist_angles, inner_fwd, inner_inv, outer_inv = tables
    length, parts_in, channels = signal_in.shape
    blocks = signal_in.reshape(length // N1, N1, parts_in, channels)
    regrouped = split_time(blocks)
    partial_sums = jnp.einsum(
        "tbpc,tpkq->kbqc", regrouped, outer_fwd[:, :parts_in], precision=highest
    )
    twisted = rotate(partial_sums, twist_angles, -1.0)
    columns = split_freq(twisted)
    return jnp.einsum("atpc,tpkq->akqc", columns, inner_fwd, precision=highest)


def signal(spectrum_input, parts_out, tables):
    outer_fwd, twist_angles, inner_fwd, inner_inv, outer_inv = tables
    rows_back = jnp.einsum("akpc,kptq->atqc", spectrum_input, inner_inv, precision=highest)
    regrouped = split_time(rows_back)
    twisted = rotate(regrouped, twist_angles, 1.0)
    positions = jnp.einsum(
        "kbpc,kptq->tbqc", twisted, outer_inv[..., :parts_out], precision=highest
    )
    blocks = split_freq(positions)
    return blocks.reshape(-1, parts_out, blocks.shape[-1])


def per_channel(group_spec, copies):
    leading = group_spec.shape[:-1]
    widened = jnp.broadcast_to(group_spec[..., None], leading + (group_spec.shape[-1], copies))
    return widened.reshape(leading + (group_spec.shape[-1] * copies,))


def on_device(qkv_in, qkv_saved, conv_saved, out_grad, filters):
    ctx_count = lax.axis_size("ctx")
    ctx_place = lax.axis_index("ctx")
    length = qkv_in.shape[1]
    groups = filters.shape[1]
    outer_rows = length // N1 * ctx_count
    outer_freqs = 2 * outer_rows
    full_size = N1 * outer_freqs
    local_cols = N1 // ctx_count
    spec_rows = 2 * (length // N1)
    filter_scale = (CPF * length * ctx_count) ** (-0.5)
    inner_ids = jnp.arange(N1, dtype=jnp.int32)
    row_ids = jnp.arange(outer_rows, dtype=jnp.int32)
    freq_ids = jnp.arange(outer_freqs, dtype=jnp.int32)
    col_ids = ctx_place * local_cols + jnp.arange(local_cols, dtype=jnp.int32)
    inner_grid = angles(inner_ids, inner_ids, N1)
    tables = (
        turn_table(angles(row_ids, freq_ids, outer_freqs), -1.0),
        angles(freq_ids, col_ids, full_size),
        turn_table(inner_grid, -1.0),
        turn_table(inner_grid, 1.0),
        turn_table(angles(freq_ids, row_ids, outer_freqs), 1.0) / full_size,
    )
    query_in = qkv_in[0, :, 0].astype(jnp.float32)
    key_in = qkv_in[0, :, 1].astype(jnp.float32)
    value_in = qkv_in[0, :, 2].astype(jnp.float32)
    mixed_in = key_in * value_in
    channels = mixed_in.shape[1]
    first_cols = jnp.concatenate([mixed_in, (filters[0] * filter_scale).T], axis=1)
    group_spectra = spectrum(first_cols[:, None, channels:], tables)
    mixed_spec = spectrum(mixed_in[:, None, :], tables)
    filter_chan = per_channel(group_spectra, CPF)
    query_back = qkv_saved[0, :, 0].astype(jnp.float32)
    key_back = qkv_saved[0, :, 1].astype(jnp.float32)
    value_back = qkv_saved[0, :, 2].astype(jnp.float32)
    mixed_back = key_back * value_back
    upstream = out_grad[0].astype(jnp.float32)
    weighted = upstream * query_back
    grad_query = upstream * conv_saved[0]
    both_spectra = spectrum(jnp.concatenate([mixed_back, weighted], axis=1)[:, None, :], tables)
    back_spec = both_spectra[..., :channels]
    weighted_spec = both_spectra[..., channels:]
    corr_spec = spectral_product(weighted_spec, filter_chan, -1.0)
    conv_out = signal(spectral_product(mixed_spec, filter_chan, 1.0), 1, tables)[:, 0, :]
    grad_mixed = signal(corr_spec, 1, tables)[:, 0, :]
    result = (query_in * conv_out).astype(jnp.bfloat16)
    next_input = from_behind(result[None], "pipe", 1)
    grad_key = grad_mixed * value_back
    grad_value = grad_mixed * key_back
    grad_stack = jnp.stack([grad_query, grad_key, grad_value], axis=1).astype(jnp.bfloat16)
    prev_grad = from_behind(grad_stack[None], "pipe", -1)
    cross_spec = spectral_product(weighted_spec, back_spec, -1.0)
    groups_spec = cross_spec.reshape(spec_rows, N1, 2, groups, CPF).sum(axis=-1)
    filter_rows = signal(groups_spec, 1, tables)[:, 0, :] * filter_scale
    filter_grad = filter_rows.T[None]
    return (next_input, prev_grad, filter_grad)


def solution(mesh):
    return jax.shard_map(
        on_device,
        mesh=mesh,
        in_specs=(
            P("pipe", "ctx", None, None),
            P("pipe", "ctx", None, None),
            P("pipe", "ctx", None),
            P("pipe", "ctx", None),
            P("pipe", None, "ctx"),
        ),
        out_specs=(P("pipe", "ctx", None), P("pipe", "ctx", None, None), P("pipe", None, "ctx")),
        check_vma=False,
    )
```

profile of v0, /device:TPU:1, one launch (start us, length us, event | category | flops | bytes accessed | tf_op | source)
XLA Modules:
  0.0 155.6 jit_solution(8360810687614214105)
XLA Ops:
  0.6 0.8 copy.103
  1.5 0.5 broadcast.551
  1.9 0.7 reduce
  2.6 0.7 reshape.538
  3.3 5.4 %all-to-all-start.2 = ((f32[4,1,512]{2,1,0:T(1,128)}), f32[4,1,512]{2,1,0:T(1,128)S(1)}, u32[]{:S(2)}, u32[]{:S(2)}) async-start(f32[4,1,512]{2,1,0:T(1,128)} %reshape.538), calls=%async_computation.2 | async-start | bytes 16384 | tf_op jit(solution)/shard_map/all_to_all | solution.py:56
  8.8 0.8 copy-done.1
  9.8 0.7 copy-done.2
  10.5 0.8 fusion.27
  11.5 1.7 %all-to-all-done.2 = f32[4,1,512]{2,1,0:T(1,128)S(1)} async-done(((f32[4,1,512]{2,1,0:T(1,128)}), f32[4,1,512]{2,1,0:T(1,128)S(1)}, u32[]{:S(2)}, u32[]{:S(2)}) %all-to-all-start.2) | async-done | bytes 8224 | tf_op jit(solution)/shard_map/all_to_all | solution.py:56
  13.2 3.3 %all-to-all-start = ((f32[1,128,1,256]{3,2,0,1:T(1,128)}), f32[1,128,1,256]{3,2,0,1:T(1,128)S(1)}, u32[]{:S(2)}, u32[]{:S(2)}) async-start(f32[1,128,1,256]{3,2,0,1:T(1,128)} %fusion.27), calls=%async_computation | async-start | bytes 262144 | tf_op jit(solution)/shard_map/all_to_all | solution.py:56
  16.5 0.6 reduce.1
  17.4 0.3 convolution_bitcast_fusion.8
  17.8 0.7 reshape.540
  18.5 2.8 %all-to-all-done = f32[1,128,1,256]{3,2,0,1:T(1,128)S(1)} async-done(((f32[1,128,1,256]{3,2,0,1:T(1,128)}), f32[1,128,1,256]{3,2,0,1:T(1,128)S(1)}, u32[]{:S(2)}, u32[]{:S(2)}) %all-to-all-start) | async-done | bytes 131104 | tf_op jit(solution)/shard_map/all_to_all | solution.py:56
  21.3 3.3 %all-to-all-start.3 = ((f32[4,1,2048]{2,1,0:T(1,128)}), f32[4,1,2048]{2,1,0:T(1,128)S(1)}, u32[]{:S(2)}, u32[]{:S(2)}) async-start(f32[4,1,2048]{2,1,0:T(1,128)} %reshape.540), calls=%async_computation.3 | async-start | bytes 65536 | tf_op jit(solution)/shard_map/all_to_all | solution.py:60
  24.6 1.0 copy.119
  25.6 3.4 %all-to-all-done.3 = f32[4,1,2048]{2,1,0:T(1,128)S(1)} async-done(((f32[4,1,2048]{2,1,0:T(1,128)}), f32[4,1,2048]{2,1,0:T(1,128)S(1)}, u32[]{:S(2)}, u32[]{:S(2)}) %all-to-all-start.3) | async-done | bytes 32800 | tf_op jit(solution)/shard_map/all_to_all | solution.py:60
  29.0 3.4 %all-to-all-start.6 = ((f32[1,128,1,512]{3,2,0,1:T(1,128)}), f32[1,128,1,512]{3,2,0,1:T(1,128)S(1)}, u32[]{:S(2)}, u32[]{:S(2)}) async-start(f32[1,128,1,512]{3,2,0,1:T(1,128)} %copy.119), calls=%async_computation.6 | async-start | bytes 524288 | tf_op jit(solution)/shard_map/all_to_all | solution.py:56
  32.4 0.6 convolution_bitcast_fusion.5
  33.3 1.0 copy.101
  34.2 3.8 %all-to-all-done.6 = f32[1,128,1,512]{3,2,0,1:T(1,128)S(1)} async-done(((f32[1,128,1,512]{3,2,0,1:T(1,128)}), f32[1,128,1,512]{3,2,0,1:T(1,128)S(1)}, u32[]{:S(2)}, u32[]{:S(2)}) %all-to-all-start.6) | async-done | bytes 262176 | tf_op jit(solution)/shard_map/all_to_all | solution.py:56
  38.0 3.5 %all-to-all-start.1 = ((f32[8,32,2,256]{3,1,2,0:T(8,128)}), f32[8,32,2,256]{3,1,2,0:T(8,128)S(1)}, u32[]{:S(2)}, u32[]{:S(2)}) async-start(f32[8,32,2,256]{3,1,2,0:T(8,128)} %copy.101), calls=%async_computation.1 | async-start | bytes 1048576 | tf_op jit(solution)/shard_map/all_to_all | solution.py:60
  41.5 1.1 convolution_bitcast_fusion.1
  42.9 1.6 %copy.121 = f32[8,32,2,512]{3,1,2,0:T(8,128)} copy(f32[8,32,2,512]{3,0,1,2:T(8,128)S(1)} %pad_maximum_fusion) | data formatting | bytes 2097152 | tf_op jit(solution)/shard_map/stack | solution.py:39
  44.5 6.2 %all-to-all-done.1 = f32[8,32,2,256]{3,1,2,0:T(8,128)S(1)} async-done(((f32[8,32,2,256]{3,1,2,0:T(8,128)}), f32[8,32,2,256]{3,1,2,0:T(8,128)S(1)}, u32[]{:S(2)}, u32[]{:S(2)}) %all-to-all-start.1) | async-done | bytes 524320 | tf_op jit(solution)/shard_map/all_to_all | solution.py:60
  50.7 3.5 %all-to-all-start.7 = ((f32[8,32,2,512]{3,1,2,0:T(8,128)}), f32[8,32,2,512]{3,1,2,0:T(8,128)S(1)}, u32[]{:S(2)}, u32[]{:S(2)}) async-start(f32[8,32,2,512]{3,1,2,0:T(8,128)} %copy.121), calls=%async_computation.7 | async-start | bytes 2097152 | tf_op jit(solution)/shard_map/all_to_all | solution.py:60
  55.1 0.6 reduce.2
  56.0 0.3 convolution_bitcast_fusion.11
  56.8 0.6 convolution_bitcast_fusion.4
  57.4 18.8 %all-to-all-done.7 = f32[8,32,2,512]{3,1,2,0:T(8,128)S(1)} async-done(((f32[8,32,2,512]{3,1,2,0:T(8,128)}), f32[8,32,2,512]{3,1,2,0:T(8,128)S(1)}, u32[]{:S(2)}, u32[]{:S(2)}) %all-to-all-start.7) | async-done | bytes 1048608 | tf_op jit(solution)/shard_map/all_to_all | solution.py:60
  76.4 1.0 convolution_bitcast_fusion
  78.0 0.3 convolution_bitcast_fusion.10
  78.5 0.9 reshape.542
  79.5 3.5 %all-to-all-start.10 = ((f32[4,1,2048]{2,1,0:T(1,128)}), f32[4,1,2048]{2,1,0:T(1,128)S(1)}, u32[]{:S(2)}, u32[]{:S(2)}) async-start(f32[4,1,2048]{2,1,0:T(1,128)} %reshape.542), calls=%async_computation.10 | async-start | bytes 65536 | tf_op jit(solution)/shard_map/all_to_all | solution.py:56
  83.0 0.6 convolution_bitcast_fusion.2
  83.6 1.2 copy.125
  84.8 2.7 %all-to-all-done.10 = f32[4,1,2048]{2,1,0:T(1,128)S(1)} async-done(((f32[4,1,2048]{2,1,0:T(1,128)}), f32[4,1,2048]{2,1,0:T(1,128)S(1)}, u32[]{:S(2)}, u32[]{:S(2)}) %all-to-all-start.10) | async-done | bytes 32800 | tf_op jit(solution)/shard_map/all_to_all | solution.py:56
  87.5 3.5 %all-to-all-start.8 = ((f32[2,128,2,256]{3,0,2,1:T(2,128)}), f32[2,128,2,256]{3,0,2,1:T(2,128)S(1)}, u32[]{:S(2)}, u32[]{:S(2)}) async-start(f32[2,128,2,256]{3,0,2,1:T(2,128)} %copy.125), calls=%async_computation.8 | async-start | bytes 1048576 | tf_op jit(solution)/shard_map/all_to_all | solution.py:56
  91.0 0.6 convolution_bitcast_fusion.3
  91.6 1.2 copy.115
  92.8 7.4 %all-to-all-done.8 = f32[2,128,2,256]{3,0,2,1:T(2,128)S(1)} async-done(((f32[2,128,2,256]{3,0,2,1:T(2,128)}), f32[2,128,2,256]{3,0,2,1:T(2,128)S(1)}, u32[]{:S(2)}, u32[]{:S(2)}) %all-to-all-start.8) | async-done | bytes 524320 | tf_op jit(solution)/shard_map/all_to_all | solution.py:56
  100.2 3.6 %all-to-all-start.4 = ((f32[2,128,2,256]{3,0,2,1:T(2,128)}), f32[2,128,2,256]{3,0,2,1:T(2,128)S(1)}, u32[]{:S(2)}, u32[]{:S(2)}) async-start(f32[2,128,2,256]{3,0,2,1:T(2,128)} %copy.115), calls=%async_computation.4 | async-start | bytes 1048576 | tf_op jit(solution)/shard_map/all_to_all | solution.py:56
  104.0 0.6 reduce.3
  104.6 0.4 reshape.543
  105.5 0.7 reshape.544
  106.4 0.4 all_to_all.143
  106.8 6.0 %all-to-all-done.4 = f32[2,128,2,256]{3,0,2,1:T(2,128)S(1)} async-done(((f32[2,128,2,256]{3,0,2,1:T(2,128)}), f32[2,128,2,256]{3,0,2,1:T(2,128)S(1)}, u32[]{:S(2)}, u32[]{:S(2)}) %all-to-all-start.4) | async-done | bytes 524320 | tf_op jit(solution)/shard_map/all_to_all | solution.py:56
  112.7 3.2 %all-to-all-start.11 = ((f32[4,1,512]{2,1,0:T(1,128)}), f32[4,1,512]{2,1,0:T(1,128)S(1)}, u32[]{:S(2)}, u32[]{:S(2)}) async-start(f32[4,1,512]{2,1,0:T(1,128)} %reshape.544), calls=%async_computation.11 | async-start | bytes 16384 | tf_op jit(solution)/shard_map/all_to_all | solution.py:60
  116.2 0.4 all_to_all.133
  116.8 0.5 convolution_bitcast_fusion.7
  117.2 0.7 copy.118
  117.9 2.5 %all-to-all-done.11 = f32[4,1,512]{2,1,0:T(1,128)S(1)} async-done(((f32[4,1,512]{2,1,0:T(1,128)}), f32[4,1,512]{2,1,0:T(1,128)S(1)}, u32[]{:S(2)}, u32[]{:S(2)}) %all-to-all-start.11) | async-done | bytes 8224 | tf_op jit(solution)/shard_map/all_to_all | solution.py:60
  120.4 3.3 %all-to-all-start.5 = ((f32[4,32,1,256]{3,1,2,0:T(8,128)}), f32[4,32,1,256]{3,1,2,0:T(8,128)S(1)}, u32[]{:S(2)}, u32[]{:S(2)}) async-start(f32[4,32,1,256]{3,1,2,0:T(8,128)} %copy.118), calls=%async_computation.5 | async-start | bytes 262144 | tf_op jit(solution)/shard_map/all_to_all | solution.py:60
  123.8 0.6 reduce.4
  124.4 0.5 convolution_bitcast_fusion.6
  124.9 0.7 copy.128
  125.6 2.9 %all-to-all-done.5 = f32[4,32,1,256]{3,1,2,0:T(8,128)S(1)} async-done(((f32[4,32,1,256]{3,1,2,0:T(8,128)}), f32[4,32,1,256]{3,1,2,0:T(8,128)S(1)}, u32[]{:S(2)}, u32[]{:S(2)}) %all-to-all-start.5) | async-done | bytes 131104 | tf_op jit(solution)/shard_map/all_to_all | solution.py:60
  128.5 3.3 %all-to-all-start.9 = ((f32[4,32,1,256]{3,1,2,0:T(8,128)}), f32[4,32,1,256]{3,1,2,0:T(8,128)S(1)}, u32[]{:S(2)}, u32[]{:S(2)}) async-start(f32[4,32,1,256]{3,1,2,0:T(8,128)} %copy.128), calls=%async_computation.9 | async-start | bytes 262144 | tf_op jit(solution)/shard_map/all_to_all | solution.py:60
  131.8 13.2 %collective-permute-start = (bf16[1,128,256]{2,1,0:T(8,128)(2,1)S(1)}, bf16[1,128,256]{2,1,0:T(8,128)(2,1)S(1)}, u32[]{:S(2)}, u32[]{:S(2)}) collective-permute-start(bf16[1,128,256]{2,1,0:T(8,128)(2,1)S(1)} %fusion.28), channel_id=1, source_target_pairs={{0,1},{1,2},{2,3},{3,4},{4,5},{5,6},{6,7},{8,9},{9,10},{10,11},{11... | collective-permute-start | bytes 196616 | tf_op jit(solution)/shard_map/ppermute | solution.py:18
  145.1 4.7 %collective-permute-start.1 = (bf16[1,128,3,256]{3,1,2,0:T(8,128)(2,1)S(1)}, bf16[1,128,3,256]{3,1,2,0:T(8,128)(2,1)S(1)}, u32[]{:S(2)}, u32[]{:S(2)}) collective-permute-start(bf16[1,128,3,256]{3,1,2,0:T(8,128)(2,1)S(1)} %pad_maximum_fusion.4), channel_id=1, source_target_pairs={{1,0},{2,1},{3,2},{4,3},{5,4},{6,5},{7,6},{9,8},{10,9},{11,10},{12... | collective-permute-start | bytes 589832 | tf_op jit(solution)/shard_map/ppermute | solution.py:18
  149.9 0.7 mul.726
  150.6 3.7 %collective-permute-done.1 = bf16[1,128,3,256]{3,1,2,0:T(8,128)(2,1)S(1)} collective-permute-done((bf16[1,128,3,256]{3,1,2,0:T(8,128)(2,1)S(1)}, bf16[1,128,3,256]{3,1,2,0:T(8,128)(2,1)S(1)}, u32[]{:S(2)}, u32[]{:S(2)}) %collective-permute-start.1) | collective-permute-done | bytes 196640 | tf_op jit(solution)/shard_map/ppermute | solution.py:18
  154.3 0.6 copy.213
  155.0 0.7 copy.214
  (66 shorter events, 4.9 us)
Async XLA Ops:
  1.4 7.3 %copy-start = (bf16[1,128,3,256]{3,1,2,0:T(8,128)(2,1)S(1)}, bf16[1,128,3,256]{3,1,2,0:T(8,128)(2,1)}, u32[]{:S(2)}) copy-start(bf16[1,128,3,256]{3,1,2,0:T(8,128)(2,1)} %param.6) | copy-start | bytes 589828
  3.3 9.9 %all-to-all-start.2 = ((f32[4,1,512]{2,1,0:T(1,128)}), f32[4,1,512]{2,1,0:T(1,128)S(1)}, u32[]{:S(2)}, u32[]{:S(2)}) async-start(f32[4,1,512]{2,1,0:T(1,128)} %reshape.538), calls=%async_computation.2 | async-start | bytes 16384 | tf_op jit(solution)/shard_map/all_to_all | solution.py:56
  8.8 0.8 copy-start.1
  9.6 0.9 copy-start.2
  13.2 8.1 %all-to-all-start = ((f32[1,128,1,256]{3,2,0,1:T(1,128)}), f32[1,128,1,256]{3,2,0,1:T(1,128)S(1)}, u32[]{:S(2)}, u32[]{:S(2)}) async-start(f32[1,128,1,256]{3,2,0,1:T(1,128)} %fusion.27), calls=%async_computation | async-start | bytes 262144 | tf_op jit(solution)/shard_map/all_to_all | solution.py:56
  21.3 7.7 %all-to-all-start.3 = ((f32[4,1,2048]{2,1,0:T(1,128)}), f32[4,1,2048]{2,1,0:T(1,128)S(1)}, u32[]{:S(2)}, u32[]{:S(2)}) async-start(f32[4,1,2048]{2,1,0:T(1,128)} %reshape.540), calls=%async_computation.3 | async-start | bytes 65536 | tf_op jit(solution)/shard_map/all_to_all | solution.py:60
  29.0 9.0 %all-to-all-start.6 = ((f32[1,128,1,512]{3,2,0,1:T(1,128)}), f32[1,128,1,512]{3,2,0,1:T(1,128)S(1)}, u32[]{:S(2)}, u32[]{:S(2)}) async-start(f32[1,128,1,512]{3,2,0,1:T(1,128)} %copy.119), calls=%async_computation.6 | async-start | bytes 524288 | tf_op jit(solution)/shard_map/all_to_all | solution.py:56
  38.0 12.7 %all-to-all-start.1 = ((f32[8,32,2,256]{3,1,2,0:T(8,128)}), f32[8,32,2,256]{3,1,2,0:T(8,128)S(1)}, u32[]{:S(2)}, u32[]{:S(2)}) async-start(f32[8,32,2,256]{3,1,2,0:T(8,128)} %copy.101), calls=%async_computation.1 | async-start | bytes 1048576 | tf_op jit(solution)/shard_map/all_to_all | solution.py:60
  50.7 25.6 %all-to-all-start.7 = ((f32[8,32,2,512]{3,1,2,0:T(8,128)}), f32[8,32,2,512]{3,1,2,0:T(8,128)S(1)}, u32[]{:S(2)}, u32[]{:S(2)}) async-start(f32[8,32,2,512]{3,1,2,0:T(8,128)} %copy.121), calls=%async_computation.7 | async-start | bytes 2097152 | tf_op jit(solution)/shard_map/all_to_all | solution.py:60
  79.5 8.0 %all-to-all-start.10 = ((f32[4,1,2048]{2,1,0:T(1,128)}), f32[4,1,2048]{2,1,0:T(1,128)S(1)}, u32[]{:S(2)}, u32[]{:S(2)}) async-start(f32[4,1,2048]{2,1,0:T(1,128)} %reshape.542), calls=%async_computation.10 | async-start | bytes 65536 | tf_op jit(solution)/shard_map/all_to_all | solution.py:56
  87.5 12.7 %all-to-all-start.8 = ((f32[2,128,2,256]{3,0,2,1:T(2,128)}), f32[2,128,2,256]{3,0,2,1:T(2,128)S(1)}, u32[]{:S(2)}, u32[]{:S(2)}) async-start(f32[2,128,2,256]{3,0,2,1:T(2,128)} %copy.125), calls=%async_computation.8 | async-start | bytes 1048576 | tf_op jit(solution)/shard_map/all_to_all | solution.py:56
  100.2 12.6 %all-to-all-start.4 = ((f32[2,128,2,256]{3,0,2,1:T(2,128)}), f32[2,128,2,256]{3,0,2,1:T(2,128)S(1)}, u32[]{:S(2)}, u32[]{:S(2)}) async-start(f32[2,128,2,256]{3,0,2,1:T(2,128)} %copy.115), calls=%async_computation.4 | async-start | bytes 1048576 | tf_op jit(solution)/shard_map/all_to_all | solution.py:56
  112.7 7.7 %all-to-all-start.11 = ((f32[4,1,512]{2,1,0:T(1,128)}), f32[4,1,512]{2,1,0:T(1,128)S(1)}, u32[]{:S(2)}, u32[]{:S(2)}) async-start(f32[4,1,512]{2,1,0:T(1,128)} %reshape.544), calls=%async_computation.11 | async-start | bytes 16384 | tf_op jit(solution)/shard_map/all_to_all | solution.py:60
  117.9 5.8 %copy-start.3 = (f32[1,128,256]{2,1,0:T(8,128)S(1)}, f32[1,128,256]{2,1,0:T(8,128)}, u32[]{:S(2)}) copy-start(f32[1,128,256]{2,1,0:T(8,128)} %param.7) | copy-start | bytes 393220
  120.4 8.1 %all-to-all-start.5 = ((f32[4,32,1,256]{3,1,2,0:T(8,128)}), f32[4,32,1,256]{3,1,2,0:T(8,128)S(1)}, u32[]{:S(2)}, u32[]{:S(2)}) async-start(f32[4,32,1,256]{3,1,2,0:T(8,128)} %copy.118), calls=%async_computation.5 | async-start | bytes 262144 | tf_op jit(solution)/shard_map/all_to_all | solution.py:60
  128.5 16.6 %all-to-all-start.9 = ((f32[4,32,1,256]{3,1,2,0:T(8,128)}), f32[4,32,1,256]{3,1,2,0:T(8,128)S(1)}, u32[]{:S(2)}, u32[]{:S(2)}) async-start(f32[4,32,1,256]{3,1,2,0:T(8,128)} %copy.128), calls=%async_computation.9 | async-start | bytes 262144 | tf_op jit(solution)/shard_map/all_to_all | solution.py:60
  131.8 18.8 %collective-permute-start = (bf16[1,128,256]{2,1,0:T(8,128)(2,1)S(1)}, bf16[1,128,256]{2,1,0:T(8,128)(2,1)S(1)}, u32[]{:S(2)}, u32[]{:S(2)}) collective-permute-start(bf16[1,128,256]{2,1,0:T(8,128)(2,1)S(1)} %fusion.28), channel_id=1, source_target_pairs={{0,1},{1,2},{2,3},{3,4},{4,5},{5,6},{6,7},{8,9},{9,10},{10,11},{11... | collective-permute-start | bytes 196616 | tf_op jit(solution)/shard_map/ppermute | solution.py:18
  145.1 9.2 %collective-permute-start.1 = (bf16[1,128,3,256]{3,1,2,0:T(8,128)(2,1)S(1)}, bf16[1,128,3,256]{3,1,2,0:T(8,128)(2,1)S(1)}, u32[]{:S(2)}, u32[]{:S(2)}) collective-permute-start(bf16[1,128,3,256]{3,1,2,0:T(8,128)(2,1)S(1)} %pad_maximum_fusion.4), channel_id=1, source_target_pairs={{1,0},{2,1},{3,2},{4,3},{5,4},{6,5},{7,6},{9,8},{10,9},{11,10},{12... | collective-permute-start | bytes 589832 | tf_op jit(solution)/shard_map/ppermute | solution.py:18
where the time goes:
time: 157 us; the launch traced here: 156 us
  waiting for transfers between devices  61.8 us (39%)
  starting transfers between devices  60.9 us (39%)
  local copies, waits for them, and re-layouts  18.7 us (12%)
  matrix products  6.82 us (4%)
  other arithmetic  6.18 us (4%)
    all_to_all x6, waiting for transfers between devices, split_freq(): lax.all_to_all(blocks, 'ctx', split_axis=0, concat_axis=1, tiled=True)  33.9 us
    all_to_all x6, waiting for transfers between devices, split_time(): lax.all_to_all(blocks, 'ctx', split_axis=1, concat_axis=0, tiled=True)  24.2 us
    all_to_all x6, starting transfers between devices, split_time(): lax.all_to_all(blocks, 'ctx', split_axis=1, concat_axis=0, tiled=True)  22.7 us
    all_to_all x6, starting transfers between devices, split_freq(): lax.all_to_all(blocks, 'ctx', split_axis=0, concat_axis=1, tiled=True)  20.1 us
    ppermute x2, starting transfers between devices, from_behind(): return lax.ppermute(x, axis, pairs)  18 us
    unnamed x24, local copies, waits for them, and re-layouts  8.2 us
    ppermute x2, waiting for transfers between devices, from_behind(): return lax.ppermute(x, axis, pairs)  3.72 us
  transfers between devices with their start and end apart: 14, of which 12 were waited for; matrix products, arithmetic and copies ran while one was open for 14% of the time, Pallas kernels for 0%

commit v1 on v0

v1 whole, which is shorter than its diff:
```python
import math

import numpy as np

import jax
import jax.numpy as jnp
from jax import lax
from jax.sharding import PartitionSpec as P

CPF = 16
CHUNK_BYTES = 36 * 2**20

highest = lax.Precision.HIGHEST


def from_behind(x, axis, by):
    devices = lax.axis_size(axis)
    pairs = [(i, i + by) for i in range(devices) if 0 <= i + by < devices]
    return lax.ppermute(x, axis, pairs)


def inner_tables(block):
    ids = np.arange(block)
    theta = 2.0 * np.pi * ((ids[:, None] * ids[None, :]) % block) / block
    cos, sin = np.cos(theta), np.sin(theta)
    fwd = np.block([[cos, -sin], [sin, cos]])
    inv = np.block([[cos, sin], [-sin, cos]])
    return jnp.asarray(fwd.T, jnp.float32), jnp.asarray(inv.T, jnp.float32)


def outer_tables(blocks, block, outer):
    size = outer * block
    pos = np.arange(blocks)[:, None, None] * block + np.arange(block)[None, :, None]
    prod = (pos * np.arange(outer)[None, None, :]) % size
    theta = 2.0 * np.pi * prod / size
    return jnp.asarray(np.cos(theta), jnp.float32), jnp.asarray(-np.sin(theta), jnp.float32)


def to_spectrum(x, cw, sw, fwd):
    blocks = x.shape[0]
    tail = (1,) * (x.ndim - 2)
    re = sum(cw[p].reshape(cw.shape[1:] + tail) * x[p][:, None] for p in range(blocks))
    im = sum(sw[p].reshape(sw.shape[1:] + tail) * x[p][:, None] for p in range(blocks))
    stacked = jnp.concatenate([re, im], axis=0)
    shape = stacked.shape
    out = jnp.dot(fwd, stacked.reshape(shape[0], -1), precision=highest)
    return out.reshape(shape)


def to_signal(spec, inv, wc, ws):
    shape = spec.shape
    block = shape[0] // 2
    z = jnp.dot(inv, spec.reshape(shape[0], -1), precision=highest).reshape(shape)
    tail = (1,) * (spec.ndim - 2)
    wc = wc.reshape(wc.shape + tail)
    ws = ws.reshape(ws.shape + tail)
    return jnp.sum(wc * z[:block] + ws * z[block:], axis=1)


def chunk_work(x3, hx, tables):
    cw, sw, fwd, inv, wc, ws = tables
    block = x3.shape[1]
    spec = to_spectrum(x3, cw, sw, fwd)
    hspec = to_spectrum(hx, cw, sw, fwd)
    hspec = jnp.repeat(hspec, CPF, axis=-1)
    hr, hi = hspec[:block], hspec[block:]
    mr, mi = spec[:block, :, 0], spec[block:, :, 0]
    wr, wi = spec[:block, :, 1], spec[block:, :, 1]
    br, bi = spec[:block, :, 2], spec[block:, :, 2]
    conv_r = hr * mr - hi * mi
    conv_i = hr * mi + hi * mr
    gm_r = hr * wr + hi * wi
    gm_i = hr * wi - hi * wr
    fg_r = br * wr + bi * wi
    fg_i = br * wi - bi * wr
    lead = fg_r.shape[:-1]
    fg_r = fg_r.reshape(lead + (-1, CPF)).sum(axis=-1)
    fg_i = fg_i.reshape(lead + (-1, CPF)).sum(axis=-1)
    pair = jnp.concatenate(
        [jnp.stack([conv_r, gm_r], axis=2), jnp.stack([conv_i, gm_i], axis=2)], axis=0
    )
    both = to_signal(pair, inv, wc, ws)
    fg = to_signal(jnp.concatenate([fg_r, fg_i], axis=0), inv, wc, ws)
    return both[:, 0], both[:, 1], fg


def on_device(qkv_in, qkv_saved, conv_saved, out_grad, filters):
    blocks = lax.axis_size("ctx")
    place = lax.axis_index("ctx")
    block = qkv_in.shape[1]
    channels = qkv_in.shape[3]
    groups = filters.shape[1]
    length = blocks * block
    outer = 2 * blocks
    size = outer * block
    filter_scale = (CPF * length) ** (-0.5)

    query_in = qkv_in[0, :, 0].astype(jnp.float32)
    mixed_in = qkv_in[0, :, 1].astype(jnp.float32) * qkv_in[0, :, 2].astype(jnp.float32)
    query_back = qkv_saved[0, :, 0].astype(jnp.float32)
    key_back = qkv_saved[0, :, 1].astype(jnp.float32)
    value_back = qkv_saved[0, :, 2].astype(jnp.float32)
    mixed_back = key_back * value_back
    upstream = out_grad[0].astype(jnp.float32)
    weighted = upstream * query_back
    grad_query = upstream * conv_saved[0]

    payload = jnp.concatenate([mixed_in, weighted, mixed_back, filters[0].T], axis=1)
    full = lax.all_gather(payload, "ctx")
    x3 = full[:, :, : 3 * channels].reshape(blocks, block, 3, channels)
    hx = full[:, :, 3 * channels :]

    cw, sw = outer_tables(blocks, block, outer)
    fwd, inv = inner_tables(block)
    pos = place * block + jnp.arange(block, dtype=jnp.int32)
    prod = (pos[:, None] * jnp.arange(outer, dtype=jnp.int32)[None, :]) % size
    theta = prod.astype(jnp.float32) * (2.0 * math.pi / size)
    wc = jnp.cos(theta) / size
    ws = -jnp.sin(theta) / size
    tables = (cw, sw, fwd, inv, wc, ws)

    per_group = 2 * block * outer * 4 * 4 * CPF * blocks
    gchunk = groups
    while gchunk > 1 and gchunk * per_group > CHUNK_BYTES and groups % (gchunk // 2) == 0:
        gchunk //= 2
    nchunk = groups // gchunk
    if nchunk == 1:
        conv, grad_mixed, fg = chunk_work(x3, hx, tables)
    else:
        cc = gchunk * CPF
        xs = x3.reshape(blocks, block, 3, nchunk, cc).transpose(3, 0, 1, 2, 4)
        hs = hx.reshape(blocks, block, nchunk, gchunk).transpose(2, 0, 1, 3)
        conv, grad_mixed, fg = lax.map(lambda a: chunk_work(a[0], a[1], tables), (xs, hs))
        conv = conv.transpose(1, 0, 2).reshape(block, channels)
        grad_mixed = grad_mixed.transpose(1, 0, 2).reshape(block, channels)
        fg = fg.transpose(1, 0, 2).reshape(block, groups)

    conv = conv * filter_scale
    grad_mixed = grad_mixed * filter_scale
    result = (query_in * conv).astype(jnp.bfloat16)
    next_input = from_behind(result[None], "pipe", 1)
    grad_key = grad_mixed * value_back
    grad_value = grad_mixed * key_back
    grad_stack = jnp.stack([grad_query, grad_key, grad_value], axis=1).astype(jnp.bfloat16)
    prev_grad = from_behind(grad_stack[None], "pipe", -1)
    filter_grad = (fg * filter_scale).T[None]
    return (next_input, prev_grad, filter_grad)


def solution(mesh):
    return jax.shard_map(
        on_device,
        mesh=mesh,
        in_specs=(
            P("pipe", "ctx", None, None),
            P("pipe", "ctx", None, None),
            P("pipe", "ctx", None),
            P("pipe", "ctx", None),
            P("pipe", None, "ctx"),
        ),
        out_specs=(P("pipe", "ctx", None), P("pipe", "ctx", None, None), P("pipe", None, "ctx")),
        check_vma=False,
    )
```

time: 157 us -> 117 us (0.75)
  the two profiles are of different devices: /device:TPU:1 before, /device:TPU:4 now
where the time goes in v1:
time: 117 us; the launch traced here: 116 us
  waiting for transfers between devices  45.9 us (39%)
  other arithmetic  19.7 us (17%)
  local copies, waits for them, and re-layouts  16.6 us (14%)
  matrix products  15 us (13%)
  between operations  14.5 us (12%)
  starting transfers between devices  4.77 us (4%)
    all_gather x1, waiting for transfers between devices, on_device(): full = lax.all_gather(payload, 'ctx')  41.2 us
    dot_general x4, matrix products, to_spectrum(): out = jnp.dot(fwd, stacked.reshape(shape[0], -1), precision=highest)  10.8 us
    slice x4, local copies, waits for them, and re-layouts, to_signal(): return jnp.sum(wc * z[:block] + ws * z[block:], axis=1)  9.32 us
    reduce_sum x2, other arithmetic, to_signal(): return jnp.sum(wc * z[:block] + ws * z[block:], axis=1)  5.45 us
    ppermute x2, starting transfers between devices, from_behind(): return lax.ppermute(x, axis, pairs)  4.73 us
    ppermute x2, waiting for transfers between devices, from_behind(): return lax.ppermute(x, axis, pairs)  4.63 us
    dot_general x2, matrix products, to_signal(): jnp.dot(inv, spec.reshape(shape[0], -1), precision=highest).reshape(shape)  4.18 us
    unnamed x42, local copies, waits for them, and re-layouts  3.82 us
  transfers between devices with their start and end apart: 3, of which 2 were waited for; matrix products, arithmetic and copies ran while one was open for 3% of the time, Pallas kernels for 0%

profile of v1, /device:TPU:4, one launch (start us, length us, event | category | flops | bytes accessed | tf_op | source)
XLA Modules:
  0.0 116.4 jit_solution(7485150374838828803)
XLA Ops:
  7.2 0.0 copy-start.4
  7.2 0.0 all-gather.3.cloned.1.call-start
  7.2 0.9 fusion.24
  8.2 0.9 fusion.5
  9.0 0.8 copy.43
  9.8 0.2 copy_multiply_fusion
  10.0 0.0 copy-start.7
  10.0 0.0 copy-start.8
  10.0 0.0 copy-start.9
  10.1 0.0 copy-start.10
  10.1 0.0 copy-start.11
  10.1 0.0 copy-start.12
  10.1 0.0 copy-start.13
  10.1 0.0 copy-start.14
  10.1 0.9 copy_bitcast_fusion.1
  11.0 0.0 copy-start.2
  11.1 0.0 copy-start.1
  11.1 0.8 pad_maximum_fusion
  11.9 0.0 all-gather.3.cloned.1.call-update
  11.9 0.1 cosine_multiply_fusion
  12.0 0.1 copy.40
  12.1 0.7 copy.45
  12.8 0.6 fusion.14
  13.5 41.2 %all-gather.3.cloned.1.call-done = f32[512,784]{1,0:T(8,128)} async-done(((f32[128,784]{1,0:T(8,128)}), f32[512,784]{1,0:T(8,128)}) %all-gather.3.cloned.1.call-update) | async-done | bytes 1605648 | tf_op jit(solution)/shard_map/all_gather | solution.py:109
  54.7 1.0 fusion.23
  55.6 1.5 %fusion.22 = (f32[1,128,768]{2,1,0:T(8,128)S(1)}, f32[1,128,768]{2,1,0:T(8,128)S(1)}, f32[1,128,768]{2,1,0:T(8,128)S(1)}, f32[1,128,768]{2,1,0:T(8,128)S(1)}) fusion(f32[4,128,784]{2,1,0:T(8,128)} %bitcast.123), kind=kLoop, calls=%fused_computation.64 | loop fusion | bytes 3145728 | tf_op jit(solution)/shard_map/slice | solution.py:42
  57.1 0.1 copy.55
  57.1 0.1 copy.52
  57.2 0.1 copy.53
  57.3 0.1 copy.54
  57.4 0.0 copy-done.9
  57.5 0.3 fusion.27
  57.8 0.3 fusion
  58.1 0.3 copy.56
  58.4 0.3 copy.57
  58.8 0.3 copy.58
  59.1 0.3 copy.59
  59.4 1.6 %multiply_add_fusion = (f32[128,8,3,256]{0,3,2,1:T(8,128)S(1)}, f32[128,8,3,256]{0,3,2,1:T(8,128)S(1)}) fusion(f32[128,8]{0,1:T(8,128)S(1)} %copy-done.14, f32[128,8]{0,1:T(8,128)S(1)} %copy-done.13, f32[128,8]{0,1:T(8,128)S(1)} %copy-done.12, f32[128,8]{0,1:T(8,128)S(1)} %copy-done.11, f32[128,3,256]{0,2,1:T(8,128)S(1)} %bitcast.127, ...), kind=kLoop, calls=%fused_computation.2 | loop fusion | flops 11010048 | bytes 7897088 | tf_op jit(solution)/shard_map/add | solution.py:43
  61.0 5.0 %fusion.28 = f32[6144,256]{1,0:T(8,128)S(1)} fusion(f32[128,6144]{0,1:T(8,128)S(1)} %bitcast.114, f32[256,128]{1,0:T(8,128)S(1)} %copy-done.2), kind=kOutput, calls=%fused_computation.70 | convolution fusion | flops 2415919104 | bytes 9568256 | tf_op jit(solution)/shard_map/dot_general | solution.py:46
  66.1 5.2 %convolution_add_fusion = f32[6144,256]{1,0:T(8,128)S(1)} fusion(f32[6144,256]{1,0:T(8,128)S(1)} %fusion.28, f32[128,6144]{0,1:T(8,128)S(1)} %bitcast.117, f32[256,128]{1,0:T(8,128)S(1)} %copy-done.1), kind=kOutput, calls=%fused_computation | convolution fusion | flops 2417491968 | bytes 15859712 | tf_op jit(solution)/shard_map/dot_general | solution.py:46
  71.4 0.1 broadcast_in_dim.12
  71.4 0.1 broadcast_in_dim.13
  71.5 0.0 copy-start
  71.5 2.3 %multiply_add_fusion.2 = (f32[128,8,1,256]{0,3,2,1:T(8,128)S(1)}, f32[128,8,1,256]{0,3,2,1:T(8,128)S(1)}, f32[128,8,1,256]{0,3,2,1:T(8,128)S(1)}, f32[128,8,1,25...) fusion(f32[256,8,3,256]{0,3,2,1:T(8,128)S(1)} %bitcast.115, ...), kind=kLoop, calls=%fused_computation.20 | loop fusion | flops 4718592 | bytes 14680064 | tf_op jit(solution)/shard_map/add | solution.py:74
  73.8 0.8 reduce_sum.37
  74.6 0.2 reduce_sum.38
  74.8 0.8 pad_maximum_fusion.2
  75.7 0.4 fusion.30
  76.1 2.1 %maximum_maximum_fusion = f32[256,8,2,256]{0,3,2,1:T(8,128)S(1)} fusion(f32[128,8,1,256]{0,3,2,1:T(8,128)S(1)} %get-tuple-element.18, f32[128,8,1,256]{0,3,2,1:T(8,128)} %get-tuple-element.19, f32[128,8,1,256]{0,3,2,1:T(8,128)} %get-tuple-element.20, f32[128,8,1,256]{0,3,2,1:T(8,128)} %get-tuple-element.21), kind=kLoop, calls=%fused_computation.1 | loop fusion | flops 3145728 | bytes 8388608 | tf_op jit(solution)/shard_map/concatenate | solution.py:79
  78.2 3.8 %fusion.29 = f32[256,4096]{1,0:T(8,128)S(1)} fusion(f32[256,256]{1,0:T(8,128)S(1)} %copy-done, f32[256,4096]{0,1:T(8,128)S(1)} %bitcast.116), kind=kOutput, calls=%fused_computation.71 | convolution fusion | flops 3221225472 | bytes 8650752 | tf_op jit(solution)/shard_map/dot_general | solution.py:53
  82.0 2.3 %fusion.21 = (f32[128,4096]{1,0:T(8,128)}, f32[128,4096]{1,0:T(8,128)}) fusion(f32[256,4096]{1,0:T(8,128)S(1)} %fusion.29), kind=kLoop, calls=%fused_computation.63 | loop fusion | bytes 8388608 | tf_op jit(solution)/shard_map/slice | solution.py:57
  84.3 3.0 %slice.197 = f32[128,8,2,256]{3,2,1,0:T(2,128)S(1)} reshape(f32[128,4096]{1,0:T(8,128)} %get-tuple-element.22) | data formatting | bytes 4194304 | tf_op jit(solution)/shard_map/slice | solution.py:57
  87.3 0.0 copy-start.3
  87.3 4.0 %slice.199 = f32[128,8,2,256]{3,2,1,0:T(2,128)} reshape(f32[128,4096]{1,0:T(8,128)} %get-tuple-element.23) | data formatting | bytes 4194304 | tf_op jit(solution)/shard_map/slice | solution.py:57
  91.4 5.4 %add_reduce_fusion = f32[128,2,256]{2,1,0:T(2,128)S(1)} fusion(f32[128,8,2,256]{3,2,1,0:T(2,128)} %slice.199, f32[128,8,2,256]{3,2,1,0:T(2,128)S(1)} %slice.197, f32[128,8]{1,0:T(8,128)S(1)} %copy-done.3, f32[128,8]{1,0:T(8,128)S(1)} %copy.40), kind=kLoop, calls=%fused_computation.12 | loop fusion | flops 2031616 | bytes 4464640 | tf_op jit(solution)/shard_map/reduce_sum | solution.py:57
  96.8 0.3 slice_multiply_fusion
  97.1 0.9 fusion.13
  98.0 2.8 %collective-permute-start.1 = (bf16[1,128,3,256]{3,1,2,0:T(8,128)(2,1)S(1)}, bf16[1,128,3,256]{3,1,2,0:T(8,128)(2,1)S(1)}, u32[]{:S(2)}, u32[]{:S(2)}) collective-permute-start(bf16[1,128,3,256]{3,1,2,0:T(8,128)(2,1)S(1)} %pad_maximum_fusion.1), channel_id=1, source_target_pairs={{1,0},{2,1},{3,2},{4,3},{5,4},{6,5},{7,6},{9,8},{10,9},{11,10},{12... | collective-permute-start | bytes 589832 | tf_op jit(solution)/shard_map/ppermute | solution.py:19
  100.8 0.2 fusion.12
  101.0 1.9 %collective-permute-start = (bf16[1,128,256]{2,0,1:T(2,128)(2,1)S(1)}, bf16[1,128,256]{2,0,1:T(2,128)(2,1)S(1)}, u32[]{:S(2)}, u32[]{:S(2)}) collective-permute-start(bf16[1,128,256]{2,0,1:T(2,128)(2,1)S(1)} %fusion.12), channel_id=1, source_target_pairs={{0,1},{1,2},{2,3},{3,4},{4,5},{5,6},{6,7},{8,9},{9,10},{10,11},{11... | collective-permute-start | bytes 196616 | tf_op jit(solution)/shard_map/ppermute | solution.py:19
  103.0 0.6 multiply_bitcast_fusion.1
  103.6 4.6 %collective-permute-done = bf16[1,128,256]{2,0,1:T(2,128)(2,1)S(1)} collective-permute-done((bf16[1,128,256]{2,0,1:T(2,128)(2,1)S(1)}, bf16[1,128,256]{2,0,1:T(2,128)(2,1)S(1)}, u32[]{:S(2)}, u32[]{:S(2)}) %collective-permute-start) | collective-permute-done | bytes 65568 | tf_op jit(solution)/shard_map/ppermute | solution.py:19
  108.2 0.6 copy.47
  108.8 0.7 copy.81
  (26 shorter events, 0.2 us)
Async XLA Ops:
  7.2 5.6 %copy-start.4 = (bf16[1,128,256]{2,1,0:T(8,128)(2,1)S(1)}, bf16[1,128,256]{2,1,0:T(8,128)(2,1)}, u32[]{:S(2)}) copy-start(bf16[1,128,256]{2,1,0:T(8,128)(2,1)} %param.12) | copy-start | bytes 196612
  7.2 5.6 %copy-start.6 = (f32[1,128,256]{2,1,0:T(8,128)S(1)}, f32[1,128,256]{2,1,0:T(8,128)}, u32[]{:S(2)}) copy-start(f32[1,128,256]{2,1,0:T(8,128)} %param.11) | copy-start | bytes 393220
  7.2 47.5 %all-gather.3.cloned.1.call-start = ((), (), s32[]{:S(2)}) async-start(), calls=%async_computation | async-start | bytes 2293760 | tf_op jit(solution)/shard_map/all_gather | solution.py:109
  10.0 47.3 %copy-start.7 = (f32[128,8]{0,1:T(8,128)S(1)}, f32[128,8]{0,1:T(8,128)}, u32[]{:S(2)}) copy-start(f32[128,8]{0,1:T(8,128)} %constant.53) | copy-start | bytes 12292
  10.0 47.3 %copy-start.8 = (f32[128,8]{0,1:T(8,128)S(1)}, f32[128,8]{0,1:T(8,128)}, u32[]{:S(2)}) copy-start(f32[128,8]{0,1:T(8,128)} %constant.55) | copy-start | bytes 12292
  10.0 47.3 %copy-start.9 = (f32[128,8]{0,1:T(8,128)S(1)}, f32[128,8]{0,1:T(8,128)}, u32[]{:S(2)}) copy-start(f32[128,8]{0,1:T(8,128)} %constant.57) | copy-start | bytes 12292
  10.1 47.3 %copy-start.10 = (f32[128,8]{0,1:T(8,128)S(1)}, f32[128,8]{0,1:T(8,128)}, u32[]{:S(2)}) copy-start(f32[128,8]{0,1:T(8,128)} %constant.59) | copy-start | bytes 12292
  10.1 47.3 %copy-start.11 = (f32[128,8]{0,1:T(8,128)S(1)}, f32[128,8]{0,1:T(8,128)}, u32[]{:S(2)}) copy-start(f32[128,8]{0,1:T(8,128)} %constant.62) | copy-start | bytes 12292
  10.1 47.3 %copy-start.12 = (f32[128,8]{0,1:T(8,128)S(1)}, f32[128,8]{0,1:T(8,128)}, u32[]{:S(2)}) copy-start(f32[128,8]{0,1:T(8,128)} %constant.64) | copy-start | bytes 12292
  10.1 47.3 %copy-start.13 = (f32[128,8]{0,1:T(8,128)S(1)}, f32[128,8]{0,1:T(8,128)}, u32[]{:S(2)}) copy-start(f32[128,8]{0,1:T(8,128)} %constant.66) | copy-start | bytes 12292
  10.1 47.3 %copy-start.14 = (f32[128,8]{0,1:T(8,128)S(1)}, f32[128,8]{0,1:T(8,128)}, u32[]{:S(2)}) copy-start(f32[128,8]{0,1:T(8,128)} %constant.68) | copy-start | bytes 12292
  11.0 46.4 %copy-start.2 = (f32[256,128]{1,0:T(8,128)S(1)}, f32[256,128]{1,0:T(8,128)}, u32[]{:S(2)}) copy-start(f32[256,128]{1,0:T(8,128)} %constant.60) | copy-start | bytes 393220
  11.1 46.7 %copy-start.1 = (f32[256,128]{1,0:T(8,128)S(1)}, f32[256,128]{1,0:T(8,128)}, u32[]{:S(2)}) copy-start(f32[256,128]{1,0:T(8,128)} %constant.69) | copy-start | bytes 393220
  71.5 4.2 %copy-start = (f32[256,256]{1,0:T(8,128)S(1)}, f32[256,256]{1,0:T(8,128)}, u32[]{:S(2)}) copy-start(f32[256,256]{1,0:T(8,128)} %constant.46.clone) | copy-start | bytes 786436
  87.3 4.0 %copy-start.3 = (f32[128,8]{1,0:T(8,128)S(1)}, f32[128,8]{1,0:T(8,128)}, u32[]{:S(2)}) copy-start(f32[128,8]{1,0:T(8,128)} %copy.45) | copy-start | bytes 12292
  91.4 6.6 %copy-start.5 = (bf16[1,128,1,256]{3,1,2,0:T(8,128)(2,1)S(1)}, bf16[1,128,1,256]{3,1,2,0:T(8,128)(2,1)}, u32[]{:S(2)}) copy-start(bf16[1,128,1,256]{3,1,2,0:T(8,128)(2,1)} %fusion.14) | copy-start | bytes 196612
  91.4 9.5 %slice-start = ((bf16[1,128,3,256]{3,1,2,0:T(8,128)(2,1)}), bf16[1,128,1,256]{3,1,2,0:T(8,128)(2,1)S(1)}, s32[]{:S(2)}) async-start(bf16[1,128,3,256]{3,1,2,0:T(8,128)(2,1)} %param.9), calls=%async_computation.1 | async-start | bytes 131072 | tf_op jit(solution)/shard_map/slice | solution.py:98
  98.0 10.8 %collective-permute-start.1 = (bf16[1,128,3,256]{3,1,2,0:T(8,128)(2,1)S(1)}, bf16[1,128,3,256]{3,1,2,0:T(8,128)(2,1)S(1)}, u32[]{:S(2)}, u32[]{:S(2)}) collective-permute-start(bf16[1,128,3,256]{3,1,2,0:T(8,128)(2,1)S(1)} %pad_maximum_fusion.1), channel_id=1, source_target_pairs={{1,0},{2,1},{3,2},{4,3},{5,4},{6,5},{7,6},{9,8},{10,9},{11,10},{12... | collective-permute-start | bytes 589832 | tf_op jit(solution)/shard_map/ppermute | solution.py:19
  101.0 7.2 %collective-permute-start = (bf16[1,128,256]{2,0,1:T(2,128)(2,1)S(1)}, bf16[1,128,256]{2,0,1:T(2,128)(2,1)S(1)}, u32[]{:S(2)}, u32[]{:S(2)}) collective-permute-start(bf16[1,128,256]{2,0,1:T(2,128)(2,1)S(1)} %fusion.12), channel_id=1, source_target_pairs={{0,1},{1,2},{2,3},{3,4},{4,5},{5,6},{6,7},{8,9},{9,10},{10,11},{11... | collective-permute-start | bytes 196616 | tf_op jit(solution)/shard_map/ppermute | solution.py:19
Sparse Core Ops, SparseCore 0:
  12.0 42.5 all-gather.2

commit v2 on v1

--- a/solution.py
+++ b/solution.py
@@ -11,6 +11,7 @@
 CHUNK_BYTES = 36 * 2**20
 
 highest = lax.Precision.HIGHEST
+precise = lax.Precision.HIGHEST
 
 
 def from_behind(x, axis, by):
@@ -47,18 +48,30 @@
     return out.reshape(shape)
 
 
-def to_signal(spec, inv, wc, ws):
+def local_signal(spec, inverse):
+    shape = spec.shape
+    flat = spec.reshape(shape[0] * shape[1], -1)
+    out = jnp.dot(inverse, flat, precision=precise)
+    return out.reshape((inverse.shape[0],) + shape[2:])
+
+
+def all_signal(spec, inv, cw, sw):
     shape = spec.shape
     block = shape[0] // 2
-    z = jnp.dot(inv, spec.reshape(shape[0], -1), precision=highest).reshape(shape)
+    size = shape[1] * block
+    z = jnp.dot(inv, spec.reshape(shape[0], -1), precision=precise).reshape(shape)
     tail = (1,) * (spec.ndim - 2)
-    wc = wc.reshape(wc.shape + tail)
-    ws = ws.reshape(ws.shape + tail)
-    return jnp.sum(wc * z[:block] + ws * z[block:], axis=1)
+    zr, zi = z[:block], z[block:]
+    rows = []
+    for p in range(cw.shape[0]):
+        c = cw[p].reshape(cw.shape[1:] + tail)
+        s = sw[p].reshape(sw.shape[1:] + tail)
+        rows.append(jnp.sum(c * zr + s * zi, axis=1))
+    return jnp.stack(rows) / size
 
 
 def chunk_work(x3, hx, tables):
-    cw, sw, fwd, inv, wc, ws = tables
+    cw, sw, fwd, inv, inverse = tables
     block = x3.shape[1]
     spec = to_spectrum(x3, cw, sw, fwd)
     hspec = to_spectrum(hx, cw, sw, fwd)
@@ -79,8 +92,8 @@
     pair = jnp.concatenate(
         [jnp.stack([conv_r, gm_r], axis=2), jnp.stack([conv_i, gm_i], axis=2)], axis=0
     )
-    both = to_signal(pair, inv, wc, ws)
-    fg = to_signal(jnp.concatenate([fg_r, fg_i], axis=0), inv, wc, ws)
+    both = local_signal(pair, inverse)
+    fg = all_signal(jnp.concatenate([fg_r, fg_i], axis=0), inv, cw, sw)
     return both[:, 0], both[:, 1], fg
 
 
@@ -104,20 +117,35 @@
     upstream = out_grad[0].astype(jnp.float32)
     weighted = upstream * query_back
     grad_query = upstream * conv_saved[0]
+    taps = filters[0].T
 
-    payload = jnp.concatenate([mixed_in, weighted, mixed_back, filters[0].T], axis=1)
-    full = lax.all_gather(payload, "ctx")
-    x3 = full[:, :, : 3 * channels].reshape(blocks, block, 3, channels)
-    hx = full[:, :, 3 * channels :]
+    ahead = jnp.concatenate([mixed_in, taps], axis=1)
+    behind = jnp.concatenate([weighted, taps], axis=1)
+    got_ahead = [from_behind(ahead, "ctx", s) for s in range(1, blocks)]
+    got_behind = [from_behind(behind, "ctx", -s) for s in range(1, blocks)]
+    pool = jnp.stack([jnp.zeros_like(ahead)] + got_ahead + got_behind)
+    ids = jnp.arange(blocks, dtype=jnp.int32)
+    pick = jnp.where(ids < place, place - ids, jnp.where(ids > place, blocks - 1 + ids - place, 0))
+    gathered = pool[pick]
+    mine = (ids == place)[:, None, None]
+    mixed_all = jnp.where(mine, mixed_in[None], gathered[:, :, :channels])
+    weighted_all = jnp.where(mine, weighted[None], gathered[:, :, :channels])
+    back_all = jnp.where(mine, mixed_back[None], 0.0)
+    hx = jnp.where(mine, taps[None], gathered[:, :, channels:])
+    x3 = jnp.stack([mixed_all, weighted_all, back_all], axis=2)
 
     cw, sw = outer_tables(blocks, block, outer)
     fwd, inv = inner_tables(block)
     pos = place * block + jnp.arange(block, dtype=jnp.int32)
-    prod = (pos[:, None] * jnp.arange(outer, dtype=jnp.int32)[None, :]) % size
+    freq = (
+        jnp.arange(outer, dtype=jnp.int32)[None, :]
+        + outer * jnp.arange(block, dtype=jnp.int32)[:, None]
+    )
+    prod = (pos[:, None, None] * freq[None]) % size
     theta = prod.astype(jnp.float32) * (2.0 * math.pi / size)
-    wc = jnp.cos(theta) / size
-    ws = -jnp.sin(theta) / size
-    tables = (cw, sw, fwd, inv, wc, ws)
+    inverse = jnp.concatenate([jnp.cos(theta), -jnp.sin(theta)], axis=1) / size
+    inverse = inverse.reshape(block, 2 * block * outer)
+    tables = (cw, sw, fwd, inv, inverse)
 
     per_group = 2 * block * outer * 4 * 4 * CPF * blocks
     gchunk = groups
@@ -133,7 +161,13 @@
         conv, grad_mixed, fg = lax.map(lambda a: chunk_work(a[0], a[1], tables), (xs, hs))
         conv = conv.transpose(1, 0, 2).reshape(block, channels)
         grad_mixed = grad_mixed.transpose(1, 0, 2).reshape(block, channels)
-        fg = fg.transpose(1, 0, 2).reshape(block, groups)
+        fg = fg.transpose(1, 2, 0, 3).reshape(blocks, block, groups)
+
+    lag_sum = fg[place]
+    for s in range(1, blocks):
+        dest = (place + s) % blocks
+        pairs = [(i, (i + s) % blocks) for i in range(blocks)]
+        lag_sum = lag_sum + lax.ppermute(fg[dest], "ctx", pairs)
 
     conv = conv * filter_scale
     grad_mixed = grad_mixed * filter_scale
@@ -143,7 +177,7 @@
     grad_value = grad_mixed * key_back
     grad_stack = jnp.stack([grad_query, grad_key, grad_value], axis=1).astype(jnp.bfloat16)
     prev_grad = from_behind(grad_stack[None], "pipe", -1)
-    filter_grad = (fg * filter_scale).T[None]
+    filter_grad = (lag_sum * filter_scale).T[None]
     return (next_input, prev_grad, filter_grad)
 
 

time: 117 us -> 86.1 us (0.74)
  waiting for transfers between devices: 45.9 us -> 9.87 us
  starting transfers between devices: 4.77 us -> 19.7 us
  between operations: 14.5 us -> 1.22 us
  other arithmetic: 19.7 us -> 13.7 us
  local copies, waits for them, and re-layouts: 16.6 us -> 21.9 us
  matrix products: 15 us -> 18.2 us
    all_gather x1 -> x0, waiting for transfers between devices: 41.2 us -> none  [on_device(): full = lax.all_gather(payload, 'ctx')]
    ppermute x2 -> x8, starting transfers between devices: 4.73 us -> 17.7 us  [from_behind(): return lax.ppermute(x, axis, pairs)]
    slice x8 -> x1, local copies, waits for them, and re-layouts: 11.8 us -> 0.01 us  [all_signal(): zr, zi = (z[:block], z[block:])]
    unnamed x42 -> x34, local copies, waits for them, and re-layouts: 3.82 us -> 12.7 us
    dot_general x0 -> x1, local copies, waits for them, and re-layouts: none -> 5.47 us  [local_signal(): out = jnp.dot(inverse, flat, precision=precise)]
    reduce_sum x2 -> x1, other arithmetic: 5.45 us -> 0.05 us  [all_signal(): rows.append(jnp.sum(c * zr + s * zi, axis=1))]
    ppermute x2 -> x8, waiting for transfers between devices: 4.63 us -> 9.71 us  [from_behind(): return lax.ppermute(x, axis, pairs)]
    dot_general x2, matrix products: 4.18 us -> 7.16 us  [the longest x1 6.76 us: local_signal(): out = jnp.dot(inverse, flat, precision=precise)]
  transfers between devices with their start and end apart: 3 -> 11, of which waited for: 2 -> 3; matrix products, arithmetic and copies ran while one was open for 3% -> 12% of each run, Pallas kernels for 0% -> 0%
where the time goes in v2:
time: 86.1 us; the launch traced here: 84.6 us
  local copies, waits for them, and re-layouts  21.9 us (25%)
  starting transfers between devices  19.7 us (23%)
  matrix products  18.2 us (21%)
  other arithmetic  13.7 us (16%)
  waiting for transfers between devices  9.87 us (11%)
  between operations  1.22 us (1%)
    ppermute x8, starting transfers between devices, from_behind(): return lax.ppermute(x, axis, pairs)  17.7 us
    unnamed x34, local copies, waits for them, and re-layouts  12.7 us
    dot_general x4, matrix products, to_spectrum(): out = jnp.dot(fwd, stacked.reshape(shape[0], -1), precision=highest)  11 us
    ppermute x8, waiting for transfers between devices, from_behind(): return lax.ppermute(x, axis, pairs)  9.71 us
    dot_general x1, matrix products, local_signal(): out = jnp.dot(inverse, flat, precision=precise)  6.76 us
    dot_general x1, local copies, waits for them, and re-layouts, local_signal(): out = jnp.dot(inverse, flat, precision=precise)  5.47 us
    concatenate x1, other arithmetic, chunk_work(): jnp.concatenate([jnp.stack([conv_r, gm_r], axis=2), jnp.stack([conv_i, gm...  2.3 us
    cos x1, other arithmetic, on_device(): inverse = jnp.concatenate([jnp.cos(theta), -jnp.sin(theta)], axis=1) / size  2.12 us
  transfers between devices with their start and end apart: 11, of which 3 were waited for; matrix products, arithmetic and copies ran while one was open for 12% of the time, Pallas kernels for 0%

profile of v2, /device:TPU:4, one launch (start us, length us, event | category | flops | bytes accessed | tf_op | source)
XLA Modules:
  0.0 84.6 jit_solution(3685147523548760715)
XLA Ops:
  0.6 0.9 %multiply_bitcast_fusion = f32[128,256]{1,0:T(8,128)S(1)} fusion(bf16[1,128,3,256]{3,1,2,0:T(8,128)(2,1)} %param.9), kind=kLoop, calls=%fused_computation.83 | loop fusion | flops 98304 | bytes 262144 | tf_op jit(solution)/shard_map/mul | solution.py:112
  1.5 0.8 copy.48
  2.3 0.9 %fusion.20 = f32[128,256]{1,0:T(8,128)S(1)} fusion(bf16[1,128,256]{2,1,0:T(8,128)(2,1)} %param.12, bf16[1,128,3,256]{3,1,2,0:T(8,128)(2,1)} %param.10), kind=kLoop, calls=%fused_computation.74 | loop fusion | flops 98304 | bytes 262144 | tf_op jit(solution)/shard_map/mul | solution.py:118
  3.2 0.8 pad_maximum_fusion.1
  4.0 4.2 %collective-permute-start = (f32[128,272]{1,0:T(8,128)}, f32[128,272]{1,0:T(8,128)}, u32[]{:S(2)}, u32[]{:S(2)}) collective-permute-start(f32[128,272]{1,0:T(8,128)} %get-tuple-element.36), channel_id=1, source_target_pairs={{0,8},{8,16},{16,24},{1,9},{9,17},{17,25},{2,10},{10,18},{18,26},{... | collective-permute-start | bytes 417800 | tf_op jit(solution)/shard_map/ppermute | solution.py:20
  8.2 3.8 %collective-permute-start.1 = (f32[128,272]{1,0:T(8,128)}, f32[128,272]{1,0:T(8,128)S(1)}, u32[]{:S(2)}, u32[]{:S(2)}) collective-permute-start(f32[128,272]{1,0:T(8,128)} %get-tuple-element.36), channel_id=1, source_target_pairs={{0,16},{8,24},{1,17},{9,25},{2,18},{10,26},{3,19},{11,27},{4,20},{... | collective-permute-start | bytes 417800 | tf_op jit(solution)/shard_map/ppermute | solution.py:20
  12.0 1.3 %collective-permute-start.2 = (f32[128,272]{1,0:T(8,128)}, f32[128,272]{1,0:T(8,128)S(1)}, u32[]{:S(2)}, u32[]{:S(2)}) collective-permute-start(f32[128,272]{1,0:T(8,128)} %get-tuple-element.36), channel_id=1, source_target_pairs={{0,24},{1,25},{2,26},{3,27},{4,28},{5,29},{6,30},{7,31}} | collective-permute-start | bytes 417800 | tf_op jit(solution)/shard_map/ppermute | solution.py:20
  13.3 1.3 %collective-permute-start.3 = (f32[128,272]{1,0:T(8,128)}, f32[128,272]{1,0:T(8,128)S(1)}, u32[]{:S(2)}, u32[]{:S(2)}) collective-permute-start(f32[128,272]{1,0:T(8,128)} %get-tuple-element.35), channel_id=1, source_target_pairs={{8,0},{16,8},{24,16},{9,1},{17,9},{25,17},{10,2},{18,10},{26,18},{... | collective-permute-start | bytes 417800 | tf_op jit(solution)/shard_map/ppermute | solution.py:20
  14.6 1.3 %collective-permute-start.4 = (f32[128,272]{1,0:T(8,128)}, f32[128,272]{1,0:T(8,128)S(1)}, u32[]{:S(2)}, u32[]{:S(2)}) collective-permute-start(f32[128,272]{1,0:T(8,128)} %get-tuple-element.35), channel_id=1, source_target_pairs={{16,0},{24,8},{17,1},{25,9},{18,2},{26,10},{19,3},{27,11},{20,4},{... | collective-permute-start | bytes 417800 | tf_op jit(solution)/shard_map/ppermute | solution.py:20
  15.9 0.9 %fusion.17 = f32[128,256]{1,0:T(8,128)S(1)} fusion(bf16[1,128,3,256]{3,1,2,0:T(8,128)(2,1)} %param.10), kind=kLoop, calls=%fused_computation.71 | loop fusion | flops 98304 | bytes 262144 | tf_op jit(solution)/shard_map/mul | solution.py:116
  16.8 1.0 %fusion.26 = (bf16[1,128,1,256]{3,1,2,0:T(8,128)(2,1)S(1)}, f32[128,256]{1,0:T(8,128)S(1)}) fusion(f32[1,128,256]{2,1,0:T(8,128)} %param.11, bf16[1,128,256]{2,1,0:T(8,128)(2,1)} %param.12, bf16[1,128,3,256]{3,1,2,0:T(8,128)(2,1)} %param.10), kind=kLoop, calls=%fused_computation.85 | loop fusion | flops 163840 | bytes 458752 | tf_op jit(solution)/shard_map/stack | solution.py:178
  17.8 0.1 iota_add_fusion
  17.9 0.1 broadcast_select_fusion
  18.0 0.0 copy-start.4
  18.0 0.0 copy-start.5
  18.0 0.0 copy-start.6
  18.1 0.0 copy-start.7
  18.1 2.1 %fusion.14 = (f32[128,128,8]{0,2,1:T(8,128)S(1)}, f32[128,128,8]{0,2,1:T(8,128)S(1)}) fusion(s32[128,8]{1,0:T(8,128)S(1)} %iota_add_fusion, s32[128]{0:T(128)S(1)} %iota_add_fusion.1), kind=kLoop, calls=%fused_computation.51 | loop fusion | flops 1966080 | bytes 1053184 | tf_op jit(solution)/shard_map/cos | solution.py:146
  20.3 0.7 broadcast_dynamic-update-slice_fusion
  21.0 1.5 %collective-permute-start.5 = (f32[128,272]{1,0:T(8,128)}, f32[128,272]{1,0:T(8,128)S(1)}, u32[]{:S(2)}, u32[]{:S(2)}) collective-permute-start(f32[128,272]{1,0:T(8,128)} %get-tuple-element.35), channel_id=1, source_target_pairs={{24,0},{25,1},{26,2},{27,3},{28,4},{29,5},{30,6},{31,7}} | collective-permute-start | bytes 417800 | tf_op jit(solution)/shard_map/ppermute | solution.py:20
  22.5 1.6 %bitcast_dynamic-update-slice_fusion.5 = f32[7,128,272]{2,1,0:T(8,128)} fusion(f32[7,128,272]{2,1,0:T(8,128)} %broadcast_dynamic-update-slice_fusion, f32[128,272]{1,0:T(8,128)} %collective-permute-done), kind=kLoop, calls=%fused_computation.60 | loop fusion | bytes 393216
  24.1 0.7 bitcast_dynamic-update-slice_fusion.4
  24.8 0.7 bitcast_dynamic-update-slice_fusion.3
  25.5 0.7 bitcast_dynamic-update-slice_fusion.2
  26.2 6.4 %collective-permute-done.4 = f32[128,272]{1,0:T(8,128)S(1)} collective-permute-done((f32[128,272]{1,0:T(8,128)}, f32[128,272]{1,0:T(8,128)S(1)}, u32[]{:S(2)}, u32[]{:S(2)}) %collective-permute-start.4) | collective-permute-done | bytes 139296 | tf_op jit(solution)/shard_map/ppermute | solution.py:20
  32.6 0.7 bitcast_dynamic-update-slice_fusion.1
  33.3 0.7 bitcast_dynamic-update-slice_fusion
  34.0 1.9 %gather_fusion = f32[4,128,272]{2,1,0:T(8,128)S(1)} fusion(f32[7,128,272]{2,1,0:T(8,128)} %bitcast_dynamic-update-slice_fusion, s32[1024]{0:T(1024)S(1)} %pad_clamp_fusion), kind=kCustom, calls=%fused_computation | custom fusion | bytes 1114128 | tf_op jit(solution)/shard_map/gather | solution.py:129
  35.9 0.1 slice_select_fusion
  36.0 0.1 copy.49
  36.1 0.1 copy.50
  36.1 0.1 copy.51
  36.2 0.1 copy.52
  36.3 0.0 copy-done.6
  36.4 0.3 fusion.38
  36.7 0.3 fusion
  37.0 0.2 select_bitcast_fusion.1
  37.2 0.1 pad_maximum_fusion
  37.3 0.1 slice_bitcast_fusion.9
  37.4 0.2 copy.53
  37.6 0.2 copy.54
  37.7 0.2 copy.55
  37.9 0.2 copy.56
  38.1 1.6 %multiply_add_fusion = (f32[128,8,3,256]{0,3,2,1:T(8,128)S(1)}, f32[128,8,3,256]{0,3,2,1:T(8,128)S(1)}) fusion(f32[128,8]{0,1:T(8,128)S(1)} %copy-done.4, f32[128,8]{0,1:T(8,128)S(1)} %copy-done.11, f32[128,8]{0,1:T(8,128)S(1)} %copy-done.10, f32[128,8]{0,1:T(8,128)S(1)} %copy-done.9, f32[128,3,256]{0,2,1:T(8,128)S(1)} %copy.56, f32[128,3,256]{0,2,1:T(8,128)S(1)} %copy.55, ...), kind=kLoop, calls=%fused_computation.3 | loop fusion | flops 11010048 | bytes 7897088 | tf_op jit(solution)/shard_map/add | solution.py:44
  39.7 5.0 %fusion.39 = f32[6144,256]{1,0:T(8,128)S(1)} fusion(f32[128,6144]{0,1:T(8,128)S(1)} %bitcast.220, f32[256,128]{1,0:T(8,128)S(1)} %copy-done.2), kind=kOutput, calls=%fused_computation.121 | convolution fusion | flops 2415919104 | bytes 9568256 | tf_op jit(solution)/shard_map/dot_general | solution.py:47
  44.7 5.4 %convolution_add_fusion = f32[6144,256]{1,0:T(8,128)S(1)} fusion(f32[6144,256]{1,0:T(8,128)S(1)} %fusion.39, f32[128,6144]{0,1:T(8,128)S(1)} %bitcast.224, f32[256,128]{1,0:T(8,128)S(1)} %copy-done.1), kind=kOutput, calls=%fused_computation.1 | convolution fusion | flops 2417491968 | bytes 15859712 | tf_op jit(solution)/shard_map/dot_general | solution.py:47
  50.2 0.7 fusion.1
  50.9 2.3 %maximum_maximum_fusion = f32[256,8,2,256]{0,3,1,2:T(8,128)} fusion(f32[128,8,1,256]{0,3,1,2:T(8,128)S(1)} %get-tuple-element.8, f32[128,8,1,256]{0,3,1,2:T(8,128)S(1)} %get-tuple-element.10, f32[128,8,1,256]{0,3,1,2:T(8,128)S(1)} %get-tuple-element.9, f32[128,8,1,256]{0,3,1,2:T(8,128)S(1)} %get-tuple-element.7), kind=kLoop, calls=%fused_computation.2 | loop fusion | flops 3145728 | bytes 8388608 | tf_op jit(solution)/shard_map/concatenate | solution.py:92
  53.2 5.5 %copy.74 = f32[256,8,2,256]{3,1,2,0:T(8,128)} copy(f32[256,8,2,256]{0,3,1,2:T(8,128)} %maximum_maximum_fusion) | data formatting | bytes 8388608
  58.7 5.5 %copy.62 = f32[512,2048]{1,0:T(8,128)} copy(f32[512,2048]{0,1:T(8,128)} %bitcast.223) | data formatting | bytes 8388608 | tf_op jit(solution)/shard_map/dot_general | solution.py:54
  64.1 6.8 %fusion.6 = f32[128,2,256]{2,0,1:T(8,128)S(1)} fusion(f32[2,256,2048]{2,1,0:T(8,128)} %bitcast.222, f32[128,128,8]{0,2,1:T(8,128)S(1)} %get-tuple-element.32, f32[128,128,8]{0,2,1:T(8,128)S(1)} %get-tuple-element.31), kind=kOutput, calls=%fused_computation.28 | convolution fusion | flops 1611137024 | bytes 5505024 | tf_op jit(solution)/shard_map/dot_general | solution.py:54
  71.0 0.9 %fusion.25 = bf16[1,128,256]{2,1,0:T(8,128)(2,1)S(1)} fusion(f32[128,2,256]{2,0,1:T(8,128)S(1)} %fusion.6, bf16[1,128,3,256]{3,1,2,0:T(8,128)(2,1)} %param.9), kind=kLoop, calls=%fused_computation.81 | loop fusion | flops 131072 | bytes 262144 | tf_op jit(solution)/shard_map/convert_element_type | solution.py:174
  71.8 0.2 reduce_sum.54
  72.0 0.2 reduce_sum.55
  72.2 0.4 fusion.40
  72.7 0.1 collective-permute-start.10
  72.8 2.0 %collective-permute-start.8 = (f32[128,16]{0,1:T(8,128)S(1)}, f32[128,16]{0,1:T(8,128)S(1)}, u32[]{:S(2)}, u32[]{:S(2)}) collective-permute-start(f32[128,16]{0,1:T(8,128)S(1)} %get-tuple-element.37), channel_id=1, source_target_pairs={{0,8},{8,16},{16,24},{24,0},{1,9},{9,17},{17,25},{25,1},{2,10},{10... | collective-permute-start | bytes 24584 | tf_op jit(solution)/shard_map/ppermute | solution.py:170
  74.8 1.9 %collective-permute-start.7 = (bf16[1,128,3,256]{3,1,2,0:T(8,128)(2,1)S(1)}, bf16[1,128,3,256]{3,1,2,0:T(8,128)(2,1)S(1)}, u32[]{:S(2)}, u32[]{:S(2)}) collective-permute-start(bf16[1,128,3,256]{3,1,2,0:T(8,128)(2,1)S(1)} %pad_maximum_fusion.3), channel_id=1, source_target_pairs={{1,0},{2,1},{3,2},{4,3},{5,4},{6,5},{7,6},{9,8},{10,9},{11,10},{12... | collective-permute-start | bytes 589832 | tf_op jit(solution)/shard_map/ppermute | solution.py:20
  76.8 2.4 %collective-permute-start.6 = (bf16[1,128,256]{2,1,0:T(8,128)(2,1)S(1)}, bf16[1,128,256]{2,1,0:T(8,128)(2,1)S(1)}, u32[]{:S(2)}, u32[]{:S(2)}) collective-permute-start(bf16[1,128,256]{2,1,0:T(8,128)(2,1)S(1)} %fusion.25), channel_id=1, source_target_pairs={{0,1},{1,2},{2,3},{3,4},{4,5},{5,6},{6,7},{8,9},{9,10},{10,11},{11... | collective-permute-start | bytes 196616 | tf_op jit(solution)/shard_map/ppermute | solution.py:20
  79.2 0.2 collective-permute-done.9
  79.4 0.6 fusion.32
  80.0 3.3 %collective-permute-done.6 = bf16[1,128,256]{2,1,0:T(8,128)(2,1)S(1)} collective-permute-done((bf16[1,128,256]{2,1,0:T(8,128)(2,1)S(1)}, bf16[1,128,256]{2,1,0:T(8,128)(2,1)S(1)}, u32[]{:S(2)}, u32[]{:S(2)}) %collective-permute-start.6) | collective-permute-done | bytes 65568 | tf_op jit(solution)/shard_map/ppermute | solution.py:20
  83.3 0.6 copy.84
  83.9 0.7 copy.85
  (43 shorter events, 0.3 us)
Async XLA Ops:
  4.0 17.0 %collective-permute-start = (f32[128,272]{1,0:T(8,128)}, f32[128,272]{1,0:T(8,128)}, u32[]{:S(2)}, u32[]{:S(2)}) collective-permute-start(f32[128,272]{1,0:T(8,128)} %get-tuple-element.36), channel_id=1, source_target_pairs={{0,8},{8,16},{16,24},{1,9},{9,17},{17,25},{2,10},{10,18},{18,26},{... | collective-permute-start | bytes 417800 | tf_op jit(solution)/shard_map/ppermute | solution.py:20
  8.2 16.0 %collective-permute-start.1 = (f32[128,272]{1,0:T(8,128)}, f32[128,272]{1,0:T(8,128)S(1)}, u32[]{:S(2)}, u32[]{:S(2)}) collective-permute-start(f32[128,272]{1,0:T(8,128)} %get-tuple-element.36), channel_id=1, source_target_pairs={{0,16},{8,24},{1,17},{9,25},{2,18},{10,26},{3,19},{11,27},{4,20},{... | collective-permute-start | bytes 417800 | tf_op jit(solution)/shard_map/ppermute | solution.py:20
  12.0 12.8 %collective-permute-start.2 = (f32[128,272]{1,0:T(8,128)}, f32[128,272]{1,0:T(8,128)S(1)}, u32[]{:S(2)}, u32[]{:S(2)}) collective-permute-start(f32[128,272]{1,0:T(8,128)} %get-tuple-element.36), channel_id=1, source_target_pairs={{0,24},{1,25},{2,26},{3,27},{4,28},{5,29},{6,30},{7,31}} | collective-permute-start | bytes 417800 | tf_op jit(solution)/shard_map/ppermute | solution.py:20
  13.3 12.2 %collective-permute-start.3 = (f32[128,272]{1,0:T(8,128)}, f32[128,272]{1,0:T(8,128)S(1)}, u32[]{:S(2)}, u32[]{:S(2)}) collective-permute-start(f32[128,272]{1,0:T(8,128)} %get-tuple-element.35), channel_id=1, source_target_pairs={{8,0},{16,8},{24,16},{9,1},{17,9},{25,17},{10,2},{18,10},{26,18},{... | collective-permute-start | bytes 417800 | tf_op jit(solution)/shard_map/ppermute | solution.py:20
  14.6 18.0 %collective-permute-start.4 = (f32[128,272]{1,0:T(8,128)}, f32[128,272]{1,0:T(8,128)S(1)}, u32[]{:S(2)}, u32[]{:S(2)}) collective-permute-start(f32[128,272]{1,0:T(8,128)} %get-tuple-element.35), channel_id=1, source_target_pairs={{16,0},{24,8},{17,1},{25,9},{18,2},{26,10},{19,3},{27,11},{20,4},{... | collective-permute-start | bytes 417800 | tf_op jit(solution)/shard_map/ppermute | solution.py:20
  18.0 18.3 %copy-start.4 = (f32[128,8]{0,1:T(8,128)S(1)}, f32[128,8]{0,1:T(8,128)}, u32[]{:S(2)}) copy-start(f32[128,8]{0,1:T(8,128)} %constant.100) | copy-start | bytes 12292
  18.0 18.3 %copy-start.5 = (f32[128,8]{0,1:T(8,128)S(1)}, f32[128,8]{0,1:T(8,128)}, u32[]{:S(2)}) copy-start(f32[128,8]{0,1:T(8,128)} %constant.85) | copy-start | bytes 12292
  18.0 18.3 %copy-start.6 = (f32[128,8]{0,1:T(8,128)S(1)}, f32[128,8]{0,1:T(8,128)}, u32[]{:S(2)}) copy-start(f32[128,8]{0,1:T(8,128)} %constant.87) | copy-start | bytes 12292
  18.1 18.3 %copy-start.7 = (f32[128,8]{0,1:T(8,128)S(1)}, f32[128,8]{0,1:T(8,128)}, u32[]{:S(2)}) copy-start(f32[128,8]{0,1:T(8,128)} %constant.89) | copy-start | bytes 12292
  18.1 18.3 %copy-start.8 = (f32[128,8]{0,1:T(8,128)S(1)}, f32[128,8]{0,1:T(8,128)}, u32[]{:S(2)}) copy-start(f32[128,8]{0,1:T(8,128)} %constant.91) | copy-start | bytes 12292
  18.1 18.3 %copy-start.9 = (f32[128,8]{0,1:T(8,128)S(1)}, f32[128,8]{0,1:T(8,128)}, u32[]{:S(2)}) copy-start(f32[128,8]{0,1:T(8,128)} %constant.94) | copy-start | bytes 12292
  18.1 18.3 %copy-start.10 = (f32[128,8]{0,1:T(8,128)S(1)}, f32[128,8]{0,1:T(8,128)}, u32[]{:S(2)}) copy-start(f32[128,8]{0,1:T(8,128)} %constant.96) | copy-start | bytes 12292
  18.1 18.3 %copy-start.11 = (f32[128,8]{0,1:T(8,128)S(1)}, f32[128,8]{0,1:T(8,128)}, u32[]{:S(2)}) copy-start(f32[128,8]{0,1:T(8,128)} %constant.98) | copy-start | bytes 12292
  20.2 16.2 %copy-start.2 = (f32[256,128]{1,0:T(8,128)S(1)}, f32[256,128]{1,0:T(8,128)}, u32[]{:S(2)}) copy-start(f32[256,128]{1,0:T(8,128)} %constant.92) | copy-start | bytes 393220
  20.3 16.5 %copy-start.1 = (f32[256,128]{1,0:T(8,128)S(1)}, f32[256,128]{1,0:T(8,128)}, u32[]{:S(2)}) copy-start(f32[256,128]{1,0:T(8,128)} %constant.101) | copy-start | bytes 393220
  21.0 12.3 %collective-permute-start.5 = (f32[128,272]{1,0:T(8,128)}, f32[128,272]{1,0:T(8,128)S(1)}, u32[]{:S(2)}, u32[]{:S(2)}) collective-permute-start(f32[128,272]{1,0:T(8,128)} %get-tuple-element.35), channel_id=1, source_target_pairs={{24,0},{25,1},{26,2},{27,3},{28,4},{29,5},{30,6},{31,7}} | collective-permute-start | bytes 417800 | tf_op jit(solution)/shard_map/ppermute | solution.py:20
  64.1 6.8 %copy-start = (bf16[1,128,3,256]{3,1,2,0:T(8,128)(2,1)S(1)}, bf16[1,128,3,256]{3,1,2,0:T(8,128)(2,1)}, u32[]{:S(2)}) copy-start(bf16[1,128,3,256]{3,1,2,0:T(8,128)(2,1)} %param.10) | copy-start | bytes 589828
  64.1 8.1 %copy-start.3 = (f32[256,256]{1,0:T(8,128)S(1)}, f32[256,256]{1,0:T(8,128)}, u32[]{:S(2)}) copy-start(f32[256,256]{1,0:T(8,128)} %constant.78.clone) | copy-start | bytes 786436
  72.7 6.5 %collective-permute-start.10 = (f32[128,16]{0,1:T(8,128)S(1)}, f32[128,16]{0,1:T(8,128)S(1)}, u32[]{:S(2)}, u32[]{:S(2)}) collective-permute-start(f32[128,16]{0,1:T(8,128)S(1)} %get-tuple-element.38), channel_id=1, source_target_pairs={{0,24},{8,0},{16,8},{24,16},{1,25},{9,1},{17,9},{25,17},{2,26},{10... | collective-permute-start | bytes 24584 | tf_op jit(solution)/shard_map/ppermute | solution.py:170
  72.8 6.4 %collective-permute-start.8 = (f32[128,16]{0,1:T(8,128)S(1)}, f32[128,16]{0,1:T(8,128)S(1)}, u32[]{:S(2)}, u32[]{:S(2)}) collective-permute-start(f32[128,16]{0,1:T(8,128)S(1)} %get-tuple-element.37), channel_id=1, source_target_pairs={{0,8},{8,16},{16,24},{24,0},{1,9},{9,17},{17,25},{25,1},{2,10},{10... | collective-permute-start | bytes 24584 | tf_op jit(solution)/shard_map/ppermute | solution.py:170
  74.8 4.5 %collective-permute-start.9 = (f32[128,16]{0,1:T(8,128)S(1)}, f32[128,16]{0,1:T(8,128)S(1)}, u32[]{:S(2)}, u32[]{:S(2)}) collective-permute-start(f32[128,16]{0,1:T(8,128)S(1)} %get-tuple-element.39), channel_id=1, source_target_pairs={{0,16},{8,24},{16,0},{24,8},{1,17},{9,25},{17,1},{25,9},{2,18},{10... | collective-permute-start | bytes 24584 | tf_op jit(solution)/shard_map/ppermute | solution.py:170
  74.8 8.4 %collective-permute-start.7 = (bf16[1,128,3,256]{3,1,2,0:T(8,128)(2,1)S(1)}, bf16[1,128,3,256]{3,1,2,0:T(8,128)(2,1)S(1)}, u32[]{:S(2)}, u32[]{:S(2)}) collective-permute-start(bf16[1,128,3,256]{3,1,2,0:T(8,128)(2,1)S(1)} %pad_maximum_fusion.3), channel_id=1, source_target_pairs={{1,0},{2,1},{3,2},{4,3},{5,4},{6,5},{7,6},{9,8},{10,9},{11,10},{12... | collective-permute-start | bytes 589832 | tf_op jit(solution)/shard_map/ppermute | solution.py:20
  76.8 6.5 %collective-permute-start.6 = (bf16[1,128,256]{2,1,0:T(8,128)(2,1)S(1)}, bf16[1,128,256]{2,1,0:T(8,128)(2,1)S(1)}, u32[]{:S(2)}, u32[]{:S(2)}) collective-permute-start(bf16[1,128,256]{2,1,0:T(8,128)(2,1)S(1)} %fusion.25), channel_id=1, source_target_pairs={{0,1},{1,2},{2,3},{3,4},{4,5},{5,6},{6,7},{8,9},{9,10},{10,11},{11... | collective-permute-start | bytes 196616 | tf_op jit(solution)/shard_map/ppermute | solution.py:20

commit v3 on v1

v3 whole, which is shorter than its diff:
```python
import math

import numpy as np

import jax
import jax.numpy as jnp
from jax import lax
from jax.sharding import PartitionSpec as P

CPF = 16
CHUNK_BYTES = 36 * 2**20
STEPWISE = 4

highest = lax.Precision.HIGHEST
precise = lax.Precision.HIGH


def from_behind(x, axis, by):
    devices = lax.axis_size(axis)
    pairs = [(i, i + by) for i in range(devices) if 0 <= i + by < devices]
    return lax.ppermute(x, axis, pairs)


def inner_tables(block):
    ids = np.arange(block)
    theta = 2.0 * np.pi * ((ids[:, None] * ids[None, :]) % block) / block
    cos, sin = np.cos(theta), np.sin(theta)
    fwd = np.block([[cos, -sin], [sin, cos]])
    inv = np.block([[cos, sin], [-sin, cos]])
    return jnp.asarray(fwd, jnp.float32), jnp.asarray(inv, jnp.float32)


def outer_tables(blocks, block, outer):
    size = outer * block
    pos = np.arange(blocks)[:, None, None] * block + np.arange(block)[None, None, :]
    prod = (pos * np.arange(outer)[None, :, None]) % size
    theta = 2.0 * np.pi * prod / size
    return jnp.asarray(np.cos(theta), jnp.float32), jnp.asarray(-np.sin(theta), jnp.float32)


def outer_step(parts, cw, sw, index):
    c = lax.dynamic_index_in_dim(cw, index, keepdims=False)
    s = lax.dynamic_index_in_dim(sw, index, keepdims=False)
    tail = (1,) * (parts.ndim - 1)
    c = c.reshape(c.shape[:1] + tail + c.shape[1:])
    s = s.reshape(s.shape[:1] + tail + s.shape[1:])
    return jnp.concatenate([c * parts[None], s * parts[None]], axis=-1)


def inner_step(y, mat):
    shape = y.shape
    return jnp.dot(y.reshape(-1, shape[-1]), mat, precision=precise).reshape(shape)


def chunk_work(local3, common, hsum, tables):
    cw, sw, fwd, inv, inverse, place = tables
    block = local3.shape[-1]
    outer = cw.shape[1]
    own = outer_step(local3, cw, sw, place)
    y = jnp.stack([own[:, 0] + common, own[:, 1] + common, own[:, 2]], axis=1)
    spec = inner_step(y, fwd)
    hspec = jnp.repeat(inner_step(hsum, fwd), CPF, axis=1)
    hr, hi = hspec[..., :block], hspec[..., block:]
    mr, mi = spec[:, 0, :, :block], spec[:, 0, :, block:]
    wr, wi = spec[:, 1, :, :block], spec[:, 1, :, block:]
    br, bi = spec[:, 2, :, :block], spec[:, 2, :, block:]
    conv = jnp.concatenate([hr * mr - hi * mi, hr * mi + hi * mr], axis=-1)
    gm = jnp.concatenate([hr * wr + hi * wi, hr * wi - hi * wr], axis=-1)
    fgs = jnp.concatenate([br * wr + bi * wi, br * wi - bi * wr], axis=-1)
    fgs = fgs.reshape(outer, -1, CPF, 2 * block).sum(axis=2)
    pair = jnp.stack([conv, gm]).transpose(0, 2, 1, 3)
    rows = pair.shape[0] * pair.shape[1]
    both = jnp.dot(pair.reshape(rows, -1), inverse, precision=precise)
    both = both.reshape(2, -1, block)
    z = inner_step(fgs, inv)
    zr, zi = z[..., :block], z[..., block:]
    fg = jnp.stack(
        [jnp.sum(cw[p][:, None] * zr + sw[p][:, None] * zi, axis=0) for p in range(cw.shape[0])]
    )
    return both[0], both[1], fg / (outer * block)


def on_device(qkv_in, qkv_saved, conv_saved, out_grad, filters):
    blocks = lax.axis_size("ctx")
    place = lax.axis_index("ctx")
    block = qkv_in.shape[1]
    channels = qkv_in.shape[3]
    groups = filters.shape[1]
    length = blocks * block
    outer = 2 * blocks
    size = outer * block
    filter_scale = (CPF * length) ** (-0.5)

    query_in = qkv_in[0, :, 0].astype(jnp.float32)
    mixed_in = qkv_in[0, :, 1].astype(jnp.float32) * qkv_in[0, :, 2].astype(jnp.float32)
    query_back = qkv_saved[0, :, 0].astype(jnp.float32)
    key_back = qkv_saved[0, :, 1].astype(jnp.float32)
    value_back = qkv_saved[0, :, 2].astype(jnp.float32)
    mixed_back = key_back * value_back
    upstream = out_grad[0].astype(jnp.float32)
    weighted = upstream * query_back
    grad_query = upstream * conv_saved[0]
    taps = filters[0]

    cw, sw = outer_tables(blocks, block, outer)
    fwd, inv = inner_tables(block)

    mixed_rows = mixed_in.T
    weighted_rows = weighted.T
    received = []
    for s in range(1, blocks):
        dest = place + s
        first = jnp.where(dest < blocks, mixed_rows, weighted_rows)
        payload = jnp.concatenate([first, taps], axis=0)
        pairs = [(i, (i + s) % blocks) for i in range(blocks)]
        received.append(lax.ppermute(payload, "ctx", pairs))
    hsum = outer_step(taps, cw, sw, place)
    if blocks <= STEPWISE:
        common = 0.0
        for s, got in enumerate(received, start=1):
            part = outer_step(got, cw, sw, (place - s) % blocks)
            common = common + part[:, :channels]
            hsum = hsum + part[:, channels:]
    else:
        got = jnp.stack(received)
        sources = (place - jnp.arange(1, blocks, dtype=jnp.int32)) % blocks
        weights = jnp.concatenate([cw[sources], sw[sources]], axis=-1)
        both = jnp.concatenate([got, got], axis=-1)
        part = jnp.einsum("sfp,scp->fcp", weights, both, precision=highest)
        common = part[:, :channels]
        hsum = hsum + part[:, channels:]
    local3 = jnp.stack([mixed_rows, weighted_rows, mixed_back.T])

    pos = place * block + jnp.arange(block, dtype=jnp.int32)
    freq = (
        jnp.arange(outer, dtype=jnp.int32)[:, None, None]
        + outer * jnp.arange(block, dtype=jnp.int32)[None, None, :]
    )
    prod = (freq * pos[None, :, None]) % size
    theta = prod.astype(jnp.float32) * (2.0 * math.pi / size)
    inverse = jnp.concatenate([jnp.cos(theta), -jnp.sin(theta)], axis=-1) / size
    inverse = inverse.transpose(0, 2, 1).reshape(outer * 2 * block, block)
    tables = (cw, sw, fwd, inv, inverse, place)

    per_group = 2 * block * outer * 4 * 4 * CPF * blocks
    gchunk = groups
    while gchunk > 1 and gchunk * per_group > CHUNK_BYTES and groups % (gchunk // 2) == 0:
        gchunk //= 2
    nchunk = groups // gchunk
    if nchunk == 1:
        conv, grad_mixed, fg = chunk_work(local3, common, hsum, tables)
    else:
        cc = gchunk * CPF
        ls = local3.reshape(3, nchunk, cc, block).transpose(1, 0, 2, 3)
        cs = common.reshape(outer, nchunk, cc, 2 * block).transpose(1, 0, 2, 3)
        hs = hsum.reshape(outer, nchunk, gchunk, 2 * block).transpose(1, 0, 2, 3)
        conv, grad_mixed, fg = lax.map(lambda a: chunk_work(a[0], a[1], a[2], tables), (ls, cs, hs))
        conv = conv.reshape(channels, block)
        grad_mixed = grad_mixed.reshape(channels, block)
        fg = fg.transpose(1, 0, 2, 3).reshape(blocks, groups, block)

    lag_sum = fg[place]
    for s in range(1, blocks):
        dest = (place + s) % blocks
        pairs = [(i, (i + s) % blocks) for i in range(blocks)]
        lag_sum = lag_sum + lax.ppermute(fg[dest], "ctx", pairs)

    conv = conv.T * filter_scale
    grad_mixed = grad_mixed.T * filter_scale
    result = (query_in * conv).astype(jnp.bfloat16)
    next_input = from_behind(result[None], "pipe", 1)
    grad_key = grad_mixed * value_back
    grad_value = grad_mixed * key_back
    grad_stack = jnp.stack([grad_query, grad_key, grad_value], axis=1).astype(jnp.bfloat16)
    prev_grad = from_behind(grad_stack[None], "pipe", -1)
    filter_grad = (lag_sum * filter_scale)[None]
    return (next_input, prev_grad, filter_grad)


def solution(mesh):
    return jax.shard_map(
        on_device,
        mesh=mesh,
        in_specs=(
            P("pipe", "ctx", None, None),
            P("pipe", "ctx", None, None),
            P("pipe", "ctx", None),
            P("pipe", "ctx", None),
            P("pipe", None, "ctx"),
        ),
        out_specs=(P("pipe", "ctx", None), P("pipe", "ctx", None, None), P("pipe", None, "ctx")),
        check_vma=False,
    )
```

time: 117 us -> 55.2 us (0.47)
  the two profiles are of different devices: /device:TPU:4 before, /device:TPU:3 now
where the time goes in v3:
time: 55.2 us; the launch traced here: 54.8 us
  other arithmetic  15.8 us (29%)
  starting transfers between devices  15.6 us (28%)
  local copies, waits for them, and re-layouts  12.3 us (22%)
  matrix products  5.21 us (9%)
  waiting for transfers between devices  4.59 us (8%)
  between operations  1.29 us (2%)
    unnamed x49, local copies, waits for them, and re-layouts  7.2 us
    ppermute x2, starting transfers between devices, from_behind(): return lax.ppermute(x, axis, pairs)  5.98 us
    mul x5, other arithmetic, outer_step(): return jnp.concatenate([c * parts[None], s * parts[None]], axis=-1)  5.7 us
    ppermute x3, starting transfers between devices, on_device(): lag_sum = lag_sum + lax.ppermute(fg[dest], 'ctx', pairs)  4.96 us
    ppermute x3, starting transfers between devices, on_device(): received.append(lax.ppermute(payload, 'ctx', pairs))  4.67 us
    ppermute x2, waiting for transfers between devices, from_behind(): return lax.ppermute(x, axis, pairs)  4.57 us
    dot_general x3, matrix products, inner_step(): jnp.dot(y.reshape(-1, shape[-1]), mat, precision=precise).reshape(shape)  3.39 us
    cos x1, other arithmetic, on_device(): inverse = jnp.concatenate([jnp.cos(theta), -jnp.sin(theta)], axis=-1) / size  3.21 us
  transfers between devices with their start and end apart: 8, of which 1 were waited for; matrix products, arithmetic and copies ran while one was open for 35% of the time, Pallas kernels for 0%

profile of v3, /device:TPU:3, one launch (start us, length us, event | category | flops | bytes accessed | tf_op | source)
XLA Modules:
  0.0 54.8 jit_solution(7422889562173073917)
XLA Ops:
  0.6 0.0 copy-start.8
  0.6 0.0 copy-start.9
  0.7 1.0 %copy.30 = bf16[1,128,256]{1,2,0:T(8,128)(2,1)S(1)} copy(bf16[1,128,256]{2,1,0:T(8,128)(2,1)} %param.12) | data formatting | bytes 131072 | tf_op args[3]
  1.7 0.9 %fusion.58 = (bf16[1,128,1,256]{3,1,2,0:T(8,128)(2,1)S(1)}, bf16[1,128,1,256]{3,1,2,0:T(8,128)(2,1)S(1)}, bf16[1,128,1,256]{3,1,2,0:T(8,128)(2,1)S(1)}) fusion(bf16[1,128,3,256]{3,1,2,0:T(8,128)(2,1)} %param.9), kind=kLoop, calls=%fused_computation.136 | loop fusion | bytes 393216 | tf_op jit(solution)/shard_map/slice | solution.py:94
  2.6 0.1 copy.45
  2.7 0.1 copy.46
  2.9 0.9 %fusion.59 = (bf16[1,128,1,256]{3,1,2,0:T(8,128)(2,1)S(1)}, bf16[1,128,1,256]{3,1,2,0:T(8,128)(2,1)S(1)}, bf16[1,128,1,256]{3,1,2,0:T(8,128)(2,1)S(1)}) fusion(bf16[1,128,3,256]{3,1,2,0:T(8,128)(2,1)} %param.10), kind=kLoop, calls=%fused_computation.137 | loop fusion | bytes 393216 | tf_op jit(solution)/shard_map/slice | solution.py:96
  3.8 0.1 copy.47
  3.9 0.1 bitcast_select_fusion.2
  4.0 1.4 %pad_maximum_fusion.6 = (f32[272,128]{1,0:T(8,128)}, f32[272,128]{1,0:T(8,128)}, f32[272,128]{1,0:T(8,128)}) fusion(f32[16,128]{1,0:T(8,128)} %bitcast.198, f32[256,128]{1,0:T(8,128)S(1)} %get-tuple-element.26, f32[256,128]{1,0:T(8,128)S(1)} %get-tuple-element.28, f32[256,128]{1,0:T(8,128)S(1)} %get-tuple-element.27), kind=kLoop, calls=%fused_computation.66 | loop fusion | flops 104448 | bytes 819200 | tf_op jit(solution)/shard_map/concatenate | solution.py:114
  5.4 1.3 %collective-permute-start = (f32[272,128]{1,0:T(8,128)}, f32[272,128]{1,0:T(8,128)}, u32[]{:S(2)}, u32[]{:S(2)}) collective-permute-start(f32[272,128]{1,0:T(8,128)} %get-tuple-element.54), channel_id=1, source_target_pairs={{0,8},{8,16},{16,24},{24,0},{1,9},{9,17},{17,25},{25,1},{2,10},{10... | collective-permute-start | bytes 417800 | tf_op jit(solution)/shard_map/ppermute | solution.py:116
  6.7 2.3 %collective-permute-start.1 = (f32[272,128]{1,0:T(8,128)}, f32[272,128]{1,0:T(8,128)}, u32[]{:S(2)}, u32[]{:S(2)}) collective-permute-start(f32[272,128]{1,0:T(8,128)} %get-tuple-element.55), channel_id=1, source_target_pairs={{0,16},{8,24},{16,0},{24,8},{1,17},{9,25},{17,1},{25,9},{2,18},{10... | collective-permute-start | bytes 417800 | tf_op jit(solution)/shard_map/ppermute | solution.py:116
  9.0 1.1 %collective-permute-start.2 = (f32[272,128]{1,0:T(8,128)}, f32[272,128]{1,0:T(8,128)}, u32[]{:S(2)}, u32[]{:S(2)}) collective-permute-start(f32[272,128]{1,0:T(8,128)} %get-tuple-element.56), channel_id=1, source_target_pairs={{0,24},{8,0},{16,8},{24,16},{1,25},{9,1},{17,9},{25,17},{2,26},{10... | collective-permute-start | bytes 417800 | tf_op jit(solution)/shard_map/ppermute | solution.py:116
  10.1 0.1 copy.40
  10.2 0.7 %fusion.49 = bf16[1,128,1,256]{1,3,2,0:T(8,128)(2,1)} fusion(f32[1,128,256]{1,2,0:T(8,128)S(1)} %copy.40, bf16[1,128,256]{1,2,0:T(8,128)(2,1)S(1)} %copy.30), kind=kLoop, calls=%fused_computation.106 | loop fusion | flops 98304 | bytes 262144 | tf_op jit(solution)/shard_map/stack | solution.py:174
  10.9 0.1 copy.48
  11.0 0.1 copy.49
  11.2 0.6 %dynamic-slice_bitcast_fusion.7 = (f32[8,128]{1,0:T(8,128)S(1)}, f32[8,128]{1,0:T(8,128)S(1)}, f32[8,128]{1,0:T(8,128)S(1)}, f32[8,128]{1,0:T(8,128)}, f32[8,128...) fusion(f32[4,8,128]{2,1,0:T(8,128)S(1)} %copy-done.8, s32[]{:T(128)S(6)} %select_n.84, ...), kind=kLoop, calls=%fused_computation.127 | loop fusion | bytes 65552 | tf_op jit(solution)/shard_map/mul | solution.py:47
  11.9 2.4 %broadcast_multiply_fusion = (f32[8,3,256,128]{3,2,1,0:T(8,128)S(1)}, f32[8,3,256,128]{3,2,1,0:T(8,128)}) fusion(f32[8,128]{1,0:T(8,128)S(1)} %get-tuple-element.49, f32[3,256,128]{2,1,0:T(8,128)S(1)} %pad_maximum_fusion.3, f32[8,128]{1,0:T(8,128)S(1)} %get-tuple-element.61), kind=kLoop, calls=%fused_computation.32 | loop fusion | flops 1572864 | bytes 6692864 | tf_op jit(solution)/shard_map/mul | solution.py:47
  14.2 3.2 %fusion.24 = (f32[8,128,128]{1,2,0:T(8,128)}, f32[8,128,128]{1,2,0:T(8,128)}) fusion(s32[128]{0:T(128)S(1)} %iota_add_fusion.1, s32[8,128]{1,0:T(8,128)S(1)} %iota_add_fusion), kind=kLoop, calls=%fused_computation.63 | loop fusion | flops 1966080 | bytes 1053184 | tf_op jit(solution)/shard_map/cos | solution.py:141
  17.5 0.1 copy.44
  17.6 0.0 copy-start.6
  17.6 1.3 %maximum_multiply_fusion = f32[8,128,256]{1,2,0:T(8,128)S(1)} fusion(f32[8,128,128]{1,2,0:T(8,128)} %get-tuple-element.58, f32[8,128,128]{1,2,0:T(8,128)} %get-tuple-element.57), kind=kLoop, calls=%fused_computation.36 | loop fusion | flops 524288 | bytes 2097152 | tf_op jit(solution)/shard_map/div | solution.py:141
  18.9 1.1 %broadcast_multiply_fusion.3 = (f32[8,272,128]{2,1,0:T(8,128)S(1)}, f32[8,272,128]{2,1,0:T(8,128)S(1)}) fusion(f32[272,128]{1,0:T(8,128)} %collective-permute-done.2, f32[8,128]{1,0:T(8,128)S(1)} %copy-done.7, f32[8,128]{1,0:T(8,128)S(1)} %copy-done.6), kind=kLoop, calls=%fused_computation.53 | loop fusion | flops 557056 | bytes 2375680 | tf_op jit(solution)/shard_map/mul | solution.py:47
  20.0 1.2 %broadcast_multiply_fusion.5 = (f32[8,272,128]{2,1,0:T(8,128)S(1)}, f32[8,272,128]{2,1,0:T(8,128)S(1)}) fusion(f32[272,128]{1,0:T(8,128)} %collective-permute-done.1, f32[8,128]{1,0:T(8,128)S(1)} %get-tuple-element.60, f32[8,128]{1,0:T(8,128)S(1)} %get-tuple-element.50), kind=kLoop, calls=%fused_computation.55 | loop fusion | flops 557056 | bytes 2375680 | tf_op jit(solution)/shard_map/mul | solution.py:47
  21.2 1.1 %broadcast_multiply_fusion.7 = (f32[8,272,128]{2,1,0:T(8,128)S(1)}, f32[8,272,128]{2,1,0:T(8,128)S(1)}) fusion(f32[272,128]{1,0:T(8,128)} %collective-permute-done, f32[8,128]{1,0:T(8,128)S(1)} %get-tuple-element.62, f32[8,128]{1,0:T(8,128)S(1)} %get-tuple-element.48), kind=kLoop, calls=%fused_computation.57 | loop fusion | flops 557056 | bytes 2375680 | tf_op jit(solution)/shard_map/mul | solution.py:47
  22.3 0.5 fusion.16
  22.8 0.0 copy-start.18
  22.8 0.3 fusion.12
  23.1 0.7 %copy-done.18 = f32[256,256,1,1]{1,0,3,2:T(8,128)S(1)} copy-done((f32[256,256,1,1]{1,0,3,2:T(8,128)S(1)}, f32[256,256,1,1]{1,0,3,2:T(8,128)}, u32[]{:S(2)}) %copy-start.18) | copy-done | bytes 262168
  23.8 2.9 %fusion.2 = f32[8,3,256,256]{3,2,1,0:T(8,128)S(1)} fusion(f32[256,256,1,1]{1,0,3,2:T(8,128)S(1)} %copy-done.18, f32[8,3,256,128]{3,2,1,0:T(8,128)S(1)} %copy-done, f32[8,3,256,128]{3,2,1,0:T(8,128)S(1)} %get-tuple-element.21, f32[8,1,256,256]{3,2,1,0:T(8,128)S(1)} %fusion.12, f32[8,1,256,256]{3,2,1,0:T(8,128)S(1)} %get-tuple-element.13), kind=kOutput, calls=%fused_computation.8 | convolution fusion | flops 2425356288 | bytes 17039360 | tf_op jit(solution)/shard_map/dot_general | solution.py:52
  26.7 0.0 copy-start.1
  26.7 0.3 multiply_add_fusion
  27.0 0.6 %copy-done.1 = f32[256,256,1]{1,0,2:T(8,128)S(1)} copy-done((f32[256,256,1]{1,0,2:T(8,128)S(1)}, f32[256,256,1]{1,0,2:T(8,128)}, u32[]{:S(2)}) %copy-start.1) | copy-done | bytes 262168
  27.7 0.2 fusion.34
  27.9 0.2 broadcast_in_dim.6
  28.1 0.5 multiply_subtract_fusion.1
  28.6 0.0 copy-start.2
  28.6 0.0 copy-start.10
  28.6 0.0 copy-start.11
  28.6 0.0 copy-start.12
  28.6 0.0 copy-start.13
  28.7 0.0 copy-start.14
  28.7 0.0 copy-start.15
  28.7 0.0 copy-start.16
  28.7 0.0 copy-start.17
  28.7 0.3 maximum_reduce_fusion
  29.1 0.5 copy-done.2
  29.5 0.2 fusion.61
  30.0 3.5 %collective-permute-start.5 = (f32[16,128]{1,0:T(8,128)S(1)}, f32[16,128]{1,0:T(8,128)S(1)}, u32[]{:S(2)}, u32[]{:S(2)}) collective-permute-start(f32[16,128]{1,0:T(8,128)S(1)} %get-tuple-element.41), channel_id=1, source_target_pairs={{0,8},{8,16},{16,24},{24,0},{1,9},{9,17},{17,25},{25,1},{2,10},{10... | collective-permute-start | bytes 24584 | tf_op jit(solution)/shard_map/ppermute | solution.py:166
  33.5 1.4 %collective-permute-start.6 = (f32[16,128]{1,0:T(8,128)S(1)}, f32[16,128]{1,0:T(8,128)S(1)}, u32[]{:S(2)}, u32[]{:S(2)}) collective-permute-start(f32[16,128]{1,0:T(8,128)S(1)} %get-tuple-element.43), channel_id=1, source_target_pairs={{0,16},{8,24},{16,0},{24,8},{1,17},{9,25},{17,1},{25,9},{2,18},{10... | collective-permute-start | bytes 24584 | tf_op jit(solution)/shard_map/ppermute | solution.py:166
  34.9 0.1 maximum_bitcast_fusion.1
  35.1 0.1 maximum_bitcast_fusion.2
  35.2 0.5 maximum_bitcast_fusion
  35.7 2.4 %copy.39 = f32[2,256,8,256]{3,2,1,0:T(8,128)S(1)} copy(f32[2,256,8,256]{3,1,2,0:T(8,128)S(1)} %maximum_bitcast_fusion) | data formatting | bytes 8388608 | tf_op jit(solution)/shard_map/transpose | solution.py:71
  38.1 2.0 %copy.53 = f32[64,8,8,256]{3,1,2,0:T(8,128)S(1)} copy(f32[64,8,8,256]{3,2,1,0:T(8,128)S(1)} %bitcast.193) | data formatting | bytes 8388608
  40.1 1.8 %fusion.60 = f32[512,128]{1,0:T(8,128)S(1)} fusion(f32[512,2048]{1,0:T(8,128)S(1)} %bitcast.192, f32[2048,128]{1,0:T(8,128)S(1)} %bitcast.195), kind=kOutput, calls=%fused_computation.138 | convolution fusion | flops 805306368 | bytes 5505024 | tf_op jit(solution)/shard_map/dot_general | solution.py:73
  41.9 0.1 fusion.48
  42.0 4.1 %collective-permute-start.3 = (bf16[1,128,256]{1,2,0:T(8,128)(2,1)S(1)}, bf16[1,128,256]{1,2,0:T(8,128)(2,1)S(1)}, u32[]{:S(2)}, u32[]{:S(2)}) collective-permute-start(bf16[1,128,256]{1,2,0:T(8,128)(2,1)S(1)} %get-tuple-element.25), channel_id=1, source_target_pairs={{0,1},{1,2},{2,3},{3,4},{4,5},{5,6},{6,7},{8,9},{9,10},{10,11},{11... | collective-permute-start | bytes 196616 | tf_op jit(solution)/shard_map/ppermute | solution.py:21
  46.1 1.9 %collective-permute-start.4 = (bf16[1,128,3,256]{1,3,2,0:T(8,128)(2,1)S(1)}, bf16[1,128,3,256]{1,3,2,0:T(8,128)(2,1)S(1)}, u32[]{:S(2)}, u32[]{:S(2)}) collective-permute-start(bf16[1,128,3,256]{1,3,2,0:T(8,128)(2,1)S(1)} %pad_maximum_fusion.7), channel_id=1, source_target_pairs={{1,0},{2,1},{3,2},{4,3},{5,4},{6,5},{7,6},{9,8},{10,9},{11,10},{12... | collective-permute-start | bytes 589832 | tf_op jit(solution)/shard_map/ppermute | solution.py:21
  48.0 0.6 %fusion.53 = f32[1,16,128]{2,1,0:T(8,128)} fusion(f32[16,128]{1,0:T(8,128)S(1)} %collective-permute-done.7, f32[16,128]{1,0:T(8,128)S(1)} %collective-permute-done.6, f32[16,128]{1,0:T(8,128)S(1)} %collective-permute-done.5, f32[4,16,128]{2,1,0:T(8,128)S(1)} %maximum_multiply_fusion.1, s32[]{:T(128)S(6)} %select_n.82), kind=kLoop, calls=%fused_computation.118 | loop fusion | flops 8192 | bytes 40964 | tf_op jit(solution)/shard_map/broadcast_in_dim | solution.py:176
  48.7 0.7 %copy.41 = bf16[1,128,256]{2,1,0:T(8,128)(2,1)} copy(bf16[1,128,256]{1,2,0:T(8,128)(2,1)S(1)} %collective-permute-done.3) | data formatting | bytes 131072
  49.4 4.6 %collective-permute-done.4 = bf16[1,128,3,256]{1,3,2,0:T(8,128)(2,1)S(1)} collective-permute-done((bf16[1,128,3,256]{1,3,2,0:T(8,128)(2,1)S(1)}, bf16[1,128,3,256]{1,3,2,0:T(8,128)(2,1)S(1)}, u32[]{:S(2)}, u32[]{:S(2)}) %collective-permute-start.4) | collective-permute-done | bytes 196640 | tf_op jit(solution)/shard_map/ppermute | solution.py:21
  54.0 0.8 %copy.42 = bf16[1,128,3,256]{3,1,2,0:T(8,128)(2,1)} copy(bf16[1,128,3,256]{1,3,2,0:T(8,128)(2,1)S(1)} %collective-permute-done.4) | data formatting | bytes 393216
  (40 shorter events, 0.3 us)
Async XLA Ops:
  0.6 10.5 %copy-start.8 = (f32[4,8,128]{2,1,0:T(8,128)S(1)}, f32[4,8,128]{2,1,0:T(8,128)}, u32[]{:S(2)}) copy-start(f32[4,8,128]{2,1,0:T(8,128)} %constant.111.clone) | copy-start | bytes 49156
  0.6 10.5 %copy-start.9 = (f32[4,8,128]{2,1,0:T(8,128)S(1)}, f32[4,8,128]{2,1,0:T(8,128)}, u32[]{:S(2)}) copy-start(f32[4,8,128]{2,1,0:T(8,128)} %constant.110.clone) | copy-start | bytes 49156
  0.7 11.1 %copy-start.5 = (f32[1,16,128]{2,1,0:T(8,128)S(1)}, f32[1,16,128]{2,1,0:T(8,128)}, u32[]{:S(2)}) copy-start(f32[1,16,128]{2,1,0:T(8,128)} %param.13) | copy-start | bytes 24580
  0.7 9.5 %copy-start.4 = (f32[1,128,256]{2,1,0:T(8,128)S(1)}, f32[1,128,256]{2,1,0:T(8,128)}, u32[]{:S(2)}) copy-start(f32[1,128,256]{2,1,0:T(8,128)} %param.11) | copy-start | bytes 393220
  5.4 15.8 %collective-permute-start = (f32[272,128]{1,0:T(8,128)}, f32[272,128]{1,0:T(8,128)}, u32[]{:S(2)}, u32[]{:S(2)}) collective-permute-start(f32[272,128]{1,0:T(8,128)} %get-tuple-element.54), channel_id=1, source_target_pairs={{0,8},{8,16},{16,24},{24,0},{1,9},{9,17},{17,25},{25,1},{2,10},{10... | collective-permute-start | bytes 417800 | tf_op jit(solution)/shard_map/ppermute | solution.py:116
  6.7 13.3 %collective-permute-start.1 = (f32[272,128]{1,0:T(8,128)}, f32[272,128]{1,0:T(8,128)}, u32[]{:S(2)}, u32[]{:S(2)}) collective-permute-start(f32[272,128]{1,0:T(8,128)} %get-tuple-element.55), channel_id=1, source_target_pairs={{0,16},{8,24},{16,0},{24,8},{1,17},{9,25},{17,1},{25,9},{2,18},{10... | collective-permute-start | bytes 417800 | tf_op jit(solution)/shard_map/ppermute | solution.py:116
  9.0 9.9 %collective-permute-start.2 = (f32[272,128]{1,0:T(8,128)}, f32[272,128]{1,0:T(8,128)}, u32[]{:S(2)}, u32[]{:S(2)}) collective-permute-start(f32[272,128]{1,0:T(8,128)} %get-tuple-element.56), channel_id=1, source_target_pairs={{0,24},{8,0},{16,8},{24,16},{1,25},{9,1},{17,9},{25,17},{2,26},{10... | collective-permute-start | bytes 417800 | tf_op jit(solution)/shard_map/ppermute | solution.py:116
  17.6 1.3 %copy-start.6 = (f32[8,128]{1,0:T(8,128)S(1)}, f32[8,128]{1,0:T(8,128)}, u32[]{:S(2)}) copy-start(f32[8,128]{1,0:T(8,128)} %get-tuple-element.51) | copy-start | bytes 12292
  17.6 1.3 %copy-start.7 = (f32[8,128]{1,0:T(8,128)S(1)}, f32[8,128]{1,0:T(8,128)}, u32[]{:S(2)}) copy-start(f32[8,128]{1,0:T(8,128)} %get-tuple-element.59) | copy-start | bytes 12292
  20.0 2.3 %copy-start = (f32[8,3,256,128]{3,2,1,0:T(8,128)S(1)}, f32[8,3,256,128]{3,2,1,0:T(8,128)}, u32[]{:S(2)}) copy-start(f32[8,3,256,128]{3,2,1,0:T(8,128)} %get-tuple-element.22) | copy-start | bytes 9437188
  22.8 1.0 %copy-start.18 = (f32[256,256,1,1]{1,0,3,2:T(8,128)S(1)}, f32[256,256,1,1]{1,0,3,2:T(8,128)}, u32[]{:S(2)}) copy-start(f32[256,256,1,1]{1,0,3,2:T(8,128)} %constant.136) | copy-start | bytes 786436
  26.7 1.0 %copy-start.1 = (f32[256,256,1]{1,0,2:T(8,128)S(1)}, f32[256,256,1]{1,0,2:T(8,128)}, u32[]{:S(2)}) copy-start(f32[256,256,1]{1,0,2:T(8,128)} %constant.135) | copy-start | bytes 786436
  28.6 1.0 %copy-start.2 = (f32[256,256,1]{1,0,2:T(8,128)S(1)}, f32[256,256,1]{1,0,2:T(8,128)}, u32[]{:S(2)}) copy-start(f32[256,256,1]{1,0,2:T(8,128)} %constant.137) | copy-start | bytes 786436
  28.6 1.2 %copy-start.10 = (f32[8,128]{1,0:T(8,128)S(1)}, f32[8,128]{1,0:T(8,128)}, u32[]{:S(2)}) copy-start(f32[8,128]{1,0:T(8,128)} %constant.134) | copy-start | bytes 12292
  28.6 1.2 %copy-start.11 = (f32[8,128]{1,0:T(8,128)S(1)}, f32[8,128]{1,0:T(8,128)}, u32[]{:S(2)}) copy-start(f32[8,128]{1,0:T(8,128)} %constant.132) | copy-start | bytes 12292
  28.6 1.2 %copy-start.12 = (f32[8,128]{1,0:T(8,128)S(1)}, f32[8,128]{1,0:T(8,128)}, u32[]{:S(2)}) copy-start(f32[8,128]{1,0:T(8,128)} %constant.130) | copy-start | bytes 12292
  28.6 1.2 %copy-start.13 = (f32[8,128]{1,0:T(8,128)S(1)}, f32[8,128]{1,0:T(8,128)}, u32[]{:S(2)}) copy-start(f32[8,128]{1,0:T(8,128)} %constant.128) | copy-start | bytes 12292
  28.7 1.2 %copy-start.14 = (f32[8,128]{1,0:T(8,128)S(1)}, f32[8,128]{1,0:T(8,128)}, u32[]{:S(2)}) copy-start(f32[8,128]{1,0:T(8,128)} %constant.126) | copy-start | bytes 12292
  28.7 1.2 %copy-start.15 = (f32[8,128]{1,0:T(8,128)S(1)}, f32[8,128]{1,0:T(8,128)}, u32[]{:S(2)}) copy-start(f32[8,128]{1,0:T(8,128)} %constant.124) | copy-start | bytes 12292
  28.7 1.2 %copy-start.16 = (f32[8,128]{1,0:T(8,128)S(1)}, f32[8,128]{1,0:T(8,128)}, u32[]{:S(2)}) copy-start(f32[8,128]{1,0:T(8,128)} %constant.122) | copy-start | bytes 12292
  28.7 1.2 %copy-start.17 = (f32[8,128]{1,0:T(8,128)S(1)}, f32[8,128]{1,0:T(8,128)}, u32[]{:S(2)}) copy-start(f32[8,128]{1,0:T(8,128)} %constant.120) | copy-start | bytes 12292
  30.0 18.1 %collective-permute-start.5 = (f32[16,128]{1,0:T(8,128)S(1)}, f32[16,128]{1,0:T(8,128)S(1)}, u32[]{:S(2)}, u32[]{:S(2)}) collective-permute-start(f32[16,128]{1,0:T(8,128)S(1)} %get-tuple-element.41), channel_id=1, source_target_pairs={{0,8},{8,16},{16,24},{24,0},{1,9},{9,17},{17,25},{25,1},{2,10},{10... | collective-permute-start | bytes 24584 | tf_op jit(solution)/shard_map/ppermute | solution.py:166
  33.5 14.5 %collective-permute-start.7 = (f32[16,128]{1,0:T(8,128)S(1)}, f32[16,128]{1,0:T(8,128)S(1)}, u32[]{:S(2)}, u32[]{:S(2)}) collective-permute-start(f32[16,128]{1,0:T(8,128)S(1)} %get-tuple-element.42), channel_id=1, source_target_pairs={{0,24},{8,0},{16,8},{24,16},{1,25},{9,1},{17,9},{25,17},{2,26},{10... | collective-permute-start | bytes 24584 | tf_op jit(solution)/shard_map/ppermute | solution.py:166
  33.5 14.5 %collective-permute-start.6 = (f32[16,128]{1,0:T(8,128)S(1)}, f32[16,128]{1,0:T(8,128)S(1)}, u32[]{:S(2)}, u32[]{:S(2)}) collective-permute-start(f32[16,128]{1,0:T(8,128)S(1)} %get-tuple-element.43), channel_id=1, source_target_pairs={{0,16},{8,24},{16,0},{24,8},{1,17},{9,25},{17,1},{25,9},{2,18},{10... | collective-permute-start | bytes 24584 | tf_op jit(solution)/shard_map/ppermute | solution.py:166
  40.1 6.0 %copy-start.3 = (bf16[1,128,1,256]{1,3,2,0:T(8,128)(2,1)S(1)}, bf16[1,128,1,256]{1,3,2,0:T(8,128)(2,1)}, u32[]{:S(2)}) copy-start(bf16[1,128,1,256]{1,3,2,0:T(8,128)(2,1)} %fusion.49) | copy-start | bytes 196612
  42.0 6.7 %collective-permute-start.3 = (bf16[1,128,256]{1,2,0:T(8,128)(2,1)S(1)}, bf16[1,128,256]{1,2,0:T(8,128)(2,1)S(1)}, u32[]{:S(2)}, u32[]{:S(2)}) collective-permute-start(bf16[1,128,256]{1,2,0:T(8,128)(2,1)S(1)} %get-tuple-element.25), channel_id=1, source_target_pairs={{0,1},{1,2},{2,3},{3,4},{4,5},{5,6},{6,7},{8,9},{9,10},{10,11},{11... | collective-permute-start | bytes 196616 | tf_op jit(solution)/shard_map/ppermute | solution.py:21
  46.1 7.9 %collective-permute-start.4 = (bf16[1,128,3,256]{1,3,2,0:T(8,128)(2,1)S(1)}, bf16[1,128,3,256]{1,3,2,0:T(8,128)(2,1)S(1)}, u32[]{:S(2)}, u32[]{:S(2)}) collective-permute-start(bf16[1,128,3,256]{1,3,2,0:T(8,128)(2,1)S(1)} %pad_maximum_fusion.7), channel_id=1, source_target_pairs={{1,0},{2,1},{3,2},{4,3},{5,4},{6,5},{7,6},{9,8},{10,9},{11,10},{12... | collective-permute-start | bytes 589832 | tf_op jit(solution)/shard_map/ppermute | solution.py:21

commit v4 on v3

--- a/solution.py
+++ b/solution.py
@@ -10,6 +10,7 @@
 CPF = 16
 CHUNK_BYTES = 36 * 2**20
 STEPWISE = 4
+DENSE = 4
 
 highest = lax.Precision.HIGHEST
 precise = lax.Precision.HIGH
@@ -50,6 +51,72 @@
 def inner_step(y, mat):
     shape = y.shape
     return jnp.dot(y.reshape(-1, shape[-1]), mat, precision=precise).reshape(shape)
+
+
+def packed_tables(blocks, block):
+    size = 2 * blocks * block
+    half = size // 2
+    ids = np.arange(block)
+    freqs = np.arange(half)
+    theta = 2.0 * np.pi * ((ids[:, None] * freqs[None, :]) % size) / size
+    phase = 2.0 * np.pi * ((np.arange(blocks)[:, None] * block * freqs[None, :]) % size) / size
+    as32 = lambda a: jnp.asarray(a, jnp.float32)
+    return as32(np.cos(theta)), as32(np.sin(theta)), as32(np.cos(phase)), as32(np.sin(phase))
+
+
+def block_table(packed, index):
+    base_c, base_s, turn_c, turn_s = packed
+    c = lax.dynamic_index_in_dim(turn_c, index, keepdims=True)
+    s = lax.dynamic_index_in_dim(turn_s, index, keepdims=True)
+    cos = base_c * c - base_s * s
+    sin = base_s * c + base_c * s
+    block, half = cos.shape
+    first = lax.broadcasted_iota(jnp.int32, (block, half), 1) == 0
+    sign = 1.0 - 2.0 * (lax.broadcasted_iota(jnp.int32, (block, half), 0) % 2).astype(jnp.float32)
+    return jnp.concatenate([cos, jnp.where(first, sign, -sin)], axis=1)
+
+
+def packed_products(h, a, conj):
+    half = h.shape[1] // 2
+    hr, hi = h[:, :half], h[:, half:]
+    ar, ai = a[:, :half], a[:, half:]
+    first = lax.broadcasted_iota(jnp.int32, hr.shape, 1) == 0
+    sign = -1.0 if conj else 1.0
+    re = hr * ar - sign * jnp.where(first, 0.0, hi * ai)
+    im = jnp.where(first, hi * ai, hr * ai + sign * (hi * ar))
+    return jnp.concatenate([re, im], axis=1)
+
+
+def dense_path(place, blocks, mixed_rows, weighted_rows, back_rows, taps):
+    channels, block = mixed_rows.shape
+    size = 2 * blocks * block
+    half = size // 2
+    packed = packed_tables(blocks, block)
+    acc = 0.0
+    for s in range(1, blocks):
+        first = jnp.where(place + s < blocks, mixed_rows, weighted_rows)
+        payload = jnp.concatenate([first, back_rows, taps], axis=0)
+        pairs = [(i, (i + s) % blocks) for i in range(blocks)]
+        got = lax.ppermute(payload, "ctx", pairs)
+        table = block_table(packed, (place - s) % blocks)
+        acc = acc + jnp.dot(got, table, precision=precise)
+    own_table = block_table(packed, place)
+    own = jnp.concatenate([mixed_rows, weighted_rows, back_rows, taps], axis=0)
+    loc = jnp.dot(own, own_table, precision=precise)
+    c = channels
+    mixed_spec = loc[:c] + acc[:c]
+    weighted_spec = loc[c : 2 * c] + acc[:c]
+    back_spec = loc[2 * c : 3 * c] + acc[c : 2 * c]
+    taps_spec = jnp.repeat(loc[3 * c :] + acc[2 * c :], CPF, axis=0)
+    conv = packed_products(taps_spec, mixed_spec, False)
+    gm = packed_products(taps_spec, weighted_spec, True)
+    fgs = packed_products(back_spec, weighted_spec, True)
+    fgs = fgs.reshape(-1, CPF, size).sum(axis=1)
+    both = jnp.concatenate([conv, gm, fgs], axis=0)
+    cols = lax.broadcasted_iota(jnp.int32, (1, size), 1)
+    weight = jnp.where((cols == 0) | (cols == half), 1.0 / size, 2.0 / size)
+    out = jnp.einsum("tf,rf->tr", own_table * weight, both, precision=precise)
+    return out[:, :c], out[:, c : 2 * c], out[:, 2 * c :].T
 
 
 def chunk_work(local3, common, hsum, tables):
@@ -80,6 +147,19 @@
     return both[0], both[1], fg / (outer * block)
 
 
+def finish(conv, grad_mixed, lag, filter_scale, query_in, grad_query, key_back, value_back):
+    conv = conv * filter_scale
+    grad_mixed = grad_mixed * filter_scale
+    result = (query_in * conv).astype(jnp.bfloat16)
+    next_input = from_behind(result[None], "pipe", 1)
+    grad_key = grad_mixed * value_back
+    grad_value = grad_mixed * key_back
+    grad_stack = jnp.stack([grad_query, grad_key, grad_value], axis=1).astype(jnp.bfloat16)
+    prev_grad = from_behind(grad_stack[None], "pipe", -1)
+    filter_grad = (lag * filter_scale)[None]
+    return (next_input, prev_grad, filter_grad)
+
+
 def on_device(qkv_in, qkv_saved, conv_saved, out_grad, filters):
     blocks = lax.axis_size("ctx")
     place = lax.axis_index("ctx")
@@ -101,6 +181,14 @@
     weighted = upstream * query_back
     grad_query = upstream * conv_saved[0]
     taps = filters[0]
+
+    if blocks <= DENSE:
+        conv, grad_mixed, lag = dense_path(
+            place, blocks, mixed_in.T, weighted.T, mixed_back.T, taps
+        )
+        return finish(
+            conv, grad_mixed, lag, filter_scale, query_in, grad_query, key_back, value_back
+        )
 
     cw, sw = outer_tables(blocks, block, outer)
     fwd, inv = inner_tables(block)
@@ -165,16 +253,9 @@
         pairs = [(i, (i + s) % blocks) for i in range(blocks)]
         lag_sum = lag_sum + lax.ppermute(fg[dest], "ctx", pairs)
 
-    conv = conv.T * filter_scale
-    grad_mixed = grad_mixed.T * filter_scale
-    result = (query_in * conv).astype(jnp.bfloat16)
-    next_input = from_behind(result[None], "pipe", 1)
-    grad_key = grad_mixed * value_back
-    grad_value = grad_mixed * key_back
-    grad_stack = jnp.stack([grad_query, grad_key, grad_value], axis=1).astype(jnp.bfloat16)
-    prev_grad = from_behind(grad_stack[None], "pipe", -1)
-    filter_grad = (lag_sum * filter_scale)[None]
-    return (next_input, prev_grad, filter_grad)
+    return finish(
+        conv.T, grad_mixed.T, lag_sum, filter_scale, query_in, grad_query, key_back, value_back
+    )
 
 
 def solution(mesh):

time: 55.2 us -> 55.7 us (level)
  the two profiles are of different devices: /device:TPU:3 before, /device:TPU:19 now
where the time goes in v4:
time: 55.7 us; the launch traced here: 55.2 us
  waiting for transfers between devices  19.3 us (35%)
  starting transfers between devices  9.58 us (17%)
  local copies, waits for them, and re-layouts  9.51 us (17%)
  matrix products  8.75 us (16%)
  other arithmetic  7.02 us (13%)
  between operations  1.09 us (2%)
    ppermute x3, waiting for transfers between devices, dense_path(): got = lax.ppermute(payload, 'ctx', pairs)  14.7 us
    unnamed x50, local copies, waits for them, and re-layouts  6.85 us
    dot_general x3, matrix products, dense_path(): acc = acc + jnp.dot(got, table, precision=precise)  6.32 us
    ppermute x2, starting transfers between devices, from_behind(): return lax.ppermute(x, axis, pairs)  6.2 us
    ppermute x2, waiting for transfers between devices, from_behind(): return lax.ppermute(x, axis, pairs)  4.61 us
    ppermute x3, starting transfers between devices, dense_path(): got = lax.ppermute(payload, 'ctx', pairs)  3.38 us
    slice x1, local copies, waits for them, and re-layouts, on_device(): query_in = qkv_in[0, :, 0].astype(jnp.float32)  1.6 us
    dot_general x1, matrix products, dense_path(): loc = jnp.dot(own, own_table, precision=precise)  1.41 us
  transfers between devices with their start and end apart: 5, of which 2 were waited for; matrix products, arithmetic and copies ran while one was open for 25% of the time, Pallas kernels for 0%

profile of v4, /device:TPU:19, one launch (start us, length us, event | category | flops | bytes accessed | tf_op | source)
XLA Modules:
  0.0 55.2 jit_solution(7525356029761303209)
XLA Ops:
  0.6 0.0 copy-start.17
  0.7 0.9 %copy.15 = bf16[1,128,256]{1,2,0:T(8,128)(2,1)S(1)} copy(bf16[1,128,256]{2,1,0:T(8,128)(2,1)} %param.12) | data formatting | bytes 131072 | tf_op args[3]
  1.6 0.0 copy-start.18
  1.6 0.0 copy-start.19
  1.6 0.0 copy-start.14
  1.6 0.0 copy-start.15
  1.7 1.6 %fusion.54 = (bf16[1,128,1,256]{3,1,2,0:T(8,128)(2,1)}, bf16[1,128,1,256]{3,1,2,0:T(8,128)(2,1)S(1)}, bf16[1,128,1,256]{3,1,2,0:T(8,128)(2,1)S(1)}) fusion(bf16[1,128,3,256]{3,1,2,0:T(8,128)(2,1)} %param.9), kind=kLoop, calls=%fused_computation.111 | loop fusion | bytes 393216 | tf_op jit(solution)/shard_map/slice | solution.py:174
  3.3 0.1 copy.23
  3.4 0.1 copy.24
  3.5 0.9 %fusion.55 = (bf16[1,128,1,256]{3,1,2,0:T(8,128)(2,1)S(1)}, bf16[1,128,1,256]{3,1,2,0:T(8,128)(2,1)S(1)}, bf16[1,128,1,256]{3,1,2,0:T(8,128)(2,1)S(1)}) fusion(bf16[1,128,3,256]{3,1,2,0:T(8,128)(2,1)} %param.10), kind=kLoop, calls=%fused_computation.112 | loop fusion | bytes 393216 | tf_op jit(solution)/shard_map/slice | solution.py:176
  4.4 0.1 copy.25
  4.5 0.1 copy.26
  4.7 0.0 copy-start.8
  4.7 0.1 copy.27
  4.8 0.0 copy-start.10
  4.8 0.1 broadcast_select_fusion
  4.9 0.0 copy-done.17
  4.9 0.9 %pad_maximum_fusion.2 = (f32[528,128]{1,0:T(8,128)}, f32[528,128]{1,0:T(8,128)}, f32[528,128]{1,0:T(8,128)}) fusion(f32[16,128]{1,0:T(8,128)S(1)} %bitcast.80, f32[256,128]{1,0:T(8,128)S(1)} %fusion.38, f32[256,128]{1,0:T(8,128)S(1)} %get-tuple-element.34, f32[256,128]{1,0:T(8,128)S(1)} %get-tuple-element.36, f32[256,128]{1,0:T(8,128)S(1)} %get-tuple-element.35), kind=kLoop, calls=%fused_computation.36 | loop fusion | flops 405504 | bytes 1343488 | tf_op jit(solution)/shard_map/concatenate | solution.py:98
  5.8 0.2 collective-permute-start.2
  6.0 3.2 %collective-permute-start.1 = (f32[528,128]{1,0:T(8,128)}, f32[528,128]{1,0:T(8,128)}, u32[]{:S(2)}, u32[]{:S(2)}) collective-permute-start(f32[528,128]{1,0:T(8,128)} %get-tuple-element.44), channel_id=1, source_target_pairs={{0,16},{8,24},{16,0},{24,8},{1,17},{9,25},{17,1},{25,9},{2,18},{10... | collective-permute-start | bytes 811016 | tf_op jit(solution)/shard_map/ppermute | solution.py:100
  9.2 0.0 collective-permute-start
  9.3 0.7 %multiply_bitcast_fusion = f32[256,128]{1,0:T(8,128)} fusion(bf16[1,128,1,256]{1,3,2,0:T(8,128)(2,1)S(1)} %copy.24, bf16[1,128,1,256]{1,3,2,0:T(8,128)(2,1)S(1)} %copy.23), kind=kLoop, calls=%fused_computation.79 | loop fusion | flops 98304 | bytes 262144 | tf_op jit(solution)/shard_map/transpose | solution.py:187
  9.9 0.7 %fusion.35 = f32[256,128]{1,0:T(8,128)} fusion(bf16[1,128,256]{1,2,0:T(8,128)(2,1)S(1)} %copy.15, bf16[1,128,1,256]{1,3,2,0:T(8,128)(2,1)S(1)} %copy.25), kind=kLoop, calls=%fused_computation.70 | loop fusion | flops 98304 | bytes 262144 | tf_op jit(solution)/shard_map/transpose | solution.py:187
  10.6 0.0 copy-done.18
  10.6 0.0 copy-done.19
  10.6 0.0 copy-done.14
  10.6 0.0 copy-done.15
  10.6 1.4 %multiply_subtract_fusion.4 = (f32[128,512]{1,0:T(8,128)}, f32[128,512]{1,0:T(8,128)}, f32[128,512]{1,0:T(8,128)S(1)}, f32[128,512]{1,0:T(8,128)S(1)}, f32[128,5...) fusion(f32[128,512]{1,0:T(8,128)S(1)} %copy-done.14, f32[128,512]{1,0:T(8,128)S(1)} %copy-done.15, ...), kind=kLoop, calls=%fused_computation.58 | loop fusion | flops 2359296 | bytes 2639488 | tf_op jit(solution)/shard_map/sub | solution.py:71
  12.0 0.0 copy-done.8
  12.0 0.0 copy-done.10
  12.0 0.0 copy-start.2
  12.0 0.0 copy-done.12
  12.0 0.0 copy-done.13
  12.0 1.4 %fusion.25 = f32[784,1024]{1,0:T(8,128)S(1)} fusion(f32[128,512]{1,0:T(8,128)S(1)} %get-tuple-element.25, f32[128,512]{1,0:T(8,128)S(1)} %get-tuple-element.26, f32[16,128]{1,0:T(8,128)S(1)} %bitcast.81, f32[256,128]{1,0:T(8,128)S(1)} %fusion.38, f32[256,128]{1,0:T(8,128)S(1)} %copy-done.13, f32[256,128]{1,0:T(8,128)S(1)} %copy-done.12), kind=kOutput, calls=%fused_computation.41 | convolution fusion | flops 616994816 | bytes 4136960 | tf_op jit(solution)/shard_map/dot_general | solution.py:105
  13.5 1.7 %copy.19 = f32[1,128,256]{1,2,0:T(8,128)} copy(f32[1,128,256]{2,1,0:T(8,128)} %param.11) | data formatting | bytes 262144 | tf_op args[2]
  15.2 1.6 %copy.22 = bf16[1,128,1,256]{1,3,2,0:T(8,128)(2,1)} copy(bf16[1,128,1,256]{3,1,2,0:T(8,128)(2,1)} %get-tuple-element.37) | data formatting | bytes 131072
  16.8 1.0 %fusion.45 = bf16[1,128,1,256]{1,3,2,0:T(8,128)(2,1)S(1)} fusion(f32[1,128,256]{1,2,0:T(8,128)} %copy.19, bf16[1,128,256]{1,2,0:T(8,128)(2,1)S(1)} %copy.15), kind=kLoop, calls=%fused_computation.83 | loop fusion | flops 98304 | bytes 262144 | tf_op jit(solution)/shard_map/stack | solution.py:157
  17.7 14.7 %collective-permute-done = f32[528,128]{1,0:T(8,128)} collective-permute-done((f32[528,128]{1,0:T(8,128)}, f32[528,128]{1,0:T(8,128)}, u32[]{:S(2)}, u32[]{:S(2)}) %collective-permute-start) | collective-permute-done | bytes 270368 | tf_op jit(solution)/shard_map/ppermute | solution.py:100
  32.4 2.1 %fusion.10 = f32[528,1024]{1,0:T(8,128)S(1)} fusion(f32[528,128]{1,0:T(8,128)} %collective-permute-done, f32[128,512]{1,0:T(8,128)} %get-tuple-element.24, f32[128,512]{1,0:T(8,128)} %get-tuple-element.23), kind=kOutput, calls=%fused_computation.17 | convolution fusion | flops 415367168 | bytes 2957312 | tf_op jit(solution)/shard_map/dot_general | solution.py:102
  34.5 0.0 collective-permute-done.1
  34.5 0.0 copy-done.6
  34.5 0.0 copy-done.7
  34.6 2.0 %fusion.14 = f32[528,1024]{1,0:T(8,128)S(1)} fusion(f32[528,128]{1,0:T(8,128)} %collective-permute-done.1, f32[128,512]{1,0:T(8,128)S(1)} %copy-done.6, f32[128,512]{1,0:T(8,128)S(1)} %copy-done.7), kind=kOutput, calls=%fused_computation.21 | convolution fusion | flops 415367168 | bytes 2957312 | tf_op jit(solution)/shard_map/dot_general | solution.py:102
  36.6 0.0 collective-permute-done.2
  36.6 2.2 %add_add_fusion = f32[528,1024]{1,0:T(8,128)S(1)} fusion(f32[528,1024]{1,0:T(8,128)S(1)} %fusion.10, f32[528,1024]{1,0:T(8,128)S(1)} %fusion.14, f32[528,128]{1,0:T(8,128)} %collective-permute-done.2, f32[128,512]{1,0:T(8,128)S(1)} %copy-done.4, f32[128,512]{1,0:T(8,128)S(1)} %copy-done.5), kind=kOutput, calls=%fused_computation.10 | convolution fusion | flops 416448512 | bytes 7282688 | tf_op jit(solution)/shard_map/dot_general | solution.py:102
  38.8 0.8 %slice_add_fusion.2 = (f32[256,1024]{1,0:T(8,128)S(1)}, f32[256,1024]{1,0:T(8,128)S(1)}, f32[256,1024]{1,0:T(8,128)S(1)}) fusion(f32[784,1024]{1,0:T(8,128)S(1)} %fusion.25, f32[528,1024]{1,0:T(8,128)S(1)} %add_add_fusion), kind=kLoop, calls=%fused_computation.13 | loop fusion | flops 786432 | bytes 8388608 | tf_op jit(solution)/shard_map/add | solution.py:107
  39.7 0.3 multiply_subtract_fusion
  39.9 0.1 broadcast_in_dim.26
  40.1 0.4 select_subtract_fusion
  40.5 0.2 bitcast_reduce_fusion
  40.7 0.3 copy-done.1
  41.0 0.1 copy-done.3
  41.1 1.0 %fusion = f32[128,528]{0,1:T(8,128)S(1)} fusion(f32[16,1024]{1,0:T(8,128)S(1)} %bitcast_reduce_fusion, f32[256,512]{1,0:T(8,128)S(1)} %get-tuple-element.15, f32[256,512]{1,0:T(8,128)S(1)} %get-tuple-element.16, f32[256,512]{1,0:T(8,128)S(1)} %get-tuple-element.10, f32[256,512]{1,0:T(8,128)S(1)} %get-tuple-element.9, f32[128,512]{1,0:T(8,128)S(1)} %copy-done.1, ...), kind=kOutput, calls=%fused_computation | convolution fusion | flops 417660928 | bytes 2961408 | tf_op jit(solution)/shard_map/tf,rf->tr/dot_general | solution.py:118
  42.1 0.0 copy-done.9
  42.1 0.0 copy-done.11
  42.1 0.0 copy-done.16
  42.1 0.1 fusion.44
  42.2 4.3 %collective-permute-start.3 = (bf16[1,128,256]{1,2,0:T(8,128)(2,1)S(1)}, bf16[1,128,256]{1,2,0:T(8,128)(2,1)S(1)}, u32[]{:S(2)}, u32[]{:S(2)}) collective-permute-start(bf16[1,128,256]{1,2,0:T(8,128)(2,1)S(1)} %get-tuple-element.33), channel_id=1, source_target_pairs={{0,1},{1,2},{2,3},{3,4},{4,5},{5,6},{6,7},{8,9},{9,10},{10,11},{11... | collective-permute-start | bytes 196616 | tf_op jit(solution)/shard_map/ppermute | solution.py:22
  46.5 1.9 %collective-permute-start.4 = (bf16[1,128,3,256]{1,3,2,0:T(8,128)(2,1)S(1)}, bf16[1,128,3,256]{1,3,2,0:T(8,128)(2,1)S(1)}, u32[]{:S(2)}, u32[]{:S(2)}) collective-permute-start(bf16[1,128,3,256]{1,3,2,0:T(8,128)(2,1)S(1)} %pad_maximum_fusion.10), channel_id=1, source_target_pairs={{1,0},{2,1},{3,2},{4,3},{5,4},{6,5},{7,6},{9,8},{10,9},{11,10},{12... | collective-permute-start | bytes 589832 | tf_op jit(solution)/shard_map/ppermute | solution.py:22
  48.4 0.6 %fusion.46 = f32[1,16,128]{2,1,0:T(8,128)} fusion(f32[128,528]{0,1:T(8,128)S(1)} %fusion), kind=kLoop, calls=%fused_computation.89 | loop fusion | flops 2048 | bytes 16384 | tf_op jit(solution)/shard_map/broadcast_in_dim | solution.py:159
  49.0 0.0 collective-permute-done.3
  49.1 0.7 %copy.20 = bf16[1,128,256]{2,1,0:T(8,128)(2,1)} copy(bf16[1,128,256]{1,2,0:T(8,128)(2,1)S(1)} %collective-permute-done.3) | data formatting | bytes 131072
  49.8 4.6 %collective-permute-done.4 = bf16[1,128,3,256]{1,3,2,0:T(8,128)(2,1)S(1)} collective-permute-done((bf16[1,128,3,256]{1,3,2,0:T(8,128)(2,1)S(1)}, bf16[1,128,3,256]{1,3,2,0:T(8,128)(2,1)S(1)}, u32[]{:S(2)}, u32[]{:S(2)}) %collective-permute-start.4) | collective-permute-done | bytes 196640 | tf_op jit(solution)/shard_map/ppermute | solution.py:22
  54.4 0.8 %copy.21 = bf16[1,128,3,256]{3,1,2,0:T(8,128)(2,1)} copy(bf16[1,128,3,256]{1,3,2,0:T(8,128)(2,1)S(1)} %collective-permute-done.4) | data formatting | bytes 393216
  (24 shorter events, 0.1 us)
Async XLA Ops:
  0.6 4.3 %copy-start.17 = (f32[1,16,128]{2,1,0:T(8,128)S(1)}, f32[1,16,128]{2,1,0:T(8,128)}, u32[]{:S(2)}) copy-start(f32[1,16,128]{2,1,0:T(8,128)} %param.13) | copy-start | bytes 24580
  1.6 9.0 %copy-start.18 = (f32[4,512]{1,0:T(4,128)S(1)}, f32[4,512]{1,0:T(4,128)}, u32[]{:S(2)}) copy-start(f32[4,512]{1,0:T(4,128)} %constant.107.clone) | copy-start | bytes 24580
  1.6 9.0 %copy-start.19 = (f32[4,512]{1,0:T(4,128)S(1)}, f32[4,512]{1,0:T(4,128)}, u32[]{:S(2)}) copy-start(f32[4,512]{1,0:T(4,128)} %constant.106.clone) | copy-start | bytes 24580
  1.6 9.0 %copy-start.14 = (f32[128,512]{1,0:T(8,128)S(1)}, f32[128,512]{1,0:T(8,128)}, u32[]{:S(2)}) copy-start(f32[128,512]{1,0:T(8,128)} %constant.105.clone) | copy-start | bytes 786436
  1.6 9.0 %copy-start.15 = (f32[128,512]{1,0:T(8,128)S(1)}, f32[128,512]{1,0:T(8,128)}, u32[]{:S(2)}) copy-start(f32[128,512]{1,0:T(8,128)} %constant.104.clone) | copy-start | bytes 786436
  4.7 7.3 %copy-start.8 = (bf16[1,128,1,256]{1,3,2,0:T(8,128)(2,1)}, bf16[1,128,1,256]{1,3,2,0:T(8,128)(2,1)S(1)}, u32[]{:S(2)}) copy-start(bf16[1,128,1,256]{1,3,2,0:T(8,128)(2,1)S(1)} %copy.26) | copy-start | bytes 196612
  4.8 7.2 %copy-start.10 = (bf16[1,128,1,256]{1,3,2,0:T(8,128)(2,1)}, bf16[1,128,1,256]{1,3,2,0:T(8,128)(2,1)S(1)}, u32[]{:S(2)}) copy-start(bf16[1,128,1,256]{1,3,2,0:T(8,128)(2,1)S(1)} %copy.27) | copy-start | bytes 196612
  5.8 30.7 %collective-permute-start.2 = (f32[528,128]{1,0:T(8,128)}, f32[528,128]{1,0:T(8,128)}, u32[]{:S(2)}, u32[]{:S(2)}) collective-permute-start(f32[528,128]{1,0:T(8,128)} %get-tuple-element.43), channel_id=1, source_target_pairs={{0,24},{8,0},{16,8},{24,16},{1,25},{9,1},{17,9},{25,17},{2,26},{10... | collective-permute-start | bytes 811016 | tf_op jit(solution)/shard_map/ppermute | solution.py:100
  6.0 28.5 %collective-permute-start.1 = (f32[528,128]{1,0:T(8,128)}, f32[528,128]{1,0:T(8,128)}, u32[]{:S(2)}, u32[]{:S(2)}) collective-permute-start(f32[528,128]{1,0:T(8,128)} %get-tuple-element.44), channel_id=1, source_target_pairs={{0,16},{8,24},{16,0},{24,8},{1,17},{9,25},{17,1},{25,9},{2,18},{10... | collective-permute-start | bytes 811016 | tf_op jit(solution)/shard_map/ppermute | solution.py:100
  9.2 23.2 %collective-permute-start = (f32[528,128]{1,0:T(8,128)}, f32[528,128]{1,0:T(8,128)}, u32[]{:S(2)}, u32[]{:S(2)}) collective-permute-start(f32[528,128]{1,0:T(8,128)} %get-tuple-element.45), channel_id=1, source_target_pairs={{0,8},{8,16},{16,24},{24,0},{1,9},{9,17},{17,25},{25,1},{2,10},{10... | collective-permute-start | bytes 811016 | tf_op jit(solution)/shard_map/ppermute | solution.py:100
  10.6 1.4 %copy-start.12 = (f32[256,128]{1,0:T(8,128)S(1)}, f32[256,128]{1,0:T(8,128)}, u32[]{:S(2)}) copy-start(f32[256,128]{1,0:T(8,128)} %multiply_bitcast_fusion) | copy-start | bytes 393220
  10.6 1.4 %copy-start.13 = (f32[256,128]{1,0:T(8,128)S(1)}, f32[256,128]{1,0:T(8,128)}, u32[]{:S(2)}) copy-start(f32[256,128]{1,0:T(8,128)} %fusion.35) | copy-start | bytes 393220
  12.0 1.5 %copy-start = (f32[128,512]{1,0:T(8,128)}, f32[128,512]{1,0:T(8,128)S(1)}, u32[]{:S(2)}) copy-start(f32[128,512]{1,0:T(8,128)S(1)} %get-tuple-element.25) | copy-start | bytes 786436
  12.0 1.5 %copy-start.2 = (f32[128,512]{1,0:T(8,128)}, f32[128,512]{1,0:T(8,128)S(1)}, u32[]{:S(2)}) copy-start(f32[128,512]{1,0:T(8,128)S(1)} %get-tuple-element.26) | copy-start | bytes 786436
  13.5 21.1 %copy-start.6 = (f32[128,512]{1,0:T(8,128)S(1)}, f32[128,512]{1,0:T(8,128)}, u32[]{:S(2)}) copy-start(f32[128,512]{1,0:T(8,128)} %get-tuple-element.29) | copy-start | bytes 786436
  16.8 17.8 %copy-start.7 = (f32[128,512]{1,0:T(8,128)S(1)}, f32[128,512]{1,0:T(8,128)}, u32[]{:S(2)}) copy-start(f32[128,512]{1,0:T(8,128)} %get-tuple-element.30) | copy-start | bytes 786436
  34.5 2.1 %copy-start.4 = (f32[128,512]{1,0:T(8,128)S(1)}, f32[128,512]{1,0:T(8,128)}, u32[]{:S(2)}) copy-start(f32[128,512]{1,0:T(8,128)} %get-tuple-element.27) | copy-start | bytes 786436
  34.5 2.1 %copy-start.5 = (f32[128,512]{1,0:T(8,128)S(1)}, f32[128,512]{1,0:T(8,128)}, u32[]{:S(2)}) copy-start(f32[128,512]{1,0:T(8,128)} %get-tuple-element.28) | copy-start | bytes 786436
  40.0 1.0 %copy-start.1 = (f32[128,512]{1,0:T(8,128)S(1)}, f32[128,512]{1,0:T(8,128)}, u32[]{:S(2)}) copy-start(f32[128,512]{1,0:T(8,128)} %copy-done) | copy-start | bytes 786436
  40.1 1.0 %copy-start.3 = (f32[128,512]{1,0:T(8,128)S(1)}, f32[128,512]{1,0:T(8,128)}, u32[]{:S(2)}) copy-start(f32[128,512]{1,0:T(8,128)} %copy-done.2) | copy-start | bytes 786436
  41.1 1.0 %copy-start.9 = (bf16[1,128,1,256]{1,3,2,0:T(8,128)(2,1)S(1)}, bf16[1,128,1,256]{1,3,2,0:T(8,128)(2,1)}, u32[]{:S(2)}) copy-start(bf16[1,128,1,256]{1,3,2,0:T(8,128)(2,1)} %copy-done.8) | copy-start | bytes 196612
  41.1 1.0 %copy-start.11 = (bf16[1,128,1,256]{1,3,2,0:T(8,128)(2,1)S(1)}, bf16[1,128,1,256]{1,3,2,0:T(8,128)(2,1)}, u32[]{:S(2)}) copy-start(bf16[1,128,1,256]{1,3,2,0:T(8,128)(2,1)} %copy-done.10) | copy-start | bytes 196612
  41.1 1.0 %copy-start.16 = (bf16[1,128,1,256]{1,3,2,0:T(8,128)(2,1)S(1)}, bf16[1,128,1,256]{1,3,2,0:T(8,128)(2,1)}, u32[]{:S(2)}) copy-start(bf16[1,128,1,256]{1,3,2,0:T(8,128)(2,1)} %copy.22) | copy-start | bytes 196612
  42.2 6.9 %collective-permute-start.3 = (bf16[1,128,256]{1,2,0:T(8,128)(2,1)S(1)}, bf16[1,128,256]{1,2,0:T(8,128)(2,1)S(1)}, u32[]{:S(2)}, u32[]{:S(2)}) collective-permute-start(bf16[1,128,256]{1,2,0:T(8,128)(2,1)S(1)} %get-tuple-element.33), channel_id=1, source_target_pairs={{0,1},{1,2},{2,3},{3,4},{4,5},{5,6},{6,7},{8,9},{9,10},{10,11},{11... | collective-permute-start | bytes 196616 | tf_op jit(solution)/shard_map/ppermute | solution.py:22
  46.5 7.9 %collective-permute-start.4 = (bf16[1,128,3,256]{1,3,2,0:T(8,128)(2,1)S(1)}, bf16[1,128,3,256]{1,3,2,0:T(8,128)(2,1)S(1)}, u32[]{:S(2)}, u32[]{:S(2)}) collective-permute-start(bf16[1,128,3,256]{1,3,2,0:T(8,128)(2,1)S(1)} %pad_maximum_fusion.10), channel_id=1, source_target_pairs={{1,0},{2,1},{3,2},{4,3},{5,4},{6,5},{7,6},{9,8},{10,9},{11,10},{12... | collective-permute-start | bytes 589832 | tf_op jit(solution)/shard_map/ppermute | solution.py:22

commit v5 on v4

--- a/solution.py
+++ b/solution.py
@@ -95,7 +95,7 @@
     acc = 0.0
     for s in range(1, blocks):
         first = jnp.where(place + s < blocks, mixed_rows, weighted_rows)
-        payload = jnp.concatenate([first, back_rows, taps], axis=0)
+        payload = jnp.concatenate([first, taps], axis=0)
         pairs = [(i, (i + s) % blocks) for i in range(blocks)]
         got = lax.ppermute(payload, "ctx", pairs)
         table = block_table(packed, (place - s) % blocks)
@@ -106,17 +106,23 @@
     c = channels
     mixed_spec = loc[:c] + acc[:c]
     weighted_spec = loc[c : 2 * c] + acc[:c]
-    back_spec = loc[2 * c : 3 * c] + acc[c : 2 * c]
-    taps_spec = jnp.repeat(loc[3 * c :] + acc[2 * c :], CPF, axis=0)
+    back_spec = loc[2 * c : 3 * c]
+    taps_spec = jnp.repeat(loc[3 * c :] + acc[c:], CPF, axis=0)
     conv = packed_products(taps_spec, mixed_spec, False)
     gm = packed_products(taps_spec, weighted_spec, True)
     fgs = packed_products(back_spec, weighted_spec, True)
     fgs = fgs.reshape(-1, CPF, size).sum(axis=1)
-    both = jnp.concatenate([conv, gm, fgs], axis=0)
     cols = lax.broadcasted_iota(jnp.int32, (1, size), 1)
     weight = jnp.where((cols == 0) | (cols == half), 1.0 / size, 2.0 / size)
+    both = jnp.concatenate([conv, gm], axis=0)
     out = jnp.einsum("tf,rf->tr", own_table * weight, both, precision=precise)
-    return out[:, :c], out[:, c : 2 * c], out[:, 2 * c :].T
+    lag = jnp.einsum("rf,tf->rt", fgs, own_table * weight, precision=precise)
+    for s in range(1, blocks):
+        table = block_table(packed, (place + s) % blocks) * weight
+        share = jnp.einsum("rf,tf->rt", fgs, table, precision=precise)
+        pairs = [(i, (i + s) % blocks) for i in range(blocks)]
+        lag = lag + lax.ppermute(share, "ctx", pairs)
+    return out[:, :c], out[:, c:], lag
 
 
 def chunk_work(local3, common, hsum, tables):

time: 55.7 us -> 43.4 us (0.78)
  the two profiles are of different devices: /device:TPU:19 before, /device:TPU:4 now
where the time goes in v5:
time: 43.4 us; the launch traced here: 43.2 us
  starting transfers between devices  17.6 us (41%)
  waiting for transfers between devices  11.5 us (26%)
  matrix products  6.62 us (15%)
  other arithmetic  3.98 us (9%)
  local copies, waits for them, and re-layouts  2.42 us (6%)
  between operations  1.01 us (2%)
    ppermute x3, starting transfers between devices, dense_path(): lag = lag + lax.ppermute(share, 'ctx', pairs)  8.37 us
    ppermute x3, waiting for transfers between devices, dense_path(): got = lax.ppermute(payload, 'ctx', pairs)  7.94 us
    ppermute x3, starting transfers between devices, dense_path(): got = lax.ppermute(payload, 'ctx', pairs)  4.68 us
    ppermute x2, starting transfers between devices, from_behind(): return lax.ppermute(x, axis, pairs)  4.59 us
    ppermute x2, waiting for transfers between devices, from_behind(): return lax.ppermute(x, axis, pairs)  3.58 us
    unnamed x19, local copies, waits for them, and re-layouts  2.27 us
    dot_general x3, matrix products, dense_path(): acc = acc + jnp.dot(got, table, precision=precise)  2.02 us
    dot_general x1, matrix products, dense_path(): loc = jnp.dot(own, own_table, precision=precise)  1.48 us
  transfers between devices with their start and end apart: 8, of which 3 were waited for; matrix products, arithmetic and copies ran while one was open for 17% of the time, Pallas kernels for 0%

profile of v5, /device:TPU:4, one launch (start us, length us, event | category | flops | bytes accessed | tf_op | source)
XLA Modules:
  0.0 43.2 jit_solution(9558910571187853738)
XLA Ops:
  0.6 0.0 copy-start.6
  0.6 0.0 copy-start.7
  0.7 0.0 copy-start
  0.7 0.0 copy-start.1
  0.7 0.0 copy-start.2
  0.7 0.0 copy-start.3
  0.7 0.0 copy-start.4
  0.7 0.0 copy-start.5
  0.7 0.9 %copy.12 = f32[1,16,128]{1,2,0:T(8,128)S(1)} copy(f32[1,16,128]{2,1,0:T(8,128)} %param.13) | data formatting | bytes 16384 | tf_op args[4]
  1.7 1.0 %broadcast_select_fusion.2 = (f32[256,128]{0,1:T(8,128)S(1)}, f32[256,128]{0,1:T(8,128)S(1)}, f32[256,128]{0,1:T(8,128)S(1)}) fusion(pred[]{:T(512)S(6)} %lt.96, bf16[1,128,3,256]{3,1,2,0:T(8,128)(2,1)} %param.10, bf16[1,128,256]{2,1,0:T(8,128)(2,1)} %param.12, bf16[1,128,3,256]{3,1,2,0:T(8,128)(2,1)} %param.9, pred[]{:T(512)S(6)} %lt.99, pred[]{:T(512)S(6)} %lt.102), kind=kLoop, calls=%fused_computation.109 | loop fusion | flops 294912 | bytes 655363 | tf_op jit(solution)/shard_map/jit(_where)/select_n | solution.py:97
  2.7 2.7 %collective-permute-start.1 = (f32[272,128]{0,1:T(8,128)S(1)}, f32[272,128]{0,1:T(8,128)S(1)}, u32[]{:S(2)}, u32[]{:S(2)}) collective-permute-start(f32[272,128]{0,1:T(8,128)S(1)} %get-tuple-element.46), channel_id=1, source_target_pairs={{0,16},{8,24},{16,0},{24,8},{1,17},{9,25},{17,1},{25,9},{2,18},{10... | collective-permute-start | bytes 417800 | tf_op jit(solution)/shard_map/ppermute | solution.py:100
  5.3 1.3 %collective-permute-start.2 = (f32[272,128]{0,1:T(8,128)S(1)}, f32[272,128]{0,1:T(8,128)S(1)}, u32[]{:S(2)}, u32[]{:S(2)}) collective-permute-start(f32[272,128]{0,1:T(8,128)S(1)} %get-tuple-element.47), channel_id=1, source_target_pairs={{0,24},{8,0},{16,8},{24,16},{1,25},{9,1},{17,9},{25,17},{2,26},{10... | collective-permute-start | bytes 417800 | tf_op jit(solution)/shard_map/ppermute | solution.py:100
  6.7 0.7 %collective-permute-start = (f32[272,128]{0,1:T(8,128)S(1)}, f32[272,128]{0,1:T(8,128)S(1)}, u32[]{:S(2)}, u32[]{:S(2)}) collective-permute-start(f32[272,128]{0,1:T(8,128)S(1)} %get-tuple-element.45), channel_id=1, source_target_pairs={{0,8},{8,16},{16,24},{24,0},{1,9},{9,17},{17,25},{25,1},{2,10},{10... | collective-permute-start | bytes 417800 | tf_op jit(solution)/shard_map/ppermute | solution.py:100
  7.4 0.0 copy-done.2
  7.4 0.9 %fusion.49 = (f32[256,128]{0,1:T(8,128)S(1)}, f32[256,128]{0,1:T(8,128)S(1)}) fusion(bf16[1,128,256]{2,1,0:T(8,128)(2,1)} %param.12, bf16[1,128,3,256]{3,1,2,0:T(8,128)(2,1)S(1)} %copy-done.2), kind=kLoop, calls=%fused_computation.92 | loop fusion | flops 196608 | bytes 524288 | tf_op jit(solution)/shard_map/transpose | solution.py:193
  8.3 0.0 copy-done.4
  8.3 0.0 copy-done.3
  8.3 0.0 copy-done.5
  8.4 0.0 copy-done.6
  8.4 0.0 copy-done.7
  8.4 0.0 copy-done
  8.5 0.0 copy-done.1
  8.5 0.1 multiply_subtract_fusion.5
  8.6 0.5 %multiply_subtract_fusion.9 = (f32[128,512]{1,0:T(8,128)S(1)}, f32[128,512]{1,0:T(8,128)S(1)}, f32[128,512]{1,0:T(8,128)S(1)}, f32[128,512]{1,0:T(8,128)S(1)}, f...) fusion(f32[128,512]{1,0:T(8,128)S(1)} %copy-done.1, ...), kind=kLoop, calls=%fused_computation.84 | loop fusion | flops 3407872 | bytes 3696256 | tf_op jit(solution)/shard_map/sub | solution.py:71
  9.1 1.5 %fusion.35 = f32[784,1024]{1,0:T(8,128)S(1)} fusion(f32[16,128]{0,1:T(8,128)S(1)} %bitcast.90, f32[256,128]{0,1:T(8,128)S(1)} %get-tuple-element.44, f32[256,128]{0,1:T(8,128)S(1)} %get-tuple-element.43, f32[256,128]{0,1:T(8,128)S(1)} %multiply_bitcast_fusion, f32[128,512]{1,0:T(8,128)S(1)} %get-tuple-element.26, f32[128,512]{1,0:T(8,128)S(1)} %get-tuple-element.25), kind=kOutput, calls=%fused_computation.53 | convolution fusion | flops 616994816 | bytes 4136960 | tf_op jit(solution)/shard_map/dot_general | solution.py:105
  10.6 6.1 %collective-permute-done.1 = f32[272,128]{0,1:T(8,128)S(1)} collective-permute-done((f32[272,128]{0,1:T(8,128)S(1)}, f32[272,128]{0,1:T(8,128)S(1)}, u32[]{:S(2)}, u32[]{:S(2)}) %collective-permute-start.1) | collective-permute-done | bytes 139296 | tf_op jit(solution)/shard_map/ppermute | solution.py:100
  16.7 0.6 %fusion.16 = f32[272,1024]{1,0:T(8,128)S(1)} fusion(f32[272,128]{0,1:T(8,128)S(1)} %collective-permute-done.1, f32[128,512]{1,0:T(8,128)S(1)} %get-tuple-element.35, f32[128,512]{1,0:T(8,128)S(1)} %get-tuple-element.36), kind=kOutput, calls=%fused_computation.23 | convolution fusion | flops 214040576 | bytes 1777664 | tf_op jit(solution)/shard_map/dot_general | solution.py:102
  17.4 0.0 collective-permute-done.2
  17.4 0.7 %fusion.20 = f32[272,1024]{1,0:T(8,128)S(1)} fusion(f32[272,128]{0,1:T(8,128)S(1)} %collective-permute-done.2, f32[128,512]{1,0:T(8,128)S(1)} %get-tuple-element.24, f32[128,512]{1,0:T(8,128)S(1)} %get-tuple-element.23), kind=kOutput, calls=%fused_computation.27 | convolution fusion | flops 214040576 | bytes 1777664 | tf_op jit(solution)/shard_map/dot_general | solution.py:102
  18.1 1.8 %collective-permute-done = f32[272,128]{0,1:T(8,128)S(1)} collective-permute-done((f32[272,128]{0,1:T(8,128)S(1)}, f32[272,128]{0,1:T(8,128)S(1)}, u32[]{:S(2)}, u32[]{:S(2)}) %collective-permute-start) | collective-permute-done | bytes 139296 | tf_op jit(solution)/shard_map/ppermute | solution.py:100
  19.9 0.7 %fusion.8 = f32[272,1024]{1,0:T(8,128)S(1)} fusion(f32[272,1024]{1,0:T(8,128)S(1)} %fusion.20, f32[272,1024]{1,0:T(8,128)S(1)} %fusion.16, f32[272,128]{0,1:T(8,128)S(1)} %collective-permute-done, f32[128,512]{1,0:T(8,128)S(1)} %get-tuple-element.33, f32[128,512]{1,0:T(8,128)S(1)} %get-tuple-element.34), kind=kOutput, calls=%fused_computation.9 | convolution fusion | flops 214597632 | bytes 4005888 | tf_op jit(solution)/shard_map/dot_general | solution.py:102
  20.6 0.4 slice_add_fusion.1
  21.1 0.1 broadcast_in_dim.26
  21.2 0.4 %multiply_subtract_fusion = (f32[256,512]{1,0:T(8,128)S(1)}, f32[256,512]{1,0:T(8,128)S(1)}, f32[256,512]{1,0:T(8,128)S(1)}, f32[256,512]{1,0:T(8,128)S(1)}) fusion(f32[784,1024]{1,0:T(8,128)S(1)} %fusion.35, f32[256,1024]{1,0:T(8,128)S(1)} %get-tuple-element.4, pred[512]{0:T(512)(128)(4,1)S(1)} %iota_compare_fusion.2, f32[256,1024]{1,0:T(8,128)S(1)} %bitcast.87), kind=kLoop, calls=%fused_computation.44 | loop fusion | flops 2621440 | bytes 5243392 | tf_op jit(solution)/shard_map/sub | solution.py:85
  21.6 0.2 bitcast_reduce_fusion
  21.8 0.3 fusion.24
  22.1 4.3 %collective-permute-start.5 = (f32[16,128]{1,0:T(8,128)S(1)}, f32[16,128]{1,0:T(8,128)S(1)}, u32[]{:S(2)}, u32[]{:S(2)}) collective-permute-start(f32[16,128]{1,0:T(8,128)S(1)} %fusion.24), channel_id=1, source_target_pairs={{0,8},{8,16},{16,24},{24,0},{1,9},{9,17},{17,25},{25,1},{2,10},{10... | collective-permute-start | bytes 24584 | tf_op jit(solution)/shard_map/ppermute | solution.py:124
  26.4 0.3 fusion.27
  26.8 1.4 %collective-permute-start.6 = (f32[16,128]{1,0:T(8,128)S(1)}, f32[16,128]{1,0:T(8,128)S(1)}, u32[]{:S(2)}, u32[]{:S(2)}) collective-permute-start(f32[16,128]{1,0:T(8,128)S(1)} %fusion.27), channel_id=1, source_target_pairs={{0,16},{8,24},{16,0},{24,8},{1,17},{9,25},{17,1},{25,9},{2,18},{10... | collective-permute-start | bytes 24584 | tf_op jit(solution)/shard_map/ppermute | solution.py:124
  28.2 0.2 select_subtract_fusion
  28.4 1.2 %fusion = f32[128,512]{1,0:T(8,128)S(1)} fusion(f32[256,512]{1,0:T(8,128)S(1)} %get-tuple-element.11, f32[256,512]{1,0:T(8,128)S(1)} %get-tuple-element.12, f32[256,512]{1,0:T(8,128)S(1)} %get-tuple-element.8, f32[256,512]{1,0:T(8,128)S(1)} %get-tuple-element.7, f32[128,512]{1,0:T(8,128)S(1)} %get-tuple-element.26, f32[128,512]{1,0:T(8,128)S(1)} %get-tuple-element.25, ...), kind=kOutput, calls=%fused_computation | convolution fusion | flops 404488192 | bytes 2887680 | tf_op jit(solution)/shard_map/tf,rf->tr/dot_general | solution.py:118
  29.6 0.1 fusion.58
  29.7 2.7 %collective-permute-start.4 = (bf16[1,128,3,256]{3,1,2,0:T(8,128)(2,1)S(1)}, bf16[1,128,3,256]{3,1,2,0:T(8,128)(2,1)S(1)}, u32[]{:S(2)}, u32[]{:S(2)}) collective-permute-start(bf16[1,128,3,256]{3,1,2,0:T(8,128)(2,1)S(1)} %pad_maximum_fusion.8), channel_id=1, source_target_pairs={{1,0},{2,1},{3,2},{4,3},{5,4},{6,5},{7,6},{9,8},{10,9},{11,10},{12... | collective-permute-start | bytes 589832 | tf_op jit(solution)/shard_map/ppermute | solution.py:22
  32.4 0.3 fusion.30
  32.8 2.7 %collective-permute-start.7 = (f32[16,128]{1,0:T(8,128)S(1)}, f32[16,128]{1,0:T(8,128)S(1)}, u32[]{:S(2)}, u32[]{:S(2)}) collective-permute-start(f32[16,128]{1,0:T(8,128)S(1)} %fusion.30), channel_id=1, source_target_pairs={{0,24},{8,0},{16,8},{24,16},{1,25},{9,1},{17,9},{25,17},{2,26},{10... | collective-permute-start | bytes 24584 | tf_op jit(solution)/shard_map/ppermute | solution.py:124
  35.4 1.9 %collective-permute-start.3 = (bf16[1,128,256]{2,1,0:T(8,128)(2,1)S(1)}, bf16[1,128,256]{2,1,0:T(8,128)(2,1)S(1)}, u32[]{:S(2)}, u32[]{:S(2)}) collective-permute-start(bf16[1,128,256]{2,1,0:T(8,128)(2,1)S(1)} %get-tuple-element.42), channel_id=1, source_target_pairs={{0,1},{1,2},{2,3},{3,4},{4,5},{5,6},{6,7},{8,9},{9,10},{10,11},{11... | collective-permute-start | bytes 196616 | tf_op jit(solution)/shard_map/ppermute | solution.py:22
  37.3 0.0 collective-permute-done.5
  37.3 0.0 collective-permute-done.6
  37.3 0.0 collective-permute-done.7
  37.4 0.9 %fusion.12 = f32[1,16,128]{2,1,0:T(8,128)} fusion(f32[16,128]{1,0:T(8,128)S(1)} %collective-permute-done.7, f32[16,128]{1,0:T(8,128)S(1)} %collective-permute-done.6, f32[16,128]{1,0:T(8,128)S(1)} %collective-permute-done.5, f32[16,1024]{1,0:T(8,128)S(1)} %bitcast_reduce_fusion, f32[128,512]{1,0:T(8,128)S(1)} %get-tuple-element.26, ...), kind=kOutput, calls=%fused_computation.14 | convolution fusion | flops 12853248 | bytes 626688 | tf_op jit(solution)/shard_map/rf,tf->rt/dot_general | solution.py:119
  38.3 3.6 %collective-permute-done.3 = bf16[1,128,256]{2,1,0:T(8,128)(2,1)S(1)} collective-permute-done((bf16[1,128,256]{2,1,0:T(8,128)(2,1)S(1)}, bf16[1,128,256]{2,1,0:T(8,128)(2,1)S(1)}, u32[]{:S(2)}, u32[]{:S(2)}) %collective-permute-start.3) | collective-permute-done | bytes 65568 | tf_op jit(solution)/shard_map/ppermute | solution.py:22
  41.9 0.0 collective-permute-done.4
  41.9 0.6 %copy.15 = bf16[1,128,256]{2,1,0:T(8,128)(2,1)} copy(bf16[1,128,256]{2,1,0:T(8,128)(2,1)S(1)} %collective-permute-done.3) | data formatting | bytes 131072
  42.5 0.7 %copy.16 = bf16[1,128,3,256]{3,1,2,0:T(8,128)(2,1)} copy(bf16[1,128,3,256]{3,1,2,0:T(8,128)(2,1)S(1)} %collective-permute-done.4) | data formatting | bytes 393216
  (10 shorter events, 0.2 us)
Async XLA Ops:
  0.6 7.8 %copy-start.6 = (f32[4,512]{1,0:T(4,128)S(1)}, f32[4,512]{1,0:T(4,128)}, u32[]{:S(2)}) copy-start(f32[4,512]{1,0:T(4,128)} %constant.139.clone) | copy-start | bytes 24580
  0.6 7.8 %copy-start.7 = (f32[4,512]{1,0:T(4,128)S(1)}, f32[4,512]{1,0:T(4,128)}, u32[]{:S(2)}) copy-start(f32[4,512]{1,0:T(4,128)} %constant.140.clone) | copy-start | bytes 24580
  0.7 7.8 %copy-start = (f32[128,512]{1,0:T(8,128)S(1)}, f32[128,512]{1,0:T(8,128)}, u32[]{:S(2)}) copy-start(f32[128,512]{1,0:T(8,128)} %constant.137.clone) | copy-start | bytes 786436
  0.7 7.8 %copy-start.1 = (f32[128,512]{1,0:T(8,128)S(1)}, f32[128,512]{1,0:T(8,128)}, u32[]{:S(2)}) copy-start(f32[128,512]{1,0:T(8,128)} %constant.138.clone) | copy-start | bytes 786436
  0.7 6.7 %copy-start.2 = (bf16[1,128,3,256]{3,1,2,0:T(8,128)(2,1)S(1)}, bf16[1,128,3,256]{3,1,2,0:T(8,128)(2,1)}, u32[]{:S(2)}) copy-start(bf16[1,128,3,256]{3,1,2,0:T(8,128)(2,1)} %param.10) | copy-start | bytes 589828
  0.7 7.6 %copy-start.3 = (bf16[1,128,256]{2,1,0:T(8,128)(2,1)S(1)}, bf16[1,128,256]{2,1,0:T(8,128)(2,1)}, u32[]{:S(2)}) copy-start(bf16[1,128,256]{2,1,0:T(8,128)(2,1)} %param.12) | copy-start | bytes 196612
  0.7 7.6 %copy-start.4 = (bf16[1,128,3,256]{3,1,2,0:T(8,128)(2,1)S(1)}, bf16[1,128,3,256]{3,1,2,0:T(8,128)(2,1)}, u32[]{:S(2)}) copy-start(bf16[1,128,3,256]{3,1,2,0:T(8,128)(2,1)} %param.9) | copy-start | bytes 589828
  0.7 7.6 %copy-start.5 = (f32[1,128,256]{2,1,0:T(8,128)S(1)}, f32[1,128,256]{2,1,0:T(8,128)}, u32[]{:S(2)}) copy-start(f32[1,128,256]{2,1,0:T(8,128)} %param.11) | copy-start | bytes 393220
  2.7 14.1 %collective-permute-start.1 = (f32[272,128]{0,1:T(8,128)S(1)}, f32[272,128]{0,1:T(8,128)S(1)}, u32[]{:S(2)}, u32[]{:S(2)}) collective-permute-start(f32[272,128]{0,1:T(8,128)S(1)} %get-tuple-element.46), channel_id=1, source_target_pairs={{0,16},{8,24},{16,0},{24,8},{1,17},{9,25},{17,1},{25,9},{2,18},{10... | collective-permute-start | bytes 417800 | tf_op jit(solution)/shard_map/ppermute | solution.py:100
  5.3 12.1 %collective-permute-start.2 = (f32[272,128]{0,1:T(8,128)S(1)}, f32[272,128]{0,1:T(8,128)S(1)}, u32[]{:S(2)}, u32[]{:S(2)}) collective-permute-start(f32[272,128]{0,1:T(8,128)S(1)} %get-tuple-element.47), channel_id=1, source_target_pairs={{0,24},{8,0},{16,8},{24,16},{1,25},{9,1},{17,9},{25,17},{2,26},{10... | collective-permute-start | bytes 417800 | tf_op jit(solution)/shard_map/ppermute | solution.py:100
  6.7 13.2 %collective-permute-start = (f32[272,128]{0,1:T(8,128)S(1)}, f32[272,128]{0,1:T(8,128)S(1)}, u32[]{:S(2)}, u32[]{:S(2)}) collective-permute-start(f32[272,128]{0,1:T(8,128)S(1)} %get-tuple-element.45), channel_id=1, source_target_pairs={{0,8},{8,16},{16,24},{24,0},{1,9},{9,17},{17,25},{25,1},{2,10},{10... | collective-permute-start | bytes 417800 | tf_op jit(solution)/shard_map/ppermute | solution.py:100
  22.1 15.2 %collective-permute-start.5 = (f32[16,128]{1,0:T(8,128)S(1)}, f32[16,128]{1,0:T(8,128)S(1)}, u32[]{:S(2)}, u32[]{:S(2)}) collective-permute-start(f32[16,128]{1,0:T(8,128)S(1)} %fusion.24), channel_id=1, source_target_pairs={{0,8},{8,16},{16,24},{24,0},{1,9},{9,17},{17,25},{25,1},{2,10},{10... | collective-permute-start | bytes 24584 | tf_op jit(solution)/shard_map/ppermute | solution.py:124
  26.8 10.6 %collective-permute-start.6 = (f32[16,128]{1,0:T(8,128)S(1)}, f32[16,128]{1,0:T(8,128)S(1)}, u32[]{:S(2)}, u32[]{:S(2)}) collective-permute-start(f32[16,128]{1,0:T(8,128)S(1)} %fusion.27), channel_id=1, source_target_pairs={{0,16},{8,24},{16,0},{24,8},{1,17},{9,25},{17,1},{25,9},{2,18},{10... | collective-permute-start | bytes 24584 | tf_op jit(solution)/shard_map/ppermute | solution.py:124
  29.7 12.1 %collective-permute-start.4 = (bf16[1,128,3,256]{3,1,2,0:T(8,128)(2,1)S(1)}, bf16[1,128,3,256]{3,1,2,0:T(8,128)(2,1)S(1)}, u32[]{:S(2)}, u32[]{:S(2)}) collective-permute-start(bf16[1,128,3,256]{3,1,2,0:T(8,128)(2,1)S(1)} %pad_maximum_fusion.8), channel_id=1, source_target_pairs={{1,0},{2,1},{3,2},{4,3},{5,4},{6,5},{7,6},{9,8},{10,9},{11,10},{12... | collective-permute-start | bytes 589832 | tf_op jit(solution)/shard_map/ppermute | solution.py:22
  32.8 4.6 %collective-permute-start.7 = (f32[16,128]{1,0:T(8,128)S(1)}, f32[16,128]{1,0:T(8,128)S(1)}, u32[]{:S(2)}, u32[]{:S(2)}) collective-permute-start(f32[16,128]{1,0:T(8,128)S(1)} %fusion.30), channel_id=1, source_target_pairs={{0,24},{8,0},{16,8},{24,16},{1,25},{9,1},{17,9},{25,17},{2,26},{10... | collective-permute-start | bytes 24584 | tf_op jit(solution)/shard_map/ppermute | solution.py:124
  35.4 6.5 %collective-permute-start.3 = (bf16[1,128,256]{2,1,0:T(8,128)(2,1)S(1)}, bf16[1,128,256]{2,1,0:T(8,128)(2,1)S(1)}, u32[]{:S(2)}, u32[]{:S(2)}) collective-permute-start(bf16[1,128,256]{2,1,0:T(8,128)(2,1)S(1)} %get-tuple-element.42), channel_id=1, source_target_pairs={{0,1},{1,2},{2,3},{3,4},{4,5},{5,6},{6,7},{8,9},{9,10},{10,11},{11... | collective-permute-start | bytes 196616 | tf_op jit(solution)/shard_map/ppermute | solution.py:22

commit v6 on v5

--- a/solution.py
+++ b/solution.py
@@ -116,12 +116,9 @@
     weight = jnp.where((cols == 0) | (cols == half), 1.0 / size, 2.0 / size)
     both = jnp.concatenate([conv, gm], axis=0)
     out = jnp.einsum("tf,rf->tr", own_table * weight, both, precision=precise)
-    lag = jnp.einsum("rf,tf->rt", fgs, own_table * weight, precision=precise)
-    for s in range(1, blocks):
-        table = block_table(packed, (place + s) % blocks) * weight
-        share = jnp.einsum("rf,tf->rt", fgs, table, precision=precise)
-        pairs = [(i, (i + s) % blocks) for i in range(blocks)]
-        lag = lag + lax.ppermute(share, "ctx", pairs)
+    tables = jnp.stack([block_table(packed, b) for b in range(blocks)]) * weight
+    shares = jnp.einsum("rf,btf->brt", fgs, tables, precision=precise)
+    lag = lax.psum_scatter(shares, "ctx", scatter_dimension=0, tiled=True)[0]
     return out[:, :c], out[:, c:], lag
 
 

time: 43.4 us -> 66.4 us (1.53)
  the two profiles are of different devices: /device:TPU:4 before, /device:TPU:0 now
where the time goes in v6:
time: 66.4 us; the launch traced here: 65.9 us
  waiting for transfers between devices  21.9 us (33%)
  between operations  14.5 us (22%)
  matrix products  9.05 us (14%)
  starting transfers between devices  8.68 us (13%)
  other arithmetic  7.82 us (12%)
  local copies, waits for them, and re-layouts  4.01 us (6%)
    reduce_scatter x1, waiting for transfers between devices, dense_path(): lag = lax.psum_scatter(shares, 'ctx', scatter_dimension=0, tiled=True)[0]  17.4 us
    ppermute x3, starting transfers between devices, dense_path(): got = lax.ppermute(payload, 'ctx', pairs)  6.06 us
    dot_general x3, matrix products, dense_path(): acc = acc + jnp.dot(got, table, precision=precise)  4.8 us
    ppermute x3, waiting for transfers between devices, dense_path(): got = lax.ppermute(payload, 'ctx', pairs)  4.43 us
    unnamed x31, local copies, waits for them, and re-layouts  3.87 us
    ppermute x2, starting transfers between devices, from_behind(): return lax.ppermute(x, axis, pairs)  2.59 us
    dot_general x1, matrix products, dense_path(): shares = jnp.einsum('rf,btf->brt', fgs, tables, precision=precise)  1.55 us
    sub x1, other arithmetic, block_table(): cos = base_c * c - base_s * s  1.51 us
  transfers between devices with their start and end apart: 6, of which 3 were waited for; matrix products, arithmetic and copies ran while one was open for 15% of the time, Pallas kernels for 0%

profile of v6, /device:TPU:0, one launch (start us, length us, event | category | flops | bytes accessed | tf_op | source)
XLA Modules:
  0.0 65.9 jit_solution(6223674630393688858)
XLA Ops:
  7.2 0.0 copy-start.12
  7.2 0.0 copy-start.13
  7.2 0.0 copy-start
  7.2 0.0 copy-start.5
  7.2 0.0 copy-start.6
  7.2 0.0 copy-start.7
  7.2 0.0 copy-start.3
  7.3 0.0 reduce-scatter.2.cloned.1.call-start
  7.3 0.9 %copy.12 = f32[1,16,128]{1,2,0:T(8,128)S(1)} copy(f32[1,16,128]{2,1,0:T(8,128)} %param.13) | data formatting | bytes 16384 | tf_op args[4]
  8.2 1.0 %broadcast_select_fusion.2 = (f32[256,128]{0,1:T(8,128)S(1)}, f32[256,128]{0,1:T(8,128)S(1)}, f32[256,128]{0,1:T(8,128)S(1)}) fusion(pred[]{:T(512)S(6)} %lt.85, bf16[1,128,3,256]{3,1,2,0:T(8,128)(2,1)} %param.10, bf16[1,128,256]{2,1,0:T(8,128)(2,1)} %param.12, bf16[1,128,3,256]{3,1,2,0:T(8,128)(2,1)} %param.9, pred[]{:T(512)S(6)} %lt.88, pred[]{:T(512)S(6)} %lt.91), kind=kLoop, calls=%fused_computation.100 | loop fusion | flops 294912 | bytes 655363 | tf_op jit(solution)/shard_map/jit(_where)/select_n | solution.py:97
  9.2 0.8 %pad_maximum_fusion.6 = (f32[272,128]{0,1:T(8,128)}, f32[272,128]{0,1:T(8,128)}, f32[272,128]{0,1:T(8,128)}) fusion(f32[16,128]{0,1:T(8,128)S(1)} %bitcast.90, f32[256,128]{0,1:T(8,128)S(1)} %get-tuple-element.29, f32[256,128]{0,1:T(8,128)S(1)} %get-tuple-element.30, f32[256,128]{0,1:T(8,128)S(1)} %get-tuple-element.31), kind=kLoop, calls=%fused_computation.60 | loop fusion | flops 104448 | bytes 819200 | tf_op jit(solution)/shard_map/concatenate | solution.py:98
  10.0 4.0 %collective-permute-start.1 = (f32[272,128]{0,1:T(8,128)}, f32[272,128]{0,1:T(8,128)}, u32[]{:S(2)}, u32[]{:S(2)}) collective-permute-start(f32[272,128]{0,1:T(8,128)} %get-tuple-element.36), channel_id=1, source_target_pairs={{0,16},{8,24},{16,0},{24,8},{1,17},{9,25},{17,1},{25,9},{2,18},{10... | collective-permute-start | bytes 417800 | tf_op jit(solution)/shard_map/ppermute | solution.py:100
  14.1 1.3 %collective-permute-start.2 = (f32[272,128]{0,1:T(8,128)}, f32[272,128]{0,1:T(8,128)}, u32[]{:S(2)}, u32[]{:S(2)}) collective-permute-start(f32[272,128]{0,1:T(8,128)} %get-tuple-element.37), channel_id=1, source_target_pairs={{0,24},{8,0},{16,8},{24,16},{1,25},{9,1},{17,9},{25,17},{2,26},{10... | collective-permute-start | bytes 417800 | tf_op jit(solution)/shard_map/ppermute | solution.py:100
  15.4 0.7 %collective-permute-start = (f32[272,128]{0,1:T(8,128)}, f32[272,128]{0,1:T(8,128)}, u32[]{:S(2)}, u32[]{:S(2)}) collective-permute-start(f32[272,128]{0,1:T(8,128)} %get-tuple-element.35), channel_id=1, source_target_pairs={{0,8},{8,16},{16,24},{24,0},{1,9},{9,17},{17,25},{25,1},{2,10},{10... | collective-permute-start | bytes 417800 | tf_op jit(solution)/shard_map/ppermute | solution.py:100
  16.1 1.0 %fusion.44 = (f32[256,128]{0,1:T(8,128)S(1)}, f32[256,128]{0,1:T(8,128)S(1)}) fusion(bf16[1,128,256]{2,1,0:T(8,128)(2,1)} %param.12, bf16[1,128,3,256]{3,1,2,0:T(8,128)(2,1)} %param.10), kind=kLoop, calls=%fused_computation.82 | loop fusion | flops 196608 | bytes 524288 | tf_op jit(solution)/shard_map/transpose | solution.py:190
  17.1 0.0 copy-done.3
  17.1 0.0 copy-done.12
  17.1 0.0 copy-done.13
  17.2 0.0 copy-done
  17.2 0.0 copy-done.5
  17.2 0.0 copy-done.6
  17.2 0.0 copy-done.7
  17.2 0.0 copy-start.2
  17.2 0.0 copy-start.11
  17.2 0.0 copy-start.10
  17.3 1.5 %multiply_subtract_fusion.6 = (f32[128,512]{1,0:T(8,128)S(1)}, f32[128,512]{1,0:T(8,128)S(1)}, f32[128,512]{1,0:T(8,128)S(1)}, f32[128,512]{1,0:T(8,128)S(1)}, f...) fusion(f32[128,512]{1,0:T(8,128)S(1)} %copy-done.5, ...), kind=kLoop, calls=%fused_computation.74 | loop fusion | flops 2621440 | bytes 4736640 | tf_op jit(solution)/shard_map/sub | solution.py:71
  18.8 0.0 copy-start.9
  18.8 0.0 copy-done.2
  18.8 0.0 copy-done.11
  18.9 0.0 copy-done.10
  18.9 0.8 %copy-done.9 = f32[128,512]{1,0:T(8,128)S(1)} copy-done((f32[128,512]{1,0:T(8,128)S(1)}, f32[128,512]{1,0:T(8,128)}, u32[]{:S(2)}) %copy-start.9) | copy-done | bytes 262168
  19.8 0.0 copy-start.8
  19.8 1.5 %fusion.30 = f32[784,1024]{1,0:T(8,128)S(1)} fusion(f32[16,128]{0,1:T(8,128)S(1)} %bitcast.91, f32[256,128]{0,1:T(8,128)S(1)} %get-tuple-element.34, f32[256,128]{0,1:T(8,128)S(1)} %get-tuple-element.33, f32[256,128]{0,1:T(8,128)S(1)} %multiply_bitcast_fusion, f32[128,512]{1,0:T(8,128)S(1)} %get-tuple-element.20, f32[128,512]{1,0:T(8,128)S(1)} %get-tuple-element.19), kind=kOutput, calls=%fused_computation.49 | convolution fusion | flops 616994816 | bytes 4136960 | tf_op jit(solution)/shard_map/dot_general | solution.py:105
  21.3 0.0 copy-done.8
  21.3 3.9 %collective-permute-done.1 = f32[272,128]{0,1:T(8,128)} collective-permute-done((f32[272,128]{0,1:T(8,128)}, f32[272,128]{0,1:T(8,128)}, u32[]{:S(2)}, u32[]{:S(2)}) %collective-permute-start.1) | collective-permute-done | bytes 139296 | tf_op jit(solution)/shard_map/ppermute | solution.py:100
  25.2 1.6 %fusion.21 = f32[272,1024]{1,0:T(8,128)S(1)} fusion(f32[272,128]{0,1:T(8,128)} %collective-permute-done.1, f32[128,512]{1,0:T(8,128)S(1)} %get-tuple-element.23, f32[128,512]{1,0:T(8,128)S(1)} %get-tuple-element.24), kind=kOutput, calls=%fused_computation.28 | convolution fusion | flops 214040576 | bytes 1777664 | tf_op jit(solution)/shard_map/dot_general | solution.py:102
  26.8 0.0 collective-permute-done.2
  26.8 1.6 %fusion.25 = f32[272,1024]{1,0:T(8,128)S(1)} fusion(f32[272,128]{0,1:T(8,128)} %collective-permute-done.2, f32[128,512]{1,0:T(8,128)S(1)} %get-tuple-element.25, f32[128,512]{1,0:T(8,128)S(1)} %get-tuple-element.26), kind=kOutput, calls=%fused_computation.32 | convolution fusion | flops 214040576 | bytes 1777664 | tf_op jit(solution)/shard_map/dot_general | solution.py:102
  28.4 0.5 collective-permute-done
  28.9 1.6 %fusion.15 = f32[272,1024]{1,0:T(8,128)S(1)} fusion(f32[272,1024]{1,0:T(8,128)S(1)} %fusion.25, f32[272,1024]{1,0:T(8,128)S(1)} %fusion.21, f32[272,128]{0,1:T(8,128)} %collective-permute-done, f32[128,512]{1,0:T(8,128)S(1)} %get-tuple-element.21, f32[128,512]{1,0:T(8,128)S(1)} %get-tuple-element.22), kind=kOutput, calls=%fused_computation.17 | convolution fusion | flops 214597632 | bytes 4005888 | tf_op jit(solution)/shard_map/dot_general | solution.py:102
  30.6 0.3 slice_add_fusion.1
  30.9 0.1 broadcast_in_dim.25
  31.1 1.2 %multiply_subtract_fusion = (f32[256,512]{1,0:T(8,128)S(1)}, f32[256,512]{1,0:T(8,128)S(1)}, f32[256,512]{1,0:T(8,128)S(1)}, f32[256,512]{1,0:T(8,128)}) fusion(f32[784,1024]{1,0:T(8,128)S(1)} %fusion.30, f32[256,1024]{1,0:T(8,128)S(1)} %get-tuple-element.4, pred[512]{0:T(512)(128)(4,1)S(1)} %iota_compare_fusion.2, f32[256,1024]{1,0:T(8,128)S(1)} %bitcast.88), kind=kLoop, calls=%fused_computation.41 | loop fusion | flops 2621440 | bytes 5243392 | tf_op jit(solution)/shard_map/sub | solution.py:85
  32.3 0.2 bitcast_reduce_fusion
  32.4 1.6 %fusion.16 = f32[4,16,128]{2,1,0:T(8,128)} fusion(f32[1,128,1024]{2,1,0:T(8,128)S(1)} %maximum_bitcast_fusion.3, f32[1,128,1024]{2,1,0:T(8,128)S(1)} %maximum_bitcast_fusion.2, f32[1,128,1024]{2,1,0:T(8,128)S(1)} %maximum_bitcast_fusion.1, f32[1,128,1024]{2,1,0:T(8,128)S(1)} %maximum_bitcast_fusion, f32[1024]{0:T(1024)S(1)} %fusion.57, ...), kind=kOutput, calls=%fused_computation.18 | convolution fusion | flops 52428800 | bytes 2199552 | tf_op jit(solution)/shard_map/rf,btf->brt/dot_general | solution.py:120
  34.0 0.0 reduce-scatter.2.cloned.1.call-update
  34.0 0.0 copy-start.4
  34.0 0.2 select_subtract_fusion
  34.3 0.8 %copy-done.4 = f32[256,512]{1,0:T(8,128)S(1)} copy-done((f32[256,512]{1,0:T(8,128)S(1)}, f32[256,512]{1,0:T(8,128)}, u32[]{:S(2)}) %copy-start.4) | copy-done | bytes 524312
  35.1 0.0 copy-start.1
  35.1 1.2 %fusion = f32[128,512]{1,0:T(8,128)S(1)} fusion(f32[256,512]{1,0:T(8,128)S(1)} %get-tuple-element.11, f32[256,512]{1,0:T(8,128)S(1)} %copy-done.4, f32[256,512]{1,0:T(8,128)S(1)} %get-tuple-element.8, f32[256,512]{1,0:T(8,128)S(1)} %get-tuple-element.7, f32[128,512]{1,0:T(8,128)S(1)} %get-tuple-element.20, f32[128,512]{1,0:T(8,128)S(1)} %get-tuple-element.19, ...), kind=kOutput, calls=%fused_computation | convolution fusion | flops 404488192 | bytes 2887680 | tf_op jit(solution)/shard_map/tf,rf->tr/dot_general | solution.py:118
  36.3 0.0 copy-done.1
  36.3 0.1 fusion.53
  36.4 1.3 %collective-permute-start.3 = (bf16[1,128,256]{2,1,0:T(8,128)(2,1)S(1)}, bf16[1,128,256]{2,1,0:T(8,128)(2,1)S(1)}, u32[]{:S(2)}, u32[]{:S(2)}) collective-permute-start(bf16[1,128,256]{2,1,0:T(8,128)(2,1)S(1)} %get-tuple-element.32), channel_id=1, source_target_pairs={{0,1},{1,2},{2,3},{3,4},{4,5},{5,6},{6,7},{8,9},{9,10},{10,11},{11... | collective-permute-start | bytes 196616 | tf_op jit(solution)/shard_map/ppermute | solution.py:22
  37.7 1.3 %collective-permute-start.4 = (bf16[1,128,3,256]{3,1,2,0:T(8,128)(2,1)S(1)}, bf16[1,128,3,256]{3,1,2,0:T(8,128)(2,1)S(1)}, u32[]{:S(2)}, u32[]{:S(2)}) collective-permute-start(bf16[1,128,3,256]{3,1,2,0:T(8,128)(2,1)S(1)} %pad_maximum_fusion.7), channel_id=1, source_target_pairs={{1,0},{2,1},{3,2},{4,3},{5,4},{6,5},{7,6},{9,8},{10,9},{11,10},{12... | collective-permute-start | bytes 589832 | tf_op jit(solution)/shard_map/ppermute | solution.py:22
  39.0 0.0 collective-permute-done.3
  39.0 17.4 %reduce-scatter.2.cloned.1.call-done = f32[1,16,128]{2,1,0:T(8,128)} async-done(((f32[4,16,128]{2,1,0:T(8,128)}), f32[1,16,128]{2,1,0:T(8,128)}) %reduce-scatter.2.cloned.1.call-update) | async-done | bytes 8208 | tf_op jit(solution)/shard_map/reduce_scatter | solution.py:121
  56.4 1.3 %broadcast_multiply_fusion = f32[1,16,128]{2,1,0:T(8,128)} fusion(f32[1,16,128]{2,1,0:T(8,128)} %reduce-scatter.2.cloned.1.call-done), kind=kLoop, calls=%fused_computation.103 | loop fusion | flops 2048 | bytes 16384 | tf_op jit(solution)/shard_map/mul | solution.py:162
  57.7 0.0 collective-permute-done.4
  57.7 0.6 copy.15
  58.4 0.7 %copy.16 = bf16[1,128,3,256]{3,1,2,0:T(8,128)(2,1)} copy(bf16[1,128,3,256]{3,1,2,0:T(8,128)(2,1)S(1)} %collective-permute-done.4) | data formatting | bytes 393216
  (13 shorter events, 0.3 us)
Async XLA Ops:
  7.2 10.0 %copy-start.12 = (f32[4,512]{1,0:T(4,128)S(1)}, f32[4,512]{1,0:T(4,128)}, u32[]{:S(2)}) copy-start(f32[4,512]{1,0:T(4,128)} %constant.141.clone) | copy-start | bytes 24580
  7.2 10.0 %copy-start.13 = (f32[4,512]{1,0:T(4,128)S(1)}, f32[4,512]{1,0:T(4,128)}, u32[]{:S(2)}) copy-start(f32[4,512]{1,0:T(4,128)} %constant.142.clone) | copy-start | bytes 24580
  7.2 10.0 %copy-start = (f32[128,512]{1,0:T(8,128)S(1)}, f32[128,512]{1,0:T(8,128)}, u32[]{:S(2)}) copy-start(f32[128,512]{1,0:T(8,128)} %constant.139.clone) | copy-start | bytes 786436
  7.2 10.0 %copy-start.5 = (f32[128,512]{1,0:T(8,128)S(1)}, f32[128,512]{1,0:T(8,128)}, u32[]{:S(2)}) copy-start(f32[128,512]{1,0:T(8,128)} %constant.140.clone) | copy-start | bytes 786436
  7.2 10.0 %copy-start.6 = (f32[128,512]{1,0:T(8,128)S(1)}, f32[128,512]{1,0:T(8,128)}, u32[]{:S(2)}) copy-start(f32[128,512]{1,0:T(8,128)} %constant.158) | copy-start | bytes 786436
  7.2 10.0 %copy-start.7 = (f32[128,512]{1,0:T(8,128)S(1)}, f32[128,512]{1,0:T(8,128)}, u32[]{:S(2)}) copy-start(f32[128,512]{1,0:T(8,128)} %constant.169) | copy-start | bytes 786436
  7.2 9.8 %copy-start.3 = (bf16[1,128,3,256]{3,1,2,0:T(8,128)(2,1)S(1)}, bf16[1,128,3,256]{3,1,2,0:T(8,128)(2,1)}, u32[]{:S(2)}) copy-start(bf16[1,128,3,256]{3,1,2,0:T(8,128)(2,1)} %param.9) | copy-start | bytes 589828
  7.3 49.2 %reduce-scatter.2.cloned.1.call-start = ((), (), s32[]{:S(2)}) async-start(), calls=%async_computation.1 | async-start | bytes 40960 | tf_op jit(solution)/shard_map/reduce_scatter | solution.py:121
  10.0 15.2 %collective-permute-start.1 = (f32[272,128]{0,1:T(8,128)}, f32[272,128]{0,1:T(8,128)}, u32[]{:S(2)}, u32[]{:S(2)}) collective-permute-start(f32[272,128]{0,1:T(8,128)} %get-tuple-element.36), channel_id=1, source_target_pairs={{0,16},{8,24},{16,0},{24,8},{1,17},{9,25},{17,1},{25,9},{2,18},{10... | collective-permute-start | bytes 417800 | tf_op jit(solution)/shard_map/ppermute | solution.py:100
  14.1 12.8 %collective-permute-start.2 = (f32[272,128]{0,1:T(8,128)}, f32[272,128]{0,1:T(8,128)}, u32[]{:S(2)}, u32[]{:S(2)}) collective-permute-start(f32[272,128]{0,1:T(8,128)} %get-tuple-element.37), channel_id=1, source_target_pairs={{0,24},{8,0},{16,8},{24,16},{1,25},{9,1},{17,9},{25,17},{2,26},{10... | collective-permute-start | bytes 417800 | tf_op jit(solution)/shard_map/ppermute | solution.py:100
  15.4 13.5 %collective-permute-start = (f32[272,128]{0,1:T(8,128)}, f32[272,128]{0,1:T(8,128)}, u32[]{:S(2)}, u32[]{:S(2)}) collective-permute-start(f32[272,128]{0,1:T(8,128)} %get-tuple-element.35), channel_id=1, source_target_pairs={{0,8},{8,16},{16,24},{24,0},{1,9},{9,17},{17,25},{25,1},{2,10},{10... | collective-permute-start | bytes 417800 | tf_op jit(solution)/shard_map/ppermute | solution.py:100
  17.2 1.6 %copy-start.2 = (bf16[1,128,256]{2,1,0:T(8,128)(2,1)S(1)}, bf16[1,128,256]{2,1,0:T(8,128)(2,1)}, u32[]{:S(2)}) copy-start(bf16[1,128,256]{2,1,0:T(8,128)(2,1)} %param.12) | copy-start | bytes 196612
  17.2 1.6 %copy-start.11 = (f32[1,128,256]{2,1,0:T(8,128)S(1)}, f32[1,128,256]{2,1,0:T(8,128)}, u32[]{:S(2)}) copy-start(f32[1,128,256]{2,1,0:T(8,128)} %param.11) | copy-start | bytes 393220
  17.2 1.6 %copy-start.10 = (f32[128,512]{1,0:T(8,128)S(1)}, f32[128,512]{1,0:T(8,128)}, u32[]{:S(2)}) copy-start(f32[128,512]{1,0:T(8,128)} %constant.165) | copy-start | bytes 786436
  18.8 1.0 %copy-start.9 = (f32[128,512]{1,0:T(8,128)S(1)}, f32[128,512]{1,0:T(8,128)}, u32[]{:S(2)}) copy-start(f32[128,512]{1,0:T(8,128)} %constant.176) | copy-start | bytes 786436
  19.8 1.5 %copy-start.8 = (f32[128,512]{1,0:T(8,128)S(1)}, f32[128,512]{1,0:T(8,128)}, u32[]{:S(2)}) copy-start(f32[128,512]{1,0:T(8,128)} %constant.187) | copy-start | bytes 786436
  34.0 1.0 %copy-start.4 = (f32[256,512]{1,0:T(8,128)S(1)}, f32[256,512]{1,0:T(8,128)}, u32[]{:S(2)}) copy-start(f32[256,512]{1,0:T(8,128)} %get-tuple-element.12) | copy-start | bytes 1572868
  35.1 1.2 %copy-start.1 = (bf16[1,128,3,256]{3,1,2,0:T(8,128)(2,1)S(1)}, bf16[1,128,3,256]{3,1,2,0:T(8,128)(2,1)}, u32[]{:S(2)}) copy-start(bf16[1,128,3,256]{3,1,2,0:T(8,128)(2,1)} %param.10) | copy-start | bytes 589828
  36.4 2.6 %collective-permute-start.3 = (bf16[1,128,256]{2,1,0:T(8,128)(2,1)S(1)}, bf16[1,128,256]{2,1,0:T(8,128)(2,1)S(1)}, u32[]{:S(2)}, u32[]{:S(2)}) collective-permute-start(bf16[1,128,256]{2,1,0:T(8,128)(2,1)S(1)} %get-tuple-element.32), channel_id=1, source_target_pairs={{0,1},{1,2},{2,3},{3,4},{4,5},{5,6},{6,7},{8,9},{9,10},{10,11},{11... | collective-permute-start | bytes 196616 | tf_op jit(solution)/shard_map/ppermute | solution.py:22
  37.7 20.0 %collective-permute-start.4 = (bf16[1,128,3,256]{3,1,2,0:T(8,128)(2,1)S(1)}, bf16[1,128,3,256]{3,1,2,0:T(8,128)(2,1)S(1)}, u32[]{:S(2)}, u32[]{:S(2)}) collective-permute-start(bf16[1,128,3,256]{3,1,2,0:T(8,128)(2,1)S(1)} %pad_maximum_fusion.7), channel_id=1, source_target_pairs={{1,0},{2,1},{3,2},{4,3},{5,4},{6,5},{7,6},{9,8},{10,9},{11,10},{12... | collective-permute-start | bytes 589832 | tf_op jit(solution)/shard_map/ppermute | solution.py:22
Sparse Core Ops, SparseCore 0:
  34.1 22.2 reduce-scatter.1

commit v7 on v5

--- a/solution.py
+++ b/solution.py
@@ -92,14 +92,13 @@
     size = 2 * blocks * block
     half = size // 2
     packed = packed_tables(blocks, block)
-    acc = 0.0
-    for s in range(1, blocks):
-        first = jnp.where(place + s < blocks, mixed_rows, weighted_rows)
-        payload = jnp.concatenate([first, taps], axis=0)
-        pairs = [(i, (i + s) % blocks) for i in range(blocks)]
-        got = lax.ppermute(payload, "ctx", pairs)
-        table = block_table(packed, (place - s) % blocks)
-        acc = acc + jnp.dot(got, table, precision=precise)
+    target = lax.broadcasted_iota(jnp.int32, (blocks, 1, 1), 0)
+    first = jnp.where(target > place, mixed_rows[None], weighted_rows[None])
+    payload = jnp.concatenate([first, jnp.broadcast_to(taps, (blocks,) + taps.shape)], axis=1)
+    payload = jnp.where(target == place, 0.0, payload)
+    got = lax.all_to_all(payload, "ctx", 0, 0, tiled=True)
+    tables = jnp.stack([block_table(packed, b) for b in range(blocks)])
+    acc = jnp.einsum("brp,bpf->rf", got, tables, precision=precise)
     own_table = block_table(packed, place)
     own = jnp.concatenate([mixed_rows, weighted_rows, back_rows, taps], axis=0)
     loc = jnp.dot(own, own_table, precision=precise)

time: 43.4 us -> 47 us (1.083)
  other arithmetic: 3.98 us -> 10.6 us
  starting transfers between devices: 17.6 us -> 12.7 us
  matrix products: 6.62 us -> 8.58 us
  waiting for transfers between devices: 11.5 us -> 10.8 us
    ppermute x3 -> x0, waiting for transfers between devices: 7.94 us -> none  [dense_path(): got = lax.ppermute(payload, 'ctx', pairs)]
    all_to_all x0 -> x1, waiting for transfers between devices: none -> 7.39 us  [dense_path(): got = lax.all_to_all(payload, 'ctx', 0, 0, tiled=True)]
    all_to_all x0 -> x1, starting transfers between devices: none -> 4.87 us  [dense_path(): got = lax.all_to_all(payload, 'ctx', 0, 0, tiled=True)]
    ppermute x3 -> x0, starting transfers between devices: 4.68 us -> none  [dense_path(): got = lax.ppermute(payload, 'ctx', pairs)]
    ppermute x3, starting transfers between devices: 8.37 us -> 3.84 us  [dense_path(): lag = lag + lax.ppermute(share, 'ctx', pairs)]
    another operation x0 -> x4, other arithmetic: none -> 3.33 us  [dense_path(): tables = jnp.stack([block_table(packed, b) for b in range(blocks)])]
    transpose x2, other arithmetic: 0.89 us -> 2.51 us  [on_device(): conv, grad_mixed, lag = dense_path(place, blocks, mixed_in.T, weighted.T,...]
    dot_general x1, matrix products: 1.48 us -> 2.62 us  [dense_path(): loc = jnp.dot(own, own_table, precision=precise)]
  transfers between devices with their start and end apart: 8 -> 6, of which waited for: 3 -> 2; matrix products, arithmetic and copies ran while one was open for 17% -> 25% of each run, Pallas kernels for 0% -> 0%
where the time goes in v7:
time: 47 us; the launch traced here: 46.6 us
  starting transfers between devices  12.7 us (27%)
  waiting for transfers between devices  10.8 us (23%)
  other arithmetic  10.6 us (23%)
  matrix products  8.58 us (18%)
  local copies, waits for them, and re-layouts  2.81 us (6%)
  between operations  1.11 us (2%)
    all_to_all x1, waiting for transfers between devices, dense_path(): got = lax.all_to_all(payload, 'ctx', 0, 0, tiled=True)  7.39 us
    all_to_all x1, starting transfers between devices, dense_path(): got = lax.all_to_all(payload, 'ctx', 0, 0, tiled=True)  4.87 us
    ppermute x2, starting transfers between devices, from_behind(): return lax.ppermute(x, axis, pairs)  4.03 us
    ppermute x3, starting transfers between devices, dense_path(): lag = lag + lax.ppermute(share, 'ctx', pairs)  3.84 us
    ppermute x2, waiting for transfers between devices, from_behind(): return lax.ppermute(x, axis, pairs)  3.34 us
    another operation x4, other arithmetic, dense_path(): tables = jnp.stack([block_table(packed, b) for b in range(blocks)])  3.33 us
    dot_general x1, matrix products, dense_path(): acc = jnp.einsum('brp,bpf->rf', got, tables, precision=precise)  2.82 us
    dot_general x1, matrix products, dense_path(): loc = jnp.dot(own, own_table, precision=precise)  2.62 us
  transfers between devices with their start and end apart: 6, of which 2 were waited for; matrix products, arithmetic and copies ran while one was open for 25% of the time, Pallas kernels for 0%

profile of v7, /device:TPU:4, one launch (start us, length us, event | category | flops | bytes accessed | tf_op | source)
XLA Modules:
  0.0 46.6 jit_solution(14378853589857068795)
XLA Ops:
  0.6 0.0 copy-start.21
  0.7 1.6 %fusion.52 = (f32[256,128]{0,1:T(8,128)S(1)}, f32[256,128]{0,1:T(8,128)}) fusion(bf16[1,128,256]{2,1,0:T(8,128)(2,1)} %param.12, bf16[1,128,3,256]{3,1,2,0:T(8,128)(2,1)} %param.10), kind=kLoop, calls=%fused_computation.89 | loop fusion | flops 196608 | bytes 524288 | tf_op jit(solution)/shard_map/transpose | solution.py:192
  2.3 0.0 copy-start.11
  2.3 0.0 copy-start.12
  2.3 0.0 copy-start.13
  2.3 0.0 copy-start.14
  2.3 0.0 copy-start.15
  2.4 0.6 %copy-done.2 = f32[256,128]{0,1:T(8,128)} copy-done((f32[256,128]{0,1:T(8,128)}, f32[256,128]{0,1:T(8,128)S(1)}, u32[]{:S(2)}) %copy-start.2) | copy-done | bytes 131096
  2.9 0.1 copy.14
  3.0 0.9 %multiply_bitcast_fusion = f32[256,128]{0,1:T(8,128)S(1)} fusion(bf16[1,128,3,256]{3,1,2,0:T(8,128)(2,1)} %param.9), kind=kLoop, calls=%fused_computation.98 | loop fusion | flops 98304 | bytes 262144 | tf_op jit(solution)/shard_map/transpose | solution.py:192
  3.9 0.0 copy-start.1
  3.9 0.1 copy.13
  4.0 0.1 broadcast_select_fusion
  4.1 0.0 copy-done.21
  4.2 0.9 %maximum_select_fusion = f32[4,272,128]{2,1,0:T(8,128)} fusion(f32[4,16,128]{2,1,0:T(8,128)S(1)} %broadcast_in_dim.72, f32[4,256,128]{2,1,0:T(8,128)S(1)} %broadcast_select_fusion, pred[4]{0:T(512)(128)(4,1)S(1)} %get-tuple-element.45), kind=kLoop, calls=%fused_computation.26 | loop fusion | flops 278528 | bytes 1114116 | tf_op jit(solution)/shard_map/jit(_where)/select_n | solution.py:98
  5.1 4.9 %all-to-all-start = ((f32[4,272,128]{2,1,0:T(8,128)}), f32[4,272,128]{2,1,0:T(8,128)}, u32[]{:S(2)}, u32[]{:S(2)}) async-start(f32[4,272,128]{2,1,0:T(8,128)} %maximum_select_fusion), calls=%async_computation | async-start | bytes 1114112 | tf_op jit(solution)/shard_map/all_to_all | solution.py:99
  10.0 0.0 copy-done.22
  10.0 0.0 copy-done.23
  10.1 0.0 copy-done.1
  10.1 0.0 copy-done.9
  10.1 0.0 copy-start.18
  10.2 1.6 %multiply_subtract_fusion.6 = (f32[128,512]{1,0:T(8,128)S(1)}, f32[128,512]{1,0:T(8,128)}, f32[128,512]{1,0:T(8,128)}, f32[128,512]{1,0:T(8,128)}, f32[128,512]{...) fusion(f32[128,512]{1,0:T(8,128)S(1)} %copy-done.11, ...), kind=kLoop, calls=%fused_computation.81 | loop fusion | flops 2621440 | bytes 4736640 | tf_op jit(solution)/shard_map/sub | solution.py:71
  11.8 0.8 %maximum_bitcast_fusion = f32[1,128,1024]{2,1,0:T(8,128)} fusion(f32[128,512]{1,0:T(8,128)S(1)} %get-tuple-element.40, f32[128,512]{1,0:T(8,128)S(1)} %copy-done.9), kind=kLoop, calls=%fused_computation.28 | loop fusion | flops 131072 | bytes 1048576 | tf_op jit(solution)/shard_map/stack | solution.py:100
  12.6 0.1 copy.12
  12.7 0.8 %maximum_bitcast_fusion.1 = f32[1,128,1024]{2,1,0:T(8,128)} fusion(f32[128,512]{1,0:T(8,128)S(1)} %get-tuple-element.41, f32[128,512]{1,0:T(8,128)S(1)} %copy-done.18), kind=kLoop, calls=%fused_computation.29 | loop fusion | flops 131072 | bytes 1048576 | tf_op jit(solution)/shard_map/stack | solution.py:100
  13.5 0.0 copy-done.17
  13.5 0.8 %maximum_bitcast_fusion.2 = f32[1,128,1024]{2,1,0:T(8,128)} fusion(f32[128,512]{1,0:T(8,128)S(1)} %get-tuple-element.42, f32[128,512]{1,0:T(8,128)S(1)} %copy-done.17), kind=kLoop, calls=%fused_computation.30 | loop fusion | flops 131072 | bytes 1048576 | tf_op jit(solution)/shard_map/stack | solution.py:100
  14.4 0.8 %maximum_bitcast_fusion.3 = f32[1,128,1024]{2,1,0:T(8,128)} fusion(f32[128,512]{1,0:T(8,128)S(1)} %get-tuple-element.43, f32[128,512]{1,0:T(8,128)S(1)} %copy-done.16), kind=kLoop, calls=%fused_computation.31 | loop fusion | flops 131072 | bytes 1048576 | tf_op jit(solution)/shard_map/stack | solution.py:100
  15.2 2.6 %fusion.34 = f32[784,1024]{1,0:T(8,128)S(1)} fusion(f32[16,128]{0,1:T(8,128)S(1)} %bitcast.68, f32[256,128]{0,1:T(8,128)} %get-tuple-element.31, f32[256,128]{0,1:T(8,128)} %copy-done.2, f32[256,128]{0,1:T(8,128)} %copy-done.1, f32[128,512]{1,0:T(8,128)} %get-tuple-element.20, f32[128,512]{1,0:T(8,128)S(1)} %get-tuple-element.19), kind=kOutput, calls=%fused_computation.54 | convolution fusion | flops 616994816 | bytes 4136960 | tf_op jit(solution)/shard_map/dot_general | solution.py:104
  17.8 0.0 copy-done.19
  17.9 0.0 copy-done.20
  17.9 7.4 %all-to-all-done = f32[4,272,128]{2,1,0:T(8,128)} async-done(((f32[4,272,128]{2,1,0:T(8,128)}), f32[4,272,128]{2,1,0:T(8,128)}, u32[]{:S(2)}, u32[]{:S(2)}) %all-to-all-start) | async-done | bytes 557088 | tf_op jit(solution)/shard_map/all_to_all | solution.py:99
  25.3 2.8 %fusion.16 = f32[272,1024]{1,0:T(8,128)S(1)} fusion(f32[4,272,128]{2,1,0:T(8,128)} %all-to-all-done, f32[1,128,1024]{2,1,0:T(8,128)} %maximum_bitcast_fusion.3, f32[1,128,1024]{2,1,0:T(8,128)} %maximum_bitcast_fusion.2, f32[1,128,1024]{2,1,0:T(8,128)} %maximum_bitcast_fusion.1, f32[1,128,1024]{2,1,0:T(8,128)} %maximum_bitcast_fusion), kind=kOutput, calls=%fused_computation.16 | convolution fusion | flops 857210880 | bytes 3768320 | tf_op jit(solution)/shard_map/brp,bpf->rf/dot_general | solution.py:101
  28.1 0.3 slice_add_fusion.1
  28.4 0.1 broadcast_in_dim.73
  28.6 0.4 multiply_subtract_fusion
  29.0 0.2 bitcast_reduce_fusion
  29.2 0.3 copy-done.7
  29.5 0.1 copy-done.8
  29.6 0.3 fusion.23
  29.9 0.0 collective-permute-start.2
  29.9 0.0 copy-done.5
  29.9 0.0 copy-done.6
  29.9 0.3 fusion.26
  30.2 2.0 %collective-permute-start.3 = (f32[16,128]{1,0:T(8,128)S(1)}, f32[16,128]{1,0:T(8,128)S(1)}, u32[]{:S(2)}, u32[]{:S(2)}) collective-permute-start(f32[16,128]{1,0:T(8,128)S(1)} %fusion.26), channel_id=1, source_target_pairs={{0,16},{8,24},{16,0},{24,8},{1,17},{9,25},{17,1},{25,9},{2,18},{10... | collective-permute-start | bytes 24584 | tf_op jit(solution)/shard_map/ppermute | solution.py:123
  32.2 0.2 select_subtract_fusion
  32.5 0.0 copy-start.10
  32.5 0.0 copy-start.3
  32.5 0.0 copy-start.4
  32.5 1.2 %fusion.8 = f32[128,512]{1,0:T(8,128)S(1)} fusion(f32[256,512]{1,0:T(8,128)S(1)} %get-tuple-element.11, f32[256,512]{1,0:T(8,128)S(1)} %get-tuple-element.12, f32[256,512]{1,0:T(8,128)S(1)} %get-tuple-element.8, f32[256,512]{1,0:T(8,128)S(1)} %get-tuple-element.7, f32[128,512]{1,0:T(8,128)S(1)} %copy-done, f32[128,512]{1,0:T(8,128)S(1)} %get-tuple-element.19, ...), kind=kOutput, calls=%fused_computation.8 | convolution fusion | flops 404488192 | bytes 2887680 | tf_op jit(solution)/shard_map/tf,rf->tr/dot_general | solution.py:117
  33.8 0.0 copy-done.10
  33.8 0.9 %fusion.61 = (bf16[1,128,1,256]{3,1,2,0:T(8,128)(2,1)S(1)}, bf16[1,128,1,256]{3,1,2,0:T(8,128)(2,1)S(1)}, bf16[1,128,256]{2,1,0:T(8,128)(2,1)S(1)}) fusion(f32[128,512]{1,0:T(8,128)S(1)} %fusion.8, bf16[1,128,3,256]{3,1,2,0:T(8,128)(2,1)S(1)} %copy-done.10, bf16[1,128,3,256]{3,1,2,0:T(8,128)(2,1)} %param.9), kind=kLoop, calls=%fused_computation.101 | loop fusion | flops 360448 | bytes 655360 | tf_op jit(solution)/shard_map/stack | solution.py:162
  34.7 1.9 %collective-permute-start.1 = (bf16[1,128,3,256]{3,1,2,0:T(8,128)(2,1)S(1)}, bf16[1,128,3,256]{3,1,2,0:T(8,128)(2,1)S(1)}, u32[]{:S(2)}, u32[]{:S(2)}) collective-permute-start(bf16[1,128,3,256]{3,1,2,0:T(8,128)(2,1)S(1)} %pad_maximum_fusion.5), channel_id=1, source_target_pairs={{1,0},{2,1},{3,2},{4,3},{5,4},{6,5},{7,6},{9,8},{10,9},{11,10},{12... | collective-permute-start | bytes 589832 | tf_op jit(solution)/shard_map/ppermute | solution.py:22
  36.7 0.3 fusion.29
  37.0 1.8 %collective-permute-start.4 = (f32[16,128]{1,0:T(8,128)S(1)}, f32[16,128]{1,0:T(8,128)S(1)}, u32[]{:S(2)}, u32[]{:S(2)}) collective-permute-start(f32[16,128]{1,0:T(8,128)S(1)} %fusion.29), channel_id=1, source_target_pairs={{0,24},{8,0},{16,8},{24,16},{1,25},{9,1},{17,9},{25,17},{2,26},{10... | collective-permute-start | bytes 24584 | tf_op jit(solution)/shard_map/ppermute | solution.py:123
  38.8 2.1 %collective-permute-start = (bf16[1,128,256]{2,1,0:T(8,128)(2,1)S(1)}, bf16[1,128,256]{2,1,0:T(8,128)(2,1)S(1)}, u32[]{:S(2)}, u32[]{:S(2)}) collective-permute-start(bf16[1,128,256]{2,1,0:T(8,128)(2,1)S(1)} %get-tuple-element.29), channel_id=1, source_target_pairs={{0,1},{1,2},{2,3},{3,4},{4,5},{5,6},{6,7},{8,9},{9,10},{10,11},{11... | collective-permute-start | bytes 196616 | tf_op jit(solution)/shard_map/ppermute | solution.py:22
  40.9 0.0 collective-permute-done.2
  40.9 0.0 collective-permute-done.3
  40.9 0.0 collective-permute-done.4
  41.0 0.9 %fusion.22 = f32[1,16,128]{2,1,0:T(8,128)} fusion(f32[16,128]{1,0:T(8,128)S(1)} %collective-permute-done.4, f32[16,128]{1,0:T(8,128)S(1)} %collective-permute-done.3, f32[16,128]{1,0:T(8,128)S(1)} %collective-permute-done.2, f32[16,1024]{1,0:T(8,128)S(1)} %bitcast_reduce_fusion, f32[128,512]{1,0:T(8,128)S(1)} %copy-done, ...), kind=kOutput, calls=%fused_computation.21 | convolution fusion | flops 12853248 | bytes 626688 | tf_op jit(solution)/shard_map/rf,tf->rt/dot_general | solution.py:118
  41.9 3.3 %collective-permute-done = bf16[1,128,256]{2,1,0:T(8,128)(2,1)S(1)} collective-permute-done((bf16[1,128,256]{2,1,0:T(8,128)(2,1)S(1)}, bf16[1,128,256]{2,1,0:T(8,128)(2,1)S(1)}, u32[]{:S(2)}, u32[]{:S(2)}) %collective-permute-start) | collective-permute-done | bytes 65568 | tf_op jit(solution)/shard_map/ppermute | solution.py:22
  45.3 0.0 collective-permute-done.1
  45.3 0.6 %copy.19 = bf16[1,128,256]{2,1,0:T(8,128)(2,1)} copy(bf16[1,128,256]{2,1,0:T(8,128)(2,1)S(1)} %collective-permute-done) | data formatting | bytes 131072
  45.9 0.7 %copy.20 = bf16[1,128,3,256]{3,1,2,0:T(8,128)(2,1)} copy(bf16[1,128,3,256]{3,1,2,0:T(8,128)(2,1)S(1)} %collective-permute-done.1) | data formatting | bytes 393216
  (33 shorter events, 0.1 us)
Async XLA Ops:
  0.6 3.5 %copy-start.21 = (f32[1,16,128]{2,1,0:T(8,128)S(1)}, f32[1,16,128]{2,1,0:T(8,128)}, u32[]{:S(2)}) copy-start(f32[1,16,128]{2,1,0:T(8,128)} %param.13) | copy-start | bytes 24580
  2.3 0.7 %copy-start.2 = (f32[256,128]{0,1:T(8,128)}, f32[256,128]{0,1:T(8,128)S(1)}, u32[]{:S(2)}) copy-start(f32[256,128]{0,1:T(8,128)S(1)} %get-tuple-element.30) | copy-start | bytes 393220
  2.3 7.7 %copy-start.22 = (f32[4,512]{1,0:T(4,128)S(1)}, f32[4,512]{1,0:T(4,128)}, u32[]{:S(2)}) copy-start(f32[4,512]{1,0:T(4,128)} %constant.135.clone) | copy-start | bytes 24580
  2.3 7.7 %copy-start.23 = (f32[4,512]{1,0:T(4,128)S(1)}, f32[4,512]{1,0:T(4,128)}, u32[]{:S(2)}) copy-start(f32[4,512]{1,0:T(4,128)} %constant.136.clone) | copy-start | bytes 24580
  2.3 7.8 %copy-start.9 = (f32[128,512]{1,0:T(8,128)S(1)}, f32[128,512]{1,0:T(8,128)}, u32[]{:S(2)}) copy-start(f32[128,512]{1,0:T(8,128)} %constant.133.clone) | copy-start | bytes 786436
  2.3 7.8 %copy-start.11 = (f32[128,512]{1,0:T(8,128)S(1)}, f32[128,512]{1,0:T(8,128)}, u32[]{:S(2)}) copy-start(f32[128,512]{1,0:T(8,128)} %constant.134.clone) | copy-start | bytes 786436
  2.3 7.8 %copy-start.12 = (f32[128,512]{1,0:T(8,128)S(1)}, f32[128,512]{1,0:T(8,128)}, u32[]{:S(2)}) copy-start(f32[128,512]{1,0:T(8,128)} %constant.152) | copy-start | bytes 786436
  2.3 7.8 %copy-start.13 = (f32[128,512]{1,0:T(8,128)S(1)}, f32[128,512]{1,0:T(8,128)}, u32[]{:S(2)}) copy-start(f32[128,512]{1,0:T(8,128)} %constant.163) | copy-start | bytes 786436
  2.3 7.8 %copy-start.14 = (f32[128,512]{1,0:T(8,128)S(1)}, f32[128,512]{1,0:T(8,128)}, u32[]{:S(2)}) copy-start(f32[128,512]{1,0:T(8,128)} %constant.174) | copy-start | bytes 786436
  2.3 7.8 %copy-start.15 = (f32[128,512]{1,0:T(8,128)S(1)}, f32[128,512]{1,0:T(8,128)}, u32[]{:S(2)}) copy-start(f32[128,512]{1,0:T(8,128)} %constant.185) | copy-start | bytes 786436
  3.9 6.1 %copy-start.1 = (f32[256,128]{0,1:T(8,128)}, f32[256,128]{0,1:T(8,128)S(1)}, u32[]{:S(2)}) copy-start(f32[256,128]{0,1:T(8,128)S(1)} %multiply_bitcast_fusion) | copy-start | bytes 393220
  5.1 20.2 %all-to-all-start = ((f32[4,272,128]{2,1,0:T(8,128)}), f32[4,272,128]{2,1,0:T(8,128)}, u32[]{:S(2)}, u32[]{:S(2)}) async-start(f32[4,272,128]{2,1,0:T(8,128)} %maximum_select_fusion), calls=%async_computation | async-start | bytes 1114112 | tf_op jit(solution)/shard_map/all_to_all | solution.py:99
  10.1 2.6 %copy-start.18 = (f32[128,512]{1,0:T(8,128)S(1)}, f32[128,512]{1,0:T(8,128)}, u32[]{:S(2)}) copy-start(f32[128,512]{1,0:T(8,128)} %constant.159) | copy-start | bytes 786436
  11.7 1.8 %copy-start.17 = (f32[128,512]{1,0:T(8,128)S(1)}, f32[128,512]{1,0:T(8,128)}, u32[]{:S(2)}) copy-start(f32[128,512]{1,0:T(8,128)} %constant.170) | copy-start | bytes 786436
  11.8 2.6 %copy-start.16 = (f32[128,512]{1,0:T(8,128)S(1)}, f32[128,512]{1,0:T(8,128)}, u32[]{:S(2)}) copy-start(f32[128,512]{1,0:T(8,128)} %constant.181) | copy-start | bytes 786436
  15.2 2.6 %copy-start.19 = (bf16[1,128,256]{2,1,0:T(8,128)(2,1)S(1)}, bf16[1,128,256]{2,1,0:T(8,128)(2,1)}, u32[]{:S(2)}) copy-start(bf16[1,128,256]{2,1,0:T(8,128)(2,1)} %param.12) | copy-start | bytes 196612
  15.2 2.6 %copy-start.20 = (f32[1,128,256]{2,1,0:T(8,128)S(1)}, f32[1,128,256]{2,1,0:T(8,128)}, u32[]{:S(2)}) copy-start(f32[1,128,256]{2,1,0:T(8,128)} %param.11) | copy-start | bytes 393220
  28.5 1.0 %copy-start.7 = (f32[128,512]{1,0:T(8,128)S(1)}, f32[128,512]{1,0:T(8,128)}, u32[]{:S(2)}) copy-start(f32[128,512]{1,0:T(8,128)} %get-tuple-element.21) | copy-start | bytes 786436
  28.5 1.0 %copy-start.8 = (f32[128,512]{1,0:T(8,128)S(1)}, f32[128,512]{1,0:T(8,128)}, u32[]{:S(2)}) copy-start(f32[128,512]{1,0:T(8,128)} %get-tuple-element.22) | copy-start | bytes 786436
  28.5 1.3 %copy-start.5 = (f32[128,512]{1,0:T(8,128)S(1)}, f32[128,512]{1,0:T(8,128)}, u32[]{:S(2)}) copy-start(f32[128,512]{1,0:T(8,128)} %get-tuple-element.23) | copy-start | bytes 786436
  28.5 1.3 %copy-start.6 = (f32[128,512]{1,0:T(8,128)S(1)}, f32[128,512]{1,0:T(8,128)}, u32[]{:S(2)}) copy-start(f32[128,512]{1,0:T(8,128)} %get-tuple-element.24) | copy-start | bytes 786436
  29.6 2.9 %copy-start = (f32[128,512]{1,0:T(8,128)S(1)}, f32[128,512]{1,0:T(8,128)}, u32[]{:S(2)}) copy-start(f32[128,512]{1,0:T(8,128)} %get-tuple-element.20) | copy-start | bytes 786436
  29.9 11.1 %collective-permute-start.2 = (f32[16,128]{1,0:T(8,128)S(1)}, f32[16,128]{1,0:T(8,128)S(1)}, u32[]{:S(2)}, u32[]{:S(2)}) collective-permute-start(f32[16,128]{1,0:T(8,128)S(1)} %fusion.23), channel_id=1, source_target_pairs={{0,8},{8,16},{16,24},{24,0},{1,9},{9,17},{17,25},{25,1},{2,10},{10... | collective-permute-start | bytes 24584 | tf_op jit(solution)/shard_map/ppermute | solution.py:123
  30.2 10.7 %collective-permute-start.3 = (f32[16,128]{1,0:T(8,128)S(1)}, f32[16,128]{1,0:T(8,128)S(1)}, u32[]{:S(2)}, u32[]{:S(2)}) collective-permute-start(f32[16,128]{1,0:T(8,128)S(1)} %fusion.26), channel_id=1, source_target_pairs={{0,16},{8,24},{16,0},{24,8},{1,17},{9,25},{17,1},{25,9},{2,18},{10... | collective-permute-start | bytes 24584 | tf_op jit(solution)/shard_map/ppermute | solution.py:123
  32.5 1.3 %copy-start.10 = (bf16[1,128,3,256]{3,1,2,0:T(8,128)(2,1)S(1)}, bf16[1,128,3,256]{3,1,2,0:T(8,128)(2,1)}, u32[]{:S(2)}) copy-start(bf16[1,128,3,256]{3,1,2,0:T(8,128)(2,1)} %param.10) | copy-start | bytes 589828
  32.5 4.1 %copy-start.3 = (f32[128,512]{1,0:T(8,128)S(1)}, f32[128,512]{1,0:T(8,128)}, u32[]{:S(2)}) copy-start(f32[128,512]{1,0:T(8,128)} %get-tuple-element.25) | copy-start | bytes 786436
  32.5 4.1 %copy-start.4 = (f32[128,512]{1,0:T(8,128)S(1)}, f32[128,512]{1,0:T(8,128)}, u32[]{:S(2)}) copy-start(f32[128,512]{1,0:T(8,128)} %get-tuple-element.26) | copy-start | bytes 786436
  34.7 10.6 %collective-permute-start.1 = (bf16[1,128,3,256]{3,1,2,0:T(8,128)(2,1)S(1)}, bf16[1,128,3,256]{3,1,2,0:T(8,128)(2,1)S(1)}, u32[]{:S(2)}, u32[]{:S(2)}) collective-permute-start(bf16[1,128,3,256]{3,1,2,0:T(8,128)(2,1)S(1)} %pad_maximum_fusion.5), channel_id=1, source_target_pairs={{1,0},{2,1},{3,2},{4,3},{5,4},{6,5},{7,6},{9,8},{10,9},{11,10},{12... | collective-permute-start | bytes 589832 | tf_op jit(solution)/shard_map/ppermute | solution.py:22
  37.0 4.0 %collective-permute-start.4 = (f32[16,128]{1,0:T(8,128)S(1)}, f32[16,128]{1,0:T(8,128)S(1)}, u32[]{:S(2)}, u32[]{:S(2)}) collective-permute-start(f32[16,128]{1,0:T(8,128)S(1)} %fusion.29), channel_id=1, source_target_pairs={{0,24},{8,0},{16,8},{24,16},{1,25},{9,1},{17,9},{25,17},{2,26},{10... | collective-permute-start | bytes 24584 | tf_op jit(solution)/shard_map/ppermute | solution.py:123
  38.8 6.5 %collective-permute-start = (bf16[1,128,256]{2,1,0:T(8,128)(2,1)S(1)}, bf16[1,128,256]{2,1,0:T(8,128)(2,1)S(1)}, u32[]{:S(2)}, u32[]{:S(2)}) collective-permute-start(bf16[1,128,256]{2,1,0:T(8,128)(2,1)S(1)} %get-tuple-element.29), channel_id=1, source_target_pairs={{0,1},{1,2},{2,3},{3,4},{4,5},{5,6},{6,7},{8,9},{9,10},{10,11},{11... | collective-permute-start | bytes 196616 | tf_op jit(solution)/shard_map/ppermute | solution.py:22

commit v8 on v6

--- a/solution.py
+++ b/solution.py
@@ -116,10 +116,26 @@
     weight = jnp.where((cols == 0) | (cols == half), 1.0 / size, 2.0 / size)
     both = jnp.concatenate([conv, gm], axis=0)
     out = jnp.einsum("tf,rf->tr", own_table * weight, both, precision=precise)
+    if blocks & (blocks - 1):
+        lag = jnp.einsum("rf,tf->rt", fgs, own_table * weight, precision=precise)
+        for s in range(1, blocks):
+            table = block_table(packed, (place + s) % blocks) * weight
+            share = jnp.einsum("rf,tf->rt", fgs, table, precision=precise)
+            pairs = [(i, (i + s) % blocks) for i in range(blocks)]
+            lag = lag + lax.ppermute(share, "ctx", pairs)
+        return out[:, :c], out[:, c:], lag
     tables = jnp.stack([block_table(packed, b) for b in range(blocks)]) * weight
     shares = jnp.einsum("rf,btf->brt", fgs, tables, precision=precise)
-    lag = lax.psum_scatter(shares, "ctx", scatter_dimension=0, tiled=True)[0]
-    return out[:, :c], out[:, c:], lag
+    bit = blocks // 2
+    while bit:
+        shares = shares.reshape((2, -1) + shares.shape[1:])
+        mine = (place // bit) % 2
+        keep = lax.dynamic_index_in_dim(shares, mine, keepdims=False)
+        give = lax.dynamic_index_in_dim(shares, 1 - mine, keepdims=False)
+        pairs = [(i, i ^ bit) for i in range(blocks)]
+        shares = keep + lax.ppermute(give, "ctx", pairs)
+        bit //= 2
+    return out[:, :c], out[:, c:], shares[0]
 
 
 def chunk_work(local3, common, hsum, tables):

time: 66.4 us -> 45.4 us (0.68)
  the two profiles are of different devices: /device:TPU:0 before, /device:TPU:4 now
where the time goes in v8:
time: 45.4 us; the launch traced here: 45 us
  starting transfers between devices  15.9 us (35%)
  other arithmetic  12.6 us (28%)
  matrix products  8.67 us (19%)
  waiting for transfers between devices  3.46 us (8%)
  local copies, waits for them, and re-layouts  3.27 us (7%)
  between operations  1.19 us (3%)
    ppermute x2, starting transfers between devices, dense_path(): shares = keep + lax.ppermute(give, 'ctx', pairs)  6.93 us
    dot_general x3, matrix products, dense_path(): acc = acc + jnp.dot(got, table, precision=precise)  5.03 us
    ppermute x3, starting transfers between devices, dense_path(): got = lax.ppermute(payload, 'ctx', pairs)  4.61 us
    ppermute x2, starting transfers between devices, from_behind(): return lax.ppermute(x, axis, pairs)  4.33 us
    another operation x4, other arithmetic, dense_path(): tables = jnp.stack([block_table(packed, b) for b in range(blocks)]) * weight  3.63 us
    ppermute x2, waiting for transfers between devices, from_behind(): return lax.ppermute(x, axis, pairs)  3.45 us
    unnamed x57, local copies, waits for them, and re-layouts  3.12 us
    transpose x2, other arithmetic, on_device(): conv, grad_mixed, lag = dense_path(place, blocks, mixed_in.T, weighted.T,...  2.33 us
  transfers between devices with their start and end apart: 7, of which 1 were waited for; matrix products, arithmetic and copies ran while one was open for 36% of the time, Pallas kernels for 0%

profile of v8, /device:TPU:4, one launch (start us, length us, event | category | flops | bytes accessed | tf_op | source)
XLA Modules:
  0.0 45.0 jit_solution(14084086926394801108)
XLA Ops:
  0.6 0.0 copy-start.25
  0.6 0.0 copy-start.26
  0.7 0.0 copy-start.6
  0.7 0.0 copy-start.16
  0.7 0.0 copy-start.17
  0.7 0.0 copy-start.18
  0.7 0.0 copy-start.19
  0.7 0.0 copy-start.20
  0.7 0.0 copy-start.9
  0.8 0.9 %copy.12 = f32[1,16,128]{1,2,0:T(8,128)S(1)} copy(f32[1,16,128]{2,1,0:T(8,128)} %param.13) | data formatting | bytes 16384 | tf_op args[4]
  1.7 1.0 %broadcast_select_fusion.2 = (f32[256,128]{0,1:T(8,128)S(1)}, f32[256,128]{0,1:T(8,128)S(1)}, f32[256,128]{0,1:T(8,128)S(1)}) fusion(pred[]{:T(512)S(6)} %lt.107, bf16[1,128,3,256]{3,1,2,0:T(8,128)(2,1)} %param.10, bf16[1,128,256]{2,1,0:T(8,128)(2,1)} %param.12, bf16[1,128,3,256]{3,1,2,0:T(8,128)(2,1)} %param.9, pred[]{:T(512)S(6)} %lt.110, pred[]{:T(512)S(6)} %lt.113), kind=kLoop, calls=%fused_computation.99 | loop fusion | flops 294912 | bytes 655363 | tf_op jit(solution)/shard_map/jit(_where)/select_n | solution.py:97
  2.7 0.8 %pad_maximum_fusion.6 = (f32[272,128]{0,1:T(8,128)}, f32[272,128]{0,1:T(8,128)}, f32[272,128]{0,1:T(8,128)}) fusion(f32[16,128]{0,1:T(8,128)S(1)} %bitcast.95, f32[256,128]{0,1:T(8,128)S(1)} %get-tuple-element.29, f32[256,128]{0,1:T(8,128)S(1)} %get-tuple-element.30, f32[256,128]{0,1:T(8,128)S(1)} %get-tuple-element.31), kind=kLoop, calls=%fused_computation.59 | loop fusion | flops 104448 | bytes 819200 | tf_op jit(solution)/shard_map/concatenate | solution.py:98
  3.5 2.6 %collective-permute-start.1 = (f32[272,128]{0,1:T(8,128)}, f32[272,128]{0,1:T(8,128)}, u32[]{:S(2)}, u32[]{:S(2)}) collective-permute-start(f32[272,128]{0,1:T(8,128)} %get-tuple-element.36), channel_id=1, source_target_pairs={{0,16},{8,24},{16,0},{24,8},{1,17},{9,25},{17,1},{25,9},{2,18},{10... | collective-permute-start | bytes 417800 | tf_op jit(solution)/shard_map/ppermute | solution.py:100
  6.1 1.3 %collective-permute-start.2 = (f32[272,128]{0,1:T(8,128)}, f32[272,128]{0,1:T(8,128)}, u32[]{:S(2)}, u32[]{:S(2)}) collective-permute-start(f32[272,128]{0,1:T(8,128)} %get-tuple-element.37), channel_id=1, source_target_pairs={{0,24},{8,0},{16,8},{24,16},{1,25},{9,1},{17,9},{25,17},{2,26},{10... | collective-permute-start | bytes 417800 | tf_op jit(solution)/shard_map/ppermute | solution.py:100
  7.4 0.7 %collective-permute-start = (f32[272,128]{0,1:T(8,128)}, f32[272,128]{0,1:T(8,128)}, u32[]{:S(2)}, u32[]{:S(2)}) collective-permute-start(f32[272,128]{0,1:T(8,128)} %get-tuple-element.35), channel_id=1, source_target_pairs={{0,8},{8,16},{16,24},{24,0},{1,9},{9,17},{17,25},{25,1},{2,10},{10... | collective-permute-start | bytes 417800 | tf_op jit(solution)/shard_map/ppermute | solution.py:100
  8.1 1.7 %fusion.43 = (f32[256,128]{0,1:T(8,128)}, f32[256,128]{0,1:T(8,128)}) fusion(bf16[1,128,256]{2,1,0:T(8,128)(2,1)} %param.12, bf16[1,128,3,256]{3,1,2,0:T(8,128)(2,1)} %param.10), kind=kLoop, calls=%fused_computation.81 | loop fusion | flops 196608 | bytes 524288 | tf_op jit(solution)/shard_map/transpose | solution.py:206
  9.8 0.0 copy-done.9
  9.8 0.7 %multiply_bitcast_fusion = f32[256,128]{0,1:T(8,128)} fusion(bf16[1,128,3,256]{3,1,2,0:T(8,128)(2,1)S(1)} %copy-done.9), kind=kLoop, calls=%fused_computation.90 | loop fusion | flops 98304 | bytes 262144 | tf_op jit(solution)/shard_map/transpose | solution.py:206
  10.5 0.0 copy-done.25
  10.5 0.0 copy-done.26
  10.6 0.0 copy-start.8
  10.6 0.0 copy-start.24
  10.6 0.0 copy-start.22
  10.6 1.5 %multiply_subtract_fusion.6 = (f32[128,512]{1,0:T(8,128)S(1)}, f32[128,512]{1,0:T(8,128)S(1)}, f32[128,512]{1,0:T(8,128)}, f32[128,512]{1,0:T(8,128)}, f32[128,5...) fusion(f32[128,512]{1,0:T(8,128)S(1)} %copy-done.16, ...), kind=kLoop, calls=%fused_computation.73 | loop fusion | flops 2621440 | bytes 4736640 | tf_op jit(solution)/shard_map/sub | solution.py:71
  12.1 0.8 %maximum_bitcast_fusion = f32[1,128,1024]{2,1,0:T(8,128)} fusion(f32[128,512]{1,0:T(8,128)S(1)} %get-tuple-element.46, f32[128,512]{1,0:T(8,128)S(1)} %copy-done.6), kind=kLoop, calls=%fused_computation.35 | loop fusion | flops 131072 | bytes 1048576 | tf_op jit(solution)/shard_map/stack | solution.py:127
  12.9 0.6 %fusion.53 = bf16[1,128,1,256]{3,1,2,0:T(8,128)(2,1)} fusion(f32[1,128,256]{2,1,0:T(8,128)S(1)} %copy-done.24, bf16[1,128,256]{2,1,0:T(8,128)(2,1)S(1)} %copy-done.8), kind=kLoop, calls=%fused_computation.94 | loop fusion | flops 98304 | bytes 262144 | tf_op jit(solution)/shard_map/stack | solution.py:176
  13.6 0.0 copy-done.22
  13.6 0.9 %maximum_bitcast_fusion.1 = f32[1,128,1024]{2,1,0:T(8,128)} fusion(f32[128,512]{1,0:T(8,128)S(1)} %get-tuple-element.47, f32[128,512]{1,0:T(8,128)S(1)} %copy-done.22), kind=kLoop, calls=%fused_computation.36 | loop fusion | flops 131072 | bytes 1048576 | tf_op jit(solution)/shard_map/stack | solution.py:127
  14.4 0.8 %maximum_bitcast_fusion.2 = f32[1,128,1024]{2,1,0:T(8,128)} fusion(f32[128,512]{1,0:T(8,128)S(1)} %get-tuple-element.48, f32[128,512]{1,0:T(8,128)S(1)} %copy-done.21), kind=kLoop, calls=%fused_computation.37 | loop fusion | flops 131072 | bytes 1048576 | tf_op jit(solution)/shard_map/stack | solution.py:127
  15.3 0.0 copy-done.14
  15.3 1.5 %fusion.29 = f32[784,1024]{1,0:T(8,128)S(1)} fusion(f32[16,128]{0,1:T(8,128)S(1)} %bitcast.96, f32[256,128]{0,1:T(8,128)S(1)} %copy-done.15, f32[256,128]{0,1:T(8,128)S(1)} %copy-done.14, f32[256,128]{0,1:T(8,128)S(1)} %copy-done.10, f32[128,512]{1,0:T(8,128)S(1)} %get-tuple-element.20, f32[128,512]{1,0:T(8,128)S(1)} %get-tuple-element.19), kind=kOutput, calls=%fused_computation.48 | convolution fusion | flops 616994816 | bytes 4136960 | tf_op jit(solution)/shard_map/dot_general | solution.py:105
  16.8 1.1 %maximum_bitcast_fusion.3 = f32[1,128,1024]{2,1,0:T(8,128)S(1)} fusion(f32[128,512]{1,0:T(8,128)} %get-tuple-element.49, f32[128,512]{1,0:T(8,128)} %constant.227), kind=kLoop, calls=%fused_computation.38 | loop fusion | flops 131072 | bytes 1048576 | tf_op jit(solution)/shard_map/stack | solution.py:127
  18.0 0.0 collective-permute-done.1
  18.0 1.8 %fusion.20 = f32[272,1024]{1,0:T(8,128)S(1)} fusion(f32[272,128]{0,1:T(8,128)} %collective-permute-done.1, f32[128,512]{1,0:T(8,128)} %get-tuple-element.23, f32[128,512]{1,0:T(8,128)} %get-tuple-element.24), kind=kOutput, calls=%fused_computation.27 | convolution fusion | flops 214040576 | bytes 1777664 | tf_op jit(solution)/shard_map/dot_general | solution.py:102
  19.8 0.0 collective-permute-done.2
  19.8 0.0 copy-done.4
  19.9 0.0 copy-done.5
  19.9 1.6 %fusion.24 = f32[272,1024]{1,0:T(8,128)S(1)} fusion(f32[272,128]{0,1:T(8,128)} %collective-permute-done.2, f32[128,512]{1,0:T(8,128)S(1)} %copy-done.4, f32[128,512]{1,0:T(8,128)S(1)} %copy-done.5), kind=kOutput, calls=%fused_computation.31 | convolution fusion | flops 214040576 | bytes 1777664 | tf_op jit(solution)/shard_map/dot_general | solution.py:102
  21.4 0.0 collective-permute-done
  21.5 1.6 %fusion.15 = f32[272,1024]{1,0:T(8,128)S(1)} fusion(f32[272,1024]{1,0:T(8,128)S(1)} %fusion.24, f32[272,1024]{1,0:T(8,128)S(1)} %fusion.20, f32[272,128]{0,1:T(8,128)} %collective-permute-done, f32[128,512]{1,0:T(8,128)S(1)} %copy-done.2, f32[128,512]{1,0:T(8,128)S(1)} %copy-done.3), kind=kOutput, calls=%fused_computation.17 | convolution fusion | flops 214597632 | bytes 4005888 | tf_op jit(solution)/shard_map/dot_general | solution.py:102
  23.1 0.3 slice_add_fusion.1
  23.4 0.1 broadcast_in_dim.25
  23.6 0.4 multiply_subtract_fusion
  24.0 0.2 bitcast_reduce_fusion
  24.2 0.4 copy-done.11
  24.6 0.2 copy-done.12
  24.7 0.2 copy-done.13
  24.9 0.9 %fusion.8 = f32[4,128,16]{1,2,0:T(8,128)S(1)} fusion(f32[1,128,1024]{2,1,0:T(8,128)S(1)} %maximum_bitcast_fusion.3, f32[1,128,1024]{2,1,0:T(8,128)S(1)} %copy-done.13, f32[1,128,1024]{2,1,0:T(8,128)S(1)} %copy-done.12, f32[1,128,1024]{2,1,0:T(8,128)S(1)} %copy-done.11, f32[1024]{0:T(1024)S(1)} %fusion.56, f32[16,1024]{1,0:T(8,128)S(1)} %bitcast_reduce_fusion), kind=kOutput, calls=%fused_computation.9 | convolution fusion | flops 52428800 | bytes 2199552 | tf_op jit(solution)/shard_map/rf,btf->brt/dot_general | solution.py:128
  25.8 5.2 %collective-permute-start.5 = (f32[2,16,128]{2,1,0:T(8,128)S(1)}, f32[2,16,128]{2,1,0:T(8,128)S(1)}, u32[]{:S(2)}, u32[]{:S(2)}) collective-permute-start(f32[2,16,128]{2,1,0:T(8,128)S(1)} %dynamic-slice_bitcast_fusion), channel_id=1, source_target_pairs={{0,16},{8,24},{16,0},{24,8},{1,17},{9,25},{17,1},{25,9},{2,18},{10... | collective-permute-start | bytes 49160 | tf_op jit(solution)/shard_map/ppermute | solution.py:136
  31.1 0.2 select_subtract_fusion
  31.3 0.0 copy-start.7
  31.3 0.0 copy-start.23
  31.4 1.3 %fusion = f32[128,512]{1,0:T(8,128)S(1)} fusion(f32[256,512]{1,0:T(8,128)S(1)} %get-tuple-element.11, f32[256,512]{1,0:T(8,128)S(1)} %get-tuple-element.12, f32[256,512]{1,0:T(8,128)S(1)} %get-tuple-element.8, f32[256,512]{1,0:T(8,128)S(1)} %get-tuple-element.7, f32[128,512]{1,0:T(8,128)S(1)} %copy-done.1, f32[128,512]{1,0:T(8,128)S(1)} %get-tuple-element.19, ...), kind=kOutput, calls=%fused_computation | convolution fusion | flops 404488192 | bytes 2887680 | tf_op jit(solution)/shard_map/tf,rf->tr/dot_general | solution.py:118
  32.6 0.9 %fusion.52 = (bf16[1,128,1,256]{3,1,2,0:T(8,128)(2,1)S(1)}, bf16[1,128,1,256]{3,1,2,0:T(8,128)(2,1)S(1)}, bf16[1,128,256]{2,1,0:T(8,128)(2,1)S(1)}) fusion(f32[128,512]{1,0:T(8,128)S(1)} %fusion, bf16[1,128,3,256]{3,1,2,0:T(8,128)(2,1)S(1)} %copy-done.7, bf16[1,128,3,256]{3,1,2,0:T(8,128)(2,1)} %param.9), kind=kLoop, calls=%fused_computation.93 | loop fusion | flops 360448 | bytes 655360 | tf_op jit(solution)/shard_map/stack | solution.py:176
  33.5 0.0 collective-permute-done.5
  33.6 1.7 %collective-permute-start.6 = (f32[1,16,128]{2,1,0:T(8,128)S(1)}, f32[1,16,128]{2,1,0:T(8,128)S(1)}, u32[]{:S(2)}, u32[]{:S(2)}) collective-permute-start(f32[1,16,128]{2,1,0:T(8,128)S(1)} %constant_dynamic-slice_fusion), channel_id=1, source_target_pairs={{0,8},{8,0},{16,24},{24,16},{1,9},{9,1},{17,25},{25,17},{2,10},{10... | collective-permute-start | bytes 24584 | tf_op jit(solution)/shard_map/ppermute | solution.py:136
  35.3 1.9 %collective-permute-start.4 = (bf16[1,128,3,256]{3,1,2,0:T(8,128)(2,1)S(1)}, bf16[1,128,3,256]{3,1,2,0:T(8,128)(2,1)S(1)}, u32[]{:S(2)}, u32[]{:S(2)}) collective-permute-start(bf16[1,128,3,256]{3,1,2,0:T(8,128)(2,1)S(1)} %pad_maximum_fusion.7), channel_id=1, source_target_pairs={{1,0},{2,1},{3,2},{4,3},{5,4},{6,5},{7,6},{9,8},{10,9},{11,10},{12... | collective-permute-start | bytes 589832 | tf_op jit(solution)/shard_map/ppermute | solution.py:22
  37.2 2.4 %collective-permute-start.3 = (bf16[1,128,256]{2,1,0:T(8,128)(2,1)S(1)}, bf16[1,128,256]{2,1,0:T(8,128)(2,1)S(1)}, u32[]{:S(2)}, u32[]{:S(2)}) collective-permute-start(bf16[1,128,256]{2,1,0:T(8,128)(2,1)S(1)} %get-tuple-element.32), channel_id=1, source_target_pairs={{0,1},{1,2},{2,3},{3,4},{4,5},{5,6},{6,7},{8,9},{9,10},{10,11},{11... | collective-permute-start | bytes 196616 | tf_op jit(solution)/shard_map/ppermute | solution.py:22
  39.6 0.0 collective-permute-done.6
  39.6 0.6 %add_multiply_fusion = f32[1,16,128]{2,1,0:T(8,128)} fusion(f32[1,16,128]{2,1,0:T(8,128)S(1)} %collective-permute-done.6, f32[2,16,128]{2,1,0:T(8,128)S(1)} %bitcast_add_fusion, s32[]{:T(128)S(6)} %select_n.216), kind=kLoop, calls=%fused_computation.102 | loop fusion | flops 4096 | bytes 24580 | tf_op jit(solution)/shard_map/mul | solution.py:178
  40.3 3.4 %collective-permute-done.3 = bf16[1,128,256]{2,1,0:T(8,128)(2,1)S(1)} collective-permute-done((bf16[1,128,256]{2,1,0:T(8,128)(2,1)S(1)}, bf16[1,128,256]{2,1,0:T(8,128)(2,1)S(1)}, u32[]{:S(2)}, u32[]{:S(2)}) %collective-permute-start.3) | collective-permute-done | bytes 65568 | tf_op jit(solution)/shard_map/ppermute | solution.py:22
  43.7 0.0 collective-permute-done.4
  43.7 0.6 %copy.15 = bf16[1,128,256]{2,1,0:T(8,128)(2,1)} copy(bf16[1,128,256]{2,1,0:T(8,128)(2,1)S(1)} %collective-permute-done.3) | data formatting | bytes 131072
  44.3 0.7 %copy.16 = bf16[1,128,3,256]{3,1,2,0:T(8,128)(2,1)} copy(bf16[1,128,3,256]{3,1,2,0:T(8,128)(2,1)S(1)} %collective-permute-done.4) | data formatting | bytes 393216
  (40 shorter events, 0.2 us)
Async XLA Ops:
  0.6 9.8 %copy-start.25 = (f32[4,512]{1,0:T(4,128)S(1)}, f32[4,512]{1,0:T(4,128)}, u32[]{:S(2)}) copy-start(f32[4,512]{1,0:T(4,128)} %constant.181.clone) | copy-start | bytes 24580
  0.6 9.8 %copy-start.26 = (f32[4,512]{1,0:T(4,128)S(1)}, f32[4,512]{1,0:T(4,128)}, u32[]{:S(2)}) copy-start(f32[4,512]{1,0:T(4,128)} %constant.182.clone) | copy-start | bytes 24580
  0.7 9.8 %copy-start.6 = (f32[128,512]{1,0:T(8,128)S(1)}, f32[128,512]{1,0:T(8,128)}, u32[]{:S(2)}) copy-start(f32[128,512]{1,0:T(8,128)} %constant.179.clone) | copy-start | bytes 786436
  0.7 9.8 %copy-start.16 = (f32[128,512]{1,0:T(8,128)S(1)}, f32[128,512]{1,0:T(8,128)}, u32[]{:S(2)}) copy-start(f32[128,512]{1,0:T(8,128)} %constant.180.clone) | copy-start | bytes 786436
  0.7 9.8 %copy-start.17 = (f32[128,512]{1,0:T(8,128)S(1)}, f32[128,512]{1,0:T(8,128)}, u32[]{:S(2)}) copy-start(f32[128,512]{1,0:T(8,128)} %constant.198) | copy-start | bytes 786436
  0.7 9.8 %copy-start.18 = (f32[128,512]{1,0:T(8,128)S(1)}, f32[128,512]{1,0:T(8,128)}, u32[]{:S(2)}) copy-start(f32[128,512]{1,0:T(8,128)} %constant.209) | copy-start | bytes 786436
  0.7 9.8 %copy-start.19 = (f32[128,512]{1,0:T(8,128)S(1)}, f32[128,512]{1,0:T(8,128)}, u32[]{:S(2)}) copy-start(f32[128,512]{1,0:T(8,128)} %constant.220) | copy-start | bytes 786436
  0.7 9.8 %copy-start.20 = (f32[128,512]{1,0:T(8,128)S(1)}, f32[128,512]{1,0:T(8,128)}, u32[]{:S(2)}) copy-start(f32[128,512]{1,0:T(8,128)} %constant.231) | copy-start | bytes 786436
  0.7 9.1 %copy-start.9 = (bf16[1,128,3,256]{3,1,2,0:T(8,128)(2,1)S(1)}, bf16[1,128,3,256]{3,1,2,0:T(8,128)(2,1)}, u32[]{:S(2)}) copy-start(bf16[1,128,3,256]{3,1,2,0:T(8,128)(2,1)} %param.9) | copy-start | bytes 589828
  3.5 14.5 %collective-permute-start.1 = (f32[272,128]{0,1:T(8,128)}, f32[272,128]{0,1:T(8,128)}, u32[]{:S(2)}, u32[]{:S(2)}) collective-permute-start(f32[272,128]{0,1:T(8,128)} %get-tuple-element.36), channel_id=1, source_target_pairs={{0,16},{8,24},{16,0},{24,8},{1,17},{9,25},{17,1},{25,9},{2,18},{10... | collective-permute-start | bytes 417800 | tf_op jit(solution)/shard_map/ppermute | solution.py:100
  6.1 13.7 %collective-permute-start.2 = (f32[272,128]{0,1:T(8,128)}, f32[272,128]{0,1:T(8,128)}, u32[]{:S(2)}, u32[]{:S(2)}) collective-permute-start(f32[272,128]{0,1:T(8,128)} %get-tuple-element.37), channel_id=1, source_target_pairs={{0,24},{8,0},{16,8},{24,16},{1,25},{9,1},{17,9},{25,17},{2,26},{10... | collective-permute-start | bytes 417800 | tf_op jit(solution)/shard_map/ppermute | solution.py:100
  7.4 14.0 %collective-permute-start = (f32[272,128]{0,1:T(8,128)}, f32[272,128]{0,1:T(8,128)}, u32[]{:S(2)}, u32[]{:S(2)}) collective-permute-start(f32[272,128]{0,1:T(8,128)} %get-tuple-element.35), channel_id=1, source_target_pairs={{0,8},{8,16},{16,24},{24,0},{1,9},{9,17},{17,25},{25,1},{2,10},{10... | collective-permute-start | bytes 417800 | tf_op jit(solution)/shard_map/ppermute | solution.py:100
  10.6 2.4 %copy-start.8 = (bf16[1,128,256]{2,1,0:T(8,128)(2,1)S(1)}, bf16[1,128,256]{2,1,0:T(8,128)(2,1)}, u32[]{:S(2)}) copy-start(bf16[1,128,256]{2,1,0:T(8,128)(2,1)} %param.12) | copy-start | bytes 196612
  10.6 2.4 %copy-start.24 = (f32[1,128,256]{2,1,0:T(8,128)S(1)}, f32[1,128,256]{2,1,0:T(8,128)}, u32[]{:S(2)}) copy-start(f32[1,128,256]{2,1,0:T(8,128)} %param.11) | copy-start | bytes 393220
  10.6 3.0 %copy-start.22 = (f32[128,512]{1,0:T(8,128)S(1)}, f32[128,512]{1,0:T(8,128)}, u32[]{:S(2)}) copy-start(f32[128,512]{1,0:T(8,128)} %constant.205) | copy-start | bytes 786436
  12.1 4.7 %copy-start = (f32[128,512]{1,0:T(8,128)}, f32[128,512]{1,0:T(8,128)S(1)}, u32[]{:S(2)}) copy-start(f32[128,512]{1,0:T(8,128)S(1)} %get-tuple-element.20) | copy-start | bytes 786436
  12.1 2.4 %copy-start.21 = (f32[128,512]{1,0:T(8,128)S(1)}, f32[128,512]{1,0:T(8,128)}, u32[]{:S(2)}) copy-start(f32[128,512]{1,0:T(8,128)} %constant.216) | copy-start | bytes 786436
  12.1 3.2 %copy-start.10 = (f32[256,128]{0,1:T(8,128)S(1)}, f32[256,128]{0,1:T(8,128)}, u32[]{:S(2)}) copy-start(f32[256,128]{0,1:T(8,128)} %multiply_bitcast_fusion) | copy-start | bytes 393220
  12.1 3.2 %copy-start.14 = (f32[256,128]{0,1:T(8,128)S(1)}, f32[256,128]{0,1:T(8,128)}, u32[]{:S(2)}) copy-start(f32[256,128]{0,1:T(8,128)} %get-tuple-element.33) | copy-start | bytes 393220
  12.1 3.2 %copy-start.15 = (f32[256,128]{0,1:T(8,128)S(1)}, f32[256,128]{0,1:T(8,128)}, u32[]{:S(2)}) copy-start(f32[256,128]{0,1:T(8,128)} %get-tuple-element.34) | copy-start | bytes 393220
  16.8 3.0 %copy-start.4 = (f32[128,512]{1,0:T(8,128)S(1)}, f32[128,512]{1,0:T(8,128)}, u32[]{:S(2)}) copy-start(f32[128,512]{1,0:T(8,128)} %get-tuple-element.25) | copy-start | bytes 786436
  16.8 3.0 %copy-start.5 = (f32[128,512]{1,0:T(8,128)S(1)}, f32[128,512]{1,0:T(8,128)}, u32[]{:S(2)}) copy-start(f32[128,512]{1,0:T(8,128)} %get-tuple-element.26) | copy-start | bytes 786436
  18.0 3.5 %copy-start.2 = (f32[128,512]{1,0:T(8,128)S(1)}, f32[128,512]{1,0:T(8,128)}, u32[]{:S(2)}) copy-start(f32[128,512]{1,0:T(8,128)} %get-tuple-element.21) | copy-start | bytes 786436
  18.0 3.5 %copy-start.3 = (f32[128,512]{1,0:T(8,128)S(1)}, f32[128,512]{1,0:T(8,128)}, u32[]{:S(2)}) copy-start(f32[128,512]{1,0:T(8,128)} %get-tuple-element.22) | copy-start | bytes 786436
  23.5 1.0 %copy-start.11 = (f32[1,128,1024]{2,1,0:T(8,128)S(1)}, f32[1,128,1024]{2,1,0:T(8,128)}, u32[]{:S(2)}) copy-start(f32[1,128,1024]{2,1,0:T(8,128)} %maximum_bitcast_fusion) | copy-start | bytes 1572868
  23.5 1.2 %copy-start.12 = (f32[1,128,1024]{2,1,0:T(8,128)S(1)}, f32[1,128,1024]{2,1,0:T(8,128)}, u32[]{:S(2)}) copy-start(f32[1,128,1024]{2,1,0:T(8,128)} %maximum_bitcast_fusion.1) | copy-start | bytes 1572868
  23.6 1.3 %copy-start.13 = (f32[1,128,1024]{2,1,0:T(8,128)S(1)}, f32[1,128,1024]{2,1,0:T(8,128)}, u32[]{:S(2)}) copy-start(f32[1,128,1024]{2,1,0:T(8,128)} %maximum_bitcast_fusion.2) | copy-start | bytes 1572868
  25.8 5.5 %copy-start.1 = (f32[128,512]{1,0:T(8,128)S(1)}, f32[128,512]{1,0:T(8,128)}, u32[]{:S(2)}) copy-start(f32[128,512]{1,0:T(8,128)} %copy-done) | copy-start | bytes 786436
  25.8 7.7 %collective-permute-start.5 = (f32[2,16,128]{2,1,0:T(8,128)S(1)}, f32[2,16,128]{2,1,0:T(8,128)S(1)}, u32[]{:S(2)}, u32[]{:S(2)}) collective-permute-start(f32[2,16,128]{2,1,0:T(8,128)S(1)} %dynamic-slice_bitcast_fusion), channel_id=1, source_target_pairs={{0,16},{8,24},{16,0},{24,8},{1,17},{9,25},{17,1},{25,9},{2,18},{10... | collective-permute-start | bytes 49160 | tf_op jit(solution)/shard_map/ppermute | solution.py:136
  31.3 1.3 %copy-start.7 = (bf16[1,128,3,256]{3,1,2,0:T(8,128)(2,1)S(1)}, bf16[1,128,3,256]{3,1,2,0:T(8,128)(2,1)}, u32[]{:S(2)}) copy-start(bf16[1,128,3,256]{3,1,2,0:T(8,128)(2,1)} %param.10) | copy-start | bytes 589828
  31.3 3.9 %copy-start.23 = (bf16[1,128,1,256]{3,1,2,0:T(8,128)(2,1)S(1)}, bf16[1,128,1,256]{3,1,2,0:T(8,128)(2,1)}, u32[]{:S(2)}) copy-start(bf16[1,128,1,256]{3,1,2,0:T(8,128)(2,1)} %fusion.53) | copy-start | bytes 196612
  33.6 6.1 %collective-permute-start.6 = (f32[1,16,128]{2,1,0:T(8,128)S(1)}, f32[1,16,128]{2,1,0:T(8,128)S(1)}, u32[]{:S(2)}, u32[]{:S(2)}) collective-permute-start(f32[1,16,128]{2,1,0:T(8,128)S(1)} %constant_dynamic-slice_fusion), channel_id=1, source_target_pairs={{0,8},{8,0},{16,24},{24,16},{1,9},{9,1},{17,25},{25,17},{2,10},{10... | collective-permute-start | bytes 24584 | tf_op jit(solution)/shard_map/ppermute | solution.py:136
  35.3 8.4 %collective-permute-start.4 = (bf16[1,128,3,256]{3,1,2,0:T(8,128)(2,1)S(1)}, bf16[1,128,3,256]{3,1,2,0:T(8,128)(2,1)S(1)}, u32[]{:S(2)}, u32[]{:S(2)}) collective-permute-start(bf16[1,128,3,256]{3,1,2,0:T(8,128)(2,1)S(1)} %pad_maximum_fusion.7), channel_id=1, source_target_pairs={{1,0},{2,1},{3,2},{4,3},{5,4},{6,5},{7,6},{9,8},{10,9},{11,10},{12... | collective-permute-start | bytes 589832 | tf_op jit(solution)/shard_map/ppermute | solution.py:22
  37.2 6.5 %collective-permute-start.3 = (bf16[1,128,256]{2,1,0:T(8,128)(2,1)S(1)}, bf16[1,128,256]{2,1,0:T(8,128)(2,1)S(1)}, u32[]{:S(2)}, u32[]{:S(2)}) collective-permute-start(bf16[1,128,256]{2,1,0:T(8,128)(2,1)S(1)} %get-tuple-element.32), channel_id=1, source_target_pairs={{0,1},{1,2},{2,3},{3,4},{4,5},{5,6},{6,7},{8,9},{9,10},{10,11},{11... | collective-permute-start | bytes 196616 | tf_op jit(solution)/shard_map/ppermute | solution.py:22

commit v9 on v5

--- a/solution.py
+++ b/solution.py
@@ -56,24 +56,16 @@
 def packed_tables(blocks, block):
     size = 2 * blocks * block
     half = size // 2
-    ids = np.arange(block)
-    freqs = np.arange(half)
-    theta = 2.0 * np.pi * ((ids[:, None] * freqs[None, :]) % size) / size
-    phase = 2.0 * np.pi * ((np.arange(blocks)[:, None] * block * freqs[None, :]) % size) / size
-    as32 = lambda a: jnp.asarray(a, jnp.float32)
-    return as32(np.cos(theta)), as32(np.sin(theta)), as32(np.cos(phase)), as32(np.sin(phase))
+    pos = np.arange(blocks * block)
+    theta = 2.0 * np.pi * ((pos[:, None] * np.arange(half)[None, :]) % size) / size
+    im = -np.sin(theta)
+    im[:, 0] = 1.0 - 2.0 * (pos % 2)
+    table = np.concatenate([np.cos(theta), im], axis=1)
+    return jnp.asarray(table.reshape(blocks, block, size), jnp.float32)
 
 
 def block_table(packed, index):
-    base_c, base_s, turn_c, turn_s = packed
-    c = lax.dynamic_index_in_dim(turn_c, index, keepdims=True)
-    s = lax.dynamic_index_in_dim(turn_s, index, keepdims=True)
-    cos = base_c * c - base_s * s
-    sin = base_s * c + base_c * s
-    block, half = cos.shape
-    first = lax.broadcasted_iota(jnp.int32, (block, half), 1) == 0
-    sign = 1.0 - 2.0 * (lax.broadcasted_iota(jnp.int32, (block, half), 0) % 2).astype(jnp.float32)
-    return jnp.concatenate([cos, jnp.where(first, sign, -sin)], axis=1)
+    return lax.dynamic_index_in_dim(packed, index, keepdims=False)
 
 
 def packed_products(h, a, conj):

time: 43.4 us -> 45.1 us (1.039)
  starting transfers between devices: 17.6 us -> 12.6 us
  matrix products: 6.62 us -> 11.2 us
  other arithmetic: 3.98 us -> 5.37 us
  waiting for transfers between devices: 11.5 us -> 12.2 us
    ppermute x3, starting transfers between devices: 8.37 us -> 3.94 us  [dense_path(): lag = lag + lax.ppermute(share, 'ctx', pairs)]
    dot_general x3, matrix products: 2.02 us -> 5.39 us  [dense_path(): acc = acc + jnp.dot(got, table, precision=precise)]
    transpose x2, other arithmetic: 0.89 us -> 2.33 us  [on_device(): conv, grad_mixed, lag = dense_path(place, blocks, mixed_in.T, weighted.T,...]
    dot_general x1, matrix products: 1.48 us -> 2.7 us  [dense_path(): loc = jnp.dot(own, own_table, precision=precise)]
    ppermute x3, waiting for transfers between devices: 7.94 us -> 8.85 us  [dense_path(): got = lax.ppermute(payload, 'ctx', pairs)]
    concatenate x1, other arithmetic: 0.05 us -> 0.84 us  [dense_path(): payload = jnp.concatenate([first, taps], axis=0)]
    sub x2 -> x0, other arithmetic: 0.65 us -> none  [block_table(): cos = base_c * c - base_s * s]
    ppermute x2, starting transfers between devices: 4.59 us -> 4.03 us  [from_behind(): return lax.ppermute(x, axis, pairs)]
  transfers between devices with their start and end apart: 8 -> 8, of which waited for: 3 -> 2; matrix products, arithmetic and copies ran while one was open for 17% -> 27% of each run, Pallas kernels for 0% -> 0%
where the time goes in v9:
time: 45.1 us; the launch traced here: 44.7 us
  starting transfers between devices  12.6 us (28%)
  waiting for transfers between devices  12.2 us (27%)
  matrix products  11.2 us (25%)
  other arithmetic  5.37 us (12%)
  local copies, waits for them, and re-layouts  2.31 us (5%)
  between operations  0.98 us (2%)
    ppermute x3, waiting for transfers between devices, dense_path(): got = lax.ppermute(payload, 'ctx', pairs)  8.85 us
    dot_general x3, matrix products, dense_path(): acc = acc + jnp.dot(got, table, precision=precise)  5.39 us
    ppermute x3, starting transfers between devices, dense_path(): got = lax.ppermute(payload, 'ctx', pairs)  4.61 us
    ppermute x2, starting transfers between devices, from_behind(): return lax.ppermute(x, axis, pairs)  4.03 us
    ppermute x3, starting transfers between devices, dense_path(): lag = lag + lax.ppermute(share, 'ctx', pairs)  3.94 us
    ppermute x2, waiting for transfers between devices, from_behind(): return lax.ppermute(x, axis, pairs)  3.37 us
    dot_general x1, matrix products, dense_path(): loc = jnp.dot(own, own_table, precision=precise)  2.7 us
    transpose x2, other arithmetic, on_device(): conv, grad_mixed, lag = dense_path(place, blocks, mixed_in.T, weighted.T,...  2.33 us
  transfers between devices with their start and end apart: 8, of which 2 were waited for; matrix products, arithmetic and copies ran while one was open for 27% of the time, Pallas kernels for 0%

profile of v9, /device:TPU:4, one launch (start us, length us, event | category | flops | bytes accessed | tf_op | source)
XLA Modules:
  0.0 44.7 jit_solution(3403275816871579971)
XLA Ops:
  0.6 0.0 copy-start.3
  0.6 0.0 copy-start.2
  0.7 0.0 copy-start.4
  0.7 0.9 %copy.9 = f32[1,16,128]{1,2,0:T(8,128)S(1)} copy(f32[1,16,128]{2,1,0:T(8,128)} %param.10) | data formatting | bytes 16384 | tf_op args[4]
  1.5 1.0 %broadcast_select_fusion.2 = (f32[256,128]{0,1:T(8,128)S(1)}, f32[256,128]{0,1:T(8,128)S(1)}, f32[256,128]{0,1:T(8,128)S(1)}) fusion(pred[]{:T(512)S(6)} %lt.58, bf16[1,128,3,256]{3,1,2,0:T(8,128)(2,1)} %param.7, bf16[1,128,256]{2,1,0:T(8,128)(2,1)} %param.9, bf16[1,128,3,256]{3,1,2,0:T(8,128)(2,1)} %param.6, pred[]{:T(512)S(6)} %lt.61, pred[]{:T(512)S(6)} %lt.64), kind=kLoop, calls=%fused_computation.88 | loop fusion | flops 294912 | bytes 655363 | tf_op jit(solution)/shard_map/jit(_where)/select_n | solution.py:89
  2.5 0.8 %pad_maximum_fusion.3 = (f32[272,128]{0,1:T(8,128)}, f32[272,128]{0,1:T(8,128)}, f32[272,128]{0,1:T(8,128)}) fusion(f32[16,128]{0,1:T(8,128)S(1)} %bitcast.99, f32[256,128]{0,1:T(8,128)S(1)} %get-tuple-element.15, f32[256,128]{0,1:T(8,128)S(1)} %get-tuple-element.16, f32[256,128]{0,1:T(8,128)S(1)} %get-tuple-element.17), kind=kLoop, calls=%fused_computation.58 | loop fusion | flops 104448 | bytes 819200 | tf_op jit(solution)/shard_map/concatenate | solution.py:90
  3.4 3.6 %collective-permute-start.2 = (f32[272,128]{0,1:T(8,128)}, f32[272,128]{0,1:T(8,128)}, u32[]{:S(2)}, u32[]{:S(2)}) collective-permute-start(f32[272,128]{0,1:T(8,128)} %get-tuple-element.23), channel_id=1, source_target_pairs={{0,24},{8,0},{16,8},{24,16},{1,25},{9,1},{17,9},{25,17},{2,26},{10... | collective-permute-start | bytes 417800 | tf_op jit(solution)/shard_map/ppermute | solution.py:92
  7.0 0.0 collective-permute-start.1
  7.0 1.0 %collective-permute-start = (f32[272,128]{0,1:T(8,128)}, f32[272,128]{0,1:T(8,128)}, u32[]{:S(2)}, u32[]{:S(2)}) collective-permute-start(f32[272,128]{0,1:T(8,128)} %get-tuple-element.21), channel_id=1, source_target_pairs={{0,8},{8,16},{16,24},{24,0},{1,9},{9,17},{17,25},{25,1},{2,10},{10... | collective-permute-start | bytes 417800 | tf_op jit(solution)/shard_map/ppermute | solution.py:92
  8.0 1.7 %fusion.43 = (f32[256,128]{0,1:T(8,128)}, f32[256,128]{0,1:T(8,128)}) fusion(bf16[1,128,256]{2,1,0:T(8,128)(2,1)} %param.9, bf16[1,128,3,256]{3,1,2,0:T(8,128)(2,1)} %param.7), kind=kLoop, calls=%fused_computation.71 | loop fusion | flops 196608 | bytes 524288 | tf_op jit(solution)/shard_map/transpose | solution.py:185
  9.7 0.0 copy-done.3
  9.7 0.7 %multiply_bitcast_fusion = f32[256,128]{0,1:T(8,128)} fusion(bf16[1,128,3,256]{3,1,2,0:T(8,128)(2,1)S(1)} %copy-done.3), kind=kLoop, calls=%fused_computation.80 | loop fusion | flops 98304 | bytes 262144 | tf_op jit(solution)/shard_map/transpose | solution.py:185
  10.3 0.0 copy-done.2
  10.3 0.0 copy-done.4
  10.3 2.7 %fusion.21 = f32[784,1024]{1,0:T(8,128)S(1)} fusion(f32[4,128,1024]{2,1,0:T(8,128)} %constant.82.clone, s32[]{:T(128)S(6)} %select_n.104, f32[16,128]{0,1:T(8,128)S(1)} %bitcast.100, f32[256,128]{0,1:T(8,128)} %get-tuple-element.20, f32[256,128]{0,1:T(8,128)} %get-tuple-element.19, f32[256,128]{0,1:T(8,128)} %multiply_bitcast_fusion), kind=kOutput, calls=%fused_computation.30 | convolution fusion | flops 616863744 | bytes 4136964 | tf_op jit(solution)/shard_map/dot_general | solution.py:97
  13.2 0.0 copy-start
  13.2 0.0 collective-permute-done.2
  13.2 1.9 %fusion.16 = f32[272,1024]{1,0:T(8,128)S(1)} fusion(f32[272,128]{0,1:T(8,128)} %collective-permute-done.2, f32[4,128,1024]{2,1,0:T(8,128)} %constant.82.clone, s32[]{:T(128)S(6)} %select_n.117), kind=kOutput, calls=%fused_computation.25 | convolution fusion | flops 213909504 | bytes 1835012 | tf_op jit(solution)/shard_map/dot_general | solution.py:94
  15.1 8.8 %collective-permute-done.1 = f32[272,128]{0,1:T(8,128)} collective-permute-done((f32[272,128]{0,1:T(8,128)}, f32[272,128]{0,1:T(8,128)}, u32[]{:S(2)}, u32[]{:S(2)}) %collective-permute-start.1) | collective-permute-done | bytes 139296 | tf_op jit(solution)/shard_map/ppermute | solution.py:92
  24.0 1.8 %fusion.18 = f32[272,1024]{1,0:T(8,128)S(1)} fusion(f32[272,128]{0,1:T(8,128)} %collective-permute-done.1, f32[4,128,1024]{2,1,0:T(8,128)} %constant.82.clone, s32[]{:T(128)S(6)} %select_n.113), kind=kOutput, calls=%fused_computation.27 | convolution fusion | flops 213909504 | bytes 1835012 | tf_op jit(solution)/shard_map/dot_general | solution.py:94
  25.8 0.0 collective-permute-done
  25.8 0.0 copy-done
  25.8 1.7 %fusion.8 = f32[272,1024]{1,0:T(8,128)S(1)} fusion(f32[272,1024]{1,0:T(8,128)S(1)} %fusion.16, f32[272,1024]{1,0:T(8,128)S(1)} %fusion.18, f32[272,128]{0,1:T(8,128)} %collective-permute-done, f32[4,128,1024]{2,1,0:T(8,128)S(1)} %copy-done, s32[]{:T(128)S(6)} %select_n.109), kind=kOutput, calls=%fused_computation.9 | convolution fusion | flops 214466560 | bytes 4005892 | tf_op jit(solution)/shard_map/dot_general | solution.py:94
  27.5 0.3 slice_add_fusion.1
  27.8 0.1 broadcast_in_dim.26
  27.9 0.4 multiply_subtract_fusion
  28.3 0.2 bitcast_reduce_fusion
  28.5 0.3 fusion.15
  28.8 0.0 collective-permute-start.5
  28.8 0.3 fusion.14
  29.1 1.0 %collective-permute-start.6 = (f32[16,128]{1,0:T(8,128)S(1)}, f32[16,128]{1,0:T(8,128)S(1)}, u32[]{:S(2)}, u32[]{:S(2)}) collective-permute-start(f32[16,128]{1,0:T(8,128)S(1)} %fusion.14), channel_id=1, source_target_pairs={{0,16},{8,24},{16,0},{24,8},{1,17},{9,25},{17,1},{25,9},{2,18},{10... | collective-permute-start | bytes 24584 | tf_op jit(solution)/shard_map/ppermute | solution.py:116
  30.1 0.2 select_subtract_fusion
  30.4 0.0 copy-start.1
  30.4 1.2 %fusion = f32[128,512]{1,0:T(8,128)S(1)} fusion(f32[256,512]{1,0:T(8,128)S(1)} %get-tuple-element.11, f32[256,512]{1,0:T(8,128)S(1)} %get-tuple-element.12, f32[256,512]{1,0:T(8,128)S(1)} %get-tuple-element.8, f32[256,512]{1,0:T(8,128)S(1)} %get-tuple-element.7, f32[4,128,1024]{2,1,0:T(8,128)S(1)} %copy-done, s32[]{:T(128)S(6)} %select_n.104, f32[1024]{0:T(1024)S(1)} %fusion.55), kind=kOutput, calls=%fused_computation | convolution fusion | flops 404357120 | bytes 2887684 | tf_op jit(solution)/shard_map/tf,rf->tr/dot_general | solution.py:110
  31.6 0.0 copy-done.1
  31.7 0.1 fusion.52
  31.7 1.9 %collective-permute-start.4 = (bf16[1,128,3,256]{3,1,2,0:T(8,128)(2,1)S(1)}, bf16[1,128,3,256]{3,1,2,0:T(8,128)(2,1)S(1)}, u32[]{:S(2)}, u32[]{:S(2)}) collective-permute-start(bf16[1,128,3,256]{3,1,2,0:T(8,128)(2,1)S(1)} %pad_maximum_fusion.4), channel_id=1, source_target_pairs={{1,0},{2,1},{3,2},{4,3},{5,4},{6,5},{7,6},{9,8},{10,9},{11,10},{12... | collective-permute-start | bytes 589832 | tf_op jit(solution)/shard_map/ppermute | solution.py:22
  33.7 0.3 fusion.13
  34.0 2.9 %collective-permute-start.7 = (f32[16,128]{1,0:T(8,128)S(1)}, f32[16,128]{1,0:T(8,128)S(1)}, u32[]{:S(2)}, u32[]{:S(2)}) collective-permute-start(f32[16,128]{1,0:T(8,128)S(1)} %fusion.13), channel_id=1, source_target_pairs={{0,24},{8,0},{16,8},{24,16},{1,25},{9,1},{17,9},{25,17},{2,26},{10... | collective-permute-start | bytes 24584 | tf_op jit(solution)/shard_map/ppermute | solution.py:116
  36.9 2.1 %collective-permute-start.3 = (bf16[1,128,256]{2,1,0:T(8,128)(2,1)S(1)}, bf16[1,128,256]{2,1,0:T(8,128)(2,1)S(1)}, u32[]{:S(2)}, u32[]{:S(2)}) collective-permute-start(bf16[1,128,256]{2,1,0:T(8,128)(2,1)S(1)} %get-tuple-element.18), channel_id=1, source_target_pairs={{0,1},{1,2},{2,3},{3,4},{4,5},{5,6},{6,7},{8,9},{9,10},{10,11},{11... | collective-permute-start | bytes 196616 | tf_op jit(solution)/shard_map/ppermute | solution.py:22
  39.1 0.0 collective-permute-done.5
  39.1 0.0 collective-permute-done.6
  39.1 0.0 collective-permute-done.7
  39.1 0.9 %fusion.12 = f32[1,16,128]{2,1,0:T(8,128)} fusion(f32[16,128]{1,0:T(8,128)S(1)} %collective-permute-done.7, f32[16,128]{1,0:T(8,128)S(1)} %collective-permute-done.6, f32[16,128]{1,0:T(8,128)S(1)} %collective-permute-done.5, f32[16,1024]{1,0:T(8,128)S(1)} %bitcast_reduce_fusion, f32[4,128,1024]{2,1,0:T(8,128)S(1)} %copy-done, s32[]{:T(128)S(6)} %select_n.104, ...), kind=kOutput, calls=%fused_computation.14 | convolution fusion | flops 12722176 | bytes 626692 | tf_op jit(solution)/shard_map/rf,tf->rt/dot_general | solution.py:111
  40.0 3.4 %collective-permute-done.3 = bf16[1,128,256]{2,1,0:T(8,128)(2,1)S(1)} collective-permute-done((bf16[1,128,256]{2,1,0:T(8,128)(2,1)S(1)}, bf16[1,128,256]{2,1,0:T(8,128)(2,1)S(1)}, u32[]{:S(2)}, u32[]{:S(2)}) %collective-permute-start.3) | collective-permute-done | bytes 65568 | tf_op jit(solution)/shard_map/ppermute | solution.py:22
  43.4 0.0 collective-permute-done.4
  43.4 0.6 %copy.12 = bf16[1,128,256]{2,1,0:T(8,128)(2,1)} copy(bf16[1,128,256]{2,1,0:T(8,128)(2,1)S(1)} %collective-permute-done.3) | data formatting | bytes 131072
  44.0 0.7 %copy.13 = bf16[1,128,3,256]{3,1,2,0:T(8,128)(2,1)} copy(bf16[1,128,3,256]{3,1,2,0:T(8,128)(2,1)S(1)} %collective-permute-done.4) | data formatting | bytes 393216
  (5 shorter events, 0.1 us)
Async XLA Ops:
  0.6 9.0 %copy-start.3 = (bf16[1,128,3,256]{3,1,2,0:T(8,128)(2,1)S(1)}, bf16[1,128,3,256]{3,1,2,0:T(8,128)(2,1)}, u32[]{:S(2)}) copy-start(bf16[1,128,3,256]{3,1,2,0:T(8,128)(2,1)} %param.6) | copy-start | bytes 589828
  0.6 9.7 %copy-start.2 = (bf16[1,128,256]{2,1,0:T(8,128)(2,1)S(1)}, bf16[1,128,256]{2,1,0:T(8,128)(2,1)}, u32[]{:S(2)}) copy-start(bf16[1,128,256]{2,1,0:T(8,128)(2,1)} %param.9) | copy-start | bytes 196612
  0.7 9.7 %copy-start.4 = (f32[1,128,256]{2,1,0:T(8,128)S(1)}, f32[1,128,256]{2,1,0:T(8,128)}, u32[]{:S(2)}) copy-start(f32[1,128,256]{2,1,0:T(8,128)} %param.8) | copy-start | bytes 393220
  3.4 9.8 %collective-permute-start.2 = (f32[272,128]{0,1:T(8,128)}, f32[272,128]{0,1:T(8,128)}, u32[]{:S(2)}, u32[]{:S(2)}) collective-permute-start(f32[272,128]{0,1:T(8,128)} %get-tuple-element.23), channel_id=1, source_target_pairs={{0,24},{8,0},{16,8},{24,16},{1,25},{9,1},{17,9},{25,17},{2,26},{10... | collective-permute-start | bytes 417800 | tf_op jit(solution)/shard_map/ppermute | solution.py:92
  7.0 17.0 %collective-permute-start.1 = (f32[272,128]{0,1:T(8,128)}, f32[272,128]{0,1:T(8,128)}, u32[]{:S(2)}, u32[]{:S(2)}) collective-permute-start(f32[272,128]{0,1:T(8,128)} %get-tuple-element.22), channel_id=1, source_target_pairs={{0,16},{8,24},{16,0},{24,8},{1,17},{9,25},{17,1},{25,9},{2,18},{10... | collective-permute-start | bytes 417800 | tf_op jit(solution)/shard_map/ppermute | solution.py:92
  7.0 18.8 %collective-permute-start = (f32[272,128]{0,1:T(8,128)}, f32[272,128]{0,1:T(8,128)}, u32[]{:S(2)}, u32[]{:S(2)}) collective-permute-start(f32[272,128]{0,1:T(8,128)} %get-tuple-element.21), channel_id=1, source_target_pairs={{0,8},{8,16},{16,24},{24,0},{1,9},{9,17},{17,25},{25,1},{2,10},{10... | collective-permute-start | bytes 417800 | tf_op jit(solution)/shard_map/ppermute | solution.py:92
  13.2 12.6 %copy-start = (f32[4,128,1024]{2,1,0:T(8,128)S(1)}, f32[4,128,1024]{2,1,0:T(8,128)}, u32[]{:S(2)}) copy-start(f32[4,128,1024]{2,1,0:T(8,128)} %constant.82.clone) | copy-start | bytes 6291460
  28.8 10.3 %collective-permute-start.5 = (f32[16,128]{1,0:T(8,128)S(1)}, f32[16,128]{1,0:T(8,128)S(1)}, u32[]{:S(2)}, u32[]{:S(2)}) collective-permute-start(f32[16,128]{1,0:T(8,128)S(1)} %fusion.15), channel_id=1, source_target_pairs={{0,8},{8,16},{16,24},{24,0},{1,9},{9,17},{17,25},{25,1},{2,10},{10... | collective-permute-start | bytes 24584 | tf_op jit(solution)/shard_map/ppermute | solution.py:116
  29.1 9.9 %collective-permute-start.6 = (f32[16,128]{1,0:T(8,128)S(1)}, f32[16,128]{1,0:T(8,128)S(1)}, u32[]{:S(2)}, u32[]{:S(2)}) collective-permute-start(f32[16,128]{1,0:T(8,128)S(1)} %fusion.14), channel_id=1, source_target_pairs={{0,16},{8,24},{16,0},{24,8},{1,17},{9,25},{17,1},{25,9},{2,18},{10... | collective-permute-start | bytes 24584 | tf_op jit(solution)/shard_map/ppermute | solution.py:116
  30.4 1.3 %copy-start.1 = (bf16[1,128,3,256]{3,1,2,0:T(8,128)(2,1)S(1)}, bf16[1,128,3,256]{3,1,2,0:T(8,128)(2,1)}, u32[]{:S(2)}) copy-start(bf16[1,128,3,256]{3,1,2,0:T(8,128)(2,1)} %param.7) | copy-start | bytes 589828
  31.7 11.7 %collective-permute-start.4 = (bf16[1,128,3,256]{3,1,2,0:T(8,128)(2,1)S(1)}, bf16[1,128,3,256]{3,1,2,0:T(8,128)(2,1)S(1)}, u32[]{:S(2)}, u32[]{:S(2)}) collective-permute-start(bf16[1,128,3,256]{3,1,2,0:T(8,128)(2,1)S(1)} %pad_maximum_fusion.4), channel_id=1, source_target_pairs={{1,0},{2,1},{3,2},{4,3},{5,4},{6,5},{7,6},{9,8},{10,9},{11,10},{12... | collective-permute-start | bytes 589832 | tf_op jit(solution)/shard_map/ppermute | solution.py:22
  34.0 5.1 %collective-permute-start.7 = (f32[16,128]{1,0:T(8,128)S(1)}, f32[16,128]{1,0:T(8,128)S(1)}, u32[]{:S(2)}, u32[]{:S(2)}) collective-permute-start(f32[16,128]{1,0:T(8,128)S(1)} %fusion.13), channel_id=1, source_target_pairs={{0,24},{8,0},{16,8},{24,16},{1,25},{9,1},{17,9},{25,17},{2,26},{10... | collective-permute-start | bytes 24584 | tf_op jit(solution)/shard_map/ppermute | solution.py:116
  36.9 6.5 %collective-permute-start.3 = (bf16[1,128,256]{2,1,0:T(8,128)(2,1)S(1)}, bf16[1,128,256]{2,1,0:T(8,128)(2,1)S(1)}, u32[]{:S(2)}, u32[]{:S(2)}) collective-permute-start(bf16[1,128,256]{2,1,0:T(8,128)(2,1)S(1)} %get-tuple-element.18), channel_id=1, source_target_pairs={{0,1},{1,2},{2,3},{3,4},{4,5},{5,6},{6,7},{8,9},{9,10},{10,11},{11... | collective-permute-start | bytes 196616 | tf_op jit(solution)/shard_map/ppermute | solution.py:22

commit v10 on v5

--- a/solution.py
+++ b/solution.py
@@ -87,22 +87,22 @@
     return jnp.concatenate([re, im], axis=1)
 
 
-def dense_path(place, blocks, mixed_rows, weighted_rows, back_rows, taps):
-    channels, block = mixed_rows.shape
+def dense_path(place, blocks, mixed, weighted, back, taps):
+    block, channels = mixed.shape
     size = 2 * blocks * block
     half = size // 2
     packed = packed_tables(blocks, block)
     acc = 0.0
     for s in range(1, blocks):
-        first = jnp.where(place + s < blocks, mixed_rows, weighted_rows)
-        payload = jnp.concatenate([first, taps], axis=0)
+        first = jnp.where(place + s < blocks, mixed, weighted)
+        payload = jnp.concatenate([first, taps], axis=1)
         pairs = [(i, (i + s) % blocks) for i in range(blocks)]
         got = lax.ppermute(payload, "ctx", pairs)
         table = block_table(packed, (place - s) % blocks)
-        acc = acc + jnp.dot(got, table, precision=precise)
+        acc = acc + jnp.einsum("pr,pf->rf", got, table, precision=precise)
     own_table = block_table(packed, place)
-    own = jnp.concatenate([mixed_rows, weighted_rows, back_rows, taps], axis=0)
-    loc = jnp.dot(own, own_table, precision=precise)
+    own = jnp.concatenate([mixed, weighted, back, taps], axis=1)
+    loc = jnp.einsum("pr,pf->rf", own, own_table, precision=precise)
     c = channels
     mixed_spec = loc[:c] + acc[:c]
     weighted_spec = loc[c : 2 * c] + acc[:c]
@@ -190,7 +190,7 @@
 
     if blocks <= DENSE:
         conv, grad_mixed, lag = dense_path(
-            place, blocks, mixed_in.T, weighted.T, mixed_back.T, taps
+            place, blocks, mixed_in, weighted, mixed_back, taps.T
         )
         return finish(
             conv, grad_mixed, lag, filter_scale, query_in, grad_query, key_back, value_back

time: 43.4 us -> 43.5 us (level)
  waiting for transfers between devices: 11.5 us -> 12.4 us
  other arithmetic: 3.98 us -> 3.18 us
    transpose x2 -> x0, other arithmetic: 0.89 us -> none  [on_device(): conv, grad_mixed, lag = dense_path(place, blocks, mixed_in.T, weighted.T,...]
    ppermute x3, waiting for transfers between devices: 7.94 us -> 8.82 us  [dense_path(): got = lax.ppermute(payload, 'ctx', pairs)]
  transfers between devices with their start and end apart: 8 -> 8, of which waited for: 3 -> 3; matrix products, arithmetic and copies ran while one was open for 17% -> 15% of each run, Pallas kernels for 0% -> 0%
where the time goes in v10:
time: 43.5 us; the launch traced here: 43.3 us
  starting transfers between devices  17.6 us (40%)
  waiting for transfers between devices  12.4 us (29%)
  matrix products  6.62 us (15%)
  other arithmetic  3.18 us (7%)
  local copies, waits for them, and re-layouts  2.42 us (6%)
  between operations  1 us (2%)
    ppermute x3, waiting for transfers between devices, dense_path(): got = lax.ppermute(payload, 'ctx', pairs)  8.82 us
    ppermute x3, starting transfers between devices, dense_path(): lag = lag + lax.ppermute(share, 'ctx', pairs)  8.37 us
    ppermute x3, starting transfers between devices, dense_path(): got = lax.ppermute(payload, 'ctx', pairs)  4.68 us
    ppermute x2, starting transfers between devices, from_behind(): return lax.ppermute(x, axis, pairs)  4.59 us
    ppermute x2, waiting for transfers between devices, from_behind(): return lax.ppermute(x, axis, pairs)  3.58 us
    unnamed x19, local copies, waits for them, and re-layouts  2.28 us
    dot_general x3, matrix products, dense_path(): acc = acc + jnp.einsum('pr,pf->rf', got, table, precision=precise)  2.02 us
    dot_general x1, matrix products, dense_path(): loc = jnp.einsum('pr,pf->rf', own, own_table, precision=precise)  1.48 us
  transfers between devices with their start and end apart: 8, of which 3 were waited for; matrix products, arithmetic and copies ran while one was open for 15% of the time, Pallas kernels for 0%

profile of v10, /device:TPU:4, one launch (start us, length us, event | category | flops | bytes accessed | tf_op | source)
XLA Modules:
  0.0 43.3 jit_solution(15666590939598089587)
XLA Ops:
  0.6 0.0 copy-start.6
  0.6 0.0 copy-start.7
  0.7 0.0 copy-start
  0.7 0.0 copy-start.1
  0.7 0.0 copy-start.4
  0.7 0.0 copy-start.3
  0.7 0.0 copy-start.5
  0.7 0.9 %copy.12 = f32[1,16,128]{1,2,0:T(8,128)S(1)} copy(f32[1,16,128]{2,1,0:T(8,128)} %param.13) | data formatting | bytes 16384 | tf_op args[4]
  1.6 1.1 %broadcast_select_fusion.2 = (f32[128,256]{1,0:T(8,128)S(1)}, f32[128,256]{1,0:T(8,128)S(1)}, f32[128,256]{1,0:T(8,128)S(1)}, f32[128,256]{1,0:T(8,128)S(1)}, f32[128,256]{1,0:T(8,128)S(1)}) fusion(pred[]{:T(512)S(6)} %lt.96, bf16[1,128,3,256]{3,1,2,0:T(8,128)(2,1)} %param.10, bf16[1,128,256]{2,1,0:T(8,128)(2,1)} %param.12, ...), kind=kLoop, calls=%fused_computation.107 | loop fusion | flops 393216 | bytes 1048579 | tf_op jit(solution)/shard_map/jit(_where)/select_n | solution.py:97
  2.8 2.7 %collective-permute-start.1 = (f32[128,272]{1,0:T(8,128)S(1)}, f32[128,272]{1,0:T(8,128)S(1)}, u32[]{:S(2)}, u32[]{:S(2)}) collective-permute-start(f32[128,272]{1,0:T(8,128)S(1)} %get-tuple-element.46), channel_id=1, source_target_pairs={{0,16},{8,24},{16,0},{24,8},{1,17},{9,25},{17,1},{25,9},{2,18},{10... | collective-permute-start | bytes 417800 | tf_op jit(solution)/shard_map/ppermute | solution.py:100
  5.4 1.3 %collective-permute-start.2 = (f32[128,272]{1,0:T(8,128)S(1)}, f32[128,272]{1,0:T(8,128)S(1)}, u32[]{:S(2)}, u32[]{:S(2)}) collective-permute-start(f32[128,272]{1,0:T(8,128)S(1)} %get-tuple-element.47), channel_id=1, source_target_pairs={{0,24},{8,0},{16,8},{24,16},{1,25},{9,1},{17,9},{25,17},{2,26},{10... | collective-permute-start | bytes 417800 | tf_op jit(solution)/shard_map/ppermute | solution.py:100
  6.8 0.7 %collective-permute-start = (f32[128,272]{1,0:T(8,128)S(1)}, f32[128,272]{1,0:T(8,128)S(1)}, u32[]{:S(2)}, u32[]{:S(2)}) collective-permute-start(f32[128,272]{1,0:T(8,128)S(1)} %get-tuple-element.45), channel_id=1, source_target_pairs={{0,8},{8,16},{16,24},{24,0},{1,9},{9,17},{17,25},{25,1},{2,10},{10... | collective-permute-start | bytes 417800 | tf_op jit(solution)/shard_map/ppermute | solution.py:100
  7.5 0.0 copy-done.3
  7.5 0.0 copy-done.4
  7.5 0.0 copy-done.5
  7.6 0.0 copy-done.6
  7.6 0.0 copy-done.7
  7.6 0.0 copy-done
  7.6 0.0 copy-done.1
  7.6 0.1 multiply_subtract_fusion.5
  7.8 0.5 %multiply_subtract_fusion.9 = (f32[128,512]{1,0:T(8,128)S(1)}, f32[128,512]{1,0:T(8,128)S(1)}, f32[128,512]{1,0:T(8,128)S(1)}, f32[128,512]{1,0:T(8,128)S(1)}, f...) fusion(f32[128,512]{1,0:T(8,128)S(1)} %copy-done.1, ...), kind=kLoop, calls=%fused_computation.84 | loop fusion | flops 3407872 | bytes 3696256 | tf_op jit(solution)/shard_map/sub | solution.py:71
  8.3 1.5 %fusion.35 = f32[784,1024]{1,0:T(8,128)S(1)} fusion(f32[128,16]{1,0:T(8,128)S(1)} %bitcast.78, f32[128,256]{1,0:T(8,128)S(1)} %get-tuple-element.44, f32[128,256]{1,0:T(8,128)S(1)} %get-tuple-element.43, f32[128,256]{1,0:T(8,128)S(1)} %multiply_bitcast_fusion, f32[128,512]{1,0:T(8,128)S(1)} %get-tuple-element.26, f32[128,512]{1,0:T(8,128)S(1)} %get-tuple-element.25), kind=kOutput, calls=%fused_computation.53 | convolution fusion | flops 616994816 | bytes 4136960 | tf_op jit(solution)/shard_map/pr,pf->rf/dot_general | solution.py:105
  9.8 7.0 %collective-permute-done.1 = f32[128,272]{1,0:T(8,128)S(1)} collective-permute-done((f32[128,272]{1,0:T(8,128)S(1)}, f32[128,272]{1,0:T(8,128)S(1)}, u32[]{:S(2)}, u32[]{:S(2)}) %collective-permute-start.1) | collective-permute-done | bytes 139296 | tf_op jit(solution)/shard_map/ppermute | solution.py:100
  16.8 0.6 %fusion.16 = f32[272,1024]{1,0:T(8,128)S(1)} fusion(f32[128,272]{1,0:T(8,128)S(1)} %collective-permute-done.1, f32[128,512]{1,0:T(8,128)S(1)} %get-tuple-element.35, f32[128,512]{1,0:T(8,128)S(1)} %get-tuple-element.36), kind=kOutput, calls=%fused_computation.23 | convolution fusion | flops 214040576 | bytes 1777664 | tf_op jit(solution)/shard_map/pr,pf->rf/dot_general | solution.py:102
  17.5 0.0 collective-permute-done.2
  17.5 0.7 %fusion.20 = f32[272,1024]{1,0:T(8,128)S(1)} fusion(f32[128,272]{1,0:T(8,128)S(1)} %collective-permute-done.2, f32[128,512]{1,0:T(8,128)S(1)} %get-tuple-element.24, f32[128,512]{1,0:T(8,128)S(1)} %get-tuple-element.23), kind=kOutput, calls=%fused_computation.27 | convolution fusion | flops 214040576 | bytes 1777664 | tf_op jit(solution)/shard_map/pr,pf->rf/dot_general | solution.py:102
  18.1 1.8 %collective-permute-done = f32[128,272]{1,0:T(8,128)S(1)} collective-permute-done((f32[128,272]{1,0:T(8,128)S(1)}, f32[128,272]{1,0:T(8,128)S(1)}, u32[]{:S(2)}, u32[]{:S(2)}) %collective-permute-start) | collective-permute-done | bytes 139296 | tf_op jit(solution)/shard_map/ppermute | solution.py:100
  20.0 0.7 %fusion.8 = f32[272,1024]{1,0:T(8,128)S(1)} fusion(f32[272,1024]{1,0:T(8,128)S(1)} %fusion.20, f32[272,1024]{1,0:T(8,128)S(1)} %fusion.16, f32[128,272]{1,0:T(8,128)S(1)} %collective-permute-done, f32[128,512]{1,0:T(8,128)S(1)} %get-tuple-element.33, f32[128,512]{1,0:T(8,128)S(1)} %get-tuple-element.34), kind=kOutput, calls=%fused_computation.9 | convolution fusion | flops 214597632 | bytes 4005888 | tf_op jit(solution)/shard_map/pr,pf->rf/dot_general | solution.py:102
  20.7 0.4 slice_add_fusion.1
  21.1 0.1 broadcast_in_dim.26
  21.2 0.4 %multiply_subtract_fusion = (f32[256,512]{1,0:T(8,128)S(1)}, f32[256,512]{1,0:T(8,128)S(1)}, f32[256,512]{1,0:T(8,128)S(1)}, f32[256,512]{1,0:T(8,128)S(1)}) fusion(f32[784,1024]{1,0:T(8,128)S(1)} %fusion.35, f32[256,1024]{1,0:T(8,128)S(1)} %get-tuple-element.4, pred[512]{0:T(512)(128)(4,1)S(1)} %iota_compare_fusion.2, f32[256,1024]{1,0:T(8,128)S(1)} %bitcast.75), kind=kLoop, calls=%fused_computation.44 | loop fusion | flops 2621440 | bytes 5243392 | tf_op jit(solution)/shard_map/sub | solution.py:85
  21.7 0.2 bitcast_reduce_fusion
  21.9 0.3 fusion.24
  22.2 4.3 %collective-permute-start.5 = (f32[16,128]{1,0:T(8,128)S(1)}, f32[16,128]{1,0:T(8,128)S(1)}, u32[]{:S(2)}, u32[]{:S(2)}) collective-permute-start(f32[16,128]{1,0:T(8,128)S(1)} %fusion.24), channel_id=1, source_target_pairs={{0,8},{8,16},{16,24},{24,0},{1,9},{9,17},{17,25},{25,1},{2,10},{10... | collective-permute-start | bytes 24584 | tf_op jit(solution)/shard_map/ppermute | solution.py:124
  26.5 0.3 fusion.27
  26.8 1.4 %collective-permute-start.6 = (f32[16,128]{1,0:T(8,128)S(1)}, f32[16,128]{1,0:T(8,128)S(1)}, u32[]{:S(2)}, u32[]{:S(2)}) collective-permute-start(f32[16,128]{1,0:T(8,128)S(1)} %fusion.27), channel_id=1, source_target_pairs={{0,16},{8,24},{16,0},{24,8},{1,17},{9,25},{17,1},{25,9},{2,18},{10... | collective-permute-start | bytes 24584 | tf_op jit(solution)/shard_map/ppermute | solution.py:124
  28.2 0.2 select_subtract_fusion
  28.5 0.0 copy-start.2
  28.5 1.2 %fusion = f32[128,512]{1,0:T(8,128)S(1)} fusion(f32[256,512]{1,0:T(8,128)S(1)} %get-tuple-element.11, f32[256,512]{1,0:T(8,128)S(1)} %get-tuple-element.12, f32[256,512]{1,0:T(8,128)S(1)} %get-tuple-element.8, f32[256,512]{1,0:T(8,128)S(1)} %get-tuple-element.7, f32[128,512]{1,0:T(8,128)S(1)} %get-tuple-element.26, f32[128,512]{1,0:T(8,128)S(1)} %get-tuple-element.25, ...), kind=kOutput, calls=%fused_computation | convolution fusion | flops 404488192 | bytes 2887680 | tf_op jit(solution)/shard_map/tf,rf->tr/dot_general | solution.py:118
  29.7 0.0 copy-done.2
  29.7 0.1 fusion.56
  29.8 2.7 %collective-permute-start.4 = (bf16[1,128,3,256]{3,1,2,0:T(8,128)(2,1)S(1)}, bf16[1,128,3,256]{3,1,2,0:T(8,128)(2,1)S(1)}, u32[]{:S(2)}, u32[]{:S(2)}) collective-permute-start(bf16[1,128,3,256]{3,1,2,0:T(8,128)(2,1)S(1)} %pad_maximum_fusion.8), channel_id=1, source_target_pairs={{1,0},{2,1},{3,2},{4,3},{5,4},{6,5},{7,6},{9,8},{10,9},{11,10},{12... | collective-permute-start | bytes 589832 | tf_op jit(solution)/shard_map/ppermute | solution.py:22
  32.5 0.3 fusion.30
  32.8 2.7 %collective-permute-start.7 = (f32[16,128]{1,0:T(8,128)S(1)}, f32[16,128]{1,0:T(8,128)S(1)}, u32[]{:S(2)}, u32[]{:S(2)}) collective-permute-start(f32[16,128]{1,0:T(8,128)S(1)} %fusion.30), channel_id=1, source_target_pairs={{0,24},{8,0},{16,8},{24,16},{1,25},{9,1},{17,9},{25,17},{2,26},{10... | collective-permute-start | bytes 24584 | tf_op jit(solution)/shard_map/ppermute | solution.py:124
  35.5 1.9 %collective-permute-start.3 = (bf16[1,128,256]{2,1,0:T(8,128)(2,1)S(1)}, bf16[1,128,256]{2,1,0:T(8,128)(2,1)S(1)}, u32[]{:S(2)}, u32[]{:S(2)}) collective-permute-start(bf16[1,128,256]{2,1,0:T(8,128)(2,1)S(1)} %get-tuple-element.42), channel_id=1, source_target_pairs={{0,1},{1,2},{2,3},{3,4},{4,5},{5,6},{6,7},{8,9},{9,10},{10,11},{11... | collective-permute-start | bytes 196616 | tf_op jit(solution)/shard_map/ppermute | solution.py:22
  37.4 0.0 collective-permute-done.5
  37.4 0.0 collective-permute-done.6
  37.4 0.0 collective-permute-done.7
  37.4 0.9 %fusion.12 = f32[1,16,128]{2,1,0:T(8,128)} fusion(f32[16,128]{1,0:T(8,128)S(1)} %collective-permute-done.7, f32[16,128]{1,0:T(8,128)S(1)} %collective-permute-done.6, f32[16,128]{1,0:T(8,128)S(1)} %collective-permute-done.5, f32[16,1024]{1,0:T(8,128)S(1)} %bitcast_reduce_fusion, f32[128,512]{1,0:T(8,128)S(1)} %get-tuple-element.26, ...), kind=kOutput, calls=%fused_computation.14 | convolution fusion | flops 12853248 | bytes 626688 | tf_op jit(solution)/shard_map/rf,tf->rt/dot_general | solution.py:119
  38.4 3.6 %collective-permute-done.3 = bf16[1,128,256]{2,1,0:T(8,128)(2,1)S(1)} collective-permute-done((bf16[1,128,256]{2,1,0:T(8,128)(2,1)S(1)}, bf16[1,128,256]{2,1,0:T(8,128)(2,1)S(1)}, u32[]{:S(2)}, u32[]{:S(2)}) %collective-permute-start.3) | collective-permute-done | bytes 65568 | tf_op jit(solution)/shard_map/ppermute | solution.py:22
  42.0 0.0 collective-permute-done.4
  42.0 0.6 %copy.15 = bf16[1,128,256]{2,1,0:T(8,128)(2,1)} copy(bf16[1,128,256]{2,1,0:T(8,128)(2,1)S(1)} %collective-permute-done.3) | data formatting | bytes 131072
  42.6 0.7 %copy.16 = bf16[1,128,3,256]{3,1,2,0:T(8,128)(2,1)} copy(bf16[1,128,3,256]{3,1,2,0:T(8,128)(2,1)S(1)} %collective-permute-done.4) | data formatting | bytes 393216
  (10 shorter events, 0.2 us)
Async XLA Ops:
  0.6 6.9 %copy-start.6 = (f32[4,512]{1,0:T(4,128)S(1)}, f32[4,512]{1,0:T(4,128)}, u32[]{:S(2)}) copy-start(f32[4,512]{1,0:T(4,128)} %constant.139.clone) | copy-start | bytes 24580
  0.6 6.9 %copy-start.7 = (f32[4,512]{1,0:T(4,128)S(1)}, f32[4,512]{1,0:T(4,128)}, u32[]{:S(2)}) copy-start(f32[4,512]{1,0:T(4,128)} %constant.140.clone) | copy-start | bytes 24580
  0.7 7.0 %copy-start = (f32[128,512]{1,0:T(8,128)S(1)}, f32[128,512]{1,0:T(8,128)}, u32[]{:S(2)}) copy-start(f32[128,512]{1,0:T(8,128)} %constant.137.clone) | copy-start | bytes 786436
  0.7 7.0 %copy-start.1 = (f32[128,512]{1,0:T(8,128)S(1)}, f32[128,512]{1,0:T(8,128)}, u32[]{:S(2)}) copy-start(f32[128,512]{1,0:T(8,128)} %constant.138.clone) | copy-start | bytes 786436
  0.7 6.8 %copy-start.4 = (bf16[1,128,256]{2,1,0:T(8,128)(2,1)S(1)}, bf16[1,128,256]{2,1,0:T(8,128)(2,1)}, u32[]{:S(2)}) copy-start(bf16[1,128,256]{2,1,0:T(8,128)(2,1)} %param.12) | copy-start | bytes 196612
  0.7 6.8 %copy-start.3 = (bf16[1,128,3,256]{3,1,2,0:T(8,128)(2,1)S(1)}, bf16[1,128,3,256]{3,1,2,0:T(8,128)(2,1)}, u32[]{:S(2)}) copy-start(bf16[1,128,3,256]{3,1,2,0:T(8,128)(2,1)} %param.9) | copy-start | bytes 589828
  0.7 6.8 %copy-start.5 = (f32[1,128,256]{2,1,0:T(8,128)S(1)}, f32[1,128,256]{2,1,0:T(8,128)}, u32[]{:S(2)}) copy-start(f32[1,128,256]{2,1,0:T(8,128)} %param.11) | copy-start | bytes 393220
  2.8 14.1 %collective-permute-start.1 = (f32[128,272]{1,0:T(8,128)S(1)}, f32[128,272]{1,0:T(8,128)S(1)}, u32[]{:S(2)}, u32[]{:S(2)}) collective-permute-start(f32[128,272]{1,0:T(8,128)S(1)} %get-tuple-element.46), channel_id=1, source_target_pairs={{0,16},{8,24},{16,0},{24,8},{1,17},{9,25},{17,1},{25,9},{2,18},{10... | collective-permute-start | bytes 417800 | tf_op jit(solution)/shard_map/ppermute | solution.py:100
  5.4 12.1 %collective-permute-start.2 = (f32[128,272]{1,0:T(8,128)S(1)}, f32[128,272]{1,0:T(8,128)S(1)}, u32[]{:S(2)}, u32[]{:S(2)}) collective-permute-start(f32[128,272]{1,0:T(8,128)S(1)} %get-tuple-element.47), channel_id=1, source_target_pairs={{0,24},{8,0},{16,8},{24,16},{1,25},{9,1},{17,9},{25,17},{2,26},{10... | collective-permute-start | bytes 417800 | tf_op jit(solution)/shard_map/ppermute | solution.py:100
  6.8 13.2 %collective-permute-start = (f32[128,272]{1,0:T(8,128)S(1)}, f32[128,272]{1,0:T(8,128)S(1)}, u32[]{:S(2)}, u32[]{:S(2)}) collective-permute-start(f32[128,272]{1,0:T(8,128)S(1)} %get-tuple-element.45), channel_id=1, source_target_pairs={{0,8},{8,16},{16,24},{24,0},{1,9},{9,17},{17,25},{25,1},{2,10},{10... | collective-permute-start | bytes 417800 | tf_op jit(solution)/shard_map/ppermute | solution.py:100
  22.2 15.2 %collective-permute-start.5 = (f32[16,128]{1,0:T(8,128)S(1)}, f32[16,128]{1,0:T(8,128)S(1)}, u32[]{:S(2)}, u32[]{:S(2)}) collective-permute-start(f32[16,128]{1,0:T(8,128)S(1)} %fusion.24), channel_id=1, source_target_pairs={{0,8},{8,16},{16,24},{24,0},{1,9},{9,17},{17,25},{25,1},{2,10},{10... | collective-permute-start | bytes 24584 | tf_op jit(solution)/shard_map/ppermute | solution.py:124
  26.8 10.6 %collective-permute-start.6 = (f32[16,128]{1,0:T(8,128)S(1)}, f32[16,128]{1,0:T(8,128)S(1)}, u32[]{:S(2)}, u32[]{:S(2)}) collective-permute-start(f32[16,128]{1,0:T(8,128)S(1)} %fusion.27), channel_id=1, source_target_pairs={{0,16},{8,24},{16,0},{24,8},{1,17},{9,25},{17,1},{25,9},{2,18},{10... | collective-permute-start | bytes 24584 | tf_op jit(solution)/shard_map/ppermute | solution.py:124
  28.5 1.2 %copy-start.2 = (bf16[1,128,3,256]{3,1,2,0:T(8,128)(2,1)S(1)}, bf16[1,128,3,256]{3,1,2,0:T(8,128)(2,1)}, u32[]{:S(2)}) copy-start(bf16[1,128,3,256]{3,1,2,0:T(8,128)(2,1)} %param.10) | copy-start | bytes 589828
  29.8 12.1 %collective-permute-start.4 = (bf16[1,128,3,256]{3,1,2,0:T(8,128)(2,1)S(1)}, bf16[1,128,3,256]{3,1,2,0:T(8,128)(2,1)S(1)}, u32[]{:S(2)}, u32[]{:S(2)}) collective-permute-start(bf16[1,128,3,256]{3,1,2,0:T(8,128)(2,1)S(1)} %pad_maximum_fusion.8), channel_id=1, source_target_pairs={{1,0},{2,1},{3,2},{4,3},{5,4},{6,5},{7,6},{9,8},{10,9},{11,10},{12... | collective-permute-start | bytes 589832 | tf_op jit(solution)/shard_map/ppermute | solution.py:22
  32.8 4.6 %collective-permute-start.7 = (f32[16,128]{1,0:T(8,128)S(1)}, f32[16,128]{1,0:T(8,128)S(1)}, u32[]{:S(2)}, u32[]{:S(2)}) collective-permute-start(f32[16,128]{1,0:T(8,128)S(1)} %fusion.30), channel_id=1, source_target_pairs={{0,24},{8,0},{16,8},{24,16},{1,25},{9,1},{17,9},{25,17},{2,26},{10... | collective-permute-start | bytes 24584 | tf_op jit(solution)/shard_map/ppermute | solution.py:124
  35.5 6.5 %collective-permute-start.3 = (bf16[1,128,256]{2,1,0:T(8,128)(2,1)S(1)}, bf16[1,128,256]{2,1,0:T(8,128)(2,1)S(1)}, u32[]{:S(2)}, u32[]{:S(2)}) collective-permute-start(bf16[1,128,256]{2,1,0:T(8,128)(2,1)S(1)} %get-tuple-element.42), channel_id=1, source_target_pairs={{0,1},{1,2},{2,3},{3,4},{4,5},{5,6},{6,7},{8,9},{9,10},{10,11},{11... | collective-permute-start | bytes 196616 | tf_op jit(solution)/shard_map/ppermute | solution.py:22

commit v11 on v10

--- a/solution.py
+++ b/solution.py
@@ -95,14 +95,27 @@
     acc = 0.0
     for s in range(1, blocks):
         first = jnp.where(place + s < blocks, mixed, weighted)
-        payload = jnp.concatenate([first, taps], axis=1)
+        payload = jnp.concatenate([first, taps.reshape(-1, channels)], axis=0)
         pairs = [(i, (i + s) % blocks) for i in range(blocks)]
         got = lax.ppermute(payload, "ctx", pairs)
         table = block_table(packed, (place - s) % blocks)
-        acc = acc + jnp.einsum("pr,pf->rf", got, table, precision=precise)
+        got_taps = got[block:].reshape(taps.shape)
+        acc = acc + jnp.concatenate(
+            [
+                jnp.einsum("pr,pf->rf", got[:block], table, precision=precise),
+                jnp.dot(got_taps, table, precision=precise),
+            ],
+            axis=0,
+        )
     own_table = block_table(packed, place)
-    own = jnp.concatenate([mixed, weighted, back, taps], axis=1)
-    loc = jnp.einsum("pr,pf->rf", own, own_table, precision=precise)
+    own = jnp.concatenate([mixed, weighted, back], axis=1)
+    loc = jnp.concatenate(
+        [
+            jnp.einsum("pr,pf->rf", own, own_table, precision=precise),
+            jnp.dot(taps, own_table, precision=precise),
+        ],
+        axis=0,
+    )
     c = channels
     mixed_spec = loc[:c] + acc[:c]
     weighted_spec = loc[c : 2 * c] + acc[:c]
@@ -190,7 +203,7 @@
 
     if blocks <= DENSE:
         conv, grad_mixed, lag = dense_path(
-            place, blocks, mixed_in, weighted, mixed_back, taps.T
+            place, blocks, mixed_in, weighted, mixed_back, taps
         )
         return finish(
             conv, grad_mixed, lag, filter_scale, query_in, grad_query, key_back, value_back

time: 43.5 us -> 49.7 us (1.14)
  waiting for transfers between devices: 12.4 us -> 4.84 us
  matrix products: 6.62 us -> 13.6 us
  other arithmetic: 3.18 us -> 8.85 us
  local copies, waits for them, and re-layouts: 2.42 us -> 5.59 us
  starting transfers between devices: 17.6 us -> 15.3 us
    ppermute x3, waiting for transfers between devices: 8.82 us -> 1.25 us  [dense_path(): got = lax.ppermute(payload, 'ctx', pairs)]
    dot_general x4 -> x8, matrix products: 3.5 us -> 10.5 us  [the longest x3 4.83 us: dense_path(): jnp.einsum('pr,pf->rf', got[:block], table, precision=precise)]
    ppermute x3, starting transfers between devices: 8.37 us -> 5.93 us  [dense_path(): lag = lag + lax.ppermute(share, 'ctx', pairs)]
    slice x0 -> x3, local copies, waits for them, and re-layouts: none -> 2.1 us  [dense_path(): got_taps = got[block:].reshape(taps.shape)]
    sub x2, other arithmetic: 0.65 us -> 2.59 us  [block_table(): cos = base_c * c - base_s * s]
    another operation x3, other arithmetic: 0.09 us -> 1.56 us  [finish(): jnp.stack([grad_query, grad_key, grad_value], axis=1).astype(jnp.bfloat16)]
    ppermute x3, waiting for transfers between devices: 0.01 us -> 0.92 us  [dense_path(): lag = lag + lax.ppermute(share, 'ctx', pairs)]
    ppermute x2, waiting for transfers between devices: 3.58 us -> 2.68 us  [from_behind(): return lax.ppermute(x, axis, pairs)]
  transfers between devices with their start and end apart: 8 -> 8, of which waited for: 3 -> 3; matrix products, arithmetic and copies ran while one was open for 15% -> 22% of each run, Pallas kernels for 0% -> 0%
where the time goes in v11:
time: 49.7 us; the launch traced here: 49.2 us
  starting transfers between devices  15.3 us (31%)
  matrix products  13.6 us (27%)
  other arithmetic  8.85 us (18%)
  local copies, waits for them, and re-layouts  5.59 us (11%)
  waiting for transfers between devices  4.84 us (10%)
  between operations  1.06 us (2%)
    ppermute x3, starting transfers between devices, dense_path(): lag = lag + lax.ppermute(share, 'ctx', pairs)  5.93 us
    ppermute x3, starting transfers between devices, dense_path(): got = lax.ppermute(payload, 'ctx', pairs)  5.51 us
    dot_general x3, matrix products, dense_path(): jnp.einsum('pr,pf->rf', got[:block], table, precision=precise)  4.83 us
    dot_general x3, matrix products, dense_path(): jnp.dot(got_taps, table, precision=precise)  3.93 us
    ppermute x2, starting transfers between devices, from_behind(): return lax.ppermute(x, axis, pairs)  3.83 us
    ppermute x2, waiting for transfers between devices, from_behind(): return lax.ppermute(x, axis, pairs)  2.68 us
    sub x2, other arithmetic, block_table(): cos = base_c * c - base_s * s  2.59 us
    unnamed x50, local copies, waits for them, and re-layouts  2.51 us
  transfers between devices with their start and end apart: 8, of which 3 were waited for; matrix products, arithmetic and copies ran while one was open for 22% of the time, Pallas kernels for 0%

profile of v11, /device:TPU:4, one launch (start us, length us, event | category | flops | bytes accessed | tf_op | source)
XLA Modules:
  0.0 49.2 jit_solution(12328049230449089488)
XLA Ops:
  0.6 0.0 copy-start.22
  0.6 0.0 copy-start.23
  0.7 0.0 copy-start.12
  0.7 0.0 copy-start.13
  0.7 0.0 copy-start.18
  0.7 0.0 copy-start.15
  0.7 0.0 copy-start.20
  0.7 0.8 %reshape_squeeze.2 = f32[8,256]{1,0:T(8,128)S(1)} reshape(f32[1,16,128]{2,1,0:T(8,128)} %param.13) | data formatting | bytes 16384 | tf_op jit(solution)/shard_map/reshape;squeeze | solution.py:98
  1.6 1.7 %broadcast_select_fusion.2 = (f32[128,256]{1,0:T(8,128)S(1)}, f32[128,256]{1,0:T(8,128)S(1)}, f32[128,256]{1,0:T(8,128)S(1)}, f32[128,256]{1,0:T(8,128)S(1)}, f32[128,256]{1,0:T(8,128)}) fusion(pred[]{:T(512)S(6)} %lt.96, bf16[1,128,3,256]{3,1,2,0:T(8,128)(2,1)} %param.10, bf16[1,128,256]{2,1,0:T(8,128)(2,1)} %param.12, bf16[1,128,3,256]{3,1,2,0:T(8,128)(2,1)} %param.9, ...), kind=kLoop, calls=%fused_computation.110 | loop fusion | flops 393216 | bytes 1048579 | tf_op jit(solution)/shard_map/jit(_where)/select_n | solution.py:97
  3.3 0.8 %pad_maximum_fusion.16 = (f32[136,256]{1,0:T(8,128)}, f32[136,256]{1,0:T(8,128)}, f32[136,256]{1,0:T(8,128)}) fusion(f32[8,256]{1,0:T(8,128)S(1)} %reshape_squeeze.2, f32[128,256]{1,0:T(8,128)S(1)} %get-tuple-element.39, f32[128,256]{1,0:T(8,128)S(1)} %get-tuple-element.40, f32[128,256]{1,0:T(8,128)S(1)} %get-tuple-element.41), kind=kLoop, calls=%fused_computation.84 | loop fusion | flops 104448 | bytes 819200 | tf_op jit(solution)/shard_map/concatenate | solution.py:98
  4.0 1.6 %collective-permute-start = (f32[136,256]{1,0:T(8,128)}, f32[136,256]{1,0:T(8,128)}, u32[]{:S(2)}, u32[]{:S(2)}) collective-permute-start(f32[136,256]{1,0:T(8,128)} %get-tuple-element.59), channel_id=1, source_target_pairs={{0,8},{8,16},{16,24},{24,0},{1,9},{9,17},{17,25},{25,1},{2,10},{10... | collective-permute-start | bytes 417800 | tf_op jit(solution)/shard_map/ppermute | solution.py:100
  5.6 2.6 %collective-permute-start.1 = (f32[136,256]{1,0:T(8,128)}, f32[136,256]{1,0:T(8,128)}, u32[]{:S(2)}, u32[]{:S(2)}) collective-permute-start(f32[136,256]{1,0:T(8,128)} %get-tuple-element.60), channel_id=1, source_target_pairs={{0,16},{8,24},{16,0},{24,8},{1,17},{9,25},{17,1},{25,9},{2,18},{10... | collective-permute-start | bytes 417800 | tf_op jit(solution)/shard_map/ppermute | solution.py:100
  8.2 1.3 %collective-permute-start.2 = (f32[136,256]{1,0:T(8,128)}, f32[136,256]{1,0:T(8,128)}, u32[]{:S(2)}, u32[]{:S(2)}) collective-permute-start(f32[136,256]{1,0:T(8,128)} %get-tuple-element.61), channel_id=1, source_target_pairs={{0,24},{8,0},{16,8},{24,16},{1,25},{9,1},{17,9},{25,17},{2,26},{10... | collective-permute-start | bytes 417800 | tf_op jit(solution)/shard_map/ppermute | solution.py:100
  9.6 0.0 copy-done.15
  9.6 0.7 %multiply_bitcast_fusion = f32[128,256]{1,0:T(8,128)} fusion(bf16[1,128,3,256]{3,1,2,0:T(8,128)(2,1)S(1)} %copy-done.15), kind=kLoop, calls=%fused_computation.102 | loop fusion | flops 98304 | bytes 262144 | tf_op jit(solution)/shard_map/mul | solution.py:194
  10.2 0.0 copy-done.20
  10.2 0.6 %fusion.54 = bf16[1,128,1,256]{3,1,2,0:T(8,128)(2,1)} fusion(f32[1,128,256]{2,1,0:T(8,128)S(1)} %copy-done.20, bf16[1,128,256]{2,1,0:T(8,128)(2,1)S(1)} %copy-done.18), kind=kLoop, calls=%fused_computation.106 | loop fusion | flops 98304 | bytes 262144 | tf_op jit(solution)/shard_map/stack | solution.py:176
  11.0 0.9 %multiply_subtract_fusion.5 = (f32[128,512]{1,0:T(8,128)}, f32[128,512]{1,0:T(8,128)}) fusion(f32[128,512]{1,0:T(8,128)S(1)} %copy-done.13, f32[128,512]{1,0:T(8,128)S(1)} %copy-done.12, f32[512]{0:T(512)S(1)} %bitcast.95, f32[512]{0:T(512)S(1)} %bitcast.96, s32[128]{0:T(128)S(1)} %get-tuple-element.69, s32[128]{0:T(128)S(1)} %get-tuple-element.70, ...), kind=kLoop, calls=%fused_computation.69 | loop fusion | flops 786432 | bytes 1054336 | tf_op jit(solution)/shard_map/sub | solution.py:71
  11.8 1.7 %multiply_subtract_fusion.9 = (f32[128,512]{1,0:T(8,128)S(1)}, f32[128,512]{1,0:T(8,128)S(1)}, f32[128,512]{1,0:T(8,128)}, f32[128,512]{1,0:T(8,128)}, f32[128,5...) fusion(f32[128,512]{1,0:T(8,128)S(1)} %copy-done.13, ...), kind=kLoop, calls=%fused_computation.81 | loop fusion | flops 3407872 | bytes 3696256 | tf_op jit(solution)/shard_map/sub | solution.py:71
  13.5 0.7 %copy-done = f32[128,512]{1,0:T(8,128)} copy-done((f32[128,512]{1,0:T(8,128)}, f32[128,512]{1,0:T(8,128)S(1)}, u32[]{:S(2)}) %copy-start) | copy-done | bytes 262168
  14.2 1.4 %fusion.31 = f32[768,1024]{1,0:T(8,128)S(1)} fusion(f32[128,256]{1,0:T(8,128)S(1)} %copy-done.16, f32[128,256]{1,0:T(8,128)S(1)} %get-tuple-element.43, f32[128,256]{1,0:T(8,128)S(1)} %copy-done.17, f32[128,512]{1,0:T(8,128)S(1)} %get-tuple-element.26, f32[128,512]{1,0:T(8,128)S(1)} %get-tuple-element.25), kind=kOutput, calls=%fused_computation.56 | convolution fusion | flops 604307456 | bytes 4063232 | tf_op jit(solution)/shard_map/pr,pf->rf/dot_general | solution.py:114
  15.7 0.0 collective-permute-done
  15.7 0.7 %slice.113 = f32[8,256]{1,0:T(8,128)S(1)} slice(f32[136,256]{1,0:T(8,128)} %collective-permute-done), slice={[128:136], [0:256]} | slice | bytes 16384 | tf_op jit(solution)/shard_map/slice | solution.py:102
  16.4 1.2 %collective-permute-done.1 = f32[136,256]{1,0:T(8,128)} collective-permute-done((f32[136,256]{1,0:T(8,128)}, f32[136,256]{1,0:T(8,128)}, u32[]{:S(2)}, u32[]{:S(2)}) %collective-permute-start.1) | collective-permute-done | bytes 139296 | tf_op jit(solution)/shard_map/ppermute | solution.py:100
  17.7 0.7 %slice.115 = f32[8,256]{1,0:T(8,128)S(1)} slice(f32[136,256]{1,0:T(8,128)} %collective-permute-done.1), slice={[128:136], [0:256]} | slice | bytes 16384 | tf_op jit(solution)/shard_map/slice | solution.py:102
  18.4 0.0 collective-permute-done.2
  18.4 0.7 %slice.117 = f32[8,256]{1,0:T(8,128)S(1)} slice(f32[136,256]{1,0:T(8,128)} %collective-permute-done.2), slice={[128:136], [0:256]} | slice | bytes 16384 | tf_op jit(solution)/shard_map/slice | solution.py:102
  19.1 1.3 %fusion.29 = f32[16,1024]{1,0:T(8,128)S(1)} fusion(f32[16,128]{1,0:T(8,128)S(1)} %reshape.123, f32[128,512]{1,0:T(8,128)} %get-tuple-element.33, f32[128,512]{1,0:T(8,128)} %get-tuple-element.34), kind=kOutput, calls=%fused_computation.53 | convolution fusion | flops 12713984 | bytes 598016 | tf_op jit(solution)/shard_map/dot_general | solution.py:106
  20.4 1.3 %fusion.27 = f32[16,1024]{1,0:T(8,128)S(1)} fusion(f32[16,128]{1,0:T(8,128)S(1)} %reshape.124, f32[128,512]{1,0:T(8,128)} %get-tuple-element.35, f32[128,512]{1,0:T(8,128)} %get-tuple-element.36), kind=kOutput, calls=%fused_computation.51 | convolution fusion | flops 12713984 | bytes 598016 | tf_op jit(solution)/shard_map/dot_general | solution.py:106
  21.7 1.3 %fusion.25 = f32[16,1024]{1,0:T(8,128)S(1)} fusion(f32[16,128]{1,0:T(8,128)S(1)} %reshape.125, f32[128,512]{1,0:T(8,128)} %get-tuple-element.24, f32[128,512]{1,0:T(8,128)} %get-tuple-element.23), kind=kOutput, calls=%fused_computation.49 | convolution fusion | flops 12713984 | bytes 598016 | tf_op jit(solution)/shard_map/dot_general | solution.py:106
  23.0 1.7 %fusion.30 = f32[256,1024]{1,0:T(8,128)S(1)} fusion(f32[128,512]{1,0:T(8,128)} %get-tuple-element.33, f32[128,512]{1,0:T(8,128)} %get-tuple-element.34, f32[136,256]{1,0:T(8,128)} %collective-permute-done), kind=kOutput, calls=%fused_computation.54 | convolution fusion | flops 201457664 | bytes 1703936 | tf_op jit(solution)/shard_map/pr,pf->rf/dot_general | solution.py:105
  24.8 0.0 copy-start.21
  24.8 1.6 %fusion.28 = f32[256,1024]{1,0:T(8,128)S(1)} fusion(f32[128,512]{1,0:T(8,128)S(1)} %copy-done.2, f32[128,512]{1,0:T(8,128)S(1)} %copy-done.3, f32[136,256]{1,0:T(8,128)} %collective-permute-done.1), kind=kOutput, calls=%fused_computation.52 | convolution fusion | flops 201457664 | bytes 1703936 | tf_op jit(solution)/shard_map/pr,pf->rf/dot_general | solution.py:105
  26.4 1.5 %fusion.26 = f32[256,1024]{1,0:T(8,128)S(1)} fusion(f32[128,512]{1,0:T(8,128)S(1)} %copy-done.5, f32[128,512]{1,0:T(8,128)S(1)} %copy-done.4, f32[136,256]{1,0:T(8,128)} %collective-permute-done.2), kind=kOutput, calls=%fused_computation.50 | convolution fusion | flops 201457664 | bytes 1703936 | tf_op jit(solution)/shard_map/pr,pf->rf/dot_general | solution.py:105
  28.0 0.2 add_add_fusion
  28.2 0.5 %slice_add_fusion.1 = (f32[256,1024]{1,0:T(8,128)S(1)}, f32[256,1024]{1,0:T(8,128)S(1)}) fusion(f32[768,1024]{1,0:T(8,128)S(1)} %fusion.31, f32[16,1024]{1,0:T(8,128)S(1)} %fusion.25, f32[256,1024]{1,0:T(8,128)S(1)} %fusion.26, f32[16,1024]{1,0:T(8,128)S(1)} %fusion.27, f32[256,1024]{1,0:T(8,128)S(1)} %fusion.28, f32[16,1024]{1,0:T(8,128)S(1)} %fusion.29, ...), kind=kLoop, calls=%fused_computation.20 | loop fusion | flops 1572864 | bytes 6488064 | tf_op jit(solution)/shard_map/add | solution.py:120
  28.8 0.2 slice_add_fusion
  28.9 0.1 broadcast_in_dim.26
  29.1 0.4 multiply_subtract_fusion
  29.5 0.2 bitcast_reduce_fusion
  29.7 0.3 copy-done.10
  30.0 0.1 copy-done.11
  30.1 0.3 fusion.14
  30.4 2.8 %collective-permute-start.5 = (f32[16,128]{1,0:T(8,128)S(1)}, f32[16,128]{1,0:T(8,128)S(1)}, u32[]{:S(2)}, u32[]{:S(2)}) collective-permute-start(f32[16,128]{1,0:T(8,128)S(1)} %fusion.14), channel_id=1, source_target_pairs={{0,8},{8,16},{16,24},{24,0},{1,9},{9,17},{17,25},{25,1},{2,10},{10... | collective-permute-start | bytes 24584 | tf_op jit(solution)/shard_map/ppermute | solution.py:137
  33.2 0.0 copy-done.9
  33.2 0.3 fusion.17
  33.5 2.3 %collective-permute-start.6 = (f32[16,128]{1,0:T(8,128)S(1)}, f32[16,128]{1,0:T(8,128)S(1)}, u32[]{:S(2)}, u32[]{:S(2)}) collective-permute-start(f32[16,128]{1,0:T(8,128)S(1)} %fusion.17), channel_id=1, source_target_pairs={{0,16},{8,24},{16,0},{24,8},{1,17},{9,25},{17,1},{25,9},{2,18},{10... | collective-permute-start | bytes 24584 | tf_op jit(solution)/shard_map/ppermute | solution.py:137
  35.8 0.2 select_subtract_fusion
  36.1 0.0 copy-start.14
  36.1 0.0 copy-start.19
  36.1 1.2 %fusion = f32[128,512]{1,0:T(8,128)S(1)} fusion(f32[256,512]{1,0:T(8,128)S(1)} %get-tuple-element.11, f32[256,512]{1,0:T(8,128)S(1)} %get-tuple-element.12, f32[256,512]{1,0:T(8,128)S(1)} %get-tuple-element.8, f32[256,512]{1,0:T(8,128)S(1)} %get-tuple-element.7, f32[1024]{0:T(1024)S(1)} %fusion.59, f32[128,512]{1,0:T(8,128)S(1)} %copy-done.1, ...), kind=kOutput, calls=%fused_computation | convolution fusion | flops 404488192 | bytes 2887680 | tf_op jit(solution)/shard_map/tf,rf->tr/dot_general | solution.py:131
  37.4 0.9 %fusion.53 = (bf16[1,128,1,256]{3,1,2,0:T(8,128)(2,1)S(1)}, bf16[1,128,1,256]{3,1,2,0:T(8,128)(2,1)S(1)}, bf16[1,128,256]{2,1,0:T(8,128)(2,1)S(1)}) fusion(f32[128,512]{1,0:T(8,128)S(1)} %fusion, bf16[1,128,3,256]{3,1,2,0:T(8,128)(2,1)S(1)} %copy-done.14, bf16[1,128,3,256]{3,1,2,0:T(8,128)(2,1)} %param.9), kind=kLoop, calls=%fused_computation.105 | loop fusion | flops 360448 | bytes 655360 | tf_op jit(solution)/shard_map/stack | solution.py:176
  38.3 1.9 %collective-permute-start.4 = (bf16[1,128,3,256]{3,1,2,0:T(8,128)(2,1)S(1)}, bf16[1,128,3,256]{3,1,2,0:T(8,128)(2,1)S(1)}, u32[]{:S(2)}, u32[]{:S(2)}) collective-permute-start(bf16[1,128,3,256]{3,1,2,0:T(8,128)(2,1)S(1)} %pad_maximum_fusion.21), channel_id=1, source_target_pairs={{1,0},{2,1},{3,2},{4,3},{5,4},{6,5},{7,6},{9,8},{10,9},{11,10},{12... | collective-permute-start | bytes 589832 | tf_op jit(solution)/shard_map/ppermute | solution.py:22
  40.3 0.3 fusion.20
  40.6 0.8 %collective-permute-start.7 = (f32[16,128]{1,0:T(8,128)S(1)}, f32[16,128]{1,0:T(8,128)S(1)}, u32[]{:S(2)}, u32[]{:S(2)}) collective-permute-start(f32[16,128]{1,0:T(8,128)S(1)} %fusion.20), channel_id=1, source_target_pairs={{0,24},{8,0},{16,8},{24,16},{1,25},{9,1},{17,9},{25,17},{2,26},{10... | collective-permute-start | bytes 24584 | tf_op jit(solution)/shard_map/ppermute | solution.py:137
  41.4 1.9 %collective-permute-start.3 = (bf16[1,128,256]{2,1,0:T(8,128)(2,1)S(1)}, bf16[1,128,256]{2,1,0:T(8,128)(2,1)S(1)}, u32[]{:S(2)}, u32[]{:S(2)}) collective-permute-start(bf16[1,128,256]{2,1,0:T(8,128)(2,1)S(1)} %get-tuple-element.42), channel_id=1, source_target_pairs={{0,1},{1,2},{2,3},{3,4},{4,5},{5,6},{6,7},{8,9},{9,10},{10,11},{11... | collective-permute-start | bytes 196616 | tf_op jit(solution)/shard_map/ppermute | solution.py:22
  43.3 0.0 collective-permute-done.5
  43.4 0.0 collective-permute-done.6
  43.4 0.9 %collective-permute-done.7 = f32[16,128]{1,0:T(8,128)S(1)} collective-permute-done((f32[16,128]{1,0:T(8,128)S(1)}, f32[16,128]{1,0:T(8,128)S(1)}, u32[]{:S(2)}, u32[]{:S(2)}) %collective-permute-start.7) | collective-permute-done | bytes 8224 | tf_op jit(solution)/shard_map/ppermute | solution.py:137
  44.3 0.9 %fusion.11 = f32[1,16,128]{2,1,0:T(8,128)} fusion(f32[16,128]{1,0:T(8,128)S(1)} %collective-permute-done.7, f32[16,128]{1,0:T(8,128)S(1)} %collective-permute-done.6, f32[16,128]{1,0:T(8,128)S(1)} %collective-permute-done.5, f32[16,1024]{1,0:T(8,128)S(1)} %bitcast_reduce_fusion, f32[1024]{0:T(1024)S(1)} %fusion.59, f32[128,512]{1,0:T(8,128)S(1)} %copy-done.1, ...), kind=kOutput, calls=%fused_computation.13 | convolution fusion | flops 12853248 | bytes 626688 | tf_op jit(solution)/shard_map/rf,tf->rt/dot_general | solution.py:132
  45.2 2.7 %collective-permute-done.3 = bf16[1,128,256]{2,1,0:T(8,128)(2,1)S(1)} collective-permute-done((bf16[1,128,256]{2,1,0:T(8,128)(2,1)S(1)}, bf16[1,128,256]{2,1,0:T(8,128)(2,1)S(1)}, u32[]{:S(2)}, u32[]{:S(2)}) %collective-permute-start.3) | collective-permute-done | bytes 65568 | tf_op jit(solution)/shard_map/ppermute | solution.py:22
  47.9 0.0 collective-permute-done.4
  47.9 0.6 %copy.14 = bf16[1,128,256]{2,1,0:T(8,128)(2,1)} copy(bf16[1,128,256]{2,1,0:T(8,128)(2,1)S(1)} %collective-permute-done.3) | data formatting | bytes 131072
  48.5 0.7 %copy.15 = bf16[1,128,3,256]{3,1,2,0:T(8,128)(2,1)} copy(bf16[1,128,3,256]{3,1,2,0:T(8,128)(2,1)S(1)} %collective-permute-done.4) | data formatting | bytes 393216
  (41 shorter events, 0.2 us)
Async XLA Ops:
  0.6 10.3 %copy-start.22 = (f32[4,512]{1,0:T(4,128)S(1)}, f32[4,512]{1,0:T(4,128)}, u32[]{:S(2)}) copy-start(f32[4,512]{1,0:T(4,128)} %constant.139.clone) | copy-start | bytes 24580
  0.6 10.3 %copy-start.23 = (f32[4,512]{1,0:T(4,128)S(1)}, f32[4,512]{1,0:T(4,128)}, u32[]{:S(2)}) copy-start(f32[4,512]{1,0:T(4,128)} %constant.140.clone) | copy-start | bytes 24580
  0.7 10.3 %copy-start.12 = (f32[128,512]{1,0:T(8,128)S(1)}, f32[128,512]{1,0:T(8,128)}, u32[]{:S(2)}) copy-start(f32[128,512]{1,0:T(8,128)} %constant.137.clone) | copy-start | bytes 786436
  0.7 10.3 %copy-start.13 = (f32[128,512]{1,0:T(8,128)S(1)}, f32[128,512]{1,0:T(8,128)}, u32[]{:S(2)}) copy-start(f32[128,512]{1,0:T(8,128)} %constant.138.clone) | copy-start | bytes 786436
  0.7 9.6 %copy-start.18 = (bf16[1,128,256]{2,1,0:T(8,128)(2,1)S(1)}, bf16[1,128,256]{2,1,0:T(8,128)(2,1)}, u32[]{:S(2)}) copy-start(bf16[1,128,256]{2,1,0:T(8,128)(2,1)} %param.12) | copy-start | bytes 196612
  0.7 8.9 %copy-start.15 = (bf16[1,128,3,256]{3,1,2,0:T(8,128)(2,1)S(1)}, bf16[1,128,3,256]{3,1,2,0:T(8,128)(2,1)}, u32[]{:S(2)}) copy-start(bf16[1,128,3,256]{3,1,2,0:T(8,128)(2,1)} %param.9) | copy-start | bytes 589828
  0.7 9.5 %copy-start.20 = (f32[1,128,256]{2,1,0:T(8,128)S(1)}, f32[1,128,256]{2,1,0:T(8,128)}, u32[]{:S(2)}) copy-start(f32[1,128,256]{2,1,0:T(8,128)} %param.11) | copy-start | bytes 393220
  4.0 11.7 %collective-permute-start = (f32[136,256]{1,0:T(8,128)}, f32[136,256]{1,0:T(8,128)}, u32[]{:S(2)}, u32[]{:S(2)}) collective-permute-start(f32[136,256]{1,0:T(8,128)} %get-tuple-element.59), channel_id=1, source_target_pairs={{0,8},{8,16},{16,24},{24,0},{1,9},{9,17},{17,25},{25,1},{2,10},{10... | collective-permute-start | bytes 417800 | tf_op jit(solution)/shard_map/ppermute | solution.py:100
  5.6 12.1 %collective-permute-start.1 = (f32[136,256]{1,0:T(8,128)}, f32[136,256]{1,0:T(8,128)}, u32[]{:S(2)}, u32[]{:S(2)}) collective-permute-start(f32[136,256]{1,0:T(8,128)} %get-tuple-element.60), channel_id=1, source_target_pairs={{0,16},{8,24},{16,0},{24,8},{1,17},{9,25},{17,1},{25,9},{2,18},{10... | collective-permute-start | bytes 417800 | tf_op jit(solution)/shard_map/ppermute | solution.py:100
  8.2 10.2 %collective-permute-start.2 = (f32[136,256]{1,0:T(8,128)}, f32[136,256]{1,0:T(8,128)}, u32[]{:S(2)}, u32[]{:S(2)}) collective-permute-start(f32[136,256]{1,0:T(8,128)} %get-tuple-element.61), channel_id=1, source_target_pairs={{0,24},{8,0},{16,8},{24,16},{1,25},{9,1},{17,9},{25,17},{2,26},{10... | collective-permute-start | bytes 417800 | tf_op jit(solution)/shard_map/ppermute | solution.py:100
  11.8 2.4 %copy-start.16 = (f32[128,256]{1,0:T(8,128)S(1)}, f32[128,256]{1,0:T(8,128)}, u32[]{:S(2)}) copy-start(f32[128,256]{1,0:T(8,128)} %get-tuple-element.44) | copy-start | bytes 393220
  11.8 2.4 %copy-start.17 = (f32[128,256]{1,0:T(8,128)S(1)}, f32[128,256]{1,0:T(8,128)}, u32[]{:S(2)}) copy-start(f32[128,256]{1,0:T(8,128)} %multiply_bitcast_fusion) | copy-start | bytes 393220
  13.5 0.7 %copy-start = (f32[128,512]{1,0:T(8,128)}, f32[128,512]{1,0:T(8,128)S(1)}, u32[]{:S(2)}) copy-start(f32[128,512]{1,0:T(8,128)S(1)} %get-tuple-element.26) | copy-start | bytes 786436
  19.1 5.7 %copy-start.2 = (f32[128,512]{1,0:T(8,128)S(1)}, f32[128,512]{1,0:T(8,128)}, u32[]{:S(2)}) copy-start(f32[128,512]{1,0:T(8,128)} %get-tuple-element.35) | copy-start | bytes 786436
  19.1 5.7 %copy-start.3 = (f32[128,512]{1,0:T(8,128)S(1)}, f32[128,512]{1,0:T(8,128)}, u32[]{:S(2)}) copy-start(f32[128,512]{1,0:T(8,128)} %get-tuple-element.36) | copy-start | bytes 786436
  21.7 4.7 %copy-start.4 = (f32[128,512]{1,0:T(8,128)S(1)}, f32[128,512]{1,0:T(8,128)}, u32[]{:S(2)}) copy-start(f32[128,512]{1,0:T(8,128)} %get-tuple-element.23) | copy-start | bytes 786436
  21.7 4.7 %copy-start.5 = (f32[128,512]{1,0:T(8,128)S(1)}, f32[128,512]{1,0:T(8,128)}, u32[]{:S(2)}) copy-start(f32[128,512]{1,0:T(8,128)} %get-tuple-element.24) | copy-start | bytes 786436
  24.8 3.2 %copy-start.1 = (f32[128,512]{1,0:T(8,128)S(1)}, f32[128,512]{1,0:T(8,128)}, u32[]{:S(2)}) copy-start(f32[128,512]{1,0:T(8,128)} %copy-done) | copy-start | bytes 786436
  24.8 3.2 %copy-start.21 = (f32[1,16,128]{2,1,0:T(8,128)S(1)}, f32[1,16,128]{2,1,0:T(8,128)}, u32[]{:S(2)}) copy-start(f32[1,16,128]{2,1,0:T(8,128)} %param.13) | copy-start | bytes 24580
  29.1 1.0 %copy-start.10 = (f32[128,512]{1,0:T(8,128)S(1)}, f32[128,512]{1,0:T(8,128)}, u32[]{:S(2)}) copy-start(f32[128,512]{1,0:T(8,128)} %get-tuple-element.27) | copy-start | bytes 786436
  29.1 1.0 %copy-start.11 = (f32[128,512]{1,0:T(8,128)S(1)}, f32[128,512]{1,0:T(8,128)}, u32[]{:S(2)}) copy-start(f32[128,512]{1,0:T(8,128)} %get-tuple-element.28) | copy-start | bytes 786436
  29.1 4.1 %copy-start.8 = (f32[128,512]{1,0:T(8,128)S(1)}, f32[128,512]{1,0:T(8,128)}, u32[]{:S(2)}) copy-start(f32[128,512]{1,0:T(8,128)} %get-tuple-element.29) | copy-start | bytes 786436
  29.1 4.1 %copy-start.9 = (f32[128,512]{1,0:T(8,128)S(1)}, f32[128,512]{1,0:T(8,128)}, u32[]{:S(2)}) copy-start(f32[128,512]{1,0:T(8,128)} %get-tuple-element.30) | copy-start | bytes 786436
  30.4 12.9 %collective-permute-start.5 = (f32[16,128]{1,0:T(8,128)S(1)}, f32[16,128]{1,0:T(8,128)S(1)}, u32[]{:S(2)}, u32[]{:S(2)}) collective-permute-start(f32[16,128]{1,0:T(8,128)S(1)} %fusion.14), channel_id=1, source_target_pairs={{0,8},{8,16},{16,24},{24,0},{1,9},{9,17},{17,25},{25,1},{2,10},{10... | collective-permute-start | bytes 24584 | tf_op jit(solution)/shard_map/ppermute | solution.py:137
  33.5 9.9 %collective-permute-start.6 = (f32[16,128]{1,0:T(8,128)S(1)}, f32[16,128]{1,0:T(8,128)S(1)}, u32[]{:S(2)}, u32[]{:S(2)}) collective-permute-start(f32[16,128]{1,0:T(8,128)S(1)} %fusion.17), channel_id=1, source_target_pairs={{0,16},{8,24},{16,0},{24,8},{1,17},{9,25},{17,1},{25,9},{2,18},{10... | collective-permute-start | bytes 24584 | tf_op jit(solution)/shard_map/ppermute | solution.py:137
  36.1 1.3 %copy-start.14 = (bf16[1,128,3,256]{3,1,2,0:T(8,128)(2,1)S(1)}, bf16[1,128,3,256]{3,1,2,0:T(8,128)(2,1)}, u32[]{:S(2)}) copy-start(bf16[1,128,3,256]{3,1,2,0:T(8,128)(2,1)} %param.10) | copy-start | bytes 589828
  36.1 2.2 %copy-start.19 = (bf16[1,128,1,256]{3,1,2,0:T(8,128)(2,1)S(1)}, bf16[1,128,1,256]{3,1,2,0:T(8,128)(2,1)}, u32[]{:S(2)}) copy-start(bf16[1,128,1,256]{3,1,2,0:T(8,128)(2,1)} %fusion.54) | copy-start | bytes 196612
  36.1 4.2 %copy-start.6 = (f32[128,512]{1,0:T(8,128)S(1)}, f32[128,512]{1,0:T(8,128)}, u32[]{:S(2)}) copy-start(f32[128,512]{1,0:T(8,128)} %get-tuple-element.31) | copy-start | bytes 786436
  36.1 4.2 %copy-start.7 = (f32[128,512]{1,0:T(8,128)S(1)}, f32[128,512]{1,0:T(8,128)}, u32[]{:S(2)}) copy-start(f32[128,512]{1,0:T(8,128)} %get-tuple-element.32) | copy-start | bytes 786436
  38.3 9.6 %collective-permute-start.4 = (bf16[1,128,3,256]{3,1,2,0:T(8,128)(2,1)S(1)}, bf16[1,128,3,256]{3,1,2,0:T(8,128)(2,1)S(1)}, u32[]{:S(2)}, u32[]{:S(2)}) collective-permute-start(bf16[1,128,3,256]{3,1,2,0:T(8,128)(2,1)S(1)} %pad_maximum_fusion.21), channel_id=1, source_target_pairs={{1,0},{2,1},{3,2},{4,3},{5,4},{6,5},{7,6},{9,8},{10,9},{11,10},{12... | collective-permute-start | bytes 589832 | tf_op jit(solution)/shard_map/ppermute | solution.py:22
  40.6 3.7 %collective-permute-start.7 = (f32[16,128]{1,0:T(8,128)S(1)}, f32[16,128]{1,0:T(8,128)S(1)}, u32[]{:S(2)}, u32[]{:S(2)}) collective-permute-start(f32[16,128]{1,0:T(8,128)S(1)} %fusion.20), channel_id=1, source_target_pairs={{0,24},{8,0},{16,8},{24,16},{1,25},{9,1},{17,9},{25,17},{2,26},{10... | collective-permute-start | bytes 24584 | tf_op jit(solution)/shard_map/ppermute | solution.py:137
  41.4 6.5 %collective-permute-start.3 = (bf16[1,128,256]{2,1,0:T(8,128)(2,1)S(1)}, bf16[1,128,256]{2,1,0:T(8,128)(2,1)S(1)}, u32[]{:S(2)}, u32[]{:S(2)}) collective-permute-start(bf16[1,128,256]{2,1,0:T(8,128)(2,1)S(1)} %get-tuple-element.42), channel_id=1, source_target_pairs={{0,1},{1,2},{2,3},{3,4},{4,5},{5,6},{6,7},{8,9},{9,10},{10,11},{11... | collective-permute-start | bytes 196616 | tf_op jit(solution)/shard_map/ppermute | solution.py:22

commit v12 on v5

--- a/solution.py
+++ b/solution.py
@@ -92,12 +92,19 @@
     size = 2 * blocks * block
     half = size // 2
     packed = packed_tables(blocks, block)
+    cols = lax.broadcasted_iota(jnp.int32, (1, size), 1)
+    weight = jnp.where((cols == 0) | (cols == half), 1.0 / size, 2.0 / size)
     acc = 0.0
+    share_tables = [None]
     for s in range(1, blocks):
         first = jnp.where(place + s < blocks, mixed_rows, weighted_rows)
         payload = jnp.concatenate([first, taps], axis=0)
         pairs = [(i, (i + s) % blocks) for i in range(blocks)]
         got = lax.ppermute(payload, "ctx", pairs)
+        got, share = lax.optimization_barrier(
+            (got, block_table(packed, (place + s) % blocks) * weight)
+        )
+        share_tables.append(share)
         table = block_table(packed, (place - s) % blocks)
         acc = acc + jnp.dot(got, table, precision=precise)
     own_table = block_table(packed, place)
@@ -112,14 +119,11 @@
     gm = packed_products(taps_spec, weighted_spec, True)
     fgs = packed_products(back_spec, weighted_spec, True)
     fgs = fgs.reshape(-1, CPF, size).sum(axis=1)
-    cols = lax.broadcasted_iota(jnp.int32, (1, size), 1)
-    weight = jnp.where((cols == 0) | (cols == half), 1.0 / size, 2.0 / size)
     both = jnp.concatenate([conv, gm], axis=0)
     out = jnp.einsum("tf,rf->tr", own_table * weight, both, precision=precise)
     lag = jnp.einsum("rf,tf->rt", fgs, own_table * weight, precision=precise)
     for s in range(1, blocks):
-        table = block_table(packed, (place + s) % blocks) * weight
-        share = jnp.einsum("rf,tf->rt", fgs, table, precision=precise)
+        share = jnp.einsum("rf,tf->rt", fgs, share_tables[s], precision=precise)
         pairs = [(i, (i + s) % blocks) for i in range(blocks)]
         lag = lag + lax.ppermute(share, "ctx", pairs)
     return out[:, :c], out[:, c:], lag

time: 43.4 us -> 44.8 us (1.032)
  starting transfers between devices: 17.6 us -> 19 us
  other arithmetic: 3.98 us -> 4.79 us
  matrix products: 6.62 us -> 5.98 us
    ppermute x3, starting transfers between devices: 4.68 us -> 6.48 us  [dense_path(): got = lax.ppermute(payload, 'ctx', pairs)]
    dot_general x1, matrix products: 0.94 us -> 0.32 us  [dense_path(): lag = jnp.einsum('rf,tf->rt', fgs, own_table * weight, precision=precise)]
    broadcast_in_dim x0 -> x1, other arithmetic: none -> 0.61 us  [finish(): filter_grad = (lag * filter_scale)[None]]
  transfers between devices with their start and end apart: 8 -> 8, of which waited for: 3 -> 3; matrix products, arithmetic and copies ran while one was open for 17% -> 14% of each run, Pallas kernels for 0% -> 0%
where the time goes in v12:
time: 44.8 us; the launch traced here: 44.5 us
  starting transfers between devices  19 us (42%)
  waiting for transfers between devices  11.3 us (25%)
  matrix products  5.98 us (13%)
  other arithmetic  4.79 us (11%)
  local copies, waits for them, and re-layouts  2.42 us (5%)
  between operations  1.01 us (2%)
    ppermute x3, starting transfers between devices, dense_path(): lag = lag + lax.ppermute(share, 'ctx', pairs)  8.22 us
    ppermute x3, waiting for transfers between devices, dense_path(): got = lax.ppermute(payload, 'ctx', pairs)  7.67 us
    ppermute x3, starting transfers between devices, dense_path(): got = lax.ppermute(payload, 'ctx', pairs)  6.48 us
    ppermute x2, starting transfers between devices, from_behind(): return lax.ppermute(x, axis, pairs)  4.33 us
    ppermute x2, waiting for transfers between devices, from_behind(): return lax.ppermute(x, axis, pairs)  3.64 us
    unnamed x19, local copies, waits for them, and re-layouts  2.27 us
    dot_general x3, matrix products, dense_path(): acc = acc + jnp.dot(got, table, precision=precise)  2.02 us
    dot_general x1, matrix products, dense_path(): loc = jnp.dot(own, own_table, precision=precise)  1.48 us
  transfers between devices with their start and end apart: 8, of which 3 were waited for; matrix products, arithmetic and copies ran while one was open for 14% of the time, Pallas kernels for 0%

profile of v12, /device:TPU:4, one launch (start us, length us, event | category | flops | bytes accessed | tf_op | source)
XLA Modules:
  0.0 44.5 jit_solution(5379807392093925673)
XLA Ops:
  0.6 0.0 copy-start.6
  0.6 0.0 copy-start.7
  0.7 0.0 copy-start
  0.7 0.0 copy-start.1
  0.7 0.0 copy-start.2
  0.7 0.0 copy-start.3
  0.7 0.0 copy-start.4
  0.7 0.0 copy-start.5
  0.7 0.9 %copy.12 = f32[1,16,128]{1,2,0:T(8,128)S(1)} copy(f32[1,16,128]{2,1,0:T(8,128)} %param.13) | data formatting | bytes 16384 | tf_op args[4]
  1.7 1.0 %broadcast_select_fusion.2 = (f32[256,128]{0,1:T(8,128)S(1)}, f32[256,128]{0,1:T(8,128)S(1)}, f32[256,128]{0,1:T(8,128)S(1)}) fusion(pred[]{:T(512)S(6)} %lt.96, bf16[1,128,3,256]{3,1,2,0:T(8,128)(2,1)} %param.10, bf16[1,128,256]{2,1,0:T(8,128)(2,1)} %param.12, bf16[1,128,3,256]{3,1,2,0:T(8,128)(2,1)} %param.9, pred[]{:T(512)S(6)} %lt.101, pred[]{:T(512)S(6)} %lt.106), kind=kLoop, calls=%fused_computation.93 | loop fusion | flops 294912 | bytes 655363 | tf_op jit(solution)/shard_map/jit(_where)/select_n | solution.py:100
  2.7 2.7 %collective-permute-start.1 = (f32[272,128]{0,1:T(8,128)S(1)}, f32[272,128]{0,1:T(8,128)S(1)}, u32[]{:S(2)}, u32[]{:S(2)}) collective-permute-start(f32[272,128]{0,1:T(8,128)S(1)} %get-tuple-element.58), channel_id=1, source_target_pairs={{0,16},{8,24},{16,0},{24,8},{1,17},{9,25},{17,1},{25,9},{2,18},{10... | collective-permute-start | bytes 417800 | tf_op jit(solution)/shard_map/ppermute | solution.py:103
  5.3 1.6 %collective-permute-start = (f32[272,128]{0,1:T(8,128)S(1)}, f32[272,128]{0,1:T(8,128)S(1)}, u32[]{:S(2)}, u32[]{:S(2)}) collective-permute-start(f32[272,128]{0,1:T(8,128)S(1)} %get-tuple-element.57), channel_id=1, source_target_pairs={{0,8},{8,16},{16,24},{24,0},{1,9},{9,17},{17,25},{25,1},{2,10},{10... | collective-permute-start | bytes 417800 | tf_op jit(solution)/shard_map/ppermute | solution.py:103
  6.9 2.2 %collective-permute-start.2 = (f32[272,128]{0,1:T(8,128)S(1)}, f32[272,128]{0,1:T(8,128)S(1)}, u32[]{:S(2)}, u32[]{:S(2)}) collective-permute-start(f32[272,128]{0,1:T(8,128)S(1)} %get-tuple-element.59), channel_id=1, source_target_pairs={{0,24},{8,0},{16,8},{24,16},{1,25},{9,1},{17,9},{25,17},{2,26},{10... | collective-permute-start | bytes 417800 | tf_op jit(solution)/shard_map/ppermute | solution.py:103
  9.2 0.0 copy-done.2
  9.2 0.9 %fusion.34 = (f32[256,128]{0,1:T(8,128)S(1)}, f32[256,128]{0,1:T(8,128)S(1)}) fusion(bf16[1,128,256]{2,1,0:T(8,128)(2,1)} %param.12, bf16[1,128,3,256]{3,1,2,0:T(8,128)(2,1)S(1)} %copy-done.2), kind=kLoop, calls=%fused_computation.76 | loop fusion | flops 196608 | bytes 524288 | tf_op jit(solution)/shard_map/transpose | solution.py:197
  10.1 0.0 copy-done.4
  10.1 0.0 copy-done.3
  10.1 0.0 copy-done.5
  10.2 0.0 copy-done.6
  10.2 0.0 copy-done.7
  10.3 0.0 copy-done
  10.3 0.0 copy-done.1
  10.3 0.1 multiply_subtract_fusion.3
  10.4 0.5 %multiply_subtract_fusion.9 = (f32[128,512]{1,0:T(8,128)S(1)}, f32[128,512]{1,0:T(8,128)S(1)}, f32[128,512]{1,0:T(8,128)S(1)}, f32[128,512]{1,0:T(8,128)S(1)}, f...) fusion(f32[128,512]{1,0:T(8,128)S(1)} %copy-done.1, ...), kind=kLoop, calls=%fused_computation.68 | loop fusion | flops 3407872 | bytes 3696256 | tf_op jit(solution)/shard_map/sub | solution.py:71
  10.9 0.2 maximum_multiply_fusion
  11.2 1.5 %fusion.23 = f32[784,1024]{1,0:T(8,128)S(1)} fusion(f32[16,128]{0,1:T(8,128)S(1)} %bitcast.93, f32[256,128]{0,1:T(8,128)S(1)} %get-tuple-element.56, f32[256,128]{0,1:T(8,128)S(1)} %get-tuple-element.55, f32[256,128]{0,1:T(8,128)S(1)} %multiply_bitcast_fusion, f32[128,512]{1,0:T(8,128)S(1)} %get-tuple-element.38, f32[128,512]{1,0:T(8,128)S(1)} %get-tuple-element.37), kind=kOutput, calls=%fused_computation.40 | convolution fusion | flops 616994816 | bytes 4136960 | tf_op jit(solution)/shard_map/dot_general | solution.py:112
  12.6 7.2 %collective-permute-done.1 = f32[272,128]{0,1:T(8,128)S(1)} collective-permute-done((f32[272,128]{0,1:T(8,128)S(1)}, f32[272,128]{0,1:T(8,128)S(1)}, u32[]{:S(2)}, u32[]{:S(2)}) %collective-permute-start.1) | collective-permute-done | bytes 139296 | tf_op jit(solution)/shard_map/ppermute | solution.py:103
  19.9 0.0 collective-permute-done
  19.9 0.4 collective-permute-done.2
  20.3 0.6 %fusion.12 = f32[272,1024]{1,0:T(8,128)S(1)} fusion(f32[272,128]{0,1:T(8,128)S(1)} %collective-permute-done.1, f32[128,512]{1,0:T(8,128)S(1)} %get-tuple-element.43, f32[128,512]{1,0:T(8,128)S(1)} %get-tuple-element.44), kind=kOutput, calls=%fused_computation.20 | convolution fusion | flops 214040576 | bytes 1777664 | tf_op jit(solution)/shard_map/dot_general | solution.py:109
  21.0 0.7 %fusion.16 = f32[272,1024]{1,0:T(8,128)S(1)} fusion(f32[272,128]{0,1:T(8,128)S(1)} %collective-permute-done.2, f32[128,512]{1,0:T(8,128)S(1)} %get-tuple-element.47, f32[128,512]{1,0:T(8,128)S(1)} %get-tuple-element.48), kind=kOutput, calls=%fused_computation.25 | convolution fusion | flops 214040576 | bytes 1777664 | tf_op jit(solution)/shard_map/dot_general | solution.py:109
  21.6 0.7 %fusion.8 = f32[272,1024]{1,0:T(8,128)S(1)} fusion(f32[272,1024]{1,0:T(8,128)S(1)} %fusion.16, f32[272,1024]{1,0:T(8,128)S(1)} %fusion.12, f32[272,128]{0,1:T(8,128)S(1)} %collective-permute-done, f32[128,512]{1,0:T(8,128)S(1)} %get-tuple-element.39, f32[128,512]{1,0:T(8,128)S(1)} %get-tuple-element.40), kind=kOutput, calls=%fused_computation.9 | convolution fusion | flops 214597632 | bytes 4005888 | tf_op jit(solution)/shard_map/dot_general | solution.py:109
  22.4 0.4 slice_add_fusion.1
  22.8 0.1 broadcast_in_dim.26
  22.9 0.4 multiply_subtract_fusion
  23.4 0.2 bitcast_reduce_fusion
  23.6 0.3 fusion.20
  23.9 0.3 fusion.53
  24.2 3.3 %collective-permute-start.5 = (f32[16,128]{1,0:T(8,128)S(1)}, f32[16,128]{1,0:T(8,128)S(1)}, u32[]{:S(2)}, u32[]{:S(2)}) collective-permute-start(f32[16,128]{1,0:T(8,128)S(1)} %fusion.53), channel_id=1, source_target_pairs={{0,8},{8,16},{16,24},{24,0},{1,9},{9,17},{17,25},{25,1},{2,10},{10... | collective-permute-start | bytes 24584 | tf_op jit(solution)/shard_map/ppermute | solution.py:128
  27.5 0.3 fusion.54
  27.8 1.9 %collective-permute-start.6 = (f32[16,128]{1,0:T(8,128)S(1)}, f32[16,128]{1,0:T(8,128)S(1)}, u32[]{:S(2)}, u32[]{:S(2)}) collective-permute-start(f32[16,128]{1,0:T(8,128)S(1)} %fusion.54), channel_id=1, source_target_pairs={{0,16},{8,24},{16,0},{24,8},{1,17},{9,25},{17,1},{25,9},{2,18},{10... | collective-permute-start | bytes 24584 | tf_op jit(solution)/shard_map/ppermute | solution.py:128
  29.8 0.3 fusion.55
  30.1 2.9 %collective-permute-start.7 = (f32[16,128]{1,0:T(8,128)S(1)}, f32[16,128]{1,0:T(8,128)S(1)}, u32[]{:S(2)}, u32[]{:S(2)}) collective-permute-start(f32[16,128]{1,0:T(8,128)S(1)} %fusion.55), channel_id=1, source_target_pairs={{0,24},{8,0},{16,8},{24,16},{1,25},{9,1},{17,9},{25,17},{2,26},{10... | collective-permute-start | bytes 24584 | tf_op jit(solution)/shard_map/ppermute | solution.py:128
  33.0 0.2 select_subtract_fusion
  33.3 1.2 %fusion = f32[128,512]{1,0:T(8,128)S(1)} fusion(f32[256,512]{1,0:T(8,128)S(1)} %get-tuple-element.23, f32[256,512]{1,0:T(8,128)S(1)} %get-tuple-element.24, f32[256,512]{1,0:T(8,128)S(1)} %get-tuple-element.20, f32[256,512]{1,0:T(8,128)S(1)} %get-tuple-element.19, f32[128,512]{1,0:T(8,128)S(1)} %get-tuple-element.38, f32[128,512]{1,0:T(8,128)S(1)} %get-tuple-element.37, ...), kind=kOutput, calls=%fused_computation | convolution fusion | flops 404488192 | bytes 2887680 | tf_op jit(solution)/shard_map/tf,rf->tr/dot_general | solution.py:123
  34.5 0.1 fusion.43
  34.6 2.1 %collective-permute-start.4 = (bf16[1,128,3,256]{3,1,2,0:T(8,128)(2,1)S(1)}, bf16[1,128,3,256]{3,1,2,0:T(8,128)(2,1)S(1)}, u32[]{:S(2)}, u32[]{:S(2)}) collective-permute-start(bf16[1,128,3,256]{3,1,2,0:T(8,128)(2,1)S(1)} %pad_maximum_fusion.8), channel_id=1, source_target_pairs={{1,0},{2,1},{3,2},{4,3},{5,4},{6,5},{7,6},{9,8},{10,9},{11,10},{12... | collective-permute-start | bytes 589832 | tf_op jit(solution)/shard_map/ppermute | solution.py:22
  36.7 2.2 %collective-permute-start.3 = (bf16[1,128,256]{2,1,0:T(8,128)(2,1)S(1)}, bf16[1,128,256]{2,1,0:T(8,128)(2,1)S(1)}, u32[]{:S(2)}, u32[]{:S(2)}) collective-permute-start(bf16[1,128,256]{2,1,0:T(8,128)(2,1)S(1)} %get-tuple-element.54), channel_id=1, source_target_pairs={{0,1},{1,2},{2,3},{3,4},{4,5},{5,6},{6,7},{8,9},{9,10},{10,11},{11... | collective-permute-start | bytes 196616 | tf_op jit(solution)/shard_map/ppermute | solution.py:22
  38.9 0.0 collective-permute-done.5
  39.0 0.0 collective-permute-done.6
  39.0 0.0 collective-permute-done.7
  39.0 0.6 %multiply_bitcast_fusion.1 = f32[1,16,128]{2,1,0:T(8,128)} fusion(f32[16,128]{1,0:T(8,128)S(1)} %collective-permute-done.7, f32[16,128]{1,0:T(8,128)S(1)} %collective-permute-done.6, f32[16,128]{1,0:T(8,128)S(1)} %fusion.20, f32[16,128]{1,0:T(8,128)S(1)} %collective-permute-done.5), kind=kLoop, calls=%fused_computation.94 | loop fusion | flops 8192 | bytes 40960 | tf_op jit(solution)/shard_map/broadcast_in_dim | solution.py:169
  39.6 3.6 %collective-permute-done.3 = bf16[1,128,256]{2,1,0:T(8,128)(2,1)S(1)} collective-permute-done((bf16[1,128,256]{2,1,0:T(8,128)(2,1)S(1)}, bf16[1,128,256]{2,1,0:T(8,128)(2,1)S(1)}, u32[]{:S(2)}, u32[]{:S(2)}) %collective-permute-start.3) | collective-permute-done | bytes 65568 | tf_op jit(solution)/shard_map/ppermute | solution.py:22
  43.2 0.0 collective-permute-done.4
  43.2 0.6 %copy.15 = bf16[1,128,256]{2,1,0:T(8,128)(2,1)} copy(bf16[1,128,256]{2,1,0:T(8,128)(2,1)S(1)} %collective-permute-done.3) | data formatting | bytes 131072
  43.9 0.7 %copy.16 = bf16[1,128,3,256]{3,1,2,0:T(8,128)(2,1)} copy(bf16[1,128,3,256]{3,1,2,0:T(8,128)(2,1)S(1)} %collective-permute-done.4) | data formatting | bytes 393216
  (10 shorter events, 0.2 us)
Async XLA Ops:
  0.6 9.6 %copy-start.6 = (f32[4,512]{1,0:T(4,128)S(1)}, f32[4,512]{1,0:T(4,128)}, u32[]{:S(2)}) copy-start(f32[4,512]{1,0:T(4,128)} %constant.139.clone) | copy-start | bytes 24580
  0.6 9.6 %copy-start.7 = (f32[4,512]{1,0:T(4,128)S(1)}, f32[4,512]{1,0:T(4,128)}, u32[]{:S(2)}) copy-start(f32[4,512]{1,0:T(4,128)} %constant.140.clone) | copy-start | bytes 24580
  0.7 9.6 %copy-start = (f32[128,512]{1,0:T(8,128)S(1)}, f32[128,512]{1,0:T(8,128)}, u32[]{:S(2)}) copy-start(f32[128,512]{1,0:T(8,128)} %constant.137.clone) | copy-start | bytes 786436
  0.7 9.6 %copy-start.1 = (f32[128,512]{1,0:T(8,128)S(1)}, f32[128,512]{1,0:T(8,128)}, u32[]{:S(2)}) copy-start(f32[128,512]{1,0:T(8,128)} %constant.138.clone) | copy-start | bytes 786436
  0.7 8.5 %copy-start.2 = (bf16[1,128,3,256]{3,1,2,0:T(8,128)(2,1)S(1)}, bf16[1,128,3,256]{3,1,2,0:T(8,128)(2,1)}, u32[]{:S(2)}) copy-start(bf16[1,128,3,256]{3,1,2,0:T(8,128)(2,1)} %param.10) | copy-start | bytes 589828
  0.7 9.4 %copy-start.3 = (bf16[1,128,256]{2,1,0:T(8,128)(2,1)S(1)}, bf16[1,128,256]{2,1,0:T(8,128)(2,1)}, u32[]{:S(2)}) copy-start(bf16[1,128,256]{2,1,0:T(8,128)(2,1)} %param.12) | copy-start | bytes 196612
  0.7 9.4 %copy-start.4 = (bf16[1,128,3,256]{3,1,2,0:T(8,128)(2,1)S(1)}, bf16[1,128,3,256]{3,1,2,0:T(8,128)(2,1)}, u32[]{:S(2)}) copy-start(bf16[1,128,3,256]{3,1,2,0:T(8,128)(2,1)} %param.9) | copy-start | bytes 589828
  0.7 9.4 %copy-start.5 = (f32[1,128,256]{2,1,0:T(8,128)S(1)}, f32[1,128,256]{2,1,0:T(8,128)}, u32[]{:S(2)}) copy-start(f32[1,128,256]{2,1,0:T(8,128)} %param.11) | copy-start | bytes 393220
  2.7 17.2 %collective-permute-start.1 = (f32[272,128]{0,1:T(8,128)S(1)}, f32[272,128]{0,1:T(8,128)S(1)}, u32[]{:S(2)}, u32[]{:S(2)}) collective-permute-start(f32[272,128]{0,1:T(8,128)S(1)} %get-tuple-element.58), channel_id=1, source_target_pairs={{0,16},{8,24},{16,0},{24,8},{1,17},{9,25},{17,1},{25,9},{2,18},{10... | collective-permute-start | bytes 417800 | tf_op jit(solution)/shard_map/ppermute | solution.py:103
  5.3 14.6 %collective-permute-start = (f32[272,128]{0,1:T(8,128)S(1)}, f32[272,128]{0,1:T(8,128)S(1)}, u32[]{:S(2)}, u32[]{:S(2)}) collective-permute-start(f32[272,128]{0,1:T(8,128)S(1)} %get-tuple-element.57), channel_id=1, source_target_pairs={{0,8},{8,16},{16,24},{24,0},{1,9},{9,17},{17,25},{25,1},{2,10},{10... | collective-permute-start | bytes 417800 | tf_op jit(solution)/shard_map/ppermute | solution.py:103
  6.9 13.4 %collective-permute-start.2 = (f32[272,128]{0,1:T(8,128)S(1)}, f32[272,128]{0,1:T(8,128)S(1)}, u32[]{:S(2)}, u32[]{:S(2)}) collective-permute-start(f32[272,128]{0,1:T(8,128)S(1)} %get-tuple-element.59), channel_id=1, source_target_pairs={{0,24},{8,0},{16,8},{24,16},{1,25},{9,1},{17,9},{25,17},{2,26},{10... | collective-permute-start | bytes 417800 | tf_op jit(solution)/shard_map/ppermute | solution.py:103
  24.2 14.7 %collective-permute-start.5 = (f32[16,128]{1,0:T(8,128)S(1)}, f32[16,128]{1,0:T(8,128)S(1)}, u32[]{:S(2)}, u32[]{:S(2)}) collective-permute-start(f32[16,128]{1,0:T(8,128)S(1)} %fusion.53), channel_id=1, source_target_pairs={{0,8},{8,16},{16,24},{24,0},{1,9},{9,17},{17,25},{25,1},{2,10},{10... | collective-permute-start | bytes 24584 | tf_op jit(solution)/shard_map/ppermute | solution.py:128
  27.8 11.1 %collective-permute-start.6 = (f32[16,128]{1,0:T(8,128)S(1)}, f32[16,128]{1,0:T(8,128)S(1)}, u32[]{:S(2)}, u32[]{:S(2)}) collective-permute-start(f32[16,128]{1,0:T(8,128)S(1)} %fusion.54), channel_id=1, source_target_pairs={{0,16},{8,24},{16,0},{24,8},{1,17},{9,25},{17,1},{25,9},{2,18},{10... | collective-permute-start | bytes 24584 | tf_op jit(solution)/shard_map/ppermute | solution.py:128
  30.1 8.9 %collective-permute-start.7 = (f32[16,128]{1,0:T(8,128)S(1)}, f32[16,128]{1,0:T(8,128)S(1)}, u32[]{:S(2)}, u32[]{:S(2)}) collective-permute-start(f32[16,128]{1,0:T(8,128)S(1)} %fusion.55), channel_id=1, source_target_pairs={{0,24},{8,0},{16,8},{24,16},{1,25},{9,1},{17,9},{25,17},{2,26},{10... | collective-permute-start | bytes 24584 | tf_op jit(solution)/shard_map/ppermute | solution.py:128
  34.6 8.6 %collective-permute-start.4 = (bf16[1,128,3,256]{3,1,2,0:T(8,128)(2,1)S(1)}, bf16[1,128,3,256]{3,1,2,0:T(8,128)(2,1)S(1)}, u32[]{:S(2)}, u32[]{:S(2)}) collective-permute-start(bf16[1,128,3,256]{3,1,2,0:T(8,128)(2,1)S(1)} %pad_maximum_fusion.8), channel_id=1, source_target_pairs={{1,0},{2,1},{3,2},{4,3},{5,4},{6,5},{7,6},{9,8},{10,9},{11,10},{12... | collective-permute-start | bytes 589832 | tf_op jit(solution)/shard_map/ppermute | solution.py:22
  36.7 6.5 %collective-permute-start.3 = (bf16[1,128,256]{2,1,0:T(8,128)(2,1)S(1)}, bf16[1,128,256]{2,1,0:T(8,128)(2,1)S(1)}, u32[]{:S(2)}, u32[]{:S(2)}) collective-permute-start(bf16[1,128,256]{2,1,0:T(8,128)(2,1)S(1)} %get-tuple-element.54), channel_id=1, source_target_pairs={{0,1},{1,2},{2,3},{3,4},{4,5},{5,6},{6,7},{8,9},{9,10},{10,11},{11... | collective-permute-start | bytes 196616 | tf_op jit(solution)/shard_map/ppermute | solution.py:22

commit v13 on v5

--- a/solution.py
+++ b/solution.py
@@ -87,27 +87,31 @@
     return jnp.concatenate([re, im], axis=1)
 
 
-def dense_path(place, blocks, mixed_rows, weighted_rows, back_rows, taps):
+def dense_path(place, blocks, mixed_rows, weighted_rows, back_rows, taps, ahead, behind):
     channels, block = mixed_rows.shape
     size = 2 * blocks * block
     half = size // 2
     packed = packed_tables(blocks, block)
+    all_taps = lax.all_gather(taps, "ctx")
     acc = 0.0
     for s in range(1, blocks):
-        first = jnp.where(place + s < blocks, mixed_rows, weighted_rows)
-        payload = jnp.concatenate([first, taps], axis=0)
+        payload = jnp.where(place + s < blocks, ahead, behind)
         pairs = [(i, (i + s) % blocks) for i in range(blocks)]
         got = lax.ppermute(payload, "ctx", pairs)
+        product = got[:, 0].astype(jnp.float32) * got[:, 1].astype(jnp.float32)
         table = block_table(packed, (place - s) % blocks)
-        acc = acc + jnp.dot(got, table, precision=precise)
+        acc = acc + jnp.einsum("pr,pf->rf", product, table, precision=precise)
     own_table = block_table(packed, place)
-    own = jnp.concatenate([mixed_rows, weighted_rows, back_rows, taps], axis=0)
+    own = jnp.concatenate([mixed_rows, weighted_rows, back_rows], axis=0)
     loc = jnp.dot(own, own_table, precision=precise)
+    taps_spec = 0.0
+    for b in range(blocks):
+        taps_spec = taps_spec + jnp.dot(all_taps[b], block_table(packed, b), precision=precise)
     c = channels
-    mixed_spec = loc[:c] + acc[:c]
-    weighted_spec = loc[c : 2 * c] + acc[:c]
+    mixed_spec = loc[:c] + acc
+    weighted_spec = loc[c : 2 * c] + acc
     back_spec = loc[2 * c : 3 * c]
-    taps_spec = jnp.repeat(loc[3 * c :] + acc[c:], CPF, axis=0)
+    taps_spec = jnp.repeat(taps_spec, CPF, axis=0)
     conv = packed_products(taps_spec, mixed_spec, False)
     gm = packed_products(taps_spec, weighted_spec, True)
     fgs = packed_products(back_spec, weighted_spec, True)
@@ -190,7 +194,14 @@
 
     if blocks <= DENSE:
         conv, grad_mixed, lag = dense_path(
-            place, blocks, mixed_in.T, weighted.T, mixed_back.T, taps
+            place,
+            blocks,
+            mixed_in.T,
+            weighted.T,
+            mixed_back.T,
+            taps,
+            qkv_in[0, :, 1:3],
+            jnp.stack([out_grad[0], qkv_saved[0, :, 0]], axis=1),
         )
         return finish(
             conv, grad_mixed, lag, filter_scale, query_in, grad_query, key_back, value_back

time: 43.4 us -> 49.8 us (1.15)
  blocking collectives: 0 us -> 13.8 us
  waiting for transfers between devices: 11.5 us -> 3.41 us
  starting transfers between devices: 17.6 us -> 14.4 us
  other arithmetic: 3.98 us -> 6.31 us
  matrix products: 6.62 us -> 7.63 us
    all_gather x0 -> x1, blocking collectives: none -> 13.8 us  [dense_path(): all_taps = lax.all_gather(taps, 'ctx')]
    ppermute x3, waiting for transfers between devices: 7.94 us -> 0.01 us  [dense_path(): got = lax.ppermute(payload, 'ctx', pairs)]
    ppermute x3, starting transfers between devices: 8.37 us -> 3.85 us  [dense_path(): lag = lag + lax.ppermute(share, 'ctx', pairs)]
    ppermute x3, starting transfers between devices: 4.68 us -> 6.48 us  [dense_path(): got = lax.ppermute(payload, 'ctx', pairs)]
    another operation x3, other arithmetic: 0.1 us -> 1.88 us  [finish(): jnp.stack([grad_query, grad_key, grad_value], axis=1).astype(jnp.bfloat16)]
    dot_general x3 -> x7, matrix products: 2.02 us -> 3.04 us  [the longest x3 2.08 us: dense_path(): acc = acc + jnp.einsum('pr,pf->rf', product, table, precision=precise)]
    transpose x2, other arithmetic: 0.89 us -> 1.9 us  [on_device(): conv, grad_mixed, lag = dense_path(place, blocks, mixed_in.T, weighted.T,...]
    another operation x0 -> x1, local copies, waits for them, and re-layouts: none -> 0.94 us  [on_device(): jnp.stack([out_grad[0], qkv_saved[0, :, 0]], axis=1)]
  transfers between devices with their start and end apart: 8 -> 8, of which waited for: 3 -> 1; matrix products, arithmetic and copies ran while one was open for 17% -> 23% of each run, Pallas kernels for 0% -> 0%
where the time goes in v13:
time: 49.8 us; the launch traced here: 49.4 us
  starting transfers between devices  14.4 us (29%)
  blocking collectives  13.8 us (28%)
  matrix products  7.63 us (15%)
  other arithmetic  6.31 us (13%)
  waiting for transfers between devices  3.41 us (7%)
  local copies, waits for them, and re-layouts  2.87 us (6%)
  between operations  1.03 us (2%)
    all_gather x1, blocking collectives, dense_path(): all_taps = lax.all_gather(taps, 'ctx')  13.8 us
    ppermute x3, starting transfers between devices, dense_path(): got = lax.ppermute(payload, 'ctx', pairs)  6.48 us
    ppermute x2, starting transfers between devices, from_behind(): return lax.ppermute(x, axis, pairs)  4.03 us
    ppermute x3, starting transfers between devices, dense_path(): lag = lag + lax.ppermute(share, 'ctx', pairs)  3.85 us
    ppermute x2, waiting for transfers between devices, from_behind(): return lax.ppermute(x, axis, pairs)  3.35 us
    dot_general x3, matrix products, dense_path(): acc = acc + jnp.einsum('pr,pf->rf', product, table, precision=precise)  2.08 us
    transpose x2, other arithmetic, on_device(): conv, grad_mixed, lag = dense_path(place, blocks, mixed_in.T, weighted.T,...  1.9 us
    another operation x3, other arithmetic, finish(): jnp.stack([grad_query, grad_key, grad_value], axis=1).astype(jnp.bfloat16)  1.88 us
  transfers between devices with their start and end apart: 8, of which 1 were waited for; matrix products, arithmetic and copies ran while one was open for 23% of the time, Pallas kernels for 0%

profile of v13, /device:TPU:4, one launch (start us, length us, event | category | flops | bytes accessed | tf_op | source)
XLA Modules:
  0.0 49.4 jit_solution(7819126999499780029)
XLA Ops:
  0.6 0.0 copy-start.10
  0.6 0.0 copy-start.11
  0.7 0.0 copy-start
  0.7 0.0 copy-start.1
  0.7 0.0 copy-start.3
  0.7 0.0 copy-start.4
  0.7 0.0 copy-start.5
  0.7 0.9 %slice_bitcast_fusion = bf16[128,1,256]{2,0,1:T(8,128)(2,1)S(1)} fusion(bf16[1,128,3,256]{3,1,2,0:T(8,128)(2,1)} %param.10), kind=kLoop, calls=%fused_computation.142 | loop fusion | bytes 131072 | tf_op jit(solution)/shard_map/stack;squeeze | solution.py:204
  1.7 0.9 %bitcast_select_fusion = (bf16[128,2,256]{2,0,1:T(8,128)(2,1)S(1)}, bf16[128,2,256]{2,0,1:T(8,128)(2,1)S(1)}, bf16[128,2,256]{2,0,1:T(8,128)(2,1)S(1)}) fusion(pred[]{:T(512)S(6)} %lt.127, bf16[1,128,3,256]{3,1,2,0:T(8,128)(2,1)} %param.9, bf16[128,1,256]{2,0,1:T(8,128)(2,1)S(1)} %slice_bitcast_fusion, bf16[128,1,256]{2,0,1:T(8,128)(2,1)} %bitcast.97, ...), kind=kLoop, calls=%fused_computation.119 | loop fusion | flops 262144 | bytes 655363 | tf_op jit(solution)/shard_map/jit(_where)/select_n | solution.py:98
  2.6 2.7 %collective-permute-start.1 = (bf16[128,2,256]{2,0,1:T(8,128)(2,1)S(1)}, bf16[128,2,256]{2,0,1:T(8,128)(2,1)S(1)}, u32[]{:S(2)}, u32[]{:S(2)}) collective-permute-start(bf16[128,2,256]{2,0,1:T(8,128)(2,1)S(1)} %get-tuple-element.40), channel_id=1, source_target_pairs={{0,16},{8,24},{16,0},{24,8},{1,17},{9,25},{17,1},{25,9},{2,18},{10... | collective-permute-start | bytes 393224 | tf_op jit(solution)/shard_map/ppermute | solution.py:100
  5.3 1.6 %collective-permute-start = (bf16[128,2,256]{2,0,1:T(8,128)(2,1)S(1)}, bf16[128,2,256]{2,0,1:T(8,128)(2,1)S(1)}, u32[]{:S(2)}, u32[]{:S(2)}) collective-permute-start(bf16[128,2,256]{2,0,1:T(8,128)(2,1)S(1)} %get-tuple-element.41), channel_id=1, source_target_pairs={{0,8},{8,16},{16,24},{24,0},{1,9},{9,17},{17,25},{25,1},{2,10},{10... | collective-permute-start | bytes 393224 | tf_op jit(solution)/shard_map/ppermute | solution.py:100
  6.8 2.2 %collective-permute-start.2 = (bf16[128,2,256]{2,0,1:T(8,128)(2,1)S(1)}, bf16[128,2,256]{2,0,1:T(8,128)(2,1)S(1)}, u32[]{:S(2)}, u32[]{:S(2)}) collective-permute-start(bf16[128,2,256]{2,0,1:T(8,128)(2,1)S(1)} %get-tuple-element.39), channel_id=1, source_target_pairs={{0,24},{8,0},{16,8},{24,16},{1,25},{9,1},{17,9},{25,17},{2,26},{10... | collective-permute-start | bytes 393224 | tf_op jit(solution)/shard_map/ppermute | solution.py:100
  9.1 0.0 copy-start.8
  9.1 1.0 %fusion.67 = (f32[256,128]{0,1:T(8,128)S(1)}, f32[256,128]{0,1:T(8,128)S(1)}) fusion(bf16[1,128,256]{2,1,0:T(8,128)(2,1)} %param.12, bf16[1,128,3,256]{3,1,2,0:T(8,128)(2,1)} %param.10), kind=kLoop, calls=%fused_computation.113 | loop fusion | flops 196608 | bytes 524288 | tf_op jit(solution)/shard_map/transpose | solution.py:200
  10.1 0.9 %multiply_bitcast_fusion = f32[256,128]{0,1:T(8,128)S(1)} fusion(bf16[1,128,3,256]{3,1,2,0:T(8,128)(2,1)} %param.9), kind=kLoop, calls=%fused_computation.131 | loop fusion | flops 98304 | bytes 262144 | tf_op jit(solution)/shard_map/transpose | solution.py:199
  11.0 13.8 %all_gather.3 = f32[4,16,128]{2,1,0:T(8,128)S(1)} all-gather(f32[1,16,128]{2,1,0:T(8,128)} %param.13), channel_id=1, replica_groups=mesh['ctx'=4,'pipe'=8] {'ctx'}, dimensions={0}, use_global_device_ids=true | all-gather | bytes 40960 | tf_op jit(solution)/shard_map/all_gather | solution.py:95
  24.8 1.0 %fusion.81 = bf16[1,128,1,256]{3,1,2,0:T(8,128)(2,1)S(1)} fusion(f32[1,128,256]{2,1,0:T(8,128)} %param.11, bf16[1,128,256]{2,1,0:T(8,128)(2,1)} %param.12), kind=kLoop, calls=%fused_computation.132 | loop fusion | flops 98304 | bytes 262144 | tf_op jit(solution)/shard_map/stack | solution.py:167
  25.8 0.0 copy-done.10
  25.8 0.0 copy-done.11
  25.9 0.0 copy-done
  25.9 0.0 copy-done.1
  25.9 0.0 copy-done.3
  25.9 0.0 copy-done.4
  25.9 0.0 copy-done.5
  25.9 0.0 copy-start.9
  25.9 0.2 multiply_subtract_fusion.7
  26.1 0.2 fusion.13
  26.3 0.0 copy-done.8
  26.3 0.2 convolution_add_fusion.4
  26.6 0.2 convolution_add_fusion.3
  26.8 0.0 copy-done.9
  26.9 0.5 %multiply_subtract_fusion.6 = (f32[128,512]{1,0:T(8,128)S(1)}, f32[128,512]{1,0:T(8,128)S(1)}, f32[128,512]{1,0:T(8,128)S(1)}, f32[128,512]{1,0:T(8,128)S(1)}, f...) fusion(f32[128,512]{1,0:T(8,128)S(1)} %copy-done.1, ...), kind=kLoop, calls=%fused_computation.85 | loop fusion | flops 3473408 | bytes 4220544 | tf_op jit(solution)/shard_map/sub | solution.py:71
  27.4 0.4 copy-done.6
  27.8 0.2 fusion.8
  28.0 1.5 %fusion.47 = f32[768,1024]{1,0:T(8,128)S(1)} fusion(f32[256,128]{0,1:T(8,128)S(1)} %get-tuple-element.44, f32[256,128]{0,1:T(8,128)S(1)} %get-tuple-element.43, f32[256,128]{0,1:T(8,128)S(1)} %multiply_bitcast_fusion, f32[128,512]{1,0:T(8,128)S(1)} %get-tuple-element.33, f32[128,512]{1,0:T(8,128)S(1)} %get-tuple-element.34), kind=kOutput, calls=%fused_computation.70 | convolution fusion | flops 604307456 | bytes 4063232 | tf_op jit(solution)/shard_map/dot_general | solution.py:106
  29.5 0.0 collective-permute-done.1
  29.5 0.6 %fusion.29 = f32[256,1024]{1,0:T(8,128)S(1)} fusion(f32[128,512]{1,0:T(8,128)S(1)} %get-tuple-element.26, f32[128,512]{1,0:T(8,128)S(1)} %get-tuple-element.25, bf16[128,2,256]{2,0,1:T(8,128)(2,1)S(1)} %collective-permute-done.1), kind=kOutput, calls=%fused_computation.40 | convolution fusion | flops 201555968 | bytes 1703936 | tf_op jit(solution)/shard_map/pr,pf->rf/dot_general | solution.py:103
  30.2 0.0 collective-permute-done
  30.2 0.7 %convolution_add_fusion.1 = f32[256,1024]{1,0:T(8,128)S(1)} fusion(f32[256,1024]{1,0:T(8,128)S(1)} %fusion.29, f32[128,512]{1,0:T(8,128)S(1)} %get-tuple-element.24, f32[128,512]{1,0:T(8,128)S(1)} %get-tuple-element.23, bf16[128,2,256]{2,0,1:T(8,128)(2,1)S(1)} %collective-permute-done), kind=kOutput, calls=%fused_computation.9 | convolution fusion | flops 201818112 | bytes 2752512 | tf_op jit(solution)/shard_map/pr,pf->rf/dot_general | solution.py:103
  30.9 0.0 collective-permute-done.2
  30.9 0.8 %slice_add_fusion.1 = (f32[256,1024]{1,0:T(8,128)S(1)}, f32[256,1024]{1,0:T(8,128)S(1)}) fusion(f32[768,1024]{1,0:T(8,128)S(1)} %fusion.47, f32[256,1024]{1,0:T(8,128)S(1)} %convolution_add_fusion.1, f32[128,512]{1,0:T(8,128)S(1)} %get-tuple-element.35, f32[128,512]{1,0:T(8,128)S(1)} %get-tuple-element.36, bf16[128,2,256]{2,0,1:T(8,128)(2,1)S(1)} %collective-permute-done.2), kind=kOutput, calls=%fused_computation.20 | convolution fusion | flops 202342400 | bytes 5898240 | tf_op jit(solution)/shard_map/pr,pf->rf/dot_general | solution.py:103
  31.7 0.1 broadcast_in_dim.26
  31.8 0.4 multiply_subtract_fusion
  32.2 0.2 bitcast_reduce_fusion
  32.4 0.3 fusion.36
  32.7 0.0 collective-permute-start.5
  32.7 0.3 fusion.39
  33.1 1.0 %collective-permute-start.6 = (f32[16,128]{1,0:T(8,128)S(1)}, f32[16,128]{1,0:T(8,128)S(1)}, u32[]{:S(2)}, u32[]{:S(2)}) collective-permute-start(f32[16,128]{1,0:T(8,128)S(1)} %fusion.39), channel_id=1, source_target_pairs={{0,16},{8,24},{16,0},{24,8},{1,17},{9,25},{17,1},{25,9},{2,18},{10... | collective-permute-start | bytes 24584 | tf_op jit(solution)/shard_map/ppermute | solution.py:128
  34.0 0.2 select_subtract_fusion
  34.3 0.0 copy-start.2
  34.3 1.2 %fusion = f32[128,512]{1,0:T(8,128)S(1)} fusion(f32[256,512]{1,0:T(8,128)S(1)} %get-tuple-element.11, f32[256,512]{1,0:T(8,128)S(1)} %get-tuple-element.12, f32[256,512]{1,0:T(8,128)S(1)} %get-tuple-element.8, f32[256,512]{1,0:T(8,128)S(1)} %get-tuple-element.7, f32[128,512]{1,0:T(8,128)S(1)} %get-tuple-element.33, f32[128,512]{1,0:T(8,128)S(1)} %get-tuple-element.34, ...), kind=kOutput, calls=%fused_computation | convolution fusion | flops 404488192 | bytes 2887680 | tf_op jit(solution)/shard_map/tf,rf->tr/dot_general | solution.py:122
  35.5 0.9 %fusion.84 = (bf16[1,128,1,256]{3,1,2,0:T(8,128)(2,1)S(1)}, bf16[1,128,1,256]{3,1,2,0:T(8,128)(2,1)S(1)}, bf16[1,128,256]{2,1,0:T(8,128)(2,1)S(1)}) fusion(f32[128,512]{1,0:T(8,128)S(1)} %fusion, bf16[1,128,3,256]{3,1,2,0:T(8,128)(2,1)S(1)} %copy-done.2, bf16[1,128,3,256]{3,1,2,0:T(8,128)(2,1)} %param.9), kind=kLoop, calls=%fused_computation.135 | loop fusion | flops 360448 | bytes 655360 | tf_op jit(solution)/shard_map/stack | solution.py:167
  36.5 1.9 %collective-permute-start.4 = (bf16[1,128,3,256]{3,1,2,0:T(8,128)(2,1)S(1)}, bf16[1,128,3,256]{3,1,2,0:T(8,128)(2,1)S(1)}, u32[]{:S(2)}, u32[]{:S(2)}) collective-permute-start(bf16[1,128,3,256]{3,1,2,0:T(8,128)(2,1)S(1)} %pad_maximum_fusion.5), channel_id=1, source_target_pairs={{1,0},{2,1},{3,2},{4,3},{5,4},{6,5},{7,6},{9,8},{10,9},{11,10},{12... | collective-permute-start | bytes 589832 | tf_op jit(solution)/shard_map/ppermute | solution.py:22
  38.4 0.3 fusion.42
  38.7 2.9 %collective-permute-start.7 = (f32[16,128]{1,0:T(8,128)S(1)}, f32[16,128]{1,0:T(8,128)S(1)}, u32[]{:S(2)}, u32[]{:S(2)}) collective-permute-start(f32[16,128]{1,0:T(8,128)S(1)} %fusion.42), channel_id=1, source_target_pairs={{0,24},{8,0},{16,8},{24,16},{1,25},{9,1},{17,9},{25,17},{2,26},{10... | collective-permute-start | bytes 24584 | tf_op jit(solution)/shard_map/ppermute | solution.py:128
  41.6 2.1 %collective-permute-start.3 = (bf16[1,128,256]{2,1,0:T(8,128)(2,1)S(1)}, bf16[1,128,256]{2,1,0:T(8,128)(2,1)S(1)}, u32[]{:S(2)}, u32[]{:S(2)}) collective-permute-start(bf16[1,128,256]{2,1,0:T(8,128)(2,1)S(1)} %get-tuple-element.42), channel_id=1, source_target_pairs={{0,1},{1,2},{2,3},{3,4},{4,5},{5,6},{6,7},{8,9},{9,10},{10,11},{11... | collective-permute-start | bytes 196616 | tf_op jit(solution)/shard_map/ppermute | solution.py:22
  43.7 0.0 collective-permute-done.5
  43.7 0.0 collective-permute-done.6
  43.7 0.0 collective-permute-done.7
  43.8 0.9 %fusion.12 = f32[1,16,128]{2,1,0:T(8,128)} fusion(f32[16,128]{1,0:T(8,128)S(1)} %collective-permute-done.7, f32[16,128]{1,0:T(8,128)S(1)} %collective-permute-done.6, f32[16,128]{1,0:T(8,128)S(1)} %collective-permute-done.5, f32[16,1024]{1,0:T(8,128)S(1)} %bitcast_reduce_fusion, f32[128,512]{1,0:T(8,128)S(1)} %get-tuple-element.33, ...), kind=kOutput, calls=%fused_computation.18 | convolution fusion | flops 12853248 | bytes 626688 | tf_op jit(solution)/shard_map/rf,tf->rt/dot_general | solution.py:123
  44.7 3.3 %collective-permute-done.3 = bf16[1,128,256]{2,1,0:T(8,128)(2,1)S(1)} collective-permute-done((bf16[1,128,256]{2,1,0:T(8,128)(2,1)S(1)}, bf16[1,128,256]{2,1,0:T(8,128)(2,1)S(1)}, u32[]{:S(2)}, u32[]{:S(2)}) %collective-permute-start.3) | collective-permute-done | bytes 65568 | tf_op jit(solution)/shard_map/ppermute | solution.py:22
  48.1 0.0 collective-permute-done.4
  48.1 0.6 %copy.14 = bf16[1,128,256]{2,1,0:T(8,128)(2,1)} copy(bf16[1,128,256]{2,1,0:T(8,128)(2,1)S(1)} %collective-permute-done.3) | data formatting | bytes 131072
  48.7 0.7 %copy.15 = bf16[1,128,3,256]{3,1,2,0:T(8,128)(2,1)} copy(bf16[1,128,3,256]{3,1,2,0:T(8,128)(2,1)S(1)} %collective-permute-done.4) | data formatting | bytes 393216
  (10 shorter events, 0.1 us)
Async XLA Ops:
  0.6 25.2 %copy-start.10 = (f32[4,512]{1,0:T(4,128)S(1)}, f32[4,512]{1,0:T(4,128)}, u32[]{:S(2)}) copy-start(f32[4,512]{1,0:T(4,128)} %constant.174.clone) | copy-start | bytes 24580
  0.6 25.2 %copy-start.11 = (f32[4,512]{1,0:T(4,128)S(1)}, f32[4,512]{1,0:T(4,128)}, u32[]{:S(2)}) copy-start(f32[4,512]{1,0:T(4,128)} %constant.175.clone) | copy-start | bytes 24580
  0.7 25.2 %copy-start = (f32[128,512]{1,0:T(8,128)S(1)}, f32[128,512]{1,0:T(8,128)}, u32[]{:S(2)}) copy-start(f32[128,512]{1,0:T(8,128)} %constant.172.clone) | copy-start | bytes 786436
  0.7 25.2 %copy-start.1 = (f32[128,512]{1,0:T(8,128)S(1)}, f32[128,512]{1,0:T(8,128)}, u32[]{:S(2)}) copy-start(f32[128,512]{1,0:T(8,128)} %constant.173.clone) | copy-start | bytes 786436
  0.7 25.2 %copy-start.3 = (f32[128,512]{1,0:T(8,128)S(1)}, f32[128,512]{1,0:T(8,128)}, u32[]{:S(2)}) copy-start(f32[128,512]{1,0:T(8,128)} %constant.191) | copy-start | bytes 786436
  0.7 25.2 %copy-start.4 = (f32[128,512]{1,0:T(8,128)S(1)}, f32[128,512]{1,0:T(8,128)}, u32[]{:S(2)}) copy-start(f32[128,512]{1,0:T(8,128)} %constant.202) | copy-start | bytes 786436
  0.7 25.2 %copy-start.5 = (f32[128,512]{1,0:T(8,128)S(1)}, f32[128,512]{1,0:T(8,128)}, u32[]{:S(2)}) copy-start(f32[128,512]{1,0:T(8,128)} %constant.213) | copy-start | bytes 786436
  2.6 26.9 %collective-permute-start.1 = (bf16[128,2,256]{2,0,1:T(8,128)(2,1)S(1)}, bf16[128,2,256]{2,0,1:T(8,128)(2,1)S(1)}, u32[]{:S(2)}, u32[]{:S(2)}) collective-permute-start(bf16[128,2,256]{2,0,1:T(8,128)(2,1)S(1)} %get-tuple-element.40), channel_id=1, source_target_pairs={{0,16},{8,24},{16,0},{24,8},{1,17},{9,25},{17,1},{25,9},{2,18},{10... | collective-permute-start | bytes 393224 | tf_op jit(solution)/shard_map/ppermute | solution.py:100
  5.3 24.9 %collective-permute-start = (bf16[128,2,256]{2,0,1:T(8,128)(2,1)S(1)}, bf16[128,2,256]{2,0,1:T(8,128)(2,1)S(1)}, u32[]{:S(2)}, u32[]{:S(2)}) collective-permute-start(bf16[128,2,256]{2,0,1:T(8,128)(2,1)S(1)} %get-tuple-element.41), channel_id=1, source_target_pairs={{0,8},{8,16},{16,24},{24,0},{1,9},{9,17},{17,25},{25,1},{2,10},{10... | collective-permute-start | bytes 393224 | tf_op jit(solution)/shard_map/ppermute | solution.py:100
  6.8 24.0 %collective-permute-start.2 = (bf16[128,2,256]{2,0,1:T(8,128)(2,1)S(1)}, bf16[128,2,256]{2,0,1:T(8,128)(2,1)S(1)}, u32[]{:S(2)}, u32[]{:S(2)}) collective-permute-start(bf16[128,2,256]{2,0,1:T(8,128)(2,1)S(1)} %get-tuple-element.39), channel_id=1, source_target_pairs={{0,24},{8,0},{16,8},{24,16},{1,25},{9,1},{17,9},{25,17},{2,26},{10... | collective-permute-start | bytes 393224 | tf_op jit(solution)/shard_map/ppermute | solution.py:100
  9.1 17.2 %copy-start.8 = (f32[128,512]{1,0:T(8,128)S(1)}, f32[128,512]{1,0:T(8,128)}, u32[]{:S(2)}) copy-start(f32[128,512]{1,0:T(8,128)} %constant.198) | copy-start | bytes 786436
  24.8 1.8 %copy-start.7 = (f32[128,512]{1,0:T(8,128)S(1)}, f32[128,512]{1,0:T(8,128)}, u32[]{:S(2)}) copy-start(f32[128,512]{1,0:T(8,128)} %constant.209) | copy-start | bytes 786436
  25.9 1.0 %copy-start.9 = (f32[128,512]{1,0:T(8,128)S(1)}, f32[128,512]{1,0:T(8,128)}, u32[]{:S(2)}) copy-start(f32[128,512]{1,0:T(8,128)} %constant.224) | copy-start | bytes 786436
  26.9 1.0 %copy-start.6 = (f32[128,512]{1,0:T(8,128)S(1)}, f32[128,512]{1,0:T(8,128)}, u32[]{:S(2)}) copy-start(f32[128,512]{1,0:T(8,128)} %constant.220) | copy-start | bytes 786436
  32.7 11.0 %collective-permute-start.5 = (f32[16,128]{1,0:T(8,128)S(1)}, f32[16,128]{1,0:T(8,128)S(1)}, u32[]{:S(2)}, u32[]{:S(2)}) collective-permute-start(f32[16,128]{1,0:T(8,128)S(1)} %fusion.36), channel_id=1, source_target_pairs={{0,8},{8,16},{16,24},{24,0},{1,9},{9,17},{17,25},{25,1},{2,10},{10... | collective-permute-start | bytes 24584 | tf_op jit(solution)/shard_map/ppermute | solution.py:128
  33.1 10.7 %collective-permute-start.6 = (f32[16,128]{1,0:T(8,128)S(1)}, f32[16,128]{1,0:T(8,128)S(1)}, u32[]{:S(2)}, u32[]{:S(2)}) collective-permute-start(f32[16,128]{1,0:T(8,128)S(1)} %fusion.39), channel_id=1, source_target_pairs={{0,16},{8,24},{16,0},{24,8},{1,17},{9,25},{17,1},{25,9},{2,18},{10... | collective-permute-start | bytes 24584 | tf_op jit(solution)/shard_map/ppermute | solution.py:128
  34.3 1.2 %copy-start.2 = (bf16[1,128,3,256]{3,1,2,0:T(8,128)(2,1)S(1)}, bf16[1,128,3,256]{3,1,2,0:T(8,128)(2,1)}, u32[]{:S(2)}) copy-start(bf16[1,128,3,256]{3,1,2,0:T(8,128)(2,1)} %param.10) | copy-start | bytes 589828
  36.5 11.6 %collective-permute-start.4 = (bf16[1,128,3,256]{3,1,2,0:T(8,128)(2,1)S(1)}, bf16[1,128,3,256]{3,1,2,0:T(8,128)(2,1)S(1)}, u32[]{:S(2)}, u32[]{:S(2)}) collective-permute-start(bf16[1,128,3,256]{3,1,2,0:T(8,128)(2,1)S(1)} %pad_maximum_fusion.5), channel_id=1, source_target_pairs={{1,0},{2,1},{3,2},{4,3},{5,4},{6,5},{7,6},{9,8},{10,9},{11,10},{12... | collective-permute-start | bytes 589832 | tf_op jit(solution)/shard_map/ppermute | solution.py:22
  38.7 5.1 %collective-permute-start.7 = (f32[16,128]{1,0:T(8,128)S(1)}, f32[16,128]{1,0:T(8,128)S(1)}, u32[]{:S(2)}, u32[]{:S(2)}) collective-permute-start(f32[16,128]{1,0:T(8,128)S(1)} %fusion.42), channel_id=1, source_target_pairs={{0,24},{8,0},{16,8},{24,16},{1,25},{9,1},{17,9},{25,17},{2,26},{10... | collective-permute-start | bytes 24584 | tf_op jit(solution)/shard_map/ppermute | solution.py:128
  41.6 6.5 %collective-permute-start.3 = (bf16[1,128,256]{2,1,0:T(8,128)(2,1)S(1)}, bf16[1,128,256]{2,1,0:T(8,128)(2,1)S(1)}, u32[]{:S(2)}, u32[]{:S(2)}) collective-permute-start(bf16[1,128,256]{2,1,0:T(8,128)(2,1)S(1)} %get-tuple-element.42), channel_id=1, source_target_pairs={{0,1},{1,2},{2,3},{3,4},{4,5},{5,6},{6,7},{8,9},{9,10},{10,11},{11... | collective-permute-start | bytes 196616 | tf_op jit(solution)/shard_map/ppermute | solution.py:22

commit v14 on v5

--- a/solution.py
+++ b/solution.py
@@ -120,7 +120,7 @@
     for s in range(1, blocks):
         table = block_table(packed, (place + s) % blocks) * weight
         share = jnp.einsum("rf,tf->rt", fgs, table, precision=precise)
-        pairs = [(i, (i + s) % blocks) for i in range(blocks)]
+        pairs = [(i, (i + s) % blocks) for i in range(blocks) if i + (i + s) % blocks < blocks]
         lag = lag + lax.ppermute(share, "ctx", pairs)
     return out[:, :c], out[:, c:], lag
 

time: 43.4 us -> 46.5 us (1.071); the launches traced: 43.2 us -> 45.7 us
  starting transfers between devices: 17.6 us -> 20.1 us
    ppermute x3, starting transfers between devices: 8.37 us -> 10.8 us  [dense_path(): lag = lag + lax.ppermute(share, 'ctx', pairs)]
    ppermute x3, waiting for transfers between devices: 0.01 us -> 1.67 us  [dense_path(): lag = lag + lax.ppermute(share, 'ctx', pairs)]
    ppermute x2, waiting for transfers between devices: 3.58 us -> 1.93 us  [from_behind(): return lax.ppermute(x, axis, pairs)]
  transfers between devices with their start and end apart: 8 -> 8, of which waited for: 3 -> 4; matrix products, arithmetic and copies ran while one was open for 17% -> 16% of each run, Pallas kernels for 0% -> 0%
where the time goes in v14:
time: 46.5 us; the launch traced here: 45.7 us
  starting transfers between devices  20.1 us (43%)
  waiting for transfers between devices  11.5 us (25%)
  matrix products  6.62 us (14%)
  other arithmetic  3.98 us (9%)
  local copies, waits for them, and re-layouts  2.42 us (5%)
  between operations  1.03 us (2%)
    ppermute x3, starting transfers between devices, dense_path(): lag = lag + lax.ppermute(share, 'ctx', pairs)  10.8 us
    ppermute x3, waiting for transfers between devices, dense_path(): got = lax.ppermute(payload, 'ctx', pairs)  7.94 us
    ppermute x3, starting transfers between devices, dense_path(): got = lax.ppermute(payload, 'ctx', pairs)  4.68 us
    ppermute x2, starting transfers between devices, from_behind(): return lax.ppermute(x, axis, pairs)  4.61 us
    unnamed x19, local copies, waits for them, and re-layouts  2.27 us
    dot_general x3, matrix products, dense_path(): acc = acc + jnp.dot(got, table, precision=precise)  2.02 us
    ppermute x2, waiting for transfers between devices, from_behind(): return lax.ppermute(x, axis, pairs)  1.93 us
    ppermute x3, waiting for transfers between devices, dense_path(): lag = lag + lax.ppermute(share, 'ctx', pairs)  1.67 us
  transfers between devices with their start and end apart: 8, of which 4 were waited for; matrix products, arithmetic and copies ran while one was open for 16% of the time, Pallas kernels for 0%

profile of v14, /device:TPU:4, one launch (start us, length us, event | category | flops | bytes accessed | tf_op | source)
XLA Modules:
  0.0 45.7 jit_solution(2708243671259040957)
XLA Ops:
  0.6 0.0 copy-start.6
  0.6 0.0 copy-start.7
  0.7 0.0 copy-start
  0.7 0.0 copy-start.1
  0.7 0.0 copy-start.2
  0.7 0.0 copy-start.3
  0.7 0.0 copy-start.4
  0.7 0.0 copy-start.5
  0.7 0.9 %copy.12 = f32[1,16,128]{1,2,0:T(8,128)S(1)} copy(f32[1,16,128]{2,1,0:T(8,128)} %param.13) | data formatting | bytes 16384 | tf_op args[4]
  1.7 1.0 %broadcast_select_fusion.2 = (f32[256,128]{0,1:T(8,128)S(1)}, f32[256,128]{0,1:T(8,128)S(1)}, f32[256,128]{0,1:T(8,128)S(1)}) fusion(pred[]{:T(512)S(6)} %lt.96, bf16[1,128,3,256]{3,1,2,0:T(8,128)(2,1)} %param.10, bf16[1,128,256]{2,1,0:T(8,128)(2,1)} %param.12, bf16[1,128,3,256]{3,1,2,0:T(8,128)(2,1)} %param.9, pred[]{:T(512)S(6)} %lt.99, pred[]{:T(512)S(6)} %lt.102), kind=kLoop, calls=%fused_computation.109 | loop fusion | flops 294912 | bytes 655363 | tf_op jit(solution)/shard_map/jit(_where)/select_n | solution.py:97
  2.7 2.7 %collective-permute-start.1 = (f32[272,128]{0,1:T(8,128)S(1)}, f32[272,128]{0,1:T(8,128)S(1)}, u32[]{:S(2)}, u32[]{:S(2)}) collective-permute-start(f32[272,128]{0,1:T(8,128)S(1)} %get-tuple-element.46), channel_id=1, source_target_pairs={{0,16},{8,24},{16,0},{24,8},{1,17},{9,25},{17,1},{25,9},{2,18},{10... | collective-permute-start | bytes 417800 | tf_op jit(solution)/shard_map/ppermute | solution.py:100
  5.3 1.3 %collective-permute-start.2 = (f32[272,128]{0,1:T(8,128)S(1)}, f32[272,128]{0,1:T(8,128)S(1)}, u32[]{:S(2)}, u32[]{:S(2)}) collective-permute-start(f32[272,128]{0,1:T(8,128)S(1)} %get-tuple-element.47), channel_id=1, source_target_pairs={{0,24},{8,0},{16,8},{24,16},{1,25},{9,1},{17,9},{25,17},{2,26},{10... | collective-permute-start | bytes 417800 | tf_op jit(solution)/shard_map/ppermute | solution.py:100
  6.7 0.7 %collective-permute-start = (f32[272,128]{0,1:T(8,128)S(1)}, f32[272,128]{0,1:T(8,128)S(1)}, u32[]{:S(2)}, u32[]{:S(2)}) collective-permute-start(f32[272,128]{0,1:T(8,128)S(1)} %get-tuple-element.45), channel_id=1, source_target_pairs={{0,8},{8,16},{16,24},{24,0},{1,9},{9,17},{17,25},{25,1},{2,10},{10... | collective-permute-start | bytes 417800 | tf_op jit(solution)/shard_map/ppermute | solution.py:100
  7.4 0.0 copy-done.2
  7.4 0.9 %fusion.49 = (f32[256,128]{0,1:T(8,128)S(1)}, f32[256,128]{0,1:T(8,128)S(1)}) fusion(bf16[1,128,256]{2,1,0:T(8,128)(2,1)} %param.12, bf16[1,128,3,256]{3,1,2,0:T(8,128)(2,1)S(1)} %copy-done.2), kind=kLoop, calls=%fused_computation.92 | loop fusion | flops 196608 | bytes 524288 | tf_op jit(solution)/shard_map/transpose | solution.py:193
  8.3 0.0 copy-done.4
  8.3 0.0 copy-done.3
  8.3 0.0 copy-done.5
  8.4 0.0 copy-done.6
  8.4 0.0 copy-done.7
  8.4 0.0 copy-done
  8.5 0.0 copy-done.1
  8.5 0.1 multiply_subtract_fusion.5
  8.6 0.5 %multiply_subtract_fusion.9 = (f32[128,512]{1,0:T(8,128)S(1)}, f32[128,512]{1,0:T(8,128)S(1)}, f32[128,512]{1,0:T(8,128)S(1)}, f32[128,512]{1,0:T(8,128)S(1)}, f...) fusion(f32[128,512]{1,0:T(8,128)S(1)} %copy-done.1, ...), kind=kLoop, calls=%fused_computation.84 | loop fusion | flops 3407872 | bytes 3696256 | tf_op jit(solution)/shard_map/sub | solution.py:71
  9.1 1.5 %fusion.35 = f32[784,1024]{1,0:T(8,128)S(1)} fusion(f32[16,128]{0,1:T(8,128)S(1)} %bitcast.90, f32[256,128]{0,1:T(8,128)S(1)} %get-tuple-element.44, f32[256,128]{0,1:T(8,128)S(1)} %get-tuple-element.43, f32[256,128]{0,1:T(8,128)S(1)} %multiply_bitcast_fusion, f32[128,512]{1,0:T(8,128)S(1)} %get-tuple-element.26, f32[128,512]{1,0:T(8,128)S(1)} %get-tuple-element.25), kind=kOutput, calls=%fused_computation.53 | convolution fusion | flops 616994816 | bytes 4136960 | tf_op jit(solution)/shard_map/dot_general | solution.py:105
  10.6 6.1 %collective-permute-done.1 = f32[272,128]{0,1:T(8,128)S(1)} collective-permute-done((f32[272,128]{0,1:T(8,128)S(1)}, f32[272,128]{0,1:T(8,128)S(1)}, u32[]{:S(2)}, u32[]{:S(2)}) %collective-permute-start.1) | collective-permute-done | bytes 139296 | tf_op jit(solution)/shard_map/ppermute | solution.py:100
  16.7 0.6 %fusion.16 = f32[272,1024]{1,0:T(8,128)S(1)} fusion(f32[272,128]{0,1:T(8,128)S(1)} %collective-permute-done.1, f32[128,512]{1,0:T(8,128)S(1)} %get-tuple-element.35, f32[128,512]{1,0:T(8,128)S(1)} %get-tuple-element.36), kind=kOutput, calls=%fused_computation.23 | convolution fusion | flops 214040576 | bytes 1777664 | tf_op jit(solution)/shard_map/dot_general | solution.py:102
  17.4 0.0 collective-permute-done.2
  17.4 0.7 %fusion.20 = f32[272,1024]{1,0:T(8,128)S(1)} fusion(f32[272,128]{0,1:T(8,128)S(1)} %collective-permute-done.2, f32[128,512]{1,0:T(8,128)S(1)} %get-tuple-element.24, f32[128,512]{1,0:T(8,128)S(1)} %get-tuple-element.23), kind=kOutput, calls=%fused_computation.27 | convolution fusion | flops 214040576 | bytes 1777664 | tf_op jit(solution)/shard_map/dot_general | solution.py:102
  18.1 1.8 %collective-permute-done = f32[272,128]{0,1:T(8,128)S(1)} collective-permute-done((f32[272,128]{0,1:T(8,128)S(1)}, f32[272,128]{0,1:T(8,128)S(1)}, u32[]{:S(2)}, u32[]{:S(2)}) %collective-permute-start) | collective-permute-done | bytes 139296 | tf_op jit(solution)/shard_map/ppermute | solution.py:100
  19.9 0.7 %fusion.8 = f32[272,1024]{1,0:T(8,128)S(1)} fusion(f32[272,1024]{1,0:T(8,128)S(1)} %fusion.20, f32[272,1024]{1,0:T(8,128)S(1)} %fusion.16, f32[272,128]{0,1:T(8,128)S(1)} %collective-permute-done, f32[128,512]{1,0:T(8,128)S(1)} %get-tuple-element.33, f32[128,512]{1,0:T(8,128)S(1)} %get-tuple-element.34), kind=kOutput, calls=%fused_computation.9 | convolution fusion | flops 214597632 | bytes 4005888 | tf_op jit(solution)/shard_map/dot_general | solution.py:102
  20.6 0.4 slice_add_fusion.1
  21.1 0.1 broadcast_in_dim.26
  21.2 0.4 multiply_subtract_fusion
  21.6 0.2 bitcast_reduce_fusion
  21.8 0.3 fusion.24
  22.1 6.2 %collective-permute-start.5 = (f32[16,128]{1,0:T(8,128)S(1)}, f32[16,128]{1,0:T(8,128)S(1)}, u32[]{:S(2)}, u32[]{:S(2)}) collective-permute-start(f32[16,128]{1,0:T(8,128)S(1)} %fusion.24), channel_id=1, source_target_pairs={{0,8},{8,16},{24,0},{1,9},{9,17},{25,1},{2,10},{10,18},{26,2},{3,1... | collective-permute-start | bytes 24584 | tf_op jit(solution)/shard_map/ppermute | solution.py:124
  28.3 0.3 fusion.27
  28.7 2.7 %collective-permute-start.6 = (f32[16,128]{1,0:T(8,128)S(1)}, f32[16,128]{1,0:T(8,128)S(1)}, u32[]{:S(2)}, u32[]{:S(2)}) collective-permute-start(f32[16,128]{1,0:T(8,128)S(1)} %fusion.27), channel_id=1, source_target_pairs={{0,16},{16,0},{1,17},{17,1},{2,18},{18,2},{3,19},{19,3},{4,20},{20... | collective-permute-start | bytes 24584 | tf_op jit(solution)/shard_map/ppermute | solution.py:124
  31.4 0.2 select_subtract_fusion
  31.6 1.2 %fusion = f32[128,512]{1,0:T(8,128)S(1)} fusion(f32[256,512]{1,0:T(8,128)S(1)} %get-tuple-element.11, f32[256,512]{1,0:T(8,128)S(1)} %get-tuple-element.12, f32[256,512]{1,0:T(8,128)S(1)} %get-tuple-element.8, f32[256,512]{1,0:T(8,128)S(1)} %get-tuple-element.7, f32[128,512]{1,0:T(8,128)S(1)} %get-tuple-element.26, f32[128,512]{1,0:T(8,128)S(1)} %get-tuple-element.25, ...), kind=kOutput, calls=%fused_computation | convolution fusion | flops 404488192 | bytes 2887680 | tf_op jit(solution)/shard_map/tf,rf->tr/dot_general | solution.py:118
  32.8 0.1 fusion.58
  32.9 2.7 %collective-permute-start.4 = (bf16[1,128,3,256]{3,1,2,0:T(8,128)(2,1)S(1)}, bf16[1,128,3,256]{3,1,2,0:T(8,128)(2,1)S(1)}, u32[]{:S(2)}, u32[]{:S(2)}) collective-permute-start(bf16[1,128,3,256]{3,1,2,0:T(8,128)(2,1)S(1)} %pad_maximum_fusion.8), channel_id=1, source_target_pairs={{1,0},{2,1},{3,2},{4,3},{5,4},{6,5},{7,6},{9,8},{10,9},{11,10},{12... | collective-permute-start | bytes 589832 | tf_op jit(solution)/shard_map/ppermute | solution.py:22
  35.6 0.3 fusion.30
  36.0 1.9 %collective-permute-start.7 = (f32[16,128]{1,0:T(8,128)S(1)}, f32[16,128]{1,0:T(8,128)S(1)}, u32[]{:S(2)}, u32[]{:S(2)}) collective-permute-start(f32[16,128]{1,0:T(8,128)S(1)} %fusion.30), channel_id=1, source_target_pairs={{0,24},{8,0},{16,8},{1,25},{9,1},{17,9},{2,26},{10,2},{18,10},{3,2... | collective-permute-start | bytes 24584 | tf_op jit(solution)/shard_map/ppermute | solution.py:124
  37.9 1.9 %collective-permute-start.3 = (bf16[1,128,256]{2,1,0:T(8,128)(2,1)S(1)}, bf16[1,128,256]{2,1,0:T(8,128)(2,1)S(1)}, u32[]{:S(2)}, u32[]{:S(2)}) collective-permute-start(bf16[1,128,256]{2,1,0:T(8,128)(2,1)S(1)} %get-tuple-element.42), channel_id=1, source_target_pairs={{0,1},{1,2},{2,3},{3,4},{4,5},{5,6},{6,7},{8,9},{9,10},{10,11},{11... | collective-permute-start | bytes 196616 | tf_op jit(solution)/shard_map/ppermute | solution.py:22
  39.8 0.0 collective-permute-done.5
  39.8 0.0 collective-permute-done.6
  39.8 1.7 %collective-permute-done.7 = f32[16,128]{1,0:T(8,128)S(1)} collective-permute-done((f32[16,128]{1,0:T(8,128)S(1)}, f32[16,128]{1,0:T(8,128)S(1)}, u32[]{:S(2)}, u32[]{:S(2)}) %collective-permute-start.7) | collective-permute-done | bytes 8224 | tf_op jit(solution)/shard_map/ppermute | solution.py:124
  41.5 0.9 %fusion.12 = f32[1,16,128]{2,1,0:T(8,128)} fusion(f32[16,128]{1,0:T(8,128)S(1)} %collective-permute-done.7, f32[16,128]{1,0:T(8,128)S(1)} %collective-permute-done.6, f32[16,128]{1,0:T(8,128)S(1)} %collective-permute-done.5, f32[16,1024]{1,0:T(8,128)S(1)} %bitcast_reduce_fusion, f32[128,512]{1,0:T(8,128)S(1)} %get-tuple-element.26, ...), kind=kOutput, calls=%fused_computation.14 | convolution fusion | flops 12853248 | bytes 626688 | tf_op jit(solution)/shard_map/rf,tf->rt/dot_general | solution.py:119
  42.4 1.9 %collective-permute-done.3 = bf16[1,128,256]{2,1,0:T(8,128)(2,1)S(1)} collective-permute-done((bf16[1,128,256]{2,1,0:T(8,128)(2,1)S(1)}, bf16[1,128,256]{2,1,0:T(8,128)(2,1)S(1)}, u32[]{:S(2)}, u32[]{:S(2)}) %collective-permute-start.3) | collective-permute-done | bytes 65568 | tf_op jit(solution)/shard_map/ppermute | solution.py:22
  44.4 0.0 collective-permute-done.4
  44.4 0.6 %copy.15 = bf16[1,128,256]{2,1,0:T(8,128)(2,1)} copy(bf16[1,128,256]{2,1,0:T(8,128)(2,1)S(1)} %collective-permute-done.3) | data formatting | bytes 131072
  45.0 0.7 %copy.16 = bf16[1,128,3,256]{3,1,2,0:T(8,128)(2,1)} copy(bf16[1,128,3,256]{3,1,2,0:T(8,128)(2,1)S(1)} %collective-permute-done.4) | data formatting | bytes 393216
  (10 shorter events, 0.2 us)
Async XLA Ops:
  0.6 7.8 %copy-start.6 = (f32[4,512]{1,0:T(4,128)S(1)}, f32[4,512]{1,0:T(4,128)}, u32[]{:S(2)}) copy-start(f32[4,512]{1,0:T(4,128)} %constant.139.clone) | copy-start | bytes 24580
  0.6 7.8 %copy-start.7 = (f32[4,512]{1,0:T(4,128)S(1)}, f32[4,512]{1,0:T(4,128)}, u32[]{:S(2)}) copy-start(f32[4,512]{1,0:T(4,128)} %constant.140.clone) | copy-start | bytes 24580
  0.7 7.8 %copy-start = (f32[128,512]{1,0:T(8,128)S(1)}, f32[128,512]{1,0:T(8,128)}, u32[]{:S(2)}) copy-start(f32[128,512]{1,0:T(8,128)} %constant.137.clone) | copy-start | bytes 786436
  0.7 7.8 %copy-start.1 = (f32[128,512]{1,0:T(8,128)S(1)}, f32[128,512]{1,0:T(8,128)}, u32[]{:S(2)}) copy-start(f32[128,512]{1,0:T(8,128)} %constant.138.clone) | copy-start | bytes 786436
  0.7 6.7 %copy-start.2 = (bf16[1,128,3,256]{3,1,2,0:T(8,128)(2,1)S(1)}, bf16[1,128,3,256]{3,1,2,0:T(8,128)(2,1)}, u32[]{:S(2)}) copy-start(bf16[1,128,3,256]{3,1,2,0:T(8,128)(2,1)} %param.10) | copy-start | bytes 589828
  0.7 7.6 %copy-start.3 = (bf16[1,128,256]{2,1,0:T(8,128)(2,1)S(1)}, bf16[1,128,256]{2,1,0:T(8,128)(2,1)}, u32[]{:S(2)}) copy-start(bf16[1,128,256]{2,1,0:T(8,128)(2,1)} %param.12) | copy-start | bytes 196612
  0.7 7.6 %copy-start.4 = (bf16[1,128,3,256]{3,1,2,0:T(8,128)(2,1)S(1)}, bf16[1,128,3,256]{3,1,2,0:T(8,128)(2,1)}, u32[]{:S(2)}) copy-start(bf16[1,128,3,256]{3,1,2,0:T(8,128)(2,1)} %param.9) | copy-start | bytes 589828
  0.7 7.6 %copy-start.5 = (f32[1,128,256]{2,1,0:T(8,128)S(1)}, f32[1,128,256]{2,1,0:T(8,128)}, u32[]{:S(2)}) copy-start(f32[1,128,256]{2,1,0:T(8,128)} %param.11) | copy-start | bytes 393220
  2.7 14.1 %collective-permute-start.1 = (f32[272,128]{0,1:T(8,128)S(1)}, f32[272,128]{0,1:T(8,128)S(1)}, u32[]{:S(2)}, u32[]{:S(2)}) collective-permute-start(f32[272,128]{0,1:T(8,128)S(1)} %get-tuple-element.46), channel_id=1, source_target_pairs={{0,16},{8,24},{16,0},{24,8},{1,17},{9,25},{17,1},{25,9},{2,18},{10... | collective-permute-start | bytes 417800 | tf_op jit(solution)/shard_map/ppermute | solution.py:100
  5.3 12.1 %collective-permute-start.2 = (f32[272,128]{0,1:T(8,128)S(1)}, f32[272,128]{0,1:T(8,128)S(1)}, u32[]{:S(2)}, u32[]{:S(2)}) collective-permute-start(f32[272,128]{0,1:T(8,128)S(1)} %get-tuple-element.47), channel_id=1, source_target_pairs={{0,24},{8,0},{16,8},{24,16},{1,25},{9,1},{17,9},{25,17},{2,26},{10... | collective-permute-start | bytes 417800 | tf_op jit(solution)/shard_map/ppermute | solution.py:100
  6.7 13.2 %collective-permute-start = (f32[272,128]{0,1:T(8,128)S(1)}, f32[272,128]{0,1:T(8,128)S(1)}, u32[]{:S(2)}, u32[]{:S(2)}) collective-permute-start(f32[272,128]{0,1:T(8,128)S(1)} %get-tuple-element.45), channel_id=1, source_target_pairs={{0,8},{8,16},{16,24},{24,0},{1,9},{9,17},{17,25},{25,1},{2,10},{10... | collective-permute-start | bytes 417800 | tf_op jit(solution)/shard_map/ppermute | solution.py:100
  22.1 17.7 %collective-permute-start.5 = (f32[16,128]{1,0:T(8,128)S(1)}, f32[16,128]{1,0:T(8,128)S(1)}, u32[]{:S(2)}, u32[]{:S(2)}) collective-permute-start(f32[16,128]{1,0:T(8,128)S(1)} %fusion.24), channel_id=1, source_target_pairs={{0,8},{8,16},{24,0},{1,9},{9,17},{25,1},{2,10},{10,18},{26,2},{3,1... | collective-permute-start | bytes 24584 | tf_op jit(solution)/shard_map/ppermute | solution.py:124
  28.7 11.2 %collective-permute-start.6 = (f32[16,128]{1,0:T(8,128)S(1)}, f32[16,128]{1,0:T(8,128)S(1)}, u32[]{:S(2)}, u32[]{:S(2)}) collective-permute-start(f32[16,128]{1,0:T(8,128)S(1)} %fusion.27), channel_id=1, source_target_pairs={{0,16},{16,0},{1,17},{17,1},{2,18},{18,2},{3,19},{19,3},{4,20},{20... | collective-permute-start | bytes 24584 | tf_op jit(solution)/shard_map/ppermute | solution.py:124
  32.9 11.4 %collective-permute-start.4 = (bf16[1,128,3,256]{3,1,2,0:T(8,128)(2,1)S(1)}, bf16[1,128,3,256]{3,1,2,0:T(8,128)(2,1)S(1)}, u32[]{:S(2)}, u32[]{:S(2)}) collective-permute-start(bf16[1,128,3,256]{3,1,2,0:T(8,128)(2,1)S(1)} %pad_maximum_fusion.8), channel_id=1, source_target_pairs={{1,0},{2,1},{3,2},{4,3},{5,4},{6,5},{7,6},{9,8},{10,9},{11,10},{12... | collective-permute-start | bytes 589832 | tf_op jit(solution)/shard_map/ppermute | solution.py:22
  36.0 5.5 %collective-permute-start.7 = (f32[16,128]{1,0:T(8,128)S(1)}, f32[16,128]{1,0:T(8,128)S(1)}, u32[]{:S(2)}, u32[]{:S(2)}) collective-permute-start(f32[16,128]{1,0:T(8,128)S(1)} %fusion.30), channel_id=1, source_target_pairs={{0,24},{8,0},{16,8},{1,25},{9,1},{17,9},{2,26},{10,2},{18,10},{3,2... | collective-permute-start | bytes 24584 | tf_op jit(solution)/shard_map/ppermute | solution.py:124
  37.9 6.5 %collective-permute-start.3 = (bf16[1,128,256]{2,1,0:T(8,128)(2,1)S(1)}, bf16[1,128,256]{2,1,0:T(8,128)(2,1)S(1)}, u32[]{:S(2)}, u32[]{:S(2)}) collective-permute-start(bf16[1,128,256]{2,1,0:T(8,128)(2,1)S(1)} %get-tuple-element.42), channel_id=1, source_target_pairs={{0,1},{1,2},{2,3},{3,4},{4,5},{5,6},{6,7},{8,9},{9,10},{10,11},{11... | collective-permute-start | bytes 196616 | tf_op jit(solution)/shard_map/ppermute | solution.py:22

commit v15 on v5

--- a/solution.py
+++ b/solution.py
@@ -18,8 +18,10 @@
 
 def from_behind(x, axis, by):
     devices = lax.axis_size(axis)
-    pairs = [(i, i + by) for i in range(devices) if 0 <= i + by < devices]
-    return lax.ppermute(x, axis, pairs)
+    pairs = [(i, (i + by) % devices) for i in range(devices)]
+    got = lax.ppermute(x, axis, pairs)
+    source = lax.axis_index(axis) - by
+    return jnp.where((source >= 0) & (source < devices), got, jnp.zeros_like(got))
 
 
 def inner_tables(block):

time: 43.4 us -> 45.8 us (1.055)
  the two profiles are of different devices: /device:TPU:4 before, /device:TPU:0 now
where the time goes in v15:
time: 45.8 us; the launch traced here: 45.5 us
  starting transfers between devices  16 us (35%)
  other arithmetic  10.7 us (23%)
  matrix products  9.81 us (21%)
  waiting for transfers between devices  5.78 us (13%)
  local copies, waits for them, and re-layouts  2.23 us (5%)
  between operations  0.99 us (2%)
    ppermute x3, starting transfers between devices, dense_path(): lag = lag + lax.ppermute(share, 'ctx', pairs)  8.64 us
    ppermute x3, starting transfers between devices, dense_path(): got = lax.ppermute(payload, 'ctx', pairs)  6.06 us
    dot_general x3, matrix products, dense_path(): acc = acc + jnp.dot(got, table, precision=precise)  5.19 us
    ppermute x2, waiting for transfers between devices, from_behind(): got = lax.ppermute(x, axis, pairs)  4.34 us
    sub x2, other arithmetic, block_table(): cos = base_c * c - base_s * s  2.62 us
    transpose x2, other arithmetic, on_device(): conv, grad_mixed, lag = dense_path(place, blocks, mixed_in.T, weighted.T,...  2.23 us
    unnamed x47, local copies, waits for them, and re-layouts  2.09 us
    another operation x3, other arithmetic, finish(): jnp.stack([grad_query, grad_key, grad_value], axis=1).astype(jnp.bfloat16)  1.56 us
  transfers between devices with their start and end apart: 8, of which 3 were waited for; matrix products, arithmetic and copies ran while one was open for 33% of the time, Pallas kernels for 0%

profile of v15, /device:TPU:0, one launch (start us, length us, event | category | flops | bytes accessed | tf_op | source)
XLA Modules:
  0.0 45.5 jit_solution(8343404622612677546)
XLA Ops:
  0.6 0.0 copy-start.21
  0.6 0.0 copy-start.22
  0.7 0.0 copy-start.10
  0.7 0.0 copy-start.11
  0.7 0.0 copy-start.12
  0.7 0.0 copy-start.14
  0.7 0.0 copy-start.15
  0.7 0.0 copy-start.20
  0.7 0.9 %copy.12 = f32[1,16,128]{1,2,0:T(8,128)S(1)} copy(f32[1,16,128]{2,1,0:T(8,128)} %param.13) | data formatting | bytes 16384 | tf_op args[4]
  1.7 1.0 %broadcast_select_fusion.3 = (f32[256,128]{0,1:T(8,128)S(1)}, f32[256,128]{0,1:T(8,128)S(1)}, f32[256,128]{0,1:T(8,128)S(1)}) fusion(pred[]{:T(512)S(6)} %lt.103, bf16[1,128,3,256]{3,1,2,0:T(8,128)(2,1)} %param.10, bf16[1,128,256]{2,1,0:T(8,128)(2,1)} %param.12, bf16[1,128,3,256]{3,1,2,0:T(8,128)(2,1)} %param.9, pred[]{:T(512)S(6)} %lt.106, pred[]{:T(512)S(6)} %lt.109), kind=kLoop, calls=%fused_computation.110 | loop fusion | flops 294912 | bytes 655363 | tf_op jit(solution)/shard_map/jit(_where)/select_n | solution.py:99
  2.6 0.8 %pad_maximum_fusion.7 = (f32[272,128]{0,1:T(8,128)}, f32[272,128]{0,1:T(8,128)}, f32[272,128]{0,1:T(8,128)}) fusion(f32[16,128]{0,1:T(8,128)S(1)} %bitcast.89, f32[256,128]{0,1:T(8,128)S(1)} %get-tuple-element.39, f32[256,128]{0,1:T(8,128)S(1)} %get-tuple-element.40, f32[256,128]{0,1:T(8,128)S(1)} %get-tuple-element.41), kind=kLoop, calls=%fused_computation.64 | loop fusion | flops 104448 | bytes 819200 | tf_op jit(solution)/shard_map/concatenate | solution.py:100
  3.5 4.0 %collective-permute-start.1 = (f32[272,128]{0,1:T(8,128)}, f32[272,128]{0,1:T(8,128)}, u32[]{:S(2)}, u32[]{:S(2)}) collective-permute-start(f32[272,128]{0,1:T(8,128)} %get-tuple-element.46), channel_id=1, source_target_pairs={{0,16},{8,24},{16,0},{24,8},{1,17},{9,25},{17,1},{25,9},{2,18},{10... | collective-permute-start | bytes 417800 | tf_op jit(solution)/shard_map/ppermute | solution.py:102
  7.5 1.3 %collective-permute-start.2 = (f32[272,128]{0,1:T(8,128)}, f32[272,128]{0,1:T(8,128)}, u32[]{:S(2)}, u32[]{:S(2)}) collective-permute-start(f32[272,128]{0,1:T(8,128)} %get-tuple-element.47), channel_id=1, source_target_pairs={{0,24},{8,0},{16,8},{24,16},{1,25},{9,1},{17,9},{25,17},{2,26},{10... | collective-permute-start | bytes 417800 | tf_op jit(solution)/shard_map/ppermute | solution.py:102
  8.8 0.7 %collective-permute-start = (f32[272,128]{0,1:T(8,128)}, f32[272,128]{0,1:T(8,128)}, u32[]{:S(2)}, u32[]{:S(2)}) collective-permute-start(f32[272,128]{0,1:T(8,128)} %get-tuple-element.45), channel_id=1, source_target_pairs={{0,8},{8,16},{16,24},{24,0},{1,9},{9,17},{17,25},{25,1},{2,10},{10... | collective-permute-start | bytes 417800 | tf_op jit(solution)/shard_map/ppermute | solution.py:102
  9.5 0.0 copy-done.12
  9.5 1.6 %fusion.49 = (f32[256,128]{0,1:T(8,128)}, f32[256,128]{0,1:T(8,128)}) fusion(bf16[1,128,256]{2,1,0:T(8,128)(2,1)} %param.12, bf16[1,128,3,256]{3,1,2,0:T(8,128)(2,1)S(1)} %copy-done.12), kind=kLoop, calls=%fused_computation.93 | loop fusion | flops 196608 | bytes 524288 | tf_op jit(solution)/shard_map/transpose | solution.py:195
  11.1 0.0 copy-done.15
  11.1 0.7 %multiply_bitcast_fusion = f32[256,128]{0,1:T(8,128)} fusion(bf16[1,128,3,256]{3,1,2,0:T(8,128)(2,1)S(1)} %copy-done.15), kind=kLoop, calls=%fused_computation.102 | loop fusion | flops 98304 | bytes 262144 | tf_op jit(solution)/shard_map/transpose | solution.py:195
  11.8 0.0 copy-done.14
  11.8 0.0 copy-done.20
  11.8 0.6 %fusion.59 = bf16[1,128,1,256]{3,1,2,0:T(8,128)(2,1)} fusion(f32[1,128,256]{2,1,0:T(8,128)S(1)} %copy-done.20, bf16[1,128,256]{2,1,0:T(8,128)(2,1)S(1)} %copy-done.14), kind=kLoop, calls=%fused_computation.106 | loop fusion | flops 98304 | bytes 262144 | tf_op jit(solution)/shard_map/stack | solution.py:165
  12.4 0.0 copy-done.21
  12.4 0.0 copy-done.22
  12.5 0.9 %multiply_subtract_fusion.5 = (f32[128,512]{1,0:T(8,128)}, f32[128,512]{1,0:T(8,128)}) fusion(f32[128,512]{1,0:T(8,128)S(1)} %copy-done.11, f32[128,512]{1,0:T(8,128)S(1)} %copy-done.10, f32[512]{0:T(512)S(1)} %bitcast.103, f32[512]{0:T(512)S(1)} %bitcast.104, s32[128]{0:T(128)S(1)} %get-tuple-element.69, s32[128]{0:T(128)S(1)} %get-tuple-element.70, ...), kind=kLoop, calls=%fused_computation.72 | loop fusion | flops 786432 | bytes 1054336 | tf_op jit(solution)/shard_map/sub | solution.py:73
  13.4 1.8 %multiply_subtract_fusion.9 = (f32[128,512]{1,0:T(8,128)S(1)}, f32[128,512]{1,0:T(8,128)S(1)}, f32[128,512]{1,0:T(8,128)}, f32[128,512]{1,0:T(8,128)}, f32[128,5...) fusion(f32[128,512]{1,0:T(8,128)S(1)} %copy-done.11, ...), kind=kLoop, calls=%fused_computation.84 | loop fusion | flops 3407872 | bytes 3696256 | tf_op jit(solution)/shard_map/sub | solution.py:73
  15.1 0.7 %copy-done = f32[128,512]{1,0:T(8,128)} copy-done((f32[128,512]{1,0:T(8,128)}, f32[128,512]{1,0:T(8,128)S(1)}, u32[]{:S(2)}) %copy-start) | copy-done | bytes 262168
  15.8 1.5 %fusion.35 = f32[784,1024]{1,0:T(8,128)S(1)} fusion(f32[16,128]{0,1:T(8,128)S(1)} %bitcast.90, f32[256,128]{0,1:T(8,128)S(1)} %copy-done.18, f32[256,128]{0,1:T(8,128)S(1)} %copy-done.17, f32[256,128]{0,1:T(8,128)S(1)} %copy-done.16, f32[128,512]{1,0:T(8,128)S(1)} %get-tuple-element.26, f32[128,512]{1,0:T(8,128)S(1)} %get-tuple-element.25), kind=kOutput, calls=%fused_computation.53 | convolution fusion | flops 616994816 | bytes 4136960 | tf_op jit(solution)/shard_map/dot_general | solution.py:107
  17.3 1.3 %collective-permute-done.1 = f32[272,128]{0,1:T(8,128)} collective-permute-done((f32[272,128]{0,1:T(8,128)}, f32[272,128]{0,1:T(8,128)}, u32[]{:S(2)}, u32[]{:S(2)}) %collective-permute-start.1) | collective-permute-done | bytes 139296 | tf_op jit(solution)/shard_map/ppermute | solution.py:102
  18.7 1.8 %fusion.16 = f32[272,1024]{1,0:T(8,128)S(1)} fusion(f32[272,128]{0,1:T(8,128)} %collective-permute-done.1, f32[128,512]{1,0:T(8,128)} %get-tuple-element.35, f32[128,512]{1,0:T(8,128)} %get-tuple-element.36), kind=kOutput, calls=%fused_computation.23 | convolution fusion | flops 214040576 | bytes 1777664 | tf_op jit(solution)/shard_map/dot_general | solution.py:104
  20.5 0.0 collective-permute-done.2
  20.5 1.8 %fusion.20 = f32[272,1024]{1,0:T(8,128)S(1)} fusion(f32[272,128]{0,1:T(8,128)} %collective-permute-done.2, f32[128,512]{1,0:T(8,128)} %get-tuple-element.24, f32[128,512]{1,0:T(8,128)} %get-tuple-element.23), kind=kOutput, calls=%fused_computation.27 | convolution fusion | flops 214040576 | bytes 1777664 | tf_op jit(solution)/shard_map/dot_general | solution.py:104
  22.2 0.1 collective-permute-done
  22.4 0.0 copy-done.2
  22.4 1.6 %fusion.8 = f32[272,1024]{1,0:T(8,128)S(1)} fusion(f32[272,1024]{1,0:T(8,128)S(1)} %fusion.20, f32[272,1024]{1,0:T(8,128)S(1)} %fusion.16, f32[272,128]{0,1:T(8,128)} %collective-permute-done, f32[128,512]{1,0:T(8,128)S(1)} %copy-done.2, f32[128,512]{1,0:T(8,128)S(1)} %copy-done.3), kind=kOutput, calls=%fused_computation.9 | convolution fusion | flops 214597632 | bytes 4005888 | tf_op jit(solution)/shard_map/dot_general | solution.py:104
  24.0 0.3 slice_add_fusion.1
  24.3 0.1 broadcast_in_dim.32
  24.5 0.4 multiply_subtract_fusion
  24.9 0.2 bitcast_reduce_fusion
  25.1 0.3 copy-done.8
  25.4 0.1 copy-done.9
  25.5 0.3 fusion.24
  25.8 5.4 %collective-permute-start.5 = (f32[16,128]{1,0:T(8,128)S(1)}, f32[16,128]{1,0:T(8,128)S(1)}, u32[]{:S(2)}, u32[]{:S(2)}) collective-permute-start(f32[16,128]{1,0:T(8,128)S(1)} %fusion.24), channel_id=1, source_target_pairs={{0,8},{8,16},{16,24},{24,0},{1,9},{9,17},{17,25},{25,1},{2,10},{10... | collective-permute-start | bytes 24584 | tf_op jit(solution)/shard_map/ppermute | solution.py:126
  31.2 0.3 fusion.27
  31.5 1.2 %collective-permute-start.6 = (f32[16,128]{1,0:T(8,128)S(1)}, f32[16,128]{1,0:T(8,128)S(1)}, u32[]{:S(2)}, u32[]{:S(2)}) collective-permute-start(f32[16,128]{1,0:T(8,128)S(1)} %fusion.27), channel_id=1, source_target_pairs={{0,16},{8,24},{16,0},{24,8},{1,17},{9,25},{17,1},{25,9},{2,18},{10... | collective-permute-start | bytes 24584 | tf_op jit(solution)/shard_map/ppermute | solution.py:126
  32.8 0.0 copy-done.5
  32.8 0.3 fusion.30
  33.1 2.0 %collective-permute-start.7 = (f32[16,128]{1,0:T(8,128)S(1)}, f32[16,128]{1,0:T(8,128)S(1)}, u32[]{:S(2)}, u32[]{:S(2)}) collective-permute-start(f32[16,128]{1,0:T(8,128)S(1)} %fusion.30), channel_id=1, source_target_pairs={{0,24},{8,0},{16,8},{24,16},{1,25},{9,1},{17,9},{25,17},{2,26},{10... | collective-permute-start | bytes 24584 | tf_op jit(solution)/shard_map/ppermute | solution.py:126
  35.1 0.2 select_subtract_fusion
  35.3 0.0 copy-done.1
  35.3 0.0 copy-start.13
  35.3 0.0 copy-start.19
  35.3 1.3 %fusion = f32[128,512]{1,0:T(8,128)S(1)} fusion(f32[256,512]{1,0:T(8,128)S(1)} %get-tuple-element.11, f32[256,512]{1,0:T(8,128)S(1)} %get-tuple-element.12, f32[256,512]{1,0:T(8,128)S(1)} %get-tuple-element.8, f32[256,512]{1,0:T(8,128)S(1)} %get-tuple-element.7, f32[128,512]{1,0:T(8,128)S(1)} %copy-done.1, f32[128,512]{1,0:T(8,128)S(1)} %get-tuple-element.25, ...), kind=kOutput, calls=%fused_computation | convolution fusion | flops 404488192 | bytes 2887680 | tf_op jit(solution)/shard_map/tf,rf->tr/dot_general | solution.py:120
  36.6 0.9 %fusion.58 = (bf16[1,128,1,256]{3,1,2,0:T(8,128)(2,1)S(1)}, bf16[1,128,1,256]{3,1,2,0:T(8,128)(2,1)S(1)}, bf16[1,128,256]{2,1,0:T(8,128)(2,1)S(1)}) fusion(f32[128,512]{1,0:T(8,128)S(1)} %fusion, bf16[1,128,3,256]{3,1,2,0:T(8,128)(2,1)S(1)} %copy-done.13, bf16[1,128,3,256]{3,1,2,0:T(8,128)(2,1)} %param.9), kind=kLoop, calls=%fused_computation.105 | loop fusion | flops 360448 | bytes 655360 | tf_op jit(solution)/shard_map/stack | solution.py:165
  37.5 0.0 copy-done.19
  37.6 1.3 %collective-permute-start.4 = (bf16[1,128,3,256]{3,1,2,0:T(8,128)(2,1)S(1)}, bf16[1,128,3,256]{3,1,2,0:T(8,128)(2,1)S(1)}, u32[]{:S(2)}, u32[]{:S(2)}) collective-permute-start(bf16[1,128,3,256]{3,1,2,0:T(8,128)(2,1)S(1)} %pad_maximum_fusion.8), channel_id=1, source_target_pairs={{0,7},{1,0},{2,1},{3,2},{4,3},{5,4},{6,5},{7,6},{8,15},{9,8},{10,9... | collective-permute-start | bytes 589832 | tf_op jit(solution)/shard_map/ppermute | solution.py:22
  38.8 0.0 collective-permute-start.3
  38.8 0.0 collective-permute-done.5
  38.8 0.0 collective-permute-done.6
  38.9 0.0 collective-permute-done.7
  38.9 1.0 %fusion.12 = f32[1,16,128]{2,1,0:T(8,128)} fusion(f32[16,128]{1,0:T(8,128)S(1)} %collective-permute-done.7, f32[16,128]{1,0:T(8,128)S(1)} %collective-permute-done.6, f32[16,128]{1,0:T(8,128)S(1)} %collective-permute-done.5, f32[16,1024]{1,0:T(8,128)S(1)} %bitcast_reduce_fusion, f32[128,512]{1,0:T(8,128)S(1)} %copy-done.1, ...), kind=kOutput, calls=%fused_computation.14 | convolution fusion | flops 12853248 | bytes 626688 | tf_op jit(solution)/shard_map/rf,tf->rt/dot_general | solution.py:121
  39.8 4.3 %collective-permute-done.3 = bf16[1,128,256]{2,1,0:T(8,128)(2,1)S(1)} collective-permute-done((bf16[1,128,256]{2,1,0:T(8,128)(2,1)S(1)}, bf16[1,128,256]{2,1,0:T(8,128)(2,1)S(1)}, u32[]{:S(2)}, u32[]{:S(2)}) %collective-permute-start.3) | collective-permute-done | bytes 65568 | tf_op jit(solution)/shard_map/ppermute | solution.py:22
  44.1 0.6 %broadcast_select_fusion.4 = bf16[1,128,256]{2,1,0:T(8,128)(2,1)} fusion(bf16[1,128,256]{2,1,0:T(8,128)(2,1)S(1)} %collective-permute-done.3, pred[]{:T(512)S(6)} %and.57), kind=kLoop, calls=%fused_computation.111 | loop fusion | flops 32768 | bytes 131073 | tf_op jit(solution)/shard_map/jit(_where)/select_n | solution.py:24
  44.8 0.0 collective-permute-done.4
  44.8 0.7 %broadcast_select_fusion = bf16[1,128,3,256]{3,1,2,0:T(8,128)(2,1)} fusion(bf16[1,128,3,256]{3,1,2,0:T(8,128)(2,1)S(1)} %collective-permute-done.4, pred[]{:T(512)S(6)} %and.62), kind=kLoop, calls=%fused_computation.86 | loop fusion | flops 98304 | bytes 393217 | tf_op jit(solution)/shard_map/jit(_where)/select_n | solution.py:24
  (30 shorter events, 0.1 us)
Async XLA Ops:
  0.6 11.8 %copy-start.21 = (f32[4,512]{1,0:T(4,128)S(1)}, f32[4,512]{1,0:T(4,128)}, u32[]{:S(2)}) copy-start(f32[4,512]{1,0:T(4,128)} %constant.151.clone) | copy-start | bytes 24580
  0.6 11.8 %copy-start.22 = (f32[4,512]{1,0:T(4,128)S(1)}, f32[4,512]{1,0:T(4,128)}, u32[]{:S(2)}) copy-start(f32[4,512]{1,0:T(4,128)} %constant.152.clone) | copy-start | bytes 24580
  0.7 11.8 %copy-start.10 = (f32[128,512]{1,0:T(8,128)S(1)}, f32[128,512]{1,0:T(8,128)}, u32[]{:S(2)}) copy-start(f32[128,512]{1,0:T(8,128)} %constant.149.clone) | copy-start | bytes 786436
  0.7 11.8 %copy-start.11 = (f32[128,512]{1,0:T(8,128)S(1)}, f32[128,512]{1,0:T(8,128)}, u32[]{:S(2)}) copy-start(f32[128,512]{1,0:T(8,128)} %constant.150.clone) | copy-start | bytes 786436
  0.7 8.9 %copy-start.12 = (bf16[1,128,3,256]{3,1,2,0:T(8,128)(2,1)S(1)}, bf16[1,128,3,256]{3,1,2,0:T(8,128)(2,1)}, u32[]{:S(2)}) copy-start(bf16[1,128,3,256]{3,1,2,0:T(8,128)(2,1)} %param.10) | copy-start | bytes 589828
  0.7 11.1 %copy-start.14 = (bf16[1,128,256]{2,1,0:T(8,128)(2,1)S(1)}, bf16[1,128,256]{2,1,0:T(8,128)(2,1)}, u32[]{:S(2)}) copy-start(bf16[1,128,256]{2,1,0:T(8,128)(2,1)} %param.12) | copy-start | bytes 196612
  0.7 10.4 %copy-start.15 = (bf16[1,128,3,256]{3,1,2,0:T(8,128)(2,1)S(1)}, bf16[1,128,3,256]{3,1,2,0:T(8,128)(2,1)}, u32[]{:S(2)}) copy-start(bf16[1,128,3,256]{3,1,2,0:T(8,128)(2,1)} %param.9) | copy-start | bytes 589828
  0.7 11.1 %copy-start.20 = (f32[1,128,256]{2,1,0:T(8,128)S(1)}, f32[1,128,256]{2,1,0:T(8,128)}, u32[]{:S(2)}) copy-start(f32[1,128,256]{2,1,0:T(8,128)} %param.11) | copy-start | bytes 393220
  3.5 15.2 %collective-permute-start.1 = (f32[272,128]{0,1:T(8,128)}, f32[272,128]{0,1:T(8,128)}, u32[]{:S(2)}, u32[]{:S(2)}) collective-permute-start(f32[272,128]{0,1:T(8,128)} %get-tuple-element.46), channel_id=1, source_target_pairs={{0,16},{8,24},{16,0},{24,8},{1,17},{9,25},{17,1},{25,9},{2,18},{10... | collective-permute-start | bytes 417800 | tf_op jit(solution)/shard_map/ppermute | solution.py:102
  7.5 13.0 %collective-permute-start.2 = (f32[272,128]{0,1:T(8,128)}, f32[272,128]{0,1:T(8,128)}, u32[]{:S(2)}, u32[]{:S(2)}) collective-permute-start(f32[272,128]{0,1:T(8,128)} %get-tuple-element.47), channel_id=1, source_target_pairs={{0,24},{8,0},{16,8},{24,16},{1,25},{9,1},{17,9},{25,17},{2,26},{10... | collective-permute-start | bytes 417800 | tf_op jit(solution)/shard_map/ppermute | solution.py:102
  8.8 13.5 %collective-permute-start = (f32[272,128]{0,1:T(8,128)}, f32[272,128]{0,1:T(8,128)}, u32[]{:S(2)}, u32[]{:S(2)}) collective-permute-start(f32[272,128]{0,1:T(8,128)} %get-tuple-element.45), channel_id=1, source_target_pairs={{0,8},{8,16},{16,24},{24,0},{1,9},{9,17},{17,25},{25,1},{2,10},{10... | collective-permute-start | bytes 417800 | tf_op jit(solution)/shard_map/ppermute | solution.py:102
  13.4 2.5 %copy-start.16 = (f32[256,128]{0,1:T(8,128)S(1)}, f32[256,128]{0,1:T(8,128)}, u32[]{:S(2)}) copy-start(f32[256,128]{0,1:T(8,128)} %multiply_bitcast_fusion) | copy-start | bytes 393220
  13.4 2.5 %copy-start.17 = (f32[256,128]{0,1:T(8,128)S(1)}, f32[256,128]{0,1:T(8,128)}, u32[]{:S(2)}) copy-start(f32[256,128]{0,1:T(8,128)} %get-tuple-element.43) | copy-start | bytes 393220
  13.4 2.5 %copy-start.18 = (f32[256,128]{0,1:T(8,128)S(1)}, f32[256,128]{0,1:T(8,128)}, u32[]{:S(2)}) copy-start(f32[256,128]{0,1:T(8,128)} %get-tuple-element.44) | copy-start | bytes 393220
  15.1 0.7 %copy-start = (f32[128,512]{1,0:T(8,128)}, f32[128,512]{1,0:T(8,128)S(1)}, u32[]{:S(2)}) copy-start(f32[128,512]{1,0:T(8,128)S(1)} %get-tuple-element.26) | copy-start | bytes 786436
  17.3 5.0 %copy-start.2 = (f32[128,512]{1,0:T(8,128)S(1)}, f32[128,512]{1,0:T(8,128)}, u32[]{:S(2)}) copy-start(f32[128,512]{1,0:T(8,128)} %get-tuple-element.33) | copy-start | bytes 786436
  17.3 5.0 %copy-start.3 = (f32[128,512]{1,0:T(8,128)S(1)}, f32[128,512]{1,0:T(8,128)}, u32[]{:S(2)}) copy-start(f32[128,512]{1,0:T(8,128)} %get-tuple-element.34) | copy-start | bytes 786436
  24.4 1.0 %copy-start.8 = (f32[128,512]{1,0:T(8,128)S(1)}, f32[128,512]{1,0:T(8,128)}, u32[]{:S(2)}) copy-start(f32[128,512]{1,0:T(8,128)} %get-tuple-element.27) | copy-start | bytes 786436
  24.4 1.0 %copy-start.9 = (f32[128,512]{1,0:T(8,128)S(1)}, f32[128,512]{1,0:T(8,128)}, u32[]{:S(2)}) copy-start(f32[128,512]{1,0:T(8,128)} %get-tuple-element.28) | copy-start | bytes 786436
  24.4 6.8 %copy-start.6 = (f32[128,512]{1,0:T(8,128)S(1)}, f32[128,512]{1,0:T(8,128)}, u32[]{:S(2)}) copy-start(f32[128,512]{1,0:T(8,128)} %get-tuple-element.29) | copy-start | bytes 786436
  24.5 6.8 %copy-start.7 = (f32[128,512]{1,0:T(8,128)S(1)}, f32[128,512]{1,0:T(8,128)}, u32[]{:S(2)}) copy-start(f32[128,512]{1,0:T(8,128)} %get-tuple-element.30) | copy-start | bytes 786436
  24.9 7.9 %copy-start.4 = (f32[128,512]{1,0:T(8,128)S(1)}, f32[128,512]{1,0:T(8,128)}, u32[]{:S(2)}) copy-start(f32[128,512]{1,0:T(8,128)} %get-tuple-element.31) | copy-start | bytes 786436
  24.9 7.9 %copy-start.5 = (f32[128,512]{1,0:T(8,128)S(1)}, f32[128,512]{1,0:T(8,128)}, u32[]{:S(2)}) copy-start(f32[128,512]{1,0:T(8,128)} %get-tuple-element.32) | copy-start | bytes 786436
  25.8 13.1 %collective-permute-start.5 = (f32[16,128]{1,0:T(8,128)S(1)}, f32[16,128]{1,0:T(8,128)S(1)}, u32[]{:S(2)}, u32[]{:S(2)}) collective-permute-start(f32[16,128]{1,0:T(8,128)S(1)} %fusion.24), channel_id=1, source_target_pairs={{0,8},{8,16},{16,24},{24,0},{1,9},{9,17},{17,25},{25,1},{2,10},{10... | collective-permute-start | bytes 24584 | tf_op jit(solution)/shard_map/ppermute | solution.py:126
  31.2 4.1 %copy-start.1 = (f32[128,512]{1,0:T(8,128)S(1)}, f32[128,512]{1,0:T(8,128)}, u32[]{:S(2)}) copy-start(f32[128,512]{1,0:T(8,128)} %copy-done) | copy-start | bytes 786436
  31.5 7.3 %collective-permute-start.6 = (f32[16,128]{1,0:T(8,128)S(1)}, f32[16,128]{1,0:T(8,128)S(1)}, u32[]{:S(2)}, u32[]{:S(2)}) collective-permute-start(f32[16,128]{1,0:T(8,128)S(1)} %fusion.27), channel_id=1, source_target_pairs={{0,16},{8,24},{16,0},{24,8},{1,17},{9,25},{17,1},{25,9},{2,18},{10... | collective-permute-start | bytes 24584 | tf_op jit(solution)/shard_map/ppermute | solution.py:126
  33.1 5.8 %collective-permute-start.7 = (f32[16,128]{1,0:T(8,128)S(1)}, f32[16,128]{1,0:T(8,128)S(1)}, u32[]{:S(2)}, u32[]{:S(2)}) collective-permute-start(f32[16,128]{1,0:T(8,128)S(1)} %fusion.30), channel_id=1, source_target_pairs={{0,24},{8,0},{16,8},{24,16},{1,25},{9,1},{17,9},{25,17},{2,26},{10... | collective-permute-start | bytes 24584 | tf_op jit(solution)/shard_map/ppermute | solution.py:126
  35.3 1.3 %copy-start.13 = (bf16[1,128,3,256]{3,1,2,0:T(8,128)(2,1)S(1)}, bf16[1,128,3,256]{3,1,2,0:T(8,128)(2,1)}, u32[]{:S(2)}) copy-start(bf16[1,128,3,256]{3,1,2,0:T(8,128)(2,1)} %param.10) | copy-start | bytes 589828
  35.3 2.2 %copy-start.19 = (bf16[1,128,1,256]{3,1,2,0:T(8,128)(2,1)S(1)}, bf16[1,128,1,256]{3,1,2,0:T(8,128)(2,1)}, u32[]{:S(2)}) copy-start(bf16[1,128,1,256]{3,1,2,0:T(8,128)(2,1)} %fusion.59) | copy-start | bytes 196612
  37.6 7.2 %collective-permute-start.4 = (bf16[1,128,3,256]{3,1,2,0:T(8,128)(2,1)S(1)}, bf16[1,128,3,256]{3,1,2,0:T(8,128)(2,1)S(1)}, u32[]{:S(2)}, u32[]{:S(2)}) collective-permute-start(bf16[1,128,3,256]{3,1,2,0:T(8,128)(2,1)S(1)} %pad_maximum_fusion.8), channel_id=1, source_target_pairs={{0,7},{1,0},{2,1},{3,2},{4,3},{5,4},{6,5},{7,6},{8,15},{9,8},{10,9... | collective-permute-start | bytes 589832 | tf_op jit(solution)/shard_map/ppermute | solution.py:22
  38.8 5.3 %collective-permute-start.3 = (bf16[1,128,256]{2,1,0:T(8,128)(2,1)S(1)}, bf16[1,128,256]{2,1,0:T(8,128)(2,1)S(1)}, u32[]{:S(2)}, u32[]{:S(2)}) collective-permute-start(bf16[1,128,256]{2,1,0:T(8,128)(2,1)S(1)} %get-tuple-element.42), channel_id=1, source_target_pairs={{0,1},{1,2},{2,3},{3,4},{4,5},{5,6},{6,7},{7,0},{8,9},{9,10},{10,1... | collective-permute-start | bytes 196616 | tf_op jit(solution)/shard_map/ppermute | solution.py:22

commit v16 on v10

--- a/solution.py
+++ b/solution.py
@@ -85,6 +85,11 @@
     re = hr * ar - sign * jnp.where(first, 0.0, hi * ai)
     im = jnp.where(first, hi * ai, hr * ai + sign * (hi * ar))
     return jnp.concatenate([re, im], axis=1)
+
+
+def turned(rows):
+    eye = jnp.eye(rows.shape[1], dtype=rows.dtype)
+    return jnp.einsum("gp,pq->qg", rows, eye, precision=highest)
 
 
 def dense_path(place, blocks, mixed, weighted, back, taps):
@@ -190,7 +195,7 @@
 
     if blocks <= DENSE:
         conv, grad_mixed, lag = dense_path(
-            place, blocks, mixed_in, weighted, mixed_back, taps.T
+            place, blocks, mixed_in, weighted, mixed_back, turned(taps)
         )
         return finish(
             conv, grad_mixed, lag, filter_scale, query_in, grad_query, key_back, value_back

time: 43.5 us -> 43.5 us (level)
    unnamed x19 -> x20, local copies, waits for them, and re-layouts: 2.28 us -> 1.95 us
where the time goes in v16:
time: 43.5 us; the launch traced here: 43.2 us
  starting transfers between devices  17.6 us (40%)
  waiting for transfers between devices  12.4 us (29%)
  matrix products  6.84 us (16%)
  other arithmetic  3.2 us (7%)
  local copies, waits for them, and re-layouts  2.1 us (5%)
  between operations  1.02 us (2%)
    ppermute x3, waiting for transfers between devices, dense_path(): got = lax.ppermute(payload, 'ctx', pairs)  8.81 us
    ppermute x3, starting transfers between devices, dense_path(): lag = lag + lax.ppermute(share, 'ctx', pairs)  8.37 us
    ppermute x3, starting transfers between devices, dense_path(): got = lax.ppermute(payload, 'ctx', pairs)  4.68 us
    ppermute x2, starting transfers between devices, from_behind(): return lax.ppermute(x, axis, pairs)  4.59 us
    ppermute x2, waiting for transfers between devices, from_behind(): return lax.ppermute(x, axis, pairs)  3.59 us
    dot_general x3, matrix products, dense_path(): acc = acc + jnp.einsum('pr,pf->rf', got, table, precision=precise)  2.01 us
    unnamed x20, local copies, waits for them, and re-layouts  1.95 us
    dot_general x1, matrix products, dense_path(): loc = jnp.einsum('pr,pf->rf', own, own_table, precision=precise)  1.48 us
  transfers between devices with their start and end apart: 8, of which 3 were waited for; matrix products, arithmetic and copies ran while one was open for 15% of the time, Pallas kernels for 0%

profile of v16, /device:TPU:4, one launch (start us, length us, event | category | flops | bytes accessed | tf_op | source)
XLA Modules:
  0.0 43.2 jit_solution(356002744972512642)
XLA Ops:
  0.6 0.0 copy-start
  0.6 0.0 copy-start.7
  0.7 0.0 copy-start.8
  0.7 0.0 copy-start.1
  0.7 0.0 copy-start.2
  0.7 0.0 copy-start.5
  0.7 0.0 copy-start.4
  0.7 0.0 copy-start.6
  0.7 0.6 %copy-done = f32[1,16,128]{2,1,0:T(8,128)S(1)} copy-done((f32[1,16,128]{2,1,0:T(8,128)S(1)}, f32[1,16,128]{2,1,0:T(8,128)}, u32[]{:S(2)}) %copy-start) | copy-done | bytes 8216
  1.3 0.2 fusion.59
  1.6 1.1 %broadcast_select_fusion.2 = (f32[128,256]{1,0:T(8,128)S(1)}, f32[128,256]{1,0:T(8,128)S(1)}, f32[128,256]{1,0:T(8,128)S(1)}, f32[128,256]{1,0:T(8,128)S(1)}, f32[128,256]{1,0:T(8,128)S(1)}) fusion(pred[]{:T(512)S(6)} %lt.96, bf16[1,128,3,256]{3,1,2,0:T(8,128)(2,1)} %param.10, bf16[1,128,256]{2,1,0:T(8,128)(2,1)} %param.12, ...), kind=kLoop, calls=%fused_computation.109 | loop fusion | flops 393216 | bytes 1048579 | tf_op jit(solution)/shard_map/jit(_where)/select_n | solution.py:102
  2.7 2.7 %collective-permute-start.1 = (f32[128,272]{1,0:T(8,128)S(1)}, f32[128,272]{1,0:T(8,128)S(1)}, u32[]{:S(2)}, u32[]{:S(2)}) collective-permute-start(f32[128,272]{1,0:T(8,128)S(1)} %get-tuple-element.46), channel_id=1, source_target_pairs={{0,16},{8,24},{16,0},{24,8},{1,17},{9,25},{17,1},{25,9},{2,18},{10... | collective-permute-start | bytes 417800 | tf_op jit(solution)/shard_map/ppermute | solution.py:105
  5.3 1.3 %collective-permute-start.2 = (f32[128,272]{1,0:T(8,128)S(1)}, f32[128,272]{1,0:T(8,128)S(1)}, u32[]{:S(2)}, u32[]{:S(2)}) collective-permute-start(f32[128,272]{1,0:T(8,128)S(1)} %get-tuple-element.47), channel_id=1, source_target_pairs={{0,24},{8,0},{16,8},{24,16},{1,25},{9,1},{17,9},{25,17},{2,26},{10... | collective-permute-start | bytes 417800 | tf_op jit(solution)/shard_map/ppermute | solution.py:105
  6.7 0.7 %collective-permute-start = (f32[128,272]{1,0:T(8,128)S(1)}, f32[128,272]{1,0:T(8,128)S(1)}, u32[]{:S(2)}, u32[]{:S(2)}) collective-permute-start(f32[128,272]{1,0:T(8,128)S(1)} %get-tuple-element.45), channel_id=1, source_target_pairs={{0,8},{8,16},{16,24},{24,0},{1,9},{9,17},{17,25},{25,1},{2,10},{10... | collective-permute-start | bytes 417800 | tf_op jit(solution)/shard_map/ppermute | solution.py:105
  7.4 0.0 copy-done.4
  7.4 0.0 copy-done.5
  7.4 0.0 copy-done.6
  7.5 0.0 copy-done.7
  7.5 0.0 copy-done.8
  7.6 0.0 copy-done.1
  7.6 0.0 copy-done.2
  7.6 0.1 multiply_subtract_fusion.5
  7.7 0.5 %multiply_subtract_fusion.9 = (f32[128,512]{1,0:T(8,128)S(1)}, f32[128,512]{1,0:T(8,128)S(1)}, f32[128,512]{1,0:T(8,128)S(1)}, f32[128,512]{1,0:T(8,128)S(1)}, f...) fusion(f32[128,512]{1,0:T(8,128)S(1)} %copy-done.2, ...), kind=kLoop, calls=%fused_computation.84 | loop fusion | flops 3407872 | bytes 3696256 | tf_op jit(solution)/shard_map/sub | solution.py:71
  8.3 1.5 %fusion.35 = f32[784,1024]{1,0:T(8,128)S(1)} fusion(f32[128,16]{1,0:T(8,128)S(1)} %fusion.59, f32[128,256]{1,0:T(8,128)S(1)} %get-tuple-element.44, f32[128,256]{1,0:T(8,128)S(1)} %get-tuple-element.43, f32[128,256]{1,0:T(8,128)S(1)} %multiply_bitcast_fusion, f32[128,512]{1,0:T(8,128)S(1)} %get-tuple-element.26, f32[128,512]{1,0:T(8,128)S(1)} %get-tuple-element.25), kind=kOutput, calls=%fused_computation.53 | convolution fusion | flops 616994816 | bytes 4136960 | tf_op jit(solution)/shard_map/pr,pf->rf/dot_general | solution.py:110
  9.8 7.0 %collective-permute-done.1 = f32[128,272]{1,0:T(8,128)S(1)} collective-permute-done((f32[128,272]{1,0:T(8,128)S(1)}, f32[128,272]{1,0:T(8,128)S(1)}, u32[]{:S(2)}, u32[]{:S(2)}) %collective-permute-start.1) | collective-permute-done | bytes 139296 | tf_op jit(solution)/shard_map/ppermute | solution.py:105
  16.8 0.6 %fusion.16 = f32[272,1024]{1,0:T(8,128)S(1)} fusion(f32[128,272]{1,0:T(8,128)S(1)} %collective-permute-done.1, f32[128,512]{1,0:T(8,128)S(1)} %get-tuple-element.35, f32[128,512]{1,0:T(8,128)S(1)} %get-tuple-element.36), kind=kOutput, calls=%fused_computation.23 | convolution fusion | flops 214040576 | bytes 1777664 | tf_op jit(solution)/shard_map/pr,pf->rf/dot_general | solution.py:107
  17.4 0.0 collective-permute-done.2
  17.4 0.6 %fusion.20 = f32[272,1024]{1,0:T(8,128)S(1)} fusion(f32[128,272]{1,0:T(8,128)S(1)} %collective-permute-done.2, f32[128,512]{1,0:T(8,128)S(1)} %get-tuple-element.24, f32[128,512]{1,0:T(8,128)S(1)} %get-tuple-element.23), kind=kOutput, calls=%fused_computation.27 | convolution fusion | flops 214040576 | bytes 1777664 | tf_op jit(solution)/shard_map/pr,pf->rf/dot_general | solution.py:107
  18.1 1.8 %collective-permute-done = f32[128,272]{1,0:T(8,128)S(1)} collective-permute-done((f32[128,272]{1,0:T(8,128)S(1)}, f32[128,272]{1,0:T(8,128)S(1)}, u32[]{:S(2)}, u32[]{:S(2)}) %collective-permute-start) | collective-permute-done | bytes 139296 | tf_op jit(solution)/shard_map/ppermute | solution.py:105
  19.9 0.7 %fusion.8 = f32[272,1024]{1,0:T(8,128)S(1)} fusion(f32[272,1024]{1,0:T(8,128)S(1)} %fusion.20, f32[272,1024]{1,0:T(8,128)S(1)} %fusion.16, f32[128,272]{1,0:T(8,128)S(1)} %collective-permute-done, f32[128,512]{1,0:T(8,128)S(1)} %get-tuple-element.33, f32[128,512]{1,0:T(8,128)S(1)} %get-tuple-element.34), kind=kOutput, calls=%fused_computation.9 | convolution fusion | flops 214597632 | bytes 4005888 | tf_op jit(solution)/shard_map/pr,pf->rf/dot_general | solution.py:107
  20.6 0.4 slice_add_fusion.1
  21.1 0.1 broadcast_in_dim.26
  21.2 0.4 %multiply_subtract_fusion = (f32[256,512]{1,0:T(8,128)S(1)}, f32[256,512]{1,0:T(8,128)S(1)}, f32[256,512]{1,0:T(8,128)S(1)}, f32[256,512]{1,0:T(8,128)S(1)}) fusion(f32[784,1024]{1,0:T(8,128)S(1)} %fusion.35, f32[256,1024]{1,0:T(8,128)S(1)} %get-tuple-element.4, pred[512]{0:T(512)(128)(4,1)S(1)} %iota_compare_fusion.3, f32[256,1024]{1,0:T(8,128)S(1)} %bitcast.75), kind=kLoop, calls=%fused_computation.44 | loop fusion | flops 2621440 | bytes 5243392 | tf_op jit(solution)/shard_map/sub | solution.py:85
  21.6 0.2 bitcast_reduce_fusion
  21.8 0.3 fusion.24
  22.1 4.3 %collective-permute-start.5 = (f32[16,128]{1,0:T(8,128)S(1)}, f32[16,128]{1,0:T(8,128)S(1)}, u32[]{:S(2)}, u32[]{:S(2)}) collective-permute-start(f32[16,128]{1,0:T(8,128)S(1)} %fusion.24), channel_id=1, source_target_pairs={{0,8},{8,16},{16,24},{24,0},{1,9},{9,17},{17,25},{25,1},{2,10},{10... | collective-permute-start | bytes 24584 | tf_op jit(solution)/shard_map/ppermute | solution.py:129
  26.4 0.3 fusion.27
  26.7 1.4 %collective-permute-start.6 = (f32[16,128]{1,0:T(8,128)S(1)}, f32[16,128]{1,0:T(8,128)S(1)}, u32[]{:S(2)}, u32[]{:S(2)}) collective-permute-start(f32[16,128]{1,0:T(8,128)S(1)} %fusion.27), channel_id=1, source_target_pairs={{0,16},{8,24},{16,0},{24,8},{1,17},{9,25},{17,1},{25,9},{2,18},{10... | collective-permute-start | bytes 24584 | tf_op jit(solution)/shard_map/ppermute | solution.py:129
  28.2 0.2 select_subtract_fusion
  28.4 0.0 copy-start.3
  28.4 1.2 %fusion = f32[128,512]{1,0:T(8,128)S(1)} fusion(f32[256,512]{1,0:T(8,128)S(1)} %get-tuple-element.11, f32[256,512]{1,0:T(8,128)S(1)} %get-tuple-element.12, f32[256,512]{1,0:T(8,128)S(1)} %get-tuple-element.8, f32[256,512]{1,0:T(8,128)S(1)} %get-tuple-element.7, f32[128,512]{1,0:T(8,128)S(1)} %get-tuple-element.26, f32[128,512]{1,0:T(8,128)S(1)} %get-tuple-element.25, ...), kind=kOutput, calls=%fused_computation | convolution fusion | flops 404488192 | bytes 2887680 | tf_op jit(solution)/shard_map/tf,rf->tr/dot_general | solution.py:123
  29.7 0.0 copy-done.3
  29.7 0.1 fusion.56
  29.8 2.7 %collective-permute-start.4 = (bf16[1,128,3,256]{3,1,2,0:T(8,128)(2,1)S(1)}, bf16[1,128,3,256]{3,1,2,0:T(8,128)(2,1)S(1)}, u32[]{:S(2)}, u32[]{:S(2)}) collective-permute-start(bf16[1,128,3,256]{3,1,2,0:T(8,128)(2,1)S(1)} %pad_maximum_fusion.8), channel_id=1, source_target_pairs={{1,0},{2,1},{3,2},{4,3},{5,4},{6,5},{7,6},{9,8},{10,9},{11,10},{12... | collective-permute-start | bytes 589832 | tf_op jit(solution)/shard_map/ppermute | solution.py:22
  32.4 0.3 fusion.30
  32.8 2.7 %collective-permute-start.7 = (f32[16,128]{1,0:T(8,128)S(1)}, f32[16,128]{1,0:T(8,128)S(1)}, u32[]{:S(2)}, u32[]{:S(2)}) collective-permute-start(f32[16,128]{1,0:T(8,128)S(1)} %fusion.30), channel_id=1, source_target_pairs={{0,24},{8,0},{16,8},{24,16},{1,25},{9,1},{17,9},{25,17},{2,26},{10... | collective-permute-start | bytes 24584 | tf_op jit(solution)/shard_map/ppermute | solution.py:129
  35.4 1.9 %collective-permute-start.3 = (bf16[1,128,256]{2,1,0:T(8,128)(2,1)S(1)}, bf16[1,128,256]{2,1,0:T(8,128)(2,1)S(1)}, u32[]{:S(2)}, u32[]{:S(2)}) collective-permute-start(bf16[1,128,256]{2,1,0:T(8,128)(2,1)S(1)} %get-tuple-element.42), channel_id=1, source_target_pairs={{0,1},{1,2},{2,3},{3,4},{4,5},{5,6},{6,7},{8,9},{9,10},{10,11},{11... | collective-permute-start | bytes 196616 | tf_op jit(solution)/shard_map/ppermute | solution.py:22
  37.3 0.0 collective-permute-done.5
  37.3 0.0 collective-permute-done.6
  37.4 0.0 collective-permute-done.7
  37.4 0.9 %fusion.12 = f32[1,16,128]{2,1,0:T(8,128)} fusion(f32[16,128]{1,0:T(8,128)S(1)} %collective-permute-done.7, f32[16,128]{1,0:T(8,128)S(1)} %collective-permute-done.6, f32[16,128]{1,0:T(8,128)S(1)} %collective-permute-done.5, f32[16,1024]{1,0:T(8,128)S(1)} %bitcast_reduce_fusion, f32[128,512]{1,0:T(8,128)S(1)} %get-tuple-element.26, ...), kind=kOutput, calls=%fused_computation.14 | convolution fusion | flops 12853248 | bytes 626688 | tf_op jit(solution)/shard_map/rf,tf->rt/dot_general | solution.py:124
  38.3 3.6 %collective-permute-done.3 = bf16[1,128,256]{2,1,0:T(8,128)(2,1)S(1)} collective-permute-done((bf16[1,128,256]{2,1,0:T(8,128)(2,1)S(1)}, bf16[1,128,256]{2,1,0:T(8,128)(2,1)S(1)}, u32[]{:S(2)}, u32[]{:S(2)}) %collective-permute-start.3) | collective-permute-done | bytes 65568 | tf_op jit(solution)/shard_map/ppermute | solution.py:22
  41.9 0.0 collective-permute-done.4
  41.9 0.6 %copy.19 = bf16[1,128,256]{2,1,0:T(8,128)(2,1)} copy(bf16[1,128,256]{2,1,0:T(8,128)(2,1)S(1)} %collective-permute-done.3) | data formatting | bytes 131072
  42.5 0.7 %copy.20 = bf16[1,128,3,256]{3,1,2,0:T(8,128)(2,1)} copy(bf16[1,128,3,256]{3,1,2,0:T(8,128)(2,1)S(1)} %collective-permute-done.4) | data formatting | bytes 393216
  (10 shorter events, 0.2 us)
Async XLA Ops:
  0.6 0.7 %copy-start = (f32[1,16,128]{2,1,0:T(8,128)S(1)}, f32[1,16,128]{2,1,0:T(8,128)}, u32[]{:S(2)}) copy-start(f32[1,16,128]{2,1,0:T(8,128)} %param.13) | copy-start | bytes 24580
  0.6 6.9 %copy-start.7 = (f32[4,512]{1,0:T(4,128)S(1)}, f32[4,512]{1,0:T(4,128)}, u32[]{:S(2)}) copy-start(f32[4,512]{1,0:T(4,128)} %constant.139.clone) | copy-start | bytes 24580
  0.7 6.9 %copy-start.8 = (f32[4,512]{1,0:T(4,128)S(1)}, f32[4,512]{1,0:T(4,128)}, u32[]{:S(2)}) copy-start(f32[4,512]{1,0:T(4,128)} %constant.140.clone) | copy-start | bytes 24580
  0.7 6.9 %copy-start.1 = (f32[128,512]{1,0:T(8,128)S(1)}, f32[128,512]{1,0:T(8,128)}, u32[]{:S(2)}) copy-start(f32[128,512]{1,0:T(8,128)} %constant.137.clone) | copy-start | bytes 786436
  0.7 6.9 %copy-start.2 = (f32[128,512]{1,0:T(8,128)S(1)}, f32[128,512]{1,0:T(8,128)}, u32[]{:S(2)}) copy-start(f32[128,512]{1,0:T(8,128)} %constant.138.clone) | copy-start | bytes 786436
  0.7 6.7 %copy-start.5 = (bf16[1,128,256]{2,1,0:T(8,128)(2,1)S(1)}, bf16[1,128,256]{2,1,0:T(8,128)(2,1)}, u32[]{:S(2)}) copy-start(bf16[1,128,256]{2,1,0:T(8,128)(2,1)} %param.12) | copy-start | bytes 196612
  0.7 6.7 %copy-start.4 = (bf16[1,128,3,256]{3,1,2,0:T(8,128)(2,1)S(1)}, bf16[1,128,3,256]{3,1,2,0:T(8,128)(2,1)}, u32[]{:S(2)}) copy-start(bf16[1,128,3,256]{3,1,2,0:T(8,128)(2,1)} %param.9) | copy-start | bytes 589828
  0.7 6.7 %copy-start.6 = (f32[1,128,256]{2,1,0:T(8,128)S(1)}, f32[1,128,256]{2,1,0:T(8,128)}, u32[]{:S(2)}) copy-start(f32[1,128,256]{2,1,0:T(8,128)} %param.11) | copy-start | bytes 393220
  2.7 14.1 %collective-permute-start.1 = (f32[128,272]{1,0:T(8,128)S(1)}, f32[128,272]{1,0:T(8,128)S(1)}, u32[]{:S(2)}, u32[]{:S(2)}) collective-permute-start(f32[128,272]{1,0:T(8,128)S(1)} %get-tuple-element.46), channel_id=1, source_target_pairs={{0,16},{8,24},{16,0},{24,8},{1,17},{9,25},{17,1},{25,9},{2,18},{10... | collective-permute-start | bytes 417800 | tf_op jit(solution)/shard_map/ppermute | solution.py:105
  5.3 12.1 %collective-permute-start.2 = (f32[128,272]{1,0:T(8,128)S(1)}, f32[128,272]{1,0:T(8,128)S(1)}, u32[]{:S(2)}, u32[]{:S(2)}) collective-permute-start(f32[128,272]{1,0:T(8,128)S(1)} %get-tuple-element.47), channel_id=1, source_target_pairs={{0,24},{8,0},{16,8},{24,16},{1,25},{9,1},{17,9},{25,17},{2,26},{10... | collective-permute-start | bytes 417800 | tf_op jit(solution)/shard_map/ppermute | solution.py:105
  6.7 13.2 %collective-permute-start = (f32[128,272]{1,0:T(8,128)S(1)}, f32[128,272]{1,0:T(8,128)S(1)}, u32[]{:S(2)}, u32[]{:S(2)}) collective-permute-start(f32[128,272]{1,0:T(8,128)S(1)} %get-tuple-element.45), channel_id=1, source_target_pairs={{0,8},{8,16},{16,24},{24,0},{1,9},{9,17},{17,25},{25,1},{2,10},{10... | collective-permute-start | bytes 417800 | tf_op jit(solution)/shard_map/ppermute | solution.py:105
  22.1 15.2 %collective-permute-start.5 = (f32[16,128]{1,0:T(8,128)S(1)}, f32[16,128]{1,0:T(8,128)S(1)}, u32[]{:S(2)}, u32[]{:S(2)}) collective-permute-start(f32[16,128]{1,0:T(8,128)S(1)} %fusion.24), channel_id=1, source_target_pairs={{0,8},{8,16},{16,24},{24,0},{1,9},{9,17},{17,25},{25,1},{2,10},{10... | collective-permute-start | bytes 24584 | tf_op jit(solution)/shard_map/ppermute | solution.py:129
  26.7 10.6 %collective-permute-start.6 = (f32[16,128]{1,0:T(8,128)S(1)}, f32[16,128]{1,0:T(8,128)S(1)}, u32[]{:S(2)}, u32[]{:S(2)}) collective-permute-start(f32[16,128]{1,0:T(8,128)S(1)} %fusion.27), channel_id=1, source_target_pairs={{0,16},{8,24},{16,0},{24,8},{1,17},{9,25},{17,1},{25,9},{2,18},{10... | collective-permute-start | bytes 24584 | tf_op jit(solution)/shard_map/ppermute | solution.py:129
  28.4 1.2 %copy-start.3 = (bf16[1,128,3,256]{3,1,2,0:T(8,128)(2,1)S(1)}, bf16[1,128,3,256]{3,1,2,0:T(8,128)(2,1)}, u32[]{:S(2)}) copy-start(bf16[1,128,3,256]{3,1,2,0:T(8,128)(2,1)} %param.10) | copy-start | bytes 589828
  29.8 12.1 %collective-permute-start.4 = (bf16[1,128,3,256]{3,1,2,0:T(8,128)(2,1)S(1)}, bf16[1,128,3,256]{3,1,2,0:T(8,128)(2,1)S(1)}, u32[]{:S(2)}, u32[]{:S(2)}) collective-permute-start(bf16[1,128,3,256]{3,1,2,0:T(8,128)(2,1)S(1)} %pad_maximum_fusion.8), channel_id=1, source_target_pairs={{1,0},{2,1},{3,2},{4,3},{5,4},{6,5},{7,6},{9,8},{10,9},{11,10},{12... | collective-permute-start | bytes 589832 | tf_op jit(solution)/shard_map/ppermute | solution.py:22
  32.8 4.6 %collective-permute-start.7 = (f32[16,128]{1,0:T(8,128)S(1)}, f32[16,128]{1,0:T(8,128)S(1)}, u32[]{:S(2)}, u32[]{:S(2)}) collective-permute-start(f32[16,128]{1,0:T(8,128)S(1)} %fusion.30), channel_id=1, source_target_pairs={{0,24},{8,0},{16,8},{24,16},{1,25},{9,1},{17,9},{25,17},{2,26},{10... | collective-permute-start | bytes 24584 | tf_op jit(solution)/shard_map/ppermute | solution.py:129
  35.4 6.5 %collective-permute-start.3 = (bf16[1,128,256]{2,1,0:T(8,128)(2,1)S(1)}, bf16[1,128,256]{2,1,0:T(8,128)(2,1)S(1)}, u32[]{:S(2)}, u32[]{:S(2)}) collective-permute-start(bf16[1,128,256]{2,1,0:T(8,128)(2,1)S(1)} %get-tuple-element.42), channel_id=1, source_target_pairs={{0,1},{1,2},{2,3},{3,4},{4,5},{5,6},{6,7},{8,9},{9,10},{10,11},{11... | collective-permute-start | bytes 196616 | tf_op jit(solution)/shard_map/ppermute | solution.py:22

commit v17 on v5

--- a/solution.py
+++ b/solution.py
@@ -117,9 +117,12 @@
     both = jnp.concatenate([conv, gm], axis=0)
     out = jnp.einsum("tf,rf->tr", own_table * weight, both, precision=precise)
     lag = jnp.einsum("rf,tf->rt", fgs, own_table * weight, precision=precise)
-    for s in range(1, blocks):
-        table = block_table(packed, (place + s) % blocks) * weight
-        share = jnp.einsum("rf,tf->rt", fgs, table, precision=precise)
+    others = jnp.concatenate(
+        [block_table(packed, (place + s) % blocks) for s in range(1, blocks)], axis=0
+    )
+    shares = jnp.einsum("rf,tf->rt", fgs, others * weight, precision=precise)
+    for s in range(1, blocks):
+        share = shares[:, (s - 1) * block : s * block]
         pairs = [(i, (i + s) % blocks) for i in range(blocks)]
         lag = lag + lax.ppermute(share, "ctx", pairs)
     return out[:, :c], out[:, c:], lag

time: 43.4 us -> 43.7 us (level)
  waiting for transfers between devices: 11.5 us -> 12.4 us
  other arithmetic: 3.98 us -> 3.14 us
  starting transfers between devices: 17.6 us -> 18.2 us
    ppermute x3, starting transfers between devices: 8.37 us -> 9.66 us  [dense_path(): lag = lag + lax.ppermute(share, 'ctx', pairs)]
    transpose x2, other arithmetic: 0.89 us -> 0.05 us  [on_device(): conv, grad_mixed, lag = dense_path(place, blocks, mixed_in.T, weighted.T,...]
    ppermute x3, waiting for transfers between devices: 7.94 us -> 8.77 us  [dense_path(): got = lax.ppermute(payload, 'ctx', pairs)]
    ppermute x2, starting transfers between devices: 4.59 us -> 3.83 us  [from_behind(): return lax.ppermute(x, axis, pairs)]
    dot_general x3 -> x1, matrix products: 0.96 us -> 0.72 us  [dense_path(): shares = jnp.einsum('rf,tf->rt', fgs, others * weight, precision=precise)]
  transfers between devices with their start and end apart: 8 -> 8, of which waited for: 3 -> 3; matrix products, arithmetic and copies ran while one was open for 17% -> 12% of each run, Pallas kernels for 0% -> 0%
where the time goes in v17:
time: 43.7 us; the launch traced here: 43.5 us
  starting transfers between devices  18.2 us (42%)
  waiting for transfers between devices  12.4 us (28%)
  matrix products  6.39 us (15%)
  other arithmetic  3.14 us (7%)
  local copies, waits for them, and re-layouts  2.39 us (5%)
  between operations  1.02 us (2%)
    ppermute x3, starting transfers between devices, dense_path(): lag = lag + lax.ppermute(share, 'ctx', pairs)  9.66 us
    ppermute x3, waiting for transfers between devices, dense_path(): got = lax.ppermute(payload, 'ctx', pairs)  8.77 us
    ppermute x3, starting transfers between devices, dense_path(): got = lax.ppermute(payload, 'ctx', pairs)  4.68 us
    ppermute x2, starting transfers between devices, from_behind(): return lax.ppermute(x, axis, pairs)  3.83 us
    ppermute x2, waiting for transfers between devices, from_behind(): return lax.ppermute(x, axis, pairs)  3.58 us
    unnamed x19, local copies, waits for them, and re-layouts  2.23 us
    dot_general x3, matrix products, dense_path(): acc = acc + jnp.dot(got, table, precision=precise)  2.02 us
    dot_general x1, matrix products, dense_path(): loc = jnp.dot(own, own_table, precision=precise)  1.48 us
  transfers between devices with their start and end apart: 8, of which 3 were waited for; matrix products, arithmetic and copies ran while one was open for 12% of the time, Pallas kernels for 0%

profile of v17, /device:TPU:4, one launch (start us, length us, event | category | flops | bytes accessed | tf_op | source)
XLA Modules:
  0.0 43.5 jit_solution(7459271940839046324)
XLA Ops:
  0.6 0.0 copy-start.6
  0.6 0.0 copy-start.7
  0.7 0.0 copy-start
  0.7 0.0 copy-start.1
  0.7 0.0 copy-start.2
  0.7 0.0 copy-start.3
  0.7 0.0 copy-start.4
  0.7 0.0 copy-start.5
  0.7 0.9 %copy.12 = f32[1,16,128]{1,2,0:T(8,128)S(1)} copy(f32[1,16,128]{2,1,0:T(8,128)} %param.13) | data formatting | bytes 16384 | tf_op args[4]
  1.6 1.0 %broadcast_select_fusion.2 = (f32[256,128]{0,1:T(8,128)S(1)}, f32[256,128]{0,1:T(8,128)S(1)}, f32[256,128]{0,1:T(8,128)S(1)}) fusion(pred[]{:T(512)S(6)} %lt.96, bf16[1,128,3,256]{3,1,2,0:T(8,128)(2,1)} %param.10, bf16[1,128,256]{2,1,0:T(8,128)(2,1)} %param.12, bf16[1,128,3,256]{3,1,2,0:T(8,128)(2,1)} %param.9, pred[]{:T(512)S(6)} %lt.99, pred[]{:T(512)S(6)} %lt.102), kind=kLoop, calls=%fused_computation.107 | loop fusion | flops 294912 | bytes 655363 | tf_op jit(solution)/shard_map/jit(_where)/select_n | solution.py:97
  2.7 2.7 %collective-permute-start.1 = (f32[272,128]{0,1:T(8,128)S(1)}, f32[272,128]{0,1:T(8,128)S(1)}, u32[]{:S(2)}, u32[]{:S(2)}) collective-permute-start(f32[272,128]{0,1:T(8,128)S(1)} %get-tuple-element.46), channel_id=1, source_target_pairs={{0,16},{8,24},{16,0},{24,8},{1,17},{9,25},{17,1},{25,9},{2,18},{10... | collective-permute-start | bytes 417800 | tf_op jit(solution)/shard_map/ppermute | solution.py:100
  5.3 1.3 %collective-permute-start.2 = (f32[272,128]{0,1:T(8,128)S(1)}, f32[272,128]{0,1:T(8,128)S(1)}, u32[]{:S(2)}, u32[]{:S(2)}) collective-permute-start(f32[272,128]{0,1:T(8,128)S(1)} %get-tuple-element.47), channel_id=1, source_target_pairs={{0,24},{8,0},{16,8},{24,16},{1,25},{9,1},{17,9},{25,17},{2,26},{10... | collective-permute-start | bytes 417800 | tf_op jit(solution)/shard_map/ppermute | solution.py:100
  6.7 0.7 %collective-permute-start = (f32[272,128]{0,1:T(8,128)S(1)}, f32[272,128]{0,1:T(8,128)S(1)}, u32[]{:S(2)}, u32[]{:S(2)}) collective-permute-start(f32[272,128]{0,1:T(8,128)S(1)} %get-tuple-element.45), channel_id=1, source_target_pairs={{0,8},{8,16},{16,24},{24,0},{1,9},{9,17},{17,25},{25,1},{2,10},{10... | collective-permute-start | bytes 417800 | tf_op jit(solution)/shard_map/ppermute | solution.py:100
  7.3 0.0 copy-done.2
  7.4 0.0 copy-done.3
  7.4 0.0 copy-done.4
  7.4 0.0 copy-done.5
  7.5 0.0 copy-done.6
  7.5 0.0 copy-done.7
  7.6 0.0 copy-done
  7.6 0.0 copy-done.1
  7.6 0.1 multiply_subtract_fusion.5
  7.7 0.5 %multiply_subtract_fusion.9 = (f32[128,512]{1,0:T(8,128)S(1)}, f32[128,512]{1,0:T(8,128)S(1)}, f32[128,512]{1,0:T(8,128)S(1)}, f32[128,512]{1,0:T(8,128)S(1)}, f...) fusion(f32[128,512]{1,0:T(8,128)S(1)} %copy-done.1, ...), kind=kLoop, calls=%fused_computation.82 | loop fusion | flops 3407872 | bytes 3696256 | tf_op jit(solution)/shard_map/sub | solution.py:71
  8.3 1.5 %fusion.38 = f32[784,1024]{1,0:T(8,128)S(1)} fusion(f32[16,128]{0,1:T(8,128)S(1)} %bitcast.88, f32[256,128]{0,1:T(8,128)S(1)} %get-tuple-element.44, f32[256,128]{0,1:T(8,128)S(1)} %get-tuple-element.43, f32[256,128]{0,1:T(8,128)S(1)} %multiply_bitcast_fusion, f32[128,512]{1,0:T(8,128)S(1)} %get-tuple-element.26, f32[128,512]{1,0:T(8,128)S(1)} %get-tuple-element.25), kind=kOutput, calls=%fused_computation.54 | convolution fusion | flops 616994816 | bytes 4136960 | tf_op jit(solution)/shard_map/dot_general | solution.py:105
  9.8 7.0 %collective-permute-done.1 = f32[272,128]{0,1:T(8,128)S(1)} collective-permute-done((f32[272,128]{0,1:T(8,128)S(1)}, f32[272,128]{0,1:T(8,128)S(1)}, u32[]{:S(2)}, u32[]{:S(2)}) %collective-permute-start.1) | collective-permute-done | bytes 139296 | tf_op jit(solution)/shard_map/ppermute | solution.py:100
  16.7 0.6 %fusion.28 = f32[272,1024]{1,0:T(8,128)S(1)} fusion(f32[272,128]{0,1:T(8,128)S(1)} %collective-permute-done.1, f32[128,512]{1,0:T(8,128)S(1)} %get-tuple-element.35, f32[128,512]{1,0:T(8,128)S(1)} %get-tuple-element.36), kind=kOutput, calls=%fused_computation.36 | convolution fusion | flops 214040576 | bytes 1777664 | tf_op jit(solution)/shard_map/dot_general | solution.py:102
  17.4 0.0 collective-permute-done.2
  17.4 0.7 %fusion.32 = f32[272,1024]{1,0:T(8,128)S(1)} fusion(f32[272,128]{0,1:T(8,128)S(1)} %collective-permute-done.2, f32[128,512]{1,0:T(8,128)S(1)} %get-tuple-element.24, f32[128,512]{1,0:T(8,128)S(1)} %get-tuple-element.23), kind=kOutput, calls=%fused_computation.40 | convolution fusion | flops 214040576 | bytes 1777664 | tf_op jit(solution)/shard_map/dot_general | solution.py:102
  18.0 1.8 %collective-permute-done = f32[272,128]{0,1:T(8,128)S(1)} collective-permute-done((f32[272,128]{0,1:T(8,128)S(1)}, f32[272,128]{0,1:T(8,128)S(1)}, u32[]{:S(2)}, u32[]{:S(2)}) %collective-permute-start) | collective-permute-done | bytes 139296 | tf_op jit(solution)/shard_map/ppermute | solution.py:100
  19.8 0.7 %fusion.19 = f32[272,1024]{1,0:T(8,128)S(1)} fusion(f32[272,1024]{1,0:T(8,128)S(1)} %fusion.32, f32[272,1024]{1,0:T(8,128)S(1)} %fusion.28, f32[272,128]{0,1:T(8,128)S(1)} %collective-permute-done, f32[128,512]{1,0:T(8,128)S(1)} %get-tuple-element.33, f32[128,512]{1,0:T(8,128)S(1)} %get-tuple-element.34), kind=kOutput, calls=%fused_computation.21 | convolution fusion | flops 214597632 | bytes 4005888 | tf_op jit(solution)/shard_map/dot_general | solution.py:102
  20.6 0.4 slice_add_fusion.1
  21.0 0.1 broadcast_in_dim.26
  21.1 0.4 %multiply_subtract_fusion = (f32[256,512]{1,0:T(8,128)S(1)}, f32[256,512]{1,0:T(8,128)S(1)}, f32[256,512]{1,0:T(8,128)S(1)}, f32[256,512]{1,0:T(8,128)S(1)}) fusion(f32[784,1024]{1,0:T(8,128)S(1)} %fusion.38, f32[256,1024]{1,0:T(8,128)S(1)} %get-tuple-element.4, pred[512]{0:T(512)(128)(4,1)S(1)} %iota_compare_fusion.2, f32[256,1024]{1,0:T(8,128)S(1)} %bitcast.85), kind=kLoop, calls=%fused_computation.45 | loop fusion | flops 2621440 | bytes 5243392 | tf_op jit(solution)/shard_map/sub | solution.py:85
  21.6 0.2 select_subtract_fusion
  21.8 1.2 %fusion = f32[128,512]{1,0:T(8,128)S(1)} fusion(f32[256,512]{1,0:T(8,128)S(1)} %get-tuple-element.11, f32[256,512]{1,0:T(8,128)S(1)} %get-tuple-element.12, f32[256,512]{1,0:T(8,128)S(1)} %get-tuple-element.8, f32[256,512]{1,0:T(8,128)S(1)} %get-tuple-element.7, f32[128,512]{1,0:T(8,128)S(1)} %get-tuple-element.26, f32[128,512]{1,0:T(8,128)S(1)} %get-tuple-element.25, ...), kind=kOutput, calls=%fused_computation | convolution fusion | flops 404488192 | bytes 2887680 | tf_op jit(solution)/shard_map/tf,rf->tr/dot_general | solution.py:118
  23.1 0.1 fusion.58
  23.2 1.9 %collective-permute-start.4 = (bf16[1,128,3,256]{3,1,2,0:T(8,128)(2,1)S(1)}, bf16[1,128,3,256]{3,1,2,0:T(8,128)(2,1)S(1)}, u32[]{:S(2)}, u32[]{:S(2)}) collective-permute-start(bf16[1,128,3,256]{3,1,2,0:T(8,128)(2,1)S(1)} %pad_maximum_fusion.8), channel_id=1, source_target_pairs={{1,0},{2,1},{3,2},{4,3},{5,4},{6,5},{7,6},{9,8},{10,9},{11,10},{12... | collective-permute-start | bytes 589832 | tf_op jit(solution)/shard_map/ppermute | solution.py:22
  25.1 0.2 bitcast_reduce_fusion
  25.3 0.7 %fusion.8 = f32[16,384]{1,0:T(8,128)S(1)} fusion(f32[16,1024]{1,0:T(8,128)S(1)} %bitcast_reduce_fusion, f32[128,512]{1,0:T(8,128)S(1)} %get-tuple-element.31, f32[128,512]{1,0:T(8,128)S(1)} %get-tuple-element.32, f32[128,512]{1,0:T(8,128)S(1)} %get-tuple-element.29, f32[128,512]{1,0:T(8,128)S(1)} %get-tuple-element.30, ...), kind=kOutput, calls=%fused_computation.9 | convolution fusion | flops 40108032 | bytes 1667072 | tf_op jit(solution)/shard_map/rf,tf->rt/dot_general | solution.py:123
  26.0 4.8 %collective-permute-start.5 = (f32[16,128]{1,0:T(8,128)S(1)}, f32[16,128]{1,0:T(8,128)S(1)}, u32[]{:S(2)}, u32[]{:S(2)}) collective-permute-start(f32[16,128]{1,0:T(8,128)S(1)} %get-tuple-element.48), channel_id=1, source_target_pairs={{0,8},{8,16},{16,24},{24,0},{1,9},{9,17},{17,25},{25,1},{2,10},{10... | collective-permute-start | bytes 24584 | tf_op jit(solution)/shard_map/ppermute | solution.py:127
  30.8 2.0 %collective-permute-start.6 = (f32[16,128]{1,0:T(8,128)S(1)}, f32[16,128]{1,0:T(8,128)S(1)}, u32[]{:S(2)}, u32[]{:S(2)}) collective-permute-start(f32[16,128]{1,0:T(8,128)S(1)} %get-tuple-element.50), channel_id=1, source_target_pairs={{0,16},{8,24},{16,0},{24,8},{1,17},{9,25},{17,1},{25,9},{2,18},{10... | collective-permute-start | bytes 24584 | tf_op jit(solution)/shard_map/ppermute | solution.py:127
  32.8 2.9 %collective-permute-start.7 = (f32[16,128]{1,0:T(8,128)S(1)}, f32[16,128]{1,0:T(8,128)S(1)}, u32[]{:S(2)}, u32[]{:S(2)}) collective-permute-start(f32[16,128]{1,0:T(8,128)S(1)} %get-tuple-element.49), channel_id=1, source_target_pairs={{0,24},{8,0},{16,8},{24,16},{1,25},{9,1},{17,9},{25,17},{2,26},{10... | collective-permute-start | bytes 24584 | tf_op jit(solution)/shard_map/ppermute | solution.py:127
  35.7 1.9 %collective-permute-start.3 = (bf16[1,128,256]{2,1,0:T(8,128)(2,1)S(1)}, bf16[1,128,256]{2,1,0:T(8,128)(2,1)S(1)}, u32[]{:S(2)}, u32[]{:S(2)}) collective-permute-start(bf16[1,128,256]{2,1,0:T(8,128)(2,1)S(1)} %get-tuple-element.42), channel_id=1, source_target_pairs={{0,1},{1,2},{2,3},{3,4},{4,5},{5,6},{6,7},{8,9},{9,10},{10,11},{11... | collective-permute-start | bytes 196616 | tf_op jit(solution)/shard_map/ppermute | solution.py:22
  37.6 0.0 collective-permute-done.5
  37.6 0.0 collective-permute-done.6
  37.6 0.0 collective-permute-done.7
  37.6 0.9 %fusion.23 = f32[1,16,128]{2,1,0:T(8,128)} fusion(f32[16,128]{1,0:T(8,128)S(1)} %collective-permute-done.7, f32[16,128]{1,0:T(8,128)S(1)} %collective-permute-done.6, f32[16,128]{1,0:T(8,128)S(1)} %collective-permute-done.5, f32[16,1024]{1,0:T(8,128)S(1)} %bitcast_reduce_fusion, f32[128,512]{1,0:T(8,128)S(1)} %get-tuple-element.26, ...), kind=kOutput, calls=%fused_computation.26 | convolution fusion | flops 12853248 | bytes 626688 | tf_op jit(solution)/shard_map/rf,tf->rt/dot_general | solution.py:119
  38.6 3.6 %collective-permute-done.3 = bf16[1,128,256]{2,1,0:T(8,128)(2,1)S(1)} collective-permute-done((bf16[1,128,256]{2,1,0:T(8,128)(2,1)S(1)}, bf16[1,128,256]{2,1,0:T(8,128)(2,1)S(1)}, u32[]{:S(2)}, u32[]{:S(2)}) %collective-permute-start.3) | collective-permute-done | bytes 65568 | tf_op jit(solution)/shard_map/ppermute | solution.py:22
  42.2 0.0 collective-permute-done.4
  42.2 0.6 %copy.15 = bf16[1,128,256]{2,1,0:T(8,128)(2,1)} copy(bf16[1,128,256]{2,1,0:T(8,128)(2,1)S(1)} %collective-permute-done.3) | data formatting | bytes 131072
  42.8 0.7 %copy.16 = bf16[1,128,3,256]{3,1,2,0:T(8,128)(2,1)} copy(bf16[1,128,3,256]{3,1,2,0:T(8,128)(2,1)S(1)} %collective-permute-done.4) | data formatting | bytes 393216
  (12 shorter events, 0.2 us)
Async XLA Ops:
  0.6 6.9 %copy-start.6 = (f32[4,512]{1,0:T(4,128)S(1)}, f32[4,512]{1,0:T(4,128)}, u32[]{:S(2)}) copy-start(f32[4,512]{1,0:T(4,128)} %constant.139.clone) | copy-start | bytes 24580
  0.6 6.9 %copy-start.7 = (f32[4,512]{1,0:T(4,128)S(1)}, f32[4,512]{1,0:T(4,128)}, u32[]{:S(2)}) copy-start(f32[4,512]{1,0:T(4,128)} %constant.140.clone) | copy-start | bytes 24580
  0.7 6.9 %copy-start = (f32[128,512]{1,0:T(8,128)S(1)}, f32[128,512]{1,0:T(8,128)}, u32[]{:S(2)}) copy-start(f32[128,512]{1,0:T(8,128)} %constant.137.clone) | copy-start | bytes 786436
  0.7 6.9 %copy-start.1 = (f32[128,512]{1,0:T(8,128)S(1)}, f32[128,512]{1,0:T(8,128)}, u32[]{:S(2)}) copy-start(f32[128,512]{1,0:T(8,128)} %constant.138.clone) | copy-start | bytes 786436
  0.7 6.7 %copy-start.2 = (bf16[1,128,3,256]{3,1,2,0:T(8,128)(2,1)S(1)}, bf16[1,128,3,256]{3,1,2,0:T(8,128)(2,1)}, u32[]{:S(2)}) copy-start(bf16[1,128,3,256]{3,1,2,0:T(8,128)(2,1)} %param.10) | copy-start | bytes 589828
  0.7 6.7 %copy-start.3 = (bf16[1,128,256]{2,1,0:T(8,128)(2,1)S(1)}, bf16[1,128,256]{2,1,0:T(8,128)(2,1)}, u32[]{:S(2)}) copy-start(bf16[1,128,256]{2,1,0:T(8,128)(2,1)} %param.12) | copy-start | bytes 196612
  0.7 6.7 %copy-start.4 = (bf16[1,128,3,256]{3,1,2,0:T(8,128)(2,1)S(1)}, bf16[1,128,3,256]{3,1,2,0:T(8,128)(2,1)}, u32[]{:S(2)}) copy-start(bf16[1,128,3,256]{3,1,2,0:T(8,128)(2,1)} %param.9) | copy-start | bytes 589828
  0.7 6.7 %copy-start.5 = (f32[1,128,256]{2,1,0:T(8,128)S(1)}, f32[1,128,256]{2,1,0:T(8,128)}, u32[]{:S(2)}) copy-start(f32[1,128,256]{2,1,0:T(8,128)} %param.11) | copy-start | bytes 393220
  2.7 14.1 %collective-permute-start.1 = (f32[272,128]{0,1:T(8,128)S(1)}, f32[272,128]{0,1:T(8,128)S(1)}, u32[]{:S(2)}, u32[]{:S(2)}) collective-permute-start(f32[272,128]{0,1:T(8,128)S(1)} %get-tuple-element.46), channel_id=1, source_target_pairs={{0,16},{8,24},{16,0},{24,8},{1,17},{9,25},{17,1},{25,9},{2,18},{10... | collective-permute-start | bytes 417800 | tf_op jit(solution)/shard_map/ppermute | solution.py:100
  5.3 12.1 %collective-permute-start.2 = (f32[272,128]{0,1:T(8,128)S(1)}, f32[272,128]{0,1:T(8,128)S(1)}, u32[]{:S(2)}, u32[]{:S(2)}) collective-permute-start(f32[272,128]{0,1:T(8,128)S(1)} %get-tuple-element.47), channel_id=1, source_target_pairs={{0,24},{8,0},{16,8},{24,16},{1,25},{9,1},{17,9},{25,17},{2,26},{10... | collective-permute-start | bytes 417800 | tf_op jit(solution)/shard_map/ppermute | solution.py:100
  6.7 13.2 %collective-permute-start = (f32[272,128]{0,1:T(8,128)S(1)}, f32[272,128]{0,1:T(8,128)S(1)}, u32[]{:S(2)}, u32[]{:S(2)}) collective-permute-start(f32[272,128]{0,1:T(8,128)S(1)} %get-tuple-element.45), channel_id=1, source_target_pairs={{0,8},{8,16},{16,24},{24,0},{1,9},{9,17},{17,25},{25,1},{2,10},{10... | collective-permute-start | bytes 417800 | tf_op jit(solution)/shard_map/ppermute | solution.py:100
  23.2 19.0 %collective-permute-start.4 = (bf16[1,128,3,256]{3,1,2,0:T(8,128)(2,1)S(1)}, bf16[1,128,3,256]{3,1,2,0:T(8,128)(2,1)S(1)}, u32[]{:S(2)}, u32[]{:S(2)}) collective-permute-start(bf16[1,128,3,256]{3,1,2,0:T(8,128)(2,1)S(1)} %pad_maximum_fusion.8), channel_id=1, source_target_pairs={{1,0},{2,1},{3,2},{4,3},{5,4},{6,5},{7,6},{9,8},{10,9},{11,10},{12... | collective-permute-start | bytes 589832 | tf_op jit(solution)/shard_map/ppermute | solution.py:22
  26.0 11.6 %collective-permute-start.5 = (f32[16,128]{1,0:T(8,128)S(1)}, f32[16,128]{1,0:T(8,128)S(1)}, u32[]{:S(2)}, u32[]{:S(2)}) collective-permute-start(f32[16,128]{1,0:T(8,128)S(1)} %get-tuple-element.48), channel_id=1, source_target_pairs={{0,8},{8,16},{16,24},{24,0},{1,9},{9,17},{17,25},{25,1},{2,10},{10... | collective-permute-start | bytes 24584 | tf_op jit(solution)/shard_map/ppermute | solution.py:127
  30.8 6.8 %collective-permute-start.6 = (f32[16,128]{1,0:T(8,128)S(1)}, f32[16,128]{1,0:T(8,128)S(1)}, u32[]{:S(2)}, u32[]{:S(2)}) collective-permute-start(f32[16,128]{1,0:T(8,128)S(1)} %get-tuple-element.50), channel_id=1, source_target_pairs={{0,16},{8,24},{16,0},{24,8},{1,17},{9,25},{17,1},{25,9},{2,18},{10... | collective-permute-start | bytes 24584 | tf_op jit(solution)/shard_map/ppermute | solution.py:127
  32.8 4.8 %collective-permute-start.7 = (f32[16,128]{1,0:T(8,128)S(1)}, f32[16,128]{1,0:T(8,128)S(1)}, u32[]{:S(2)}, u32[]{:S(2)}) collective-permute-start(f32[16,128]{1,0:T(8,128)S(1)} %get-tuple-element.49), channel_id=1, source_target_pairs={{0,24},{8,0},{16,8},{24,16},{1,25},{9,1},{17,9},{25,17},{2,26},{10... | collective-permute-start | bytes 24584 | tf_op jit(solution)/shard_map/ppermute | solution.py:127
  35.7 6.5 %collective-permute-start.3 = (bf16[1,128,256]{2,1,0:T(8,128)(2,1)S(1)}, bf16[1,128,256]{2,1,0:T(8,128)(2,1)S(1)}, u32[]{:S(2)}, u32[]{:S(2)}) collective-permute-start(bf16[1,128,256]{2,1,0:T(8,128)(2,1)S(1)} %get-tuple-element.42), channel_id=1, source_target_pairs={{0,1},{1,2},{2,3},{3,4},{4,5},{5,6},{6,7},{8,9},{9,10},{10,11},{11... | collective-permute-start | bytes 196616 | tf_op jit(solution)/shard_map/ppermute | solution.py:22

commit v18 on v14

--- a/solution.py
+++ b/solution.py
@@ -92,13 +92,16 @@
     size = 2 * blocks * block
     half = size // 2
     packed = packed_tables(blocks, block)
+    swap = blocks & (blocks - 1) == 0
+    dest = (lambda i, s: i ^ s) if swap else (lambda i, s: (i + s) % blocks)
+    source = (lambda i, s: i ^ s) if swap else (lambda i, s: (i - s) % blocks)
     acc = 0.0
     for s in range(1, blocks):
-        first = jnp.where(place + s < blocks, mixed_rows, weighted_rows)
+        first = jnp.where(dest(place, s) > place, mixed_rows, weighted_rows)
         payload = jnp.concatenate([first, taps], axis=0)
-        pairs = [(i, (i + s) % blocks) for i in range(blocks)]
+        pairs = [(i, dest(i, s)) for i in range(blocks)]
         got = lax.ppermute(payload, "ctx", pairs)
-        table = block_table(packed, (place - s) % blocks)
+        table = block_table(packed, source(place, s))
         acc = acc + jnp.dot(got, table, precision=precise)
     own_table = block_table(packed, place)
     own = jnp.concatenate([mixed_rows, weighted_rows, back_rows, taps], axis=0)
@@ -118,9 +121,9 @@
     out = jnp.einsum("tf,rf->tr", own_table * weight, both, precision=precise)
     lag = jnp.einsum("rf,tf->rt", fgs, own_table * weight, precision=precise)
     for s in range(1, blocks):
-        table = block_table(packed, (place + s) % blocks) * weight
+        table = block_table(packed, dest(place, s)) * weight
         share = jnp.einsum("rf,tf->rt", fgs, table, precision=precise)
-        pairs = [(i, (i + s) % blocks) for i in range(blocks) if i + (i + s) % blocks < blocks]
+        pairs = [(i, dest(i, s)) for i in range(blocks)]
         lag = lag + lax.ppermute(share, "ctx", pairs)
     return out[:, :c], out[:, c:], lag
 

time: 46.5 us -> 43.2 us (0.929); the launches traced: 45.7 us -> 43 us
  starting transfers between devices: 20.1 us -> 15.6 us
  waiting for transfers between devices: 11.5 us -> 13.6 us
    ppermute x3, starting transfers between devices: 10.8 us -> 7.53 us  [dense_path(): lag = lag + lax.ppermute(share, 'ctx', pairs)]
    ppermute x3, waiting for transfers between devices: 7.94 us -> 9.97 us  [dense_path(): got = lax.ppermute(payload, 'ctx', pairs)]
    ppermute x2, starting transfers between devices: 4.61 us -> 3.83 us  [from_behind(): return lax.ppermute(x, axis, pairs)]
  transfers between devices with their start and end apart: 8 -> 8, of which waited for: 4 -> 3; matrix products, arithmetic and copies ran while one was open for 16% -> 13% of each run, Pallas kernels for 0% -> 0%
where the time goes in v18:
time: 43.2 us; the launch traced here: 43 us
  starting transfers between devices  15.6 us (36%)
  waiting for transfers between devices  13.6 us (31%)
  matrix products  6.64 us (15%)
  other arithmetic  3.77 us (9%)
  local copies, waits for them, and re-layouts  2.42 us (6%)
  between operations  0.99 us (2%)
    ppermute x3, waiting for transfers between devices, dense_path(): got = lax.ppermute(payload, 'ctx', pairs)  9.97 us
    ppermute x3, starting transfers between devices, dense_path(): lag = lag + lax.ppermute(share, 'ctx', pairs)  7.53 us
    ppermute x3, starting transfers between devices, dense_path(): got = lax.ppermute(payload, 'ctx', pairs)  4.23 us
    ppermute x2, starting transfers between devices, from_behind(): return lax.ppermute(x, axis, pairs)  3.83 us
    unnamed x19, local copies, waits for them, and re-layouts  2.28 us
    ppermute x3, waiting for transfers between devices, dense_path(): lag = lag + lax.ppermute(share, 'ctx', pairs)  2.11 us
    dot_general x3, matrix products, dense_path(): acc = acc + jnp.dot(got, table, precision=precise)  2.02 us
    ppermute x2, waiting for transfers between devices, from_behind(): return lax.ppermute(x, axis, pairs)  1.5 us
  transfers between devices with their start and end apart: 8, of which 3 were waited for; matrix products, arithmetic and copies ran while one was open for 13% of the time, Pallas kernels for 0%

profile of v18, /device:TPU:4, one launch (start us, length us, event | category | flops | bytes accessed | tf_op | source)
XLA Modules:
  0.0 43.0 jit_solution(12180604708665301356)
XLA Ops:
  0.6 0.0 copy-start.6
  0.6 0.0 copy-start.7
  0.7 0.0 copy-start.3
  0.7 0.0 copy-start.4
  0.7 0.0 copy-start.1
  0.7 0.0 copy-start.2
  0.7 0.0 copy-start.5
  0.7 0.9 %copy.12 = f32[1,16,128]{1,2,0:T(8,128)S(1)} copy(f32[1,16,128]{2,1,0:T(8,128)} %param.13) | data formatting | bytes 16384 | tf_op args[4]
  1.7 1.0 %broadcast_select_fusion.2 = (f32[256,128]{0,1:T(8,128)S(1)}, f32[256,128]{0,1:T(8,128)S(1)}, f32[256,128]{0,1:T(8,128)S(1)}) fusion(pred[]{:T(512)S(6)} %gt.9, bf16[1,128,3,256]{3,1,2,0:T(8,128)(2,1)} %param.10, bf16[1,128,256]{2,1,0:T(8,128)(2,1)} %param.12, bf16[1,128,3,256]{3,1,2,0:T(8,128)(2,1)} %param.9, pred[]{:T(512)S(6)} %gt.10, pred[]{:T(512)S(6)} %gt.11), kind=kLoop, calls=%fused_computation.91 | loop fusion | flops 294912 | bytes 655363 | tf_op jit(solution)/shard_map/jit(_where)/select_n | solution.py:100
  2.7 2.7 %collective-permute-start.1 = (f32[272,128]{0,1:T(8,128)S(1)}, f32[272,128]{0,1:T(8,128)S(1)}, u32[]{:S(2)}, u32[]{:S(2)}) collective-permute-start(f32[272,128]{0,1:T(8,128)S(1)} %get-tuple-element.36), channel_id=1, source_target_pairs={{0,16},{8,24},{16,0},{24,8},{1,17},{9,25},{17,1},{25,9},{2,18},{10... | collective-permute-start | bytes 417800 | tf_op jit(solution)/shard_map/ppermute | solution.py:103
  5.3 1.3 %collective-permute-start.2 = (f32[272,128]{0,1:T(8,128)S(1)}, f32[272,128]{0,1:T(8,128)S(1)}, u32[]{:S(2)}, u32[]{:S(2)}) collective-permute-start(f32[272,128]{0,1:T(8,128)S(1)} %get-tuple-element.37), channel_id=1, source_target_pairs={{0,24},{8,16},{16,8},{24,0},{1,25},{9,17},{17,9},{25,1},{2,26},{10... | collective-permute-start | bytes 417800 | tf_op jit(solution)/shard_map/ppermute | solution.py:103
  6.7 0.2 collective-permute-start
  6.9 1.0 %fusion.37 = (f32[256,128]{0,1:T(8,128)S(1)}, f32[256,128]{0,1:T(8,128)S(1)}) fusion(bf16[1,128,256]{2,1,0:T(8,128)(2,1)} %param.12, bf16[1,128,3,256]{3,1,2,0:T(8,128)(2,1)} %param.10), kind=kLoop, calls=%fused_computation.74 | loop fusion | flops 196608 | bytes 524288 | tf_op jit(solution)/shard_map/transpose | solution.py:196
  7.9 0.0 copy-done.2
  7.9 0.0 copy-done.1
  8.0 0.0 copy-done.5
  8.0 0.0 copy-done.6
  8.0 0.0 copy-done.7
  8.1 0.0 copy-done.3
  8.1 0.0 copy-done.4
  8.1 0.3 multiply_subtract_fusion.6
  8.4 1.5 %fusion.21 = f32[784,1024]{1,0:T(8,128)S(1)} fusion(f32[16,128]{0,1:T(8,128)S(1)} %bitcast.84, f32[256,128]{0,1:T(8,128)S(1)} %get-tuple-element.34, f32[256,128]{0,1:T(8,128)S(1)} %get-tuple-element.33, f32[256,128]{0,1:T(8,128)S(1)} %multiply_bitcast_fusion, f32[128,512]{1,0:T(8,128)S(1)} %get-tuple-element.20, f32[128,512]{1,0:T(8,128)S(1)} %get-tuple-element.19), kind=kOutput, calls=%fused_computation.39 | convolution fusion | flops 616994816 | bytes 4136960 | tf_op jit(solution)/shard_map/dot_general | solution.py:108
  9.9 10.0 %collective-permute-done.1 = f32[272,128]{0,1:T(8,128)S(1)} collective-permute-done((f32[272,128]{0,1:T(8,128)S(1)}, f32[272,128]{0,1:T(8,128)S(1)}, u32[]{:S(2)}, u32[]{:S(2)}) %collective-permute-start.1) | collective-permute-done | bytes 139296 | tf_op jit(solution)/shard_map/ppermute | solution.py:103
  19.9 0.6 %fusion.30 = f32[272,1024]{1,0:T(8,128)S(1)} fusion(f32[272,128]{0,1:T(8,128)S(1)} %collective-permute-done.1, f32[128,512]{1,0:T(8,128)S(1)} %get-tuple-element.23, f32[128,512]{1,0:T(8,128)S(1)} %get-tuple-element.24), kind=kOutput, calls=%fused_computation.48 | convolution fusion | flops 214040576 | bytes 1777664 | tf_op jit(solution)/shard_map/dot_general | solution.py:105
  20.5 0.0 collective-permute-done.2
  20.6 0.7 %fusion.29 = f32[272,1024]{1,0:T(8,128)S(1)} fusion(f32[272,128]{0,1:T(8,128)S(1)} %collective-permute-done.2, f32[128,512]{1,0:T(8,128)S(1)} %get-tuple-element.25, f32[128,512]{1,0:T(8,128)S(1)} %get-tuple-element.26), kind=kOutput, calls=%fused_computation.47 | convolution fusion | flops 214040576 | bytes 1777664 | tf_op jit(solution)/shard_map/dot_general | solution.py:105
  21.2 0.0 collective-permute-done
  21.2 0.7 %fusion.8 = f32[272,1024]{1,0:T(8,128)S(1)} fusion(f32[272,1024]{1,0:T(8,128)S(1)} %fusion.29, f32[272,1024]{1,0:T(8,128)S(1)} %fusion.30, f32[272,128]{0,1:T(8,128)S(1)} %collective-permute-done, f32[128,512]{1,0:T(8,128)S(1)} %get-tuple-element.21, f32[128,512]{1,0:T(8,128)S(1)} %get-tuple-element.22), kind=kOutput, calls=%fused_computation.9 | convolution fusion | flops 214597632 | bytes 4005888 | tf_op jit(solution)/shard_map/dot_general | solution.py:105
  22.0 0.4 slice_add_fusion.1
  22.4 0.1 broadcast_in_dim.26
  22.5 0.4 %multiply_subtract_fusion = (f32[256,512]{1,0:T(8,128)S(1)}, f32[256,512]{1,0:T(8,128)S(1)}, f32[256,512]{1,0:T(8,128)S(1)}, f32[256,512]{1,0:T(8,128)S(1)}) fusion(f32[784,1024]{1,0:T(8,128)S(1)} %fusion.21, f32[256,1024]{1,0:T(8,128)S(1)} %get-tuple-element.4, pred[512]{0:T(512)(128)(4,1)S(1)} %iota_compare_fusion.2, f32[256,1024]{1,0:T(8,128)S(1)} %bitcast.81), kind=kLoop, calls=%fused_computation.30 | loop fusion | flops 2621440 | bytes 5243392 | tf_op jit(solution)/shard_map/sub | solution.py:85
  23.0 0.2 bitcast_reduce_fusion
  23.2 0.3 fusion.17
  23.5 0.3 fusion.15
  23.8 0.3 select_subtract_fusion
  24.1 0.0 copy-start
  24.1 1.2 %fusion = f32[128,512]{1,0:T(8,128)S(1)} fusion(f32[256,512]{1,0:T(8,128)S(1)} %get-tuple-element.11, f32[256,512]{1,0:T(8,128)S(1)} %get-tuple-element.12, f32[256,512]{1,0:T(8,128)S(1)} %get-tuple-element.8, f32[256,512]{1,0:T(8,128)S(1)} %get-tuple-element.7, f32[128,512]{1,0:T(8,128)S(1)} %get-tuple-element.20, f32[128,512]{1,0:T(8,128)S(1)} %get-tuple-element.19, ...), kind=kOutput, calls=%fused_computation | convolution fusion | flops 404488192 | bytes 2887680 | tf_op jit(solution)/shard_map/tf,rf->tr/dot_general | solution.py:121
  25.3 0.0 copy-done
  25.3 0.1 fusion.46
  25.4 1.9 %collective-permute-start.4 = (bf16[1,128,3,256]{3,1,2,0:T(8,128)(2,1)S(1)}, bf16[1,128,3,256]{3,1,2,0:T(8,128)(2,1)S(1)}, u32[]{:S(2)}, u32[]{:S(2)}) collective-permute-start(bf16[1,128,3,256]{3,1,2,0:T(8,128)(2,1)S(1)} %pad_maximum_fusion.17), channel_id=1, source_target_pairs={{1,0},{2,1},{3,2},{4,3},{5,4},{6,5},{7,6},{9,8},{10,9},{11,10},{12... | collective-permute-start | bytes 589832 | tf_op jit(solution)/shard_map/ppermute | solution.py:22
  27.3 0.3 fusion.13
  27.7 4.2 %collective-permute-start.5 = (f32[16,128]{1,0:T(8,128)S(1)}, f32[16,128]{1,0:T(8,128)S(1)}, u32[]{:S(2)}, u32[]{:S(2)}) collective-permute-start(f32[16,128]{1,0:T(8,128)S(1)} %fusion.17), channel_id=1, source_target_pairs={{0,8},{8,0},{16,24},{24,16},{1,9},{9,1},{17,25},{25,17},{2,10},{10... | collective-permute-start | bytes 24584 | tf_op jit(solution)/shard_map/ppermute | solution.py:127
  31.8 2.0 %collective-permute-start.6 = (f32[16,128]{1,0:T(8,128)S(1)}, f32[16,128]{1,0:T(8,128)S(1)}, u32[]{:S(2)}, u32[]{:S(2)}) collective-permute-start(f32[16,128]{1,0:T(8,128)S(1)} %fusion.15), channel_id=1, source_target_pairs={{0,16},{8,24},{16,0},{24,8},{1,17},{9,25},{17,1},{25,9},{2,18},{10... | collective-permute-start | bytes 24584 | tf_op jit(solution)/shard_map/ppermute | solution.py:127
  33.8 1.4 %collective-permute-start.7 = (f32[16,128]{1,0:T(8,128)S(1)}, f32[16,128]{1,0:T(8,128)S(1)}, u32[]{:S(2)}, u32[]{:S(2)}) collective-permute-start(f32[16,128]{1,0:T(8,128)S(1)} %fusion.13), channel_id=1, source_target_pairs={{0,24},{8,16},{16,8},{24,0},{1,25},{9,17},{17,9},{25,1},{2,26},{10... | collective-permute-start | bytes 24584 | tf_op jit(solution)/shard_map/ppermute | solution.py:127
  35.2 1.9 %collective-permute-start.3 = (bf16[1,128,256]{2,1,0:T(8,128)(2,1)S(1)}, bf16[1,128,256]{2,1,0:T(8,128)(2,1)S(1)}, u32[]{:S(2)}, u32[]{:S(2)}) collective-permute-start(bf16[1,128,256]{2,1,0:T(8,128)(2,1)S(1)} %get-tuple-element.32), channel_id=1, source_target_pairs={{0,1},{1,2},{2,3},{3,4},{4,5},{5,6},{6,7},{8,9},{9,10},{10,11},{11... | collective-permute-start | bytes 196616 | tf_op jit(solution)/shard_map/ppermute | solution.py:22
  37.1 0.0 collective-permute-done.5
  37.1 0.0 collective-permute-done.6
  37.1 2.1 %collective-permute-done.7 = f32[16,128]{1,0:T(8,128)S(1)} collective-permute-done((f32[16,128]{1,0:T(8,128)S(1)}, f32[16,128]{1,0:T(8,128)S(1)}, u32[]{:S(2)}, u32[]{:S(2)}) %collective-permute-start.7) | collective-permute-done | bytes 8224 | tf_op jit(solution)/shard_map/ppermute | solution.py:127
  39.2 0.9 %fusion.12 = f32[1,16,128]{2,1,0:T(8,128)} fusion(f32[16,128]{1,0:T(8,128)S(1)} %collective-permute-done.7, f32[16,128]{1,0:T(8,128)S(1)} %collective-permute-done.6, f32[16,128]{1,0:T(8,128)S(1)} %collective-permute-done.5, f32[16,1024]{1,0:T(8,128)S(1)} %bitcast_reduce_fusion, f32[128,512]{1,0:T(8,128)S(1)} %get-tuple-element.20, ...), kind=kOutput, calls=%fused_computation.14 | convolution fusion | flops 12853248 | bytes 626688 | tf_op jit(solution)/shard_map/rf,tf->rt/dot_general | solution.py:122
  40.2 1.5 %collective-permute-done.3 = bf16[1,128,256]{2,1,0:T(8,128)(2,1)S(1)} collective-permute-done((bf16[1,128,256]{2,1,0:T(8,128)(2,1)S(1)}, bf16[1,128,256]{2,1,0:T(8,128)(2,1)S(1)}, u32[]{:S(2)}, u32[]{:S(2)}) %collective-permute-start.3) | collective-permute-done | bytes 65568 | tf_op jit(solution)/shard_map/ppermute | solution.py:22
  41.7 0.0 collective-permute-done.4
  41.7 0.6 %copy.15 = bf16[1,128,256]{2,1,0:T(8,128)(2,1)} copy(bf16[1,128,256]{2,1,0:T(8,128)(2,1)S(1)} %collective-permute-done.3) | data formatting | bytes 131072
  42.3 0.7 %copy.16 = bf16[1,128,3,256]{3,1,2,0:T(8,128)(2,1)} copy(bf16[1,128,3,256]{3,1,2,0:T(8,128)(2,1)S(1)} %collective-permute-done.4) | data formatting | bytes 393216
  (10 shorter events, 0.2 us)
Async XLA Ops:
  0.6 7.4 %copy-start.6 = (f32[4,512]{1,0:T(4,128)S(1)}, f32[4,512]{1,0:T(4,128)}, u32[]{:S(2)}) copy-start(f32[4,512]{1,0:T(4,128)} %constant.103.clone) | copy-start | bytes 24580
  0.6 7.4 %copy-start.7 = (f32[4,512]{1,0:T(4,128)S(1)}, f32[4,512]{1,0:T(4,128)}, u32[]{:S(2)}) copy-start(f32[4,512]{1,0:T(4,128)} %constant.104.clone) | copy-start | bytes 24580
  0.7 7.4 %copy-start.3 = (f32[128,512]{1,0:T(8,128)S(1)}, f32[128,512]{1,0:T(8,128)}, u32[]{:S(2)}) copy-start(f32[128,512]{1,0:T(8,128)} %constant.101.clone) | copy-start | bytes 786436
  0.7 7.4 %copy-start.4 = (f32[128,512]{1,0:T(8,128)S(1)}, f32[128,512]{1,0:T(8,128)}, u32[]{:S(2)}) copy-start(f32[128,512]{1,0:T(8,128)} %constant.102.clone) | copy-start | bytes 786436
  0.7 7.3 %copy-start.1 = (bf16[1,128,256]{2,1,0:T(8,128)(2,1)S(1)}, bf16[1,128,256]{2,1,0:T(8,128)(2,1)}, u32[]{:S(2)}) copy-start(bf16[1,128,256]{2,1,0:T(8,128)(2,1)} %param.12) | copy-start | bytes 196612
  0.7 7.2 %copy-start.2 = (bf16[1,128,3,256]{3,1,2,0:T(8,128)(2,1)S(1)}, bf16[1,128,3,256]{3,1,2,0:T(8,128)(2,1)}, u32[]{:S(2)}) copy-start(bf16[1,128,3,256]{3,1,2,0:T(8,128)(2,1)} %param.9) | copy-start | bytes 589828
  0.7 7.2 %copy-start.5 = (f32[1,128,256]{2,1,0:T(8,128)S(1)}, f32[1,128,256]{2,1,0:T(8,128)}, u32[]{:S(2)}) copy-start(f32[1,128,256]{2,1,0:T(8,128)} %param.11) | copy-start | bytes 393220
  2.7 17.2 %collective-permute-start.1 = (f32[272,128]{0,1:T(8,128)S(1)}, f32[272,128]{0,1:T(8,128)S(1)}, u32[]{:S(2)}, u32[]{:S(2)}) collective-permute-start(f32[272,128]{0,1:T(8,128)S(1)} %get-tuple-element.36), channel_id=1, source_target_pairs={{0,16},{8,24},{16,0},{24,8},{1,17},{9,25},{17,1},{25,9},{2,18},{10... | collective-permute-start | bytes 417800 | tf_op jit(solution)/shard_map/ppermute | solution.py:103
  5.3 15.2 %collective-permute-start.2 = (f32[272,128]{0,1:T(8,128)S(1)}, f32[272,128]{0,1:T(8,128)S(1)}, u32[]{:S(2)}, u32[]{:S(2)}) collective-permute-start(f32[272,128]{0,1:T(8,128)S(1)} %get-tuple-element.37), channel_id=1, source_target_pairs={{0,24},{8,16},{16,8},{24,0},{1,25},{9,17},{17,9},{25,1},{2,26},{10... | collective-permute-start | bytes 417800 | tf_op jit(solution)/shard_map/ppermute | solution.py:103
  6.7 14.5 %collective-permute-start = (f32[272,128]{0,1:T(8,128)S(1)}, f32[272,128]{0,1:T(8,128)S(1)}, u32[]{:S(2)}, u32[]{:S(2)}) collective-permute-start(f32[272,128]{0,1:T(8,128)S(1)} %get-tuple-element.35), channel_id=1, source_target_pairs={{0,8},{8,0},{16,24},{24,16},{1,9},{9,1},{17,25},{25,17},{2,10},{10... | collective-permute-start | bytes 417800 | tf_op jit(solution)/shard_map/ppermute | solution.py:103
  24.1 1.2 %copy-start = (bf16[1,128,3,256]{3,1,2,0:T(8,128)(2,1)S(1)}, bf16[1,128,3,256]{3,1,2,0:T(8,128)(2,1)}, u32[]{:S(2)}) copy-start(bf16[1,128,3,256]{3,1,2,0:T(8,128)(2,1)} %param.10) | copy-start | bytes 589828
  25.4 16.3 %collective-permute-start.4 = (bf16[1,128,3,256]{3,1,2,0:T(8,128)(2,1)S(1)}, bf16[1,128,3,256]{3,1,2,0:T(8,128)(2,1)S(1)}, u32[]{:S(2)}, u32[]{:S(2)}) collective-permute-start(bf16[1,128,3,256]{3,1,2,0:T(8,128)(2,1)S(1)} %pad_maximum_fusion.17), channel_id=1, source_target_pairs={{1,0},{2,1},{3,2},{4,3},{5,4},{6,5},{7,6},{9,8},{10,9},{11,10},{12... | collective-permute-start | bytes 589832 | tf_op jit(solution)/shard_map/ppermute | solution.py:22
  27.7 9.5 %collective-permute-start.5 = (f32[16,128]{1,0:T(8,128)S(1)}, f32[16,128]{1,0:T(8,128)S(1)}, u32[]{:S(2)}, u32[]{:S(2)}) collective-permute-start(f32[16,128]{1,0:T(8,128)S(1)} %fusion.17), channel_id=1, source_target_pairs={{0,8},{8,0},{16,24},{24,16},{1,9},{9,1},{17,25},{25,17},{2,10},{10... | collective-permute-start | bytes 24584 | tf_op jit(solution)/shard_map/ppermute | solution.py:127
  31.8 5.3 %collective-permute-start.6 = (f32[16,128]{1,0:T(8,128)S(1)}, f32[16,128]{1,0:T(8,128)S(1)}, u32[]{:S(2)}, u32[]{:S(2)}) collective-permute-start(f32[16,128]{1,0:T(8,128)S(1)} %fusion.15), channel_id=1, source_target_pairs={{0,16},{8,24},{16,0},{24,8},{1,17},{9,25},{17,1},{25,9},{2,18},{10... | collective-permute-start | bytes 24584 | tf_op jit(solution)/shard_map/ppermute | solution.py:127
  33.8 5.4 %collective-permute-start.7 = (f32[16,128]{1,0:T(8,128)S(1)}, f32[16,128]{1,0:T(8,128)S(1)}, u32[]{:S(2)}, u32[]{:S(2)}) collective-permute-start(f32[16,128]{1,0:T(8,128)S(1)} %fusion.13), channel_id=1, source_target_pairs={{0,24},{8,16},{16,8},{24,0},{1,25},{9,17},{17,9},{25,1},{2,26},{10... | collective-permute-start | bytes 24584 | tf_op jit(solution)/shard_map/ppermute | solution.py:127
  35.2 6.5 %collective-permute-start.3 = (bf16[1,128,256]{2,1,0:T(8,128)(2,1)S(1)}, bf16[1,128,256]{2,1,0:T(8,128)(2,1)S(1)}, u32[]{:S(2)}, u32[]{:S(2)}) collective-permute-start(bf16[1,128,256]{2,1,0:T(8,128)(2,1)S(1)} %get-tuple-element.32), channel_id=1, source_target_pairs={{0,1},{1,2},{2,3},{3,4},{4,5},{5,6},{6,7},{8,9},{9,10},{10,11},{11... | collective-permute-start | bytes 196616 | tf_op jit(solution)/shard_map/ppermute | solution.py:22
